TPU v7x, 32 devices: a whole 2x2x4 slice. The times are simulated.
32 devices in a mesh: req: 16 (over z, y, x), head: 2 (over core).
Axes of the slice: x: 2, y: 2, z: 4, core: 2. Of those that a mesh axis runs over, the one named last changes fastest.
Arguments:
- hidden: bfloat16 [384, 1024], P('req', 'head'), may hold values from -6 to 6
- norm_gain: float32 [1024], replicated, may hold values from 0.1 to 1.9
- qkv_weight: bfloat16 [1024, 8, 3, 128], P(None, 'head'), may hold values from -0.1875 to 0.1875
- conv_weight: float32 [4, 8, 3, 128], P(None, 'head'), may hold values from -1.5 to 1.5
- conv_state: bfloat16 [384, 3, 8, 3, 128], P('req', None, 'head'), may hold values from -6 to 6
- gate_weight: bfloat16 [1024, 2, 8], P(None, None, 'head'), may hold values from -0.1875 to 0.1875
- prompt_weight: float32 [384, 8], P('req', 'head'), may hold values from 0.2 to 1
- ridge_term: float32 [8], P('head'), may hold values from 0.25 to 1
- own_keys: float32 [384, 8, 128, 128], P('req', 'head'), as said below
- own_values: float32 [384, 8, 128, 128], P('req', 'head')
- prompt_keys: float32 [32, 8, 128, 128], P('req', 'head'), as said below
- prompt_values: float32 [32, 8, 128, 128], P('req', 'head')
- group_ids: int32 [384], P('req'), may hold values from 0 to 31, as said below
- lengths: int32 [384], P('req'), may hold values from 0 to 32768, as said below
- out_weight: bfloat16 [8, 128, 1024], P('head'), may hold values from -0.1875 to 0.1875
Outputs:
- combined: bfloat16 [384, 1024], P('req', 'head')
Inputs may be any that keep to these rules, and one draw needn't show every extreme that they name: `group_ids`: group g's prompt states are row g of prompt_keys and prompt_values. Every group holds 8 to 16 request slots, some group exactly 8 and some exactly 16. The groups held by one index of req hold exactly 24 slots in all. The slots of one index of req form runs of 6 consecutive slots; the groups of one run are all held by one index of req, and different runs of one index by different indices. So at most 6 live requests of one index of req belong to groups held by one index of req, and some pair of indices reaches it. `lengths`: 0 marks an empty slot. At most half of the slots of one index of req are empty; some index has none empty and some exactly half. Some live requests hold 1 token and some 2. `own_keys`: each [128, 128] matrix is symmetric positive semidefinite. `prompt_keys`: each [128, 128] matrix is symmetric positive semidefinite.
All inputs are finite; a program needn't handle non-finite values.
Results may differ from a plain program's by a relative error of at most 0.008.
Values may be sent and summed in bfloat16 or wider, within the bound.
No kernel may reach another device: no remote copies, remote signals or barrier semaphores. Data moves between devices by JAX's collectives and lax.ppermute only.
A program may use at most 128 MiB of HBM per device.

v0:
```python
import jax
import jax.numpy as jnp
from jax import lax
from jax.sharding import PartitionSpec as P

KW = 4
ITERS = 8
CAP = 6


epsilon = 1e-06
highest = lax.Precision.HIGHEST


def own_matvec(matrices, vectors):
    return jnp.sum(matrices * vectors[:, :, None, :], axis=3)


def on_device(
    hidden,
    norm_gain,
    qkv_weight,
    conv_weight,
    conv_state,
    gate_weight,
    prompt_weight,
    ridge_term,
    own_keys,
    own_values,
    prompt_keys,
    prompt_values,
    group_ids,
    lengths,
    out_weight,
):
    gathered = lax.all_gather(hidden, "head", axis=1, tiled=True)
    widened = gathered.astype(jnp.float32)
    scaled = (
        widened
        * lax.rsqrt(jnp.mean(widened * widened, axis=1, keepdims=True) + epsilon)
        * norm_gain
    )
    normed = scaled.astype(jnp.bfloat16)
    row_count, model_width = gathered.shape
    head_count = qkv_weight.shape[1]
    head_size = qkv_weight.shape[3]
    projected = jnp.dot(
        normed,
        qkv_weight.reshape(model_width, head_count * 3 * head_size),
        preferred_element_type=jnp.float32,
    ).reshape(row_count, head_count, 3, head_size)
    mixing = conv_weight[0] * projected
    for offset in range(1, KW):
        usable = (lengths >= offset).astype(jnp.float32)[:, None, None, None]
        mixing = (
            mixing + conv_weight[offset] * conv_state[:, offset - 1].astype(jnp.float32) * usable
        )
    active = jax.nn.silu(mixing)
    queries = active[:, :, 0]
    queries = queries * lax.rsqrt(jnp.sum(queries * queries, axis=2, keepdims=True) + epsilon)
    key_now = active[:, :, 1]
    key_now = key_now * lax.rsqrt(jnp.sum(key_now * key_now, axis=2, keepdims=True) + epsilon)
    value_now = active[:, :, 2]
    gate_logit = jnp.dot(
        normed, gate_weight.reshape(model_width, 2 * head_count), preferred_element_type=jnp.float32
    ).reshape(row_count, 2, head_count)
    decay_col = jax.nn.sigmoid(gate_logit[:, 0])[:, :, None]
    write_col = jax.nn.sigmoid(gate_logit[:, 1])[:, :, None]
    weight_col = prompt_weight[:, :, None]
    ridge_col = ridge_term[None, :, None]

    peer_count = lax.axis_size("req")
    group_count = prompt_keys.shape[0]
    capacity = CAP
    slot_count = peer_count * capacity
    mask_of_live = lengths > 0
    owner_of = group_ids // group_count
    local_group = group_ids % group_count
    order_ids = jnp.arange(row_count)
    earlier = (
        (order_ids[None, :] < order_ids[:, None])
        & (owner_of[None, :] == owner_of[:, None])
        & mask_of_live[None, :]
    )
    rank_of = jnp.sum(earlier.astype(jnp.int32), axis=1)
    routed = mask_of_live & (rank_of < capacity)
    slot_of = jnp.where(routed, owner_of * capacity + rank_of, 0)
    hits = (slot_of[:, None] == jnp.arange(slot_count)[None, :]) & routed[:, None]
    filled = jnp.any(hits, axis=0)
    source = jnp.sum(jnp.where(hits, order_ids[:, None], 0), axis=0) + jnp.where(
        filled, 0, row_count
    )
    slot_label = jnp.sum(jnp.where(hits, (local_group + 1)[:, None], 0), axis=0)

    def pack(vectors):
        padded = jnp.concatenate(
            [vectors, jnp.zeros((1,) + vectors.shape[1:], vectors.dtype)], axis=0
        )
        return jnp.take(padded, source, axis=0)

    def exchange(slots):
        shaped = slots.reshape((peer_count, capacity) + slots.shape[1:])
        moved = lax.all_to_all(shaped, "req", split_axis=0, concat_axis=0, tiled=True)
        return moved.reshape(slots.shape)

    def unpack(slots):
        taken = jnp.take(slots, slot_of, axis=0)
        return jnp.where(routed[:, None, None], taken, 0.0)

    def owner_apply(states, incoming, chosen):
        products = jnp.einsum("shj,ghij->gshi", incoming, states, precision=highest)
        total = jnp.zeros_like(incoming)
        for group in range(group_count):
            total = total + jnp.where(chosen[group][:, None, None], products[group], 0.0)
        return total

    solution = jnp.zeros_like(queries)
    residual = queries
    direction = queries
    norm_now = jnp.sum(residual * residual, axis=2, keepdims=True)
    chosen = None
    for iteration in range(ITERS):
        outgoing = pack(direction)
        if iteration == 0:
            label_row = jnp.broadcast_to(
                slot_label.astype(jnp.float32)[:, None, None], (slot_count, 1, head_size)
            )
            arrived = exchange(jnp.concatenate([outgoing, label_row], axis=1))
            labels_in = arrived[:, head_count, 0]
            chosen = [labels_in == float(group + 1) for group in range(group_count)]
            arrived = arrived[:, :head_count]
        else:
            arrived = exchange(outgoing)
        shares = unpack(exchange(owner_apply(prompt_keys, arrived, chosen)))
        shared = weight_col * shares + own_matvec(own_keys, direction)
        product = (
            decay_col * shared
            + write_col * key_now * jnp.sum(key_now * direction, axis=2, keepdims=True)
            + ridge_col * direction
        )
        step_size = norm_now / jnp.sum(direction * product, axis=2, keepdims=True)
        solution = solution + step_size * direction
        residual = residual - step_size * product
        norm_next = jnp.sum(residual * residual, axis=2, keepdims=True)
        direction = residual + norm_next / norm_now * direction
        norm_now = norm_next
    value_sum = unpack(exchange(owner_apply(prompt_values, exchange(pack(solution)), chosen)))
    shared_out = weight_col * value_sum + own_matvec(own_values, solution)
    readout = decay_col * shared_out + write_col * value_now * jnp.sum(
        key_now * solution, axis=2, keepdims=True
    )
    normalized = (
        readout * lax.rsqrt(jnp.mean(readout * readout, axis=2, keepdims=True) + epsilon)
    ).astype(jnp.bfloat16)
    partial_value = jnp.dot(
        normalized.reshape(row_count, head_count * head_size),
        out_weight.reshape(head_count * head_size, model_width),
        preferred_element_type=jnp.float32,
    )
    head_peers = lax.axis_size("head")
    if head_peers == 2:
        me = lax.axis_index("head")
        width = model_width // 2
        mine = lax.dynamic_slice_in_dim(partial_value, me * width, width, axis=1)
        theirs = lax.dynamic_slice_in_dim(partial_value, (1 - me) * width, width, axis=1)
        attended = mine + lax.ppermute(theirs, "head", [(0, 1), (1, 0)])
    else:
        attended = lax.psum_scatter(
            partial_value.astype(jnp.bfloat16), "head", scatter_dimension=1, tiled=True
        ).astype(jnp.float32)
    widened_own = hidden.astype(jnp.float32)
    combined = jnp.where(mask_of_live[:, None], widened_own + attended, widened_own)
    return combined.astype(jnp.bfloat16)


def solution(mesh):
    in_specs = (
        P("req", "head"),
        P(),
        P(None, "head", None, None),
        P(None, "head", None, None),
        P("req", None, "head", None, None),
        P(None, None, "head"),
        P("req", "head"),
        P("head"),
        P("req", "head", None, None),
        P("req", "head", None, None),
        P("req", "head", None, None),
        P("req", "head", None, None),
        P("req"),
        P("req"),
        P("head", None, None),
    )
    out_specs = P("req", "head")
    return jax.shard_map(
        on_device, mesh=mesh, in_specs=in_specs, out_specs=out_specs, check_vma=False
    )
```

profile of v0, /device:TPU:0, one launch (start us, length us, event | category | flops | bytes accessed | tf_op | source)
XLA Modules:
  0.0 283.2 jit_solution(17922766164927195069)
XLA Ops:
  6.6 6.0 %copy.201 = bf16[1024,4,3,128]{0,3,2,1:T(8,128)(2,1)} copy(bf16[1024,4,3,128]{3,1,2,0:T(4,128)(2,1)} %param.21) | data formatting | bytes 6291456 | tf_op args[2]
  17.9 8.3 %all-to-all-start = ((f32[16,6,5,128]{3,1,2,0:T(8,128)}), f32[16,6,5,128]{3,1,2,0:T(8,128)S(1)}, u32[]{:S(2)}, u32[]{:S(2)}) async-start(f32[16,6,5,128]{3,1,2,0:T(8,128)} %copy.211), calls=%async_computation | async-start | bytes 655360 | tf_op jit(solution)/shard_map/all_to_all | solution.py:103
  26.6 11.3 %all-to-all-done = f32[16,6,5,128]{3,1,2,0:T(8,128)S(1)} async-done(((f32[16,6,5,128]{3,1,2,0:T(8,128)}), f32[16,6,5,128]{3,1,2,0:T(8,128)S(1)}, u32[]{:S(2)}, u32[]{:S(2)}) %all-to-all-start) | async-done | bytes 245792 | tf_op jit(solution)/shard_map/all_to_all | solution.py:103
  40.2 3.5 %all-to-all-start.1 = ((f32[16,6,4,128]{3,2,1,0:T(4,128)}), f32[16,6,4,128]{3,2,1,0:T(4,128)S(1)}, u32[]{:S(2)}, u32[]{:S(2)}) async-start(f32[16,6,4,128]{3,2,1,0:T(4,128)} %select_add_fusion.8), calls=%async_computation.1 | async-start | bytes 393216 | tf_op jit(solution)/shard_map/all_to_all | solution.py:103
  43.8 4.5 %multiply_reduce_fusion.8 = f32[24,4,128]{2,1,0:T(4,128)S(1)} fusion(f32[24,4,128,128]{3,2,1,0:T(8,128)} %param.27, f32[24,4,128]{2,1,0:T(4,128)S(1)} %copy.217), kind=kLoop, calls=%fused_computation.35 | loop fusion | flops 3133440 | bytes 6389760 | tf_op jit(solution)/shard_map/reduce_sum | solution.py:16
  48.2 3.5 %all-to-all-done.1 = f32[16,6,4,128]{3,2,1,0:T(4,128)S(1)} async-done(((f32[16,6,4,128]{3,2,1,0:T(4,128)}), f32[16,6,4,128]{3,2,1,0:T(4,128)S(1)}, u32[]{:S(2)}, u32[]{:S(2)}) %all-to-all-start.1) | async-done | bytes 196640 | tf_op jit(solution)/shard_map/all_to_all | solution.py:103
  54.1 11.3 %all_to_all.90 = f32[16,6,4,128]{3,2,1,0:T(4,128)S(1)} all-to-all(f32[16,6,4,128]{3,2,1,0:T(4,128)S(1)} %bitcast.267), channel_id=1, replica_groups=mesh['req'=16,'head'=2] {'req'}, dimensions={0} | all-to-all | bytes 393216 | tf_op jit(solution)/shard_map/all_to_all | solution.py:103
  70.9 4.5 %multiply_reduce_fusion.7 = f32[24,4,128]{2,1,0:T(4,128)S(1)} fusion(f32[24,4,128,128]{3,2,1,0:T(8,128)} %param.27, f32[24,4,128]{2,1,0:T(4,128)S(1)} %copy.318), kind=kLoop, calls=%fused_computation.34 | loop fusion | flops 3133440 | bytes 6389760 | tf_op jit(solution)/shard_map/reduce_sum | solution.py:16
  75.4 3.5 %all-to-all-done.3 = f32[16,6,4,128]{3,2,1,0:T(4,128)S(1)} async-done(((f32[16,6,4,128]{3,2,1,0:T(4,128)}), f32[16,6,4,128]{3,2,1,0:T(4,128)S(1)}, u32[]{:S(2)}, u32[]{:S(2)}) %all-to-all-start.3) | async-done | bytes 196640 | tf_op jit(solution)/shard_map/all_to_all | solution.py:103
  81.2 11.2 %all_to_all.91 = f32[16,6,4,128]{3,2,1,0:T(4,128)S(1)} all-to-all(f32[16,6,4,128]{3,2,1,0:T(4,128)S(1)} %bitcast.268), channel_id=1, replica_groups=mesh['req'=16,'head'=2] {'req'}, dimensions={0} | all-to-all | bytes 393216 | tf_op jit(solution)/shard_map/all_to_all | solution.py:103
  94.3 3.8 %all-to-all-start.5 = ((f32[16,6,4,128]{3,2,1,0:T(4,128)}), f32[16,6,4,128]{3,2,1,0:T(4,128)S(1)}, u32[]{:S(2)}, u32[]{:S(2)}) async-start(f32[16,6,4,128]{3,2,1,0:T(4,128)} %select_add_fusion.6), calls=%async_computation.5 | async-start | bytes 393216 | tf_op jit(solution)/shard_map/all_to_all | solution.py:103
  98.1 4.5 %multiply_reduce_fusion.6 = f32[24,4,128]{2,1,0:T(4,128)S(1)} fusion(f32[24,4,128,128]{3,2,1,0:T(8,128)} %param.27, f32[24,4,128]{2,1,0:T(4,128)S(1)} %copy.319), kind=kLoop, calls=%fused_computation.33 | loop fusion | flops 3133440 | bytes 6389760 | tf_op jit(solution)/shard_map/reduce_sum | solution.py:16
  102.6 3.5 %all-to-all-done.5 = f32[16,6,4,128]{3,2,1,0:T(4,128)S(1)} async-done(((f32[16,6,4,128]{3,2,1,0:T(4,128)}), f32[16,6,4,128]{3,2,1,0:T(4,128)S(1)}, u32[]{:S(2)}, u32[]{:S(2)}) %all-to-all-start.5) | async-done | bytes 196640 | tf_op jit(solution)/shard_map/all_to_all | solution.py:103
  108.4 11.3 %all_to_all.92 = f32[16,6,4,128]{3,2,1,0:T(4,128)S(1)} all-to-all(f32[16,6,4,128]{3,2,1,0:T(4,128)S(1)} %bitcast.269), channel_id=1, replica_groups=mesh['req'=16,'head'=2] {'req'}, dimensions={0} | all-to-all | bytes 393216 | tf_op jit(solution)/shard_map/all_to_all | solution.py:103
  125.2 4.5 %multiply_reduce_fusion.5 = f32[24,4,128]{2,1,0:T(4,128)S(1)} fusion(f32[24,4,128,128]{3,2,1,0:T(8,128)} %param.27, f32[24,4,128]{2,1,0:T(4,128)S(1)} %copy.320), kind=kLoop, calls=%fused_computation.32 | loop fusion | flops 3133440 | bytes 6389760 | tf_op jit(solution)/shard_map/reduce_sum | solution.py:16
  129.7 3.5 %all-to-all-done.7 = f32[16,6,4,128]{3,2,1,0:T(4,128)S(1)} async-done(((f32[16,6,4,128]{3,2,1,0:T(4,128)}), f32[16,6,4,128]{3,2,1,0:T(4,128)S(1)}, u32[]{:S(2)}, u32[]{:S(2)}) %all-to-all-start.7) | async-done | bytes 196640 | tf_op jit(solution)/shard_map/all_to_all | solution.py:103
  135.5 11.2 %all_to_all.93 = f32[16,6,4,128]{3,2,1,0:T(4,128)S(1)} all-to-all(f32[16,6,4,128]{3,2,1,0:T(4,128)S(1)} %bitcast.270), channel_id=1, replica_groups=mesh['req'=16,'head'=2] {'req'}, dimensions={0} | all-to-all | bytes 393216 | tf_op jit(solution)/shard_map/all_to_all | solution.py:103
  152.1 4.5 %multiply_reduce_fusion.4 = f32[24,4,128]{2,1,0:T(4,128)S(1)} fusion(f32[24,4,128,128]{3,2,1,0:T(8,128)} %param.27, f32[24,4,128]{2,1,0:T(4,128)S(1)} %copy.321), kind=kLoop, calls=%fused_computation.31 | loop fusion | flops 3133440 | bytes 6389760 | tf_op jit(solution)/shard_map/reduce_sum | solution.py:16
  156.6 3.5 %all-to-all-done.9 = f32[16,6,4,128]{3,2,1,0:T(4,128)S(1)} async-done(((f32[16,6,4,128]{3,2,1,0:T(4,128)}), f32[16,6,4,128]{3,2,1,0:T(4,128)S(1)}, u32[]{:S(2)}, u32[]{:S(2)}) %all-to-all-start.9) | async-done | bytes 196640 | tf_op jit(solution)/shard_map/all_to_all | solution.py:103
  162.4 11.2 %all_to_all.94 = f32[16,6,4,128]{3,2,1,0:T(4,128)S(1)} all-to-all(f32[16,6,4,128]{3,2,1,0:T(4,128)S(1)} %bitcast.271), channel_id=1, replica_groups=mesh['req'=16,'head'=2] {'req'}, dimensions={0} | all-to-all | bytes 393216 | tf_op jit(solution)/shard_map/all_to_all | solution.py:103
  175.5 13.1 %all-to-all-start.11 = ((f32[16,6,4,128]{3,2,1,0:T(4,128)}), f32[16,6,4,128]{3,2,1,0:T(4,128)S(1)}, u32[]{:S(2)}, u32[]{:S(2)}) async-start(f32[16,6,4,128]{3,2,1,0:T(4,128)} %select_add_fusion.3), calls=%async_computation.11 | async-start | bytes 393216 | tf_op jit(solution)/shard_map/all_to_all | solution.py:103
  188.6 4.5 %multiply_reduce_fusion.3 = f32[24,4,128]{2,1,0:T(4,128)S(1)} fusion(f32[24,4,128,128]{3,2,1,0:T(8,128)} %param.27, f32[24,4,128]{2,1,0:T(4,128)S(1)} %copy.322), kind=kLoop, calls=%fused_computation.30 | loop fusion | flops 3133440 | bytes 6389760 | tf_op jit(solution)/shard_map/reduce_sum | solution.py:16
  198.7 11.4 %all_to_all.95 = f32[16,6,4,128]{3,2,1,0:T(4,128)S(1)} all-to-all(f32[16,6,4,128]{3,2,1,0:T(4,128)S(1)} %bitcast.272), channel_id=1, replica_groups=mesh['req'=16,'head'=2] {'req'}, dimensions={0} | all-to-all | bytes 393216 | tf_op jit(solution)/shard_map/all_to_all | solution.py:103
  215.5 4.5 %multiply_reduce_fusion.2 = f32[24,4,128]{2,1,0:T(4,128)S(1)} fusion(f32[24,4,128,128]{3,2,1,0:T(8,128)} %param.27, f32[24,4,128]{2,1,0:T(4,128)S(1)} %copy.323), kind=kLoop, calls=%fused_computation.29 | loop fusion | flops 3133440 | bytes 6389760 | tf_op jit(solution)/shard_map/reduce_sum | solution.py:16
  220.0 3.5 %all-to-all-done.13 = f32[16,6,4,128]{3,2,1,0:T(4,128)S(1)} async-done(((f32[16,6,4,128]{3,2,1,0:T(4,128)}), f32[16,6,4,128]{3,2,1,0:T(4,128)S(1)}, u32[]{:S(2)}, u32[]{:S(2)}) %all-to-all-start.13) | async-done | bytes 196640 | tf_op jit(solution)/shard_map/all_to_all | solution.py:103
  225.8 11.3 %all_to_all.96 = f32[16,6,4,128]{3,2,1,0:T(4,128)S(1)} all-to-all(f32[16,6,4,128]{3,2,1,0:T(4,128)S(1)} %bitcast.273), channel_id=1, replica_groups=mesh['req'=16,'head'=2] {'req'}, dimensions={0} | all-to-all | bytes 393216 | tf_op jit(solution)/shard_map/all_to_all | solution.py:103
  242.5 4.5 %multiply_reduce_fusion.1 = f32[24,4,128]{2,1,0:T(4,128)S(1)} fusion(f32[24,4,128,128]{3,2,1,0:T(8,128)} %param.27, f32[24,4,128]{2,1,0:T(4,128)S(1)} %copy.324), kind=kLoop, calls=%fused_computation.28 | loop fusion | flops 3133440 | bytes 6389760 | tf_op jit(solution)/shard_map/reduce_sum | solution.py:16
  247.0 3.5 %all-to-all-done.15 = f32[16,6,4,128]{3,2,1,0:T(4,128)S(1)} async-done(((f32[16,6,4,128]{3,2,1,0:T(4,128)}), f32[16,6,4,128]{3,2,1,0:T(4,128)S(1)}, u32[]{:S(2)}, u32[]{:S(2)}) %all-to-all-start.15) | async-done | bytes 196640 | tf_op jit(solution)/shard_map/all_to_all | solution.py:103
  252.8 13.0 %all_to_all.97 = f32[16,6,4,128]{3,2,1,0:T(4,128)S(1)} all-to-all(f32[16,6,4,128]{3,2,1,0:T(4,128)S(1)} %bitcast.266), channel_id=1, replica_groups=mesh['req'=16,'head'=2] {'req'}, dimensions={0} | all-to-all | bytes 393216 | tf_op jit(solution)/shard_map/all_to_all | solution.py:103
  267.7 3.9 %all-to-all-start.17 = ((f32[16,6,4,128]{3,2,1,0:T(4,128)}), f32[16,6,4,128]{3,2,1,0:T(4,128)S(1)}, u32[]{:S(2)}, u32[]{:S(2)}) async-start(f32[16,6,4,128]{3,2,1,0:T(4,128)} %select_add_fusion), calls=%async_computation.17 | async-start | bytes 393216 | tf_op jit(solution)/shard_map/all_to_all | solution.py:103
  271.6 4.5 %multiply_reduce_fusion = f32[24,4,128]{2,1,0:T(4,128)S(1)} fusion(f32[24,4,128,128]{3,2,1,0:T(8,128)} %param.28, f32[24,4,128]{2,1,0:T(4,128)S(1)} %copy.325), kind=kLoop, calls=%fused_computation.27 | loop fusion | flops 3133440 | bytes 6389760 | tf_op jit(solution)/shard_map/reduce_sum | solution.py:16
  276.1 3.6 %all-to-all-done.17 = f32[16,6,4,128]{3,2,1,0:T(4,128)S(1)} async-done(((f32[16,6,4,128]{3,2,1,0:T(4,128)}), f32[16,6,4,128]{3,2,1,0:T(4,128)S(1)}, u32[]{:S(2)}, u32[]{:S(2)}) %all-to-all-start.17) | async-done | bytes 196640 | tf_op jit(solution)/shard_map/all_to_all | solution.py:103
  (196 shorter events, 71.2 us)
Async XLA Ops:
  0.0 280.7 %copy-start = (bf16[4,128,1024]{2,1,0:T(8,128)(2,1)S(1)}, bf16[4,128,1024]{2,1,0:T(8,128)(2,1)}, u32[]{:S(2)}) copy-start(bf16[4,128,1024]{2,1,0:T(8,128)(2,1)} %param.33) | copy-start | bytes 3145732
  0.0 12.7 %copy-start.5 = (f32[1024]{0:T(1024)S(1)}, f32[1024]{0:T(1024)}, u32[]{:S(2)}) copy-start(f32[1024]{0:T(1024)} %param.20) | copy-start | bytes 12292
  6.6 19.7 %copy-start.4 = (bf16[1024,2,4]{0,2,1:T(4,128)(2,1)S(1)}, bf16[1024,2,4]{0,2,1:T(4,128)(2,1)}, u32[]{:S(2)}) copy-start(bf16[1024,2,4]{0,2,1:T(4,128)(2,1)} %param.24) | copy-start | bytes 49156
  6.6 31.7 %copy-start.1 = (f32[2,4,128,128]{3,2,1,0:T(8,128)S(1)}, f32[2,4,128,128]{3,2,1,0:T(8,128)}, u32[]{:S(2)}) copy-start(f32[2,4,128,128]{3,2,1,0:T(8,128)} %param.29) | copy-start | bytes 1572868
  17.9 34.5 %copy-start.6 = (f32[24,4]{0,1:T(4,128)S(1)}, f32[24,4]{0,1:T(4,128)}, u32[]{:S(2)}) copy-start(f32[24,4]{0,1:T(4,128)} %param.25) | copy-start | bytes 1156
  17.9 34.5 %copy-start.7 = (f32[4]{0:T(128)S(1)}, f32[4]{0:T(128)}, u32[]{:S(2)}) copy-start(f32[4]{0:T(128)} %param.26) | copy-start | bytes 52
  17.9 20.0 %all-to-all-start = ((f32[16,6,5,128]{3,1,2,0:T(8,128)}), f32[16,6,5,128]{3,1,2,0:T(8,128)S(1)}, u32[]{:S(2)}, u32[]{:S(2)}) async-start(f32[16,6,5,128]{3,1,2,0:T(8,128)} %copy.211), calls=%async_computation | async-start | bytes 655360 | tf_op jit(solution)/shard_map/all_to_all | solution.py:103
  40.2 11.6 %all-to-all-start.1 = ((f32[16,6,4,128]{3,2,1,0:T(4,128)}), f32[16,6,4,128]{3,2,1,0:T(4,128)S(1)}, u32[]{:S(2)}, u32[]{:S(2)}) async-start(f32[16,6,4,128]{3,2,1,0:T(4,128)} %select_add_fusion.8), calls=%async_computation.1 | async-start | bytes 393216 | tf_op jit(solution)/shard_map/all_to_all | solution.py:103
  67.3 11.6 %all-to-all-start.3 = ((f32[16,6,4,128]{3,2,1,0:T(4,128)}), f32[16,6,4,128]{3,2,1,0:T(4,128)S(1)}, u32[]{:S(2)}, u32[]{:S(2)}) async-start(f32[16,6,4,128]{3,2,1,0:T(4,128)} %select_add_fusion.7), calls=%async_computation.3 | async-start | bytes 393216 | tf_op jit(solution)/shard_map/all_to_all | solution.py:103
  94.3 11.8 %all-to-all-start.5 = ((f32[16,6,4,128]{3,2,1,0:T(4,128)}), f32[16,6,4,128]{3,2,1,0:T(4,128)S(1)}, u32[]{:S(2)}, u32[]{:S(2)}) async-start(f32[16,6,4,128]{3,2,1,0:T(4,128)} %select_add_fusion.6), calls=%async_computation.5 | async-start | bytes 393216 | tf_op jit(solution)/shard_map/all_to_all | solution.py:103
  121.6 11.6 %all-to-all-start.7 = ((f32[16,6,4,128]{3,2,1,0:T(4,128)}), f32[16,6,4,128]{3,2,1,0:T(4,128)S(1)}, u32[]{:S(2)}, u32[]{:S(2)}) async-start(f32[16,6,4,128]{3,2,1,0:T(4,128)} %select_add_fusion.5), calls=%async_computation.7 | async-start | bytes 393216 | tf_op jit(solution)/shard_map/all_to_all | solution.py:103
  148.6 11.6 %all-to-all-start.9 = ((f32[16,6,4,128]{3,2,1,0:T(4,128)}), f32[16,6,4,128]{3,2,1,0:T(4,128)S(1)}, u32[]{:S(2)}, u32[]{:S(2)}) async-start(f32[16,6,4,128]{3,2,1,0:T(4,128)} %select_add_fusion.4), calls=%async_computation.9 | async-start | bytes 393216 | tf_op jit(solution)/shard_map/all_to_all | solution.py:103
  175.5 20.9 %all-to-all-start.11 = ((f32[16,6,4,128]{3,2,1,0:T(4,128)}), f32[16,6,4,128]{3,2,1,0:T(4,128)S(1)}, u32[]{:S(2)}, u32[]{:S(2)}) async-start(f32[16,6,4,128]{3,2,1,0:T(4,128)} %select_add_fusion.3), calls=%async_computation.11 | async-start | bytes 393216 | tf_op jit(solution)/shard_map/all_to_all | solution.py:103
  211.9 11.6 %all-to-all-start.13 = ((f32[16,6,4,128]{3,2,1,0:T(4,128)}), f32[16,6,4,128]{3,2,1,0:T(4,128)S(1)}, u32[]{:S(2)}, u32[]{:S(2)}) async-start(f32[16,6,4,128]{3,2,1,0:T(4,128)} %select_add_fusion.2), calls=%async_computation.13 | async-start | bytes 393216 | tf_op jit(solution)/shard_map/all_to_all | solution.py:103
  237.1 28.7 %copy-start.2 = (f32[2,4,128,128]{3,2,1,0:T(8,128)S(1)}, f32[2,4,128,128]{3,2,1,0:T(8,128)}, u32[]{:S(2)}) copy-start(f32[2,4,128,128]{3,2,1,0:T(8,128)} %param.30) | copy-start | bytes 1572868
  239.0 11.6 %all-to-all-start.15 = ((f32[16,6,4,128]{3,2,1,0:T(4,128)}), f32[16,6,4,128]{3,2,1,0:T(4,128)S(1)}, u32[]{:S(2)}, u32[]{:S(2)}) async-start(f32[16,6,4,128]{3,2,1,0:T(4,128)} %select_add_fusion.1), calls=%async_computation.15 | async-start | bytes 393216 | tf_op jit(solution)/shard_map/all_to_all | solution.py:103
  252.6 29.8 %copy-start.3 = (bf16[24,512]{1,0:T(8,128)(2,1)S(1)}, bf16[24,512]{1,0:T(8,128)(2,1)}, u32[]{:S(2)}) copy-start(bf16[24,512]{1,0:T(8,128)(2,1)} %param.19) | copy-start | bytes 73732
  267.7 12.0 %all-to-all-start.17 = ((f32[16,6,4,128]{3,2,1,0:T(4,128)}), f32[16,6,4,128]{3,2,1,0:T(4,128)S(1)}, u32[]{:S(2)}, u32[]{:S(2)}) async-start(f32[16,6,4,128]{3,2,1,0:T(4,128)} %select_add_fusion), calls=%async_computation.17 | async-start | bytes 393216 | tf_op jit(solution)/shard_map/all_to_all | solution.py:103
  281.1 1.3 collective-permute-start
where the time goes:
time: 289 us; the launch traced here: 283 us
  blocking collectives  94.4 us (33%)
  other arithmetic  60.5 us (21%)
  starting transfers between devices  50.3 us (17%)
  waiting for transfers between devices  44.1 us (15%)
  local copies, waits for them, and re-layouts  23.6 us (8%)
  matrix products  9.04 us (3%)
    all_to_all x8, blocking collectives, exchange(): lax.all_to_all(shaped, 'req', split_axis=0, concat_axis=0, tiled=True)  92 us
    all_to_all x10, starting transfers between devices, exchange(): lax.all_to_all(shaped, 'req', split_axis=0, concat_axis=0, tiled=True)  50.3 us
    all_to_all x10, waiting for transfers between devices, exchange(): lax.all_to_all(shaped, 'req', split_axis=0, concat_axis=0, tiled=True)  42.9 us
    reduce_sum x9, other arithmetic, own_matvec(): return jnp.sum(matrices * vectors[:, :, None, :], axis=3)  40.4 us
    add x9, other arithmetic, owner_apply(): total + jnp.where(chosen[group][:, None, None], products[group], 0.0)  8.5 us
    gather x9, local copies, waits for them, and re-layouts, pack(): return jnp.take(padded, source, axis=0)  6.35 us
    unnamed x26, local copies, waits for them, and re-layouts  6.21 us
  transfers between devices with their start and end apart: 11, of which 11 were waited for; matrix products, arithmetic and copies ran while one was open for 14% of the time, Pallas kernels for 0%

commit v1 on v0

--- a/solution.py
+++ b/solution.py
@@ -1,6 +1,8 @@
 import jax
 import jax.numpy as jnp
 from jax import lax
+from jax.experimental import pallas as pl
+from jax.experimental.pallas import tpu as pltpu
 from jax.sharding import PartitionSpec as P
 
 KW = 4
@@ -14,6 +16,26 @@
 
 def own_matvec(matrices, vectors):
     return jnp.sum(matrices * vectors[:, :, None, :], axis=3)
+
+
+def project_kernel(rows_ref, weight_ref, out_ref):
+    out_ref[...] = jnp.dot(rows_ref[...], weight_ref[...], preferred_element_type=jnp.float32)
+
+
+def project(rows, weight):
+    row_count, depth = rows.shape
+    width = weight.shape[1]
+    return pl.pallas_call(
+        project_kernel,
+        out_shape=jax.ShapeDtypeStruct((row_count, width), jnp.float32),
+        in_specs=[pl.BlockSpec(memory_space=pltpu.VMEM)] * 2,
+        out_specs=pl.BlockSpec(memory_space=pltpu.VMEM),
+        cost_estimate=pl.CostEstimate(
+            flops=2 * row_count * depth * width,
+            bytes_accessed=2 * (row_count * depth + depth * width) + 4 * row_count * width,
+            transcendentals=0,
+        ),
+    )(rows, weight)
 
 
 def on_device(
@@ -44,10 +66,8 @@
     row_count, model_width = gathered.shape
     head_count = qkv_weight.shape[1]
     head_size = qkv_weight.shape[3]
-    projected = jnp.dot(
-        normed,
-        qkv_weight.reshape(model_width, head_count * 3 * head_size),
-        preferred_element_type=jnp.float32,
+    projected = project(
+        normed, qkv_weight.reshape(model_width, head_count * 3 * head_size)
     ).reshape(row_count, head_count, 3, head_size)
     mixing = conv_weight[0] * projected
     for offset in range(1, KW):
@@ -108,29 +128,13 @@
         return jnp.where(routed[:, None, None], taken, 0.0)
 
     def owner_apply(states, incoming, chosen):
-        products = jnp.einsum("shj,ghij->gshi", incoming, states, precision=highest)
-        total = jnp.zeros_like(incoming)
-        for group in range(group_count):
-            total = total + jnp.where(chosen[group][:, None, None], products[group], 0.0)
-        return total
-
-    solution = jnp.zeros_like(queries)
-    residual = queries
-    direction = queries
-    norm_now = jnp.sum(residual * residual, axis=2, keepdims=True)
-    chosen = None
-    for iteration in range(ITERS):
-        outgoing = pack(direction)
-        if iteration == 0:
-            label_row = jnp.broadcast_to(
-                slot_label.astype(jnp.float32)[:, None, None], (slot_count, 1, head_size)
-            )
-            arrived = exchange(jnp.concatenate([outgoing, label_row], axis=1))
-            labels_in = arrived[:, head_count, 0]
-            chosen = [labels_in == float(group + 1) for group in range(group_count)]
-            arrived = arrived[:, :head_count]
-        else:
-            arrived = exchange(outgoing)
+        split = jnp.stack(
+            [jnp.where(chosen[group][:, None, None], incoming, 0.0) for group in range(group_count)]
+        )
+        return jnp.einsum("gshj,ghij->shi", split, states, precision=highest)
+
+    def cg_step(arrived, carry):
+        solution, residual, direction, norm_now = carry
         shares = unpack(exchange(owner_apply(prompt_keys, arrived, chosen)))
         shared = weight_col * shares + own_matvec(own_keys, direction)
         product = (
@@ -143,7 +147,25 @@
         residual = residual - step_size * product
         norm_next = jnp.sum(residual * residual, axis=2, keepdims=True)
         direction = residual + norm_next / norm_now * direction
-        norm_now = norm_next
+        return solution, residual, direction, norm_next
+
+    label_row = jnp.broadcast_to(
+        slot_label.astype(jnp.float32)[:, None, None], (slot_count, 1, head_size)
+    )
+    first = exchange(jnp.concatenate([pack(queries), label_row], axis=1))
+    labels_in = first[:, head_count, 0]
+    chosen = [labels_in == float(group + 1) for group in range(group_count)]
+    carry = (
+        jnp.zeros_like(queries),
+        queries,
+        queries,
+        jnp.sum(queries * queries, axis=2, keepdims=True),
+    )
+    carry = cg_step(first[:, :head_count], carry)
+    carry = lax.fori_loop(
+        1, ITERS, lambda _, state: cg_step(exchange(pack(state[2])), state), carry
+    )
+    solution = carry[0]
     value_sum = unpack(exchange(owner_apply(prompt_values, exchange(pack(solution)), chosen)))
     shared_out = weight_col * value_sum + own_matvec(own_values, solution)
     readout = decay_col * shared_out + write_col * value_now * jnp.sum(

time: 289 us -> 290 us (level); the launches traced: 283 us -> 288 us
  blocking collectives: 94.4 us -> 13.9 us
  waiting for transfers between devices: 44.1 us -> 99.3 us
  starting transfers between devices: 50.3 us -> 67.4 us
  local copies, waits for them, and re-layouts: 23.6 us -> 36.5 us
  Pallas kernels: 0 us -> 3.23 us
    all_to_all x8 -> x1, blocking collectives: 92 us -> 11.4 us  [exchange(): lax.all_to_all(shaped, 'req', split_axis=0, concat_axis=0, tiled=True)]
    all_to_all x10 -> x17, waiting for transfers between devices: 42.9 us -> 98.1 us  [exchange(): lax.all_to_all(shaped, 'req', split_axis=0, concat_axis=0, tiled=True)]
    all_to_all x10 -> x17, starting transfers between devices: 50.3 us -> 67.4 us  [exchange(): lax.all_to_all(shaped, 'req', split_axis=0, concat_axis=0, tiled=True)]
    add x17 -> x8, other arithmetic: 9.36 us -> 1.51 us  [cg_step(): direction = residual + norm_next / norm_now * direction]
    transpose x0 -> x9, local copies, waits for them, and re-layouts: none -> 7.23 us  [owner_apply(): return jnp.einsum('gshj,ghij->shi', split, states, precision=highest)]
    reshape x0 -> x2, local copies, waits for them, and re-layouts: none -> 5.72 us  [the longest x1 4.69 us: on_device(): qkv_weight.reshape(model_width, head_count * 3 * head_size)]
    select_n x9 -> x17, other arithmetic: 1.51 us -> 6.26 us  [pack(): return jnp.take(padded, source, axis=0)]
    pallas_call x0 -> x1, Pallas kernels: none -> 3.23 us  [project(): pl.pallas_call(project_kernel, out_shape=jax.ShapeDtypeStruct((row_count,...]
  transfers between devices with their start and end apart: 11 -> 18, of which waited for: 11 -> 18; matrix products, arithmetic and copies ran while one was open for 14% -> 15% of each run, Pallas kernels for 0% -> 0%
where the time goes in v1:
time: 290 us; the launch traced here: 288 us
  waiting for transfers between devices  99.3 us (34%)
  starting transfers between devices  67.4 us (23%)
  other arithmetic  59 us (20%)
  local copies, waits for them, and re-layouts  36.5 us (13%)
  blocking collectives  13.9 us (5%)
  matrix products  7.17 us (2%)
  Pallas kernels  3.23 us (1%)
    all_to_all x17, waiting for transfers between devices, exchange(): lax.all_to_all(shaped, 'req', split_axis=0, concat_axis=0, tiled=True)  98.1 us
    all_to_all x17, starting transfers between devices, exchange(): lax.all_to_all(shaped, 'req', split_axis=0, concat_axis=0, tiled=True)  67.4 us
    reduce_sum x9, other arithmetic, own_matvec(): return jnp.sum(matrices * vectors[:, :, None, :], axis=3)  40.4 us
    all_to_all x1, blocking collectives, exchange(): lax.all_to_all(shaped, 'req', split_axis=0, concat_axis=0, tiled=True)  11.4 us
    transpose x9, local copies, waits for them, and re-layouts, owner_apply(): return jnp.einsum('gshj,ghij->shi', split, states, precision=highest)  7.23 us
    gather x9, local copies, waits for them, and re-layouts, pack(): return jnp.take(padded, source, axis=0)  6.35 us
    select_n x17, other arithmetic, pack(): return jnp.take(padded, source, axis=0)  6.26 us
    unnamed x27, local copies, waits for them, and re-layouts  6.18 us
  transfers between devices with their start and end apart: 18, of which 18 were waited for; matrix products, arithmetic and copies ran while one was open for 15% of the time, Pallas kernels for 0%

profile of v1, /device:TPU:0, one launch (start us, length us, event | category | flops | bytes accessed | tf_op | source)
XLA Modules:
  0.0 287.7 jit_solution(15288833724251689835)
XLA Ops:
  2.6 6.0 %copy.101 = bf16[1024,4,3,128]{0,3,2,1:T(8,128)(2,1)} copy(bf16[1024,4,3,128]{3,1,2,0:T(4,128)(2,1)} %param.23) | data formatting | bytes 6291456 | tf_op args[2]
  8.6 4.7 %copy.102.weight_ref = bf16[1024,1536]{1,0:T(8,128)(2,1)} copy(bf16[1024,1536]{0,1:T(8,128)(2,1)} %bitcast.144) | data formatting | bytes 6291456 | tf_op jit(solution)/shard_map/reshape | solution.py:70
  22.3 8.2 %all-to-all-start.2 = ((f32[16,6,5,128]{3,1,2,0:T(8,128)}), f32[16,6,5,128]{3,1,2,0:T(8,128)S(1)}, u32[]{:S(2)}, u32[]{:S(2)}) async-start(f32[16,6,5,128]{3,1,2,0:T(8,128)} %copy.108), calls=%async_computation.2 | async-start | bytes 655360 | tf_op jit(solution)/shard_map/all_to_all | solution.py:123
  30.7 11.5 %all-to-all-done.2 = f32[16,6,5,128]{3,1,2,0:T(8,128)S(1)} async-done(((f32[16,6,5,128]{3,1,2,0:T(8,128)}), f32[16,6,5,128]{3,1,2,0:T(8,128)S(1)}, u32[]{:S(2)}, u32[]{:S(2)}) %all-to-all-start.2) | async-done | bytes 245792 | tf_op jit(solution)/shard_map/all_to_all | solution.py:123
  44.0 3.5 %all-to-all-start.3 = ((f32[16,6,4,128]{3,2,1,0:T(4,128)}), f32[16,6,4,128]{3,2,1,0:T(4,128)S(1)}, u32[]{:S(2)}, u32[]{:S(2)}) async-start(f32[16,6,4,128]{3,2,1,0:T(4,128)} %bitcast.34), calls=%async_computation.3 | async-start | bytes 393216 | tf_op jit(solution)/shard_map/all_to_all | solution.py:123
  47.8 4.5 %multiply_reduce_fusion.5 = f32[24,4,128]{2,1,0:T(4,128)S(1)} fusion(f32[24,4,128,128]{3,2,1,0:T(8,128)} %param.29, f32[24,4,128]{2,1,0:T(4,128)S(1)} %multiply_bitcast_fusion), kind=kLoop, calls=%fused_computation.42 | loop fusion | flops 3133440 | bytes 6389760 | tf_op jit(solution)/shard_map/reduce_sum | solution.py:18
  57.2 201.5 %while.16 = (s32[]{:T(128)}, f32[24,4,128]{2,1,0:T(4,128)S(1)}, f32[24,4,128]{2,1,0:T(4,128)S(1)}, f32[24,4,128]{2,1,0:T(4,128)S(1)}, f32[24,4,1]{0,1,2:T(4,128)...) while((s32[]{:T(128)}, f32[24,4,128]{2,1,0:T(4,128)S(1)}, ...), condition=%wide.region_17.20_spmd, body=%wide.region_12.19_spmd.sunk | while | flops 154635536 | bytes 11313449 | solution.py:165
  58.8 3.6 %all-to-all-start = ((f32[16,6,4,128]{3,2,1,0:T(4,128)}), f32[16,6,4,128]{3,2,1,0:T(4,128)S(1)}, u32[]{:S(2)}, u32[]{:S(2)}) async-start(f32[16,6,4,128]{3,2,1,0:T(4,128)} %bitcast.136), calls=%async_computation | async-start | bytes 393216 | tf_op jit(solution)/shard_map/while/body/eval_jaxpr/all_to_all | solution.py:123
  62.5 8.1 %all-to-all-done = f32[16,6,4,128]{3,2,1,0:T(4,128)S(1)} async-done(((f32[16,6,4,128]{3,2,1,0:T(4,128)}), f32[16,6,4,128]{3,2,1,0:T(4,128)S(1)}, u32[]{:S(2)}, u32[]{:S(2)}) %all-to-all-start) | async-done | bytes 196640 | tf_op jit(solution)/shard_map/while/body/eval_jaxpr/all_to_all | solution.py:123
  75.9 4.5 %multiply_reduce_fusion.16 = f32[24,4,128]{2,1,0:T(4,128)S(1)} fusion(f32[24,4,128,128]{3,2,1,0:T(8,128)} %get-tuple-element.418, f32[24,4,128]{2,1,0:T(4,128)S(1)} %get-tuple-element.389), kind=kLoop, calls=%fused_computation.7.clone.1 | loop fusion | flops 3133440 | bytes 6389760 | tf_op jit(solution)/shard_map/while/body/eval_jaxpr/reduce_sum | solution.py:18
  87.3 3.6 %all-to-all-start = ((f32[16,6,4,128]{3,2,1,0:T(4,128)}), f32[16,6,4,128]{3,2,1,0:T(4,128)S(1)}, u32[]{:S(2)}, u32[]{:S(2)}) async-start(f32[16,6,4,128]{3,2,1,0:T(4,128)} %bitcast.136), calls=%async_computation | async-start | bytes 393216 | tf_op jit(solution)/shard_map/while/body/eval_jaxpr/all_to_all | solution.py:123
  90.9 8.1 %all-to-all-done = f32[16,6,4,128]{3,2,1,0:T(4,128)S(1)} async-done(((f32[16,6,4,128]{3,2,1,0:T(4,128)}), f32[16,6,4,128]{3,2,1,0:T(4,128)S(1)}, u32[]{:S(2)}, u32[]{:S(2)}) %all-to-all-start) | async-done | bytes 196640 | tf_op jit(solution)/shard_map/while/body/eval_jaxpr/all_to_all | solution.py:123
  104.3 4.5 %multiply_reduce_fusion.16 = f32[24,4,128]{2,1,0:T(4,128)S(1)} fusion(f32[24,4,128,128]{3,2,1,0:T(8,128)} %get-tuple-element.418, f32[24,4,128]{2,1,0:T(4,128)S(1)} %get-tuple-element.389), kind=kLoop, calls=%fused_computation.7.clone.1 | loop fusion | flops 3133440 | bytes 6389760 | tf_op jit(solution)/shard_map/while/body/eval_jaxpr/reduce_sum | solution.py:18
  115.7 3.6 %all-to-all-start = ((f32[16,6,4,128]{3,2,1,0:T(4,128)}), f32[16,6,4,128]{3,2,1,0:T(4,128)S(1)}, u32[]{:S(2)}, u32[]{:S(2)}) async-start(f32[16,6,4,128]{3,2,1,0:T(4,128)} %bitcast.136), calls=%async_computation | async-start | bytes 393216 | tf_op jit(solution)/shard_map/while/body/eval_jaxpr/all_to_all | solution.py:123
  119.3 8.1 %all-to-all-done = f32[16,6,4,128]{3,2,1,0:T(4,128)S(1)} async-done(((f32[16,6,4,128]{3,2,1,0:T(4,128)}), f32[16,6,4,128]{3,2,1,0:T(4,128)S(1)}, u32[]{:S(2)}, u32[]{:S(2)}) %all-to-all-start) | async-done | bytes 196640 | tf_op jit(solution)/shard_map/while/body/eval_jaxpr/all_to_all | solution.py:123
  132.7 4.5 %multiply_reduce_fusion.16 = f32[24,4,128]{2,1,0:T(4,128)S(1)} fusion(f32[24,4,128,128]{3,2,1,0:T(8,128)} %get-tuple-element.418, f32[24,4,128]{2,1,0:T(4,128)S(1)} %get-tuple-element.389), kind=kLoop, calls=%fused_computation.7.clone.1 | loop fusion | flops 3133440 | bytes 6389760 | tf_op jit(solution)/shard_map/while/body/eval_jaxpr/reduce_sum | solution.py:18
  144.1 3.6 %all-to-all-start = ((f32[16,6,4,128]{3,2,1,0:T(4,128)}), f32[16,6,4,128]{3,2,1,0:T(4,128)S(1)}, u32[]{:S(2)}, u32[]{:S(2)}) async-start(f32[16,6,4,128]{3,2,1,0:T(4,128)} %bitcast.136), calls=%async_computation | async-start | bytes 393216 | tf_op jit(solution)/shard_map/while/body/eval_jaxpr/all_to_all | solution.py:123
  147.7 8.1 %all-to-all-done = f32[16,6,4,128]{3,2,1,0:T(4,128)S(1)} async-done(((f32[16,6,4,128]{3,2,1,0:T(4,128)}), f32[16,6,4,128]{3,2,1,0:T(4,128)S(1)}, u32[]{:S(2)}, u32[]{:S(2)}) %all-to-all-start) | async-done | bytes 196640 | tf_op jit(solution)/shard_map/while/body/eval_jaxpr/all_to_all | solution.py:123
  161.1 4.5 %multiply_reduce_fusion.16 = f32[24,4,128]{2,1,0:T(4,128)S(1)} fusion(f32[24,4,128,128]{3,2,1,0:T(8,128)} %get-tuple-element.418, f32[24,4,128]{2,1,0:T(4,128)S(1)} %get-tuple-element.389), kind=kLoop, calls=%fused_computation.7.clone.1 | loop fusion | flops 3133440 | bytes 6389760 | tf_op jit(solution)/shard_map/while/body/eval_jaxpr/reduce_sum | solution.py:18
  172.5 3.6 %all-to-all-start = ((f32[16,6,4,128]{3,2,1,0:T(4,128)}), f32[16,6,4,128]{3,2,1,0:T(4,128)S(1)}, u32[]{:S(2)}, u32[]{:S(2)}) async-start(f32[16,6,4,128]{3,2,1,0:T(4,128)} %bitcast.136), calls=%async_computation | async-start | bytes 393216 | tf_op jit(solution)/shard_map/while/body/eval_jaxpr/all_to_all | solution.py:123
  176.1 8.2 %all-to-all-done = f32[16,6,4,128]{3,2,1,0:T(4,128)S(1)} async-done(((f32[16,6,4,128]{3,2,1,0:T(4,128)}), f32[16,6,4,128]{3,2,1,0:T(4,128)S(1)}, u32[]{:S(2)}, u32[]{:S(2)}) %all-to-all-start) | async-done | bytes 196640 | tf_op jit(solution)/shard_map/while/body/eval_jaxpr/all_to_all | solution.py:123
  189.6 4.5 %multiply_reduce_fusion.16 = f32[24,4,128]{2,1,0:T(4,128)S(1)} fusion(f32[24,4,128,128]{3,2,1,0:T(8,128)} %get-tuple-element.418, f32[24,4,128]{2,1,0:T(4,128)S(1)} %get-tuple-element.389), kind=kLoop, calls=%fused_computation.7.clone.1 | loop fusion | flops 3133440 | bytes 6389760 | tf_op jit(solution)/shard_map/while/body/eval_jaxpr/reduce_sum | solution.py:18
  201.0 3.6 %all-to-all-start = ((f32[16,6,4,128]{3,2,1,0:T(4,128)}), f32[16,6,4,128]{3,2,1,0:T(4,128)S(1)}, u32[]{:S(2)}, u32[]{:S(2)}) async-start(f32[16,6,4,128]{3,2,1,0:T(4,128)} %bitcast.136), calls=%async_computation | async-start | bytes 393216 | tf_op jit(solution)/shard_map/while/body/eval_jaxpr/all_to_all | solution.py:123
  204.6 8.3 %all-to-all-done = f32[16,6,4,128]{3,2,1,0:T(4,128)S(1)} async-done(((f32[16,6,4,128]{3,2,1,0:T(4,128)}), f32[16,6,4,128]{3,2,1,0:T(4,128)S(1)}, u32[]{:S(2)}, u32[]{:S(2)}) %all-to-all-start) | async-done | bytes 196640 | tf_op jit(solution)/shard_map/while/body/eval_jaxpr/all_to_all | solution.py:123
  214.4 4.6 %all-to-all-start.1 = ((f32[16,6,4,128]{3,2,1,0:T(4,128)}), f32[16,6,4,128]{3,2,1,0:T(4,128)S(1)}, u32[]{:S(2)}, u32[]{:S(2)}) async-start(f32[16,6,4,128]{3,2,1,0:T(4,128)} %bitcast.138), calls=%async_computation.1 | async-start | bytes 393216 | tf_op jit(solution)/shard_map/while/body/eval_jaxpr/all_to_all | solution.py:123
  219.3 4.5 %multiply_reduce_fusion.16 = f32[24,4,128]{2,1,0:T(4,128)S(1)} fusion(f32[24,4,128,128]{3,2,1,0:T(8,128)} %get-tuple-element.418, f32[24,4,128]{2,1,0:T(4,128)S(1)} %get-tuple-element.389), kind=kLoop, calls=%fused_computation.7.clone.1 | loop fusion | flops 3133440 | bytes 6389760 | tf_op jit(solution)/shard_map/while/body/eval_jaxpr/reduce_sum | solution.py:18
  230.7 4.7 %all-to-all-start = ((f32[16,6,4,128]{3,2,1,0:T(4,128)}), f32[16,6,4,128]{3,2,1,0:T(4,128)S(1)}, u32[]{:S(2)}, u32[]{:S(2)}) async-start(f32[16,6,4,128]{3,2,1,0:T(4,128)} %bitcast.136), calls=%async_computation | async-start | bytes 393216 | tf_op jit(solution)/shard_map/while/body/eval_jaxpr/all_to_all | solution.py:123
  235.5 8.1 %all-to-all-done = f32[16,6,4,128]{3,2,1,0:T(4,128)S(1)} async-done(((f32[16,6,4,128]{3,2,1,0:T(4,128)}), f32[16,6,4,128]{3,2,1,0:T(4,128)S(1)}, u32[]{:S(2)}, u32[]{:S(2)}) %all-to-all-start) | async-done | bytes 196640 | tf_op jit(solution)/shard_map/while/body/eval_jaxpr/all_to_all | solution.py:123
  248.9 4.5 %multiply_reduce_fusion.16 = f32[24,4,128]{2,1,0:T(4,128)S(1)} fusion(f32[24,4,128,128]{3,2,1,0:T(8,128)} %get-tuple-element.418, f32[24,4,128]{2,1,0:T(4,128)S(1)} %get-tuple-element.389), kind=kLoop, calls=%fused_computation.7.clone.1 | loop fusion | flops 3133440 | bytes 6389760 | tf_op jit(solution)/shard_map/while/body/eval_jaxpr/reduce_sum | solution.py:18
  259.6 11.4 %all_to_all.32 = f32[16,6,4,128]{3,2,1,0:T(4,128)S(1)} all-to-all(f32[16,6,4,128]{3,2,1,0:T(4,128)S(1)} %bitcast.147), channel_id=1, replica_groups=mesh['req'=16,'head'=2] {'req'}, dimensions={0} | all-to-all | bytes 393216 | tf_op jit(solution)/shard_map/all_to_all | solution.py:123
  276.2 4.5 %multiply_reduce_fusion.4 = f32[24,4,128]{2,1,0:T(4,128)S(1)} fusion(f32[24,4,128,128]{3,2,1,0:T(8,128)} %param.30, f32[24,4,128]{2,1,0:T(4,128)S(1)} %get-tuple-element.94), kind=kLoop, calls=%fused_computation.41 | loop fusion | flops 3133440 | bytes 6389760 | tf_op jit(solution)/shard_map/reduce_sum | solution.py:18
  280.7 3.5 %all-to-all-done.5 = f32[16,6,4,128]{3,2,1,0:T(4,128)S(1)} async-done(((f32[16,6,4,128]{3,2,1,0:T(4,128)}), f32[16,6,4,128]{3,2,1,0:T(4,128)S(1)}, u32[]{:S(2)}, u32[]{:S(2)}) %all-to-all-start.5) | async-done | bytes 196640 | tf_op jit(solution)/shard_map/all_to_all | solution.py:123
  (288 shorter events, 109.4 us)
Async XLA Ops:
  0.0 285.4 %copy-start = (bf16[4,128,1024]{2,1,0:T(8,128)(2,1)S(1)}, bf16[4,128,1024]{2,1,0:T(8,128)(2,1)}, u32[]{:S(2)}) copy-start(bf16[4,128,1024]{2,1,0:T(8,128)(2,1)} %param.35) | copy-start | bytes 3145732
  2.6 10.7 %copy-start.8 = (f32[1024]{0:T(1024)S(1)}, f32[1024]{0:T(1024)}, u32[]{:S(2)}) copy-start(f32[1024]{0:T(1024)} %param.22) | copy-start | bytes 12292
  8.6 9.7 %copy-start.3 = (bf16[24,3,4,3,128]{4,2,3,1,0:T(4,128)(2,1)S(1)}, bf16[24,3,4,3,128]{4,2,3,1,0:T(4,128)(2,1)}, u32[]{:S(2)}) copy-start(bf16[24,3,4,3,128]{4,2,3,1,0:T(4,128)(2,1)} %param.25) | copy-start | bytes 663556
  8.6 9.8 %copy-start.10 = (s32[24]{0:T(128)S(1)}, s32[24]{0:T(128)}, u32[]{:S(2)}) copy-start(s32[24]{0:T(128)} %param.33) | copy-start | bytes 292
  8.6 9.8 %copy-start.9 = (s32[24]{0:T(128)S(1)}, s32[24]{0:T(128)}, u32[]{:S(2)}) copy-start(s32[24]{0:T(128)} %param.34) | copy-start | bytes 292
  8.6 10.0 %copy-start.6 = (f32[4,4,3,128]{3,1,2,0:T(4,128)S(1)}, f32[4,4,3,128]{3,1,2,0:T(4,128)}, u32[]{:S(2)}) copy-start(f32[4,4,3,128]{3,1,2,0:T(4,128)} %param.24) | copy-start | bytes 73732
  8.6 10.4 %copy-start.7 = (bf16[1024,2,4]{0,2,1:T(4,128)(2,1)S(1)}, bf16[1024,2,4]{0,2,1:T(4,128)(2,1)}, u32[]{:S(2)}) copy-start(bf16[1024,2,4]{0,2,1:T(4,128)(2,1)} %param.26) | copy-start | bytes 49156
  13.3 29.2 %copy-start.1 = (f32[2,4,128,128]{3,2,1,0:T(8,128)S(1)}, f32[2,4,128,128]{3,2,1,0:T(8,128)}, u32[]{:S(2)}) copy-start(f32[2,4,128,128]{3,2,1,0:T(8,128)} %param.31) | copy-start | bytes 1572868
  14.0 33.6 %copy-start.5 = (f32[24,4]{0,1:T(4,128)S(1)}, f32[24,4]{0,1:T(4,128)}, u32[]{:S(2)}) copy-start(f32[24,4]{0,1:T(4,128)} %param.27) | copy-start | bytes 1156
  21.6 34.6 %copy-start.11 = (f32[4]{0:T(128)S(1)}, f32[4]{0:T(128)}, u32[]{:S(2)}) copy-start(f32[4]{0:T(128)} %param.28) | copy-start | bytes 52
  22.3 19.9 %all-to-all-start.2 = ((f32[16,6,5,128]{3,1,2,0:T(8,128)}), f32[16,6,5,128]{3,1,2,0:T(8,128)S(1)}, u32[]{:S(2)}, u32[]{:S(2)}) async-start(f32[16,6,5,128]{3,1,2,0:T(8,128)} %copy.108), calls=%async_computation.2 | async-start | bytes 655360 | tf_op jit(solution)/shard_map/all_to_all | solution.py:123
  44.0 11.6 %all-to-all-start.3 = ((f32[16,6,4,128]{3,2,1,0:T(4,128)}), f32[16,6,4,128]{3,2,1,0:T(4,128)S(1)}, u32[]{:S(2)}, u32[]{:S(2)}) async-start(f32[16,6,4,128]{3,2,1,0:T(4,128)} %bitcast.34), calls=%async_computation.3 | async-start | bytes 393216 | tf_op jit(solution)/shard_map/all_to_all | solution.py:123
  57.2 214.0 %copy-start.2 = (f32[2,4,128,128]{3,2,1,0:T(8,128)S(1)}, f32[2,4,128,128]{3,2,1,0:T(8,128)}, u32[]{:S(2)}) copy-start(f32[2,4,128,128]{3,2,1,0:T(8,128)} %param.32) | copy-start | bytes 1572868
  58.8 11.7 %all-to-all-start = ((f32[16,6,4,128]{3,2,1,0:T(4,128)}), f32[16,6,4,128]{3,2,1,0:T(4,128)S(1)}, u32[]{:S(2)}, u32[]{:S(2)}) async-start(f32[16,6,4,128]{3,2,1,0:T(4,128)} %bitcast.136), calls=%async_computation | async-start | bytes 393216 | tf_op jit(solution)/shard_map/while/body/eval_jaxpr/all_to_all | solution.py:123
  72.1 11.6 %all-to-all-start.1 = ((f32[16,6,4,128]{3,2,1,0:T(4,128)}), f32[16,6,4,128]{3,2,1,0:T(4,128)S(1)}, u32[]{:S(2)}, u32[]{:S(2)}) async-start(f32[16,6,4,128]{3,2,1,0:T(4,128)} %bitcast.138), calls=%async_computation.1 | async-start | bytes 393216 | tf_op jit(solution)/shard_map/while/body/eval_jaxpr/all_to_all | solution.py:123
  87.3 11.7 %all-to-all-start = ((f32[16,6,4,128]{3,2,1,0:T(4,128)}), f32[16,6,4,128]{3,2,1,0:T(4,128)S(1)}, u32[]{:S(2)}, u32[]{:S(2)}) async-start(f32[16,6,4,128]{3,2,1,0:T(4,128)} %bitcast.136), calls=%async_computation | async-start | bytes 393216 | tf_op jit(solution)/shard_map/while/body/eval_jaxpr/all_to_all | solution.py:123
  100.5 11.6 %all-to-all-start.1 = ((f32[16,6,4,128]{3,2,1,0:T(4,128)}), f32[16,6,4,128]{3,2,1,0:T(4,128)S(1)}, u32[]{:S(2)}, u32[]{:S(2)}) async-start(f32[16,6,4,128]{3,2,1,0:T(4,128)} %bitcast.138), calls=%async_computation.1 | async-start | bytes 393216 | tf_op jit(solution)/shard_map/while/body/eval_jaxpr/all_to_all | solution.py:123
  115.7 11.7 %all-to-all-start = ((f32[16,6,4,128]{3,2,1,0:T(4,128)}), f32[16,6,4,128]{3,2,1,0:T(4,128)S(1)}, u32[]{:S(2)}, u32[]{:S(2)}) async-start(f32[16,6,4,128]{3,2,1,0:T(4,128)} %bitcast.136), calls=%async_computation | async-start | bytes 393216 | tf_op jit(solution)/shard_map/while/body/eval_jaxpr/all_to_all | solution.py:123
  128.9 11.6 %all-to-all-start.1 = ((f32[16,6,4,128]{3,2,1,0:T(4,128)}), f32[16,6,4,128]{3,2,1,0:T(4,128)S(1)}, u32[]{:S(2)}, u32[]{:S(2)}) async-start(f32[16,6,4,128]{3,2,1,0:T(4,128)} %bitcast.138), calls=%async_computation.1 | async-start | bytes 393216 | tf_op jit(solution)/shard_map/while/body/eval_jaxpr/all_to_all | solution.py:123
  144.1 11.7 %all-to-all-start = ((f32[16,6,4,128]{3,2,1,0:T(4,128)}), f32[16,6,4,128]{3,2,1,0:T(4,128)S(1)}, u32[]{:S(2)}, u32[]{:S(2)}) async-start(f32[16,6,4,128]{3,2,1,0:T(4,128)} %bitcast.136), calls=%async_computation | async-start | bytes 393216 | tf_op jit(solution)/shard_map/while/body/eval_jaxpr/all_to_all | solution.py:123
  157.3 11.6 %all-to-all-start.1 = ((f32[16,6,4,128]{3,2,1,0:T(4,128)}), f32[16,6,4,128]{3,2,1,0:T(4,128)S(1)}, u32[]{:S(2)}, u32[]{:S(2)}) async-start(f32[16,6,4,128]{3,2,1,0:T(4,128)} %bitcast.138), calls=%async_computation.1 | async-start | bytes 393216 | tf_op jit(solution)/shard_map/while/body/eval_jaxpr/all_to_all | solution.py:123
  172.5 11.8 %all-to-all-start = ((f32[16,6,4,128]{3,2,1,0:T(4,128)}), f32[16,6,4,128]{3,2,1,0:T(4,128)S(1)}, u32[]{:S(2)}, u32[]{:S(2)}) async-start(f32[16,6,4,128]{3,2,1,0:T(4,128)} %bitcast.136), calls=%async_computation | async-start | bytes 393216 | tf_op jit(solution)/shard_map/while/body/eval_jaxpr/all_to_all | solution.py:123
  185.8 11.6 %all-to-all-start.1 = ((f32[16,6,4,128]{3,2,1,0:T(4,128)}), f32[16,6,4,128]{3,2,1,0:T(4,128)S(1)}, u32[]{:S(2)}, u32[]{:S(2)}) async-start(f32[16,6,4,128]{3,2,1,0:T(4,128)} %bitcast.138), calls=%async_computation.1 | async-start | bytes 393216 | tf_op jit(solution)/shard_map/while/body/eval_jaxpr/all_to_all | solution.py:123
  201.0 11.9 %all-to-all-start = ((f32[16,6,4,128]{3,2,1,0:T(4,128)}), f32[16,6,4,128]{3,2,1,0:T(4,128)S(1)}, u32[]{:S(2)}, u32[]{:S(2)}) async-start(f32[16,6,4,128]{3,2,1,0:T(4,128)} %bitcast.136), calls=%async_computation | async-start | bytes 393216 | tf_op jit(solution)/shard_map/while/body/eval_jaxpr/all_to_all | solution.py:123
  214.4 12.7 %all-to-all-start.1 = ((f32[16,6,4,128]{3,2,1,0:T(4,128)}), f32[16,6,4,128]{3,2,1,0:T(4,128)S(1)}, u32[]{:S(2)}, u32[]{:S(2)}) async-start(f32[16,6,4,128]{3,2,1,0:T(4,128)} %bitcast.138), calls=%async_computation.1 | async-start | bytes 393216 | tf_op jit(solution)/shard_map/while/body/eval_jaxpr/all_to_all | solution.py:123
  230.7 12.8 %all-to-all-start = ((f32[16,6,4,128]{3,2,1,0:T(4,128)}), f32[16,6,4,128]{3,2,1,0:T(4,128)S(1)}, u32[]{:S(2)}, u32[]{:S(2)}) async-start(f32[16,6,4,128]{3,2,1,0:T(4,128)} %bitcast.136), calls=%async_computation | async-start | bytes 393216 | tf_op jit(solution)/shard_map/while/body/eval_jaxpr/all_to_all | solution.py:123
  245.1 11.7 %all-to-all-start.1 = ((f32[16,6,4,128]{3,2,1,0:T(4,128)}), f32[16,6,4,128]{3,2,1,0:T(4,128)S(1)}, u32[]{:S(2)}, u32[]{:S(2)}) async-start(f32[16,6,4,128]{3,2,1,0:T(4,128)} %bitcast.138), calls=%async_computation.1 | async-start | bytes 393216 | tf_op jit(solution)/shard_map/while/body/eval_jaxpr/all_to_all | solution.py:123
  258.7 28.3 %copy-start.4 = (bf16[24,512]{1,0:T(8,128)(2,1)S(1)}, bf16[24,512]{1,0:T(8,128)(2,1)}, u32[]{:S(2)}) copy-start(bf16[24,512]{1,0:T(8,128)(2,1)} %param.21) | copy-start | bytes 73732
  272.6 11.6 %all-to-all-start.5 = ((f32[16,6,4,128]{3,2,1,0:T(4,128)}), f32[16,6,4,128]{3,2,1,0:T(4,128)S(1)}, u32[]{:S(2)}, u32[]{:S(2)}) async-start(f32[16,6,4,128]{3,2,1,0:T(4,128)} %bitcast.49), calls=%async_computation.5 | async-start | bytes 393216 | tf_op jit(solution)/shard_map/all_to_all | solution.py:123
  285.7 1.3 collective-permute-start

commit v2 on v1

--- a/solution.py
+++ b/solution.py
@@ -1,8 +1,6 @@
 import jax
 import jax.numpy as jnp
 from jax import lax
-from jax.experimental import pallas as pl
-from jax.experimental.pallas import tpu as pltpu
 from jax.sharding import PartitionSpec as P
 
 KW = 4
@@ -16,26 +14,6 @@
 
 def own_matvec(matrices, vectors):
     return jnp.sum(matrices * vectors[:, :, None, :], axis=3)
-
-
-def project_kernel(rows_ref, weight_ref, out_ref):
-    out_ref[...] = jnp.dot(rows_ref[...], weight_ref[...], preferred_element_type=jnp.float32)
-
-
-def project(rows, weight):
-    row_count, depth = rows.shape
-    width = weight.shape[1]
-    return pl.pallas_call(
-        project_kernel,
-        out_shape=jax.ShapeDtypeStruct((row_count, width), jnp.float32),
-        in_specs=[pl.BlockSpec(memory_space=pltpu.VMEM)] * 2,
-        out_specs=pl.BlockSpec(memory_space=pltpu.VMEM),
-        cost_estimate=pl.CostEstimate(
-            flops=2 * row_count * depth * width,
-            bytes_accessed=2 * (row_count * depth + depth * width) + 4 * row_count * width,
-            transcendentals=0,
-        ),
-    )(rows, weight)
 
 
 def on_device(
@@ -66,8 +44,10 @@
     row_count, model_width = gathered.shape
     head_count = qkv_weight.shape[1]
     head_size = qkv_weight.shape[3]
-    projected = project(
-        normed, qkv_weight.reshape(model_width, head_count * 3 * head_size)
+    projected = jnp.dot(
+        normed,
+        qkv_weight.reshape(model_width, head_count * 3 * head_size),
+        preferred_element_type=jnp.float32,
     ).reshape(row_count, head_count, 3, head_size)
     mixing = conv_weight[0] * projected
     for offset in range(1, KW):
@@ -119,9 +99,9 @@
         return jnp.take(padded, source, axis=0)
 
     def exchange(slots):
-        shaped = slots.reshape((peer_count, capacity) + slots.shape[1:])
+        shaped = slots.astype(jnp.bfloat16).reshape((peer_count, capacity) + slots.shape[1:])
         moved = lax.all_to_all(shaped, "req", split_axis=0, concat_axis=0, tiled=True)
-        return moved.reshape(slots.shape)
+        return moved.reshape(slots.shape).astype(jnp.float32)
 
     def unpack(slots):
         taken = jnp.take(slots, slot_of, axis=0)

time: 290 us -> 279 us (0.962)
  blocking collectives: 13.9 us -> 2.35 us
  local copies, waits for them, and re-layouts: 36.5 us -> 31.1 us
  starting transfers between devices: 67.4 us -> 71.1 us
  Pallas kernels: 3.23 us -> 0 us
    all_to_all x1 -> x0, blocking collectives: 11.4 us -> none  [exchange(): lax.all_to_all(shaped, 'req', split_axis=0, concat_axis=0, tiled=True)]
    transpose x9 -> x0, local copies, waits for them, and re-layouts: 7.23 us -> none  [owner_apply(): return jnp.einsum('gshj,ghij->shi', split, states, precision=highest)]
    reshape x4 -> x0, local copies, waits for them, and re-layouts: 6.52 us -> none  [the longest x1 4.69 us: on_device(): qkv_weight.reshape(model_width, head_count * 3 * head_size)]
    select_n x17 -> x8, other arithmetic: 6.26 us -> 0.03 us  [pack(): return jnp.take(padded, source, axis=0)]
    convert_element_type x0 -> x11, local copies, waits for them, and re-layouts: none -> 6.21 us  [the longest x9 6.1 us: exchange(): slots.astype(jnp.bfloat16).reshape((peer_count, capacity) + slots.shape[1:])]
    convert_element_type x3 -> x26, other arithmetic: 0.8 us -> 6.76 us  [the longest x8 6.35 us: exchange(): slots.astype(jnp.bfloat16).reshape((peer_count, capacity) + slots.shape[1:])]
    all_to_all x17 -> x18, starting transfers between devices: 67.4 us -> 71 us  [exchange(): lax.all_to_all(shaped, 'req', split_axis=0, concat_axis=0, tiled=True)]
    pallas_call x1 -> x0, Pallas kernels: 3.23 us -> none  [project(): pl.pallas_call(project_kernel, out_shape=jax.ShapeDtypeStruct((row_count,...]
  transfers between devices with their start and end apart: 18 -> 19, of which waited for: 18 -> 19; matrix products, arithmetic and copies ran while one was open for 15% -> 14% of each run, Pallas kernels for 0% -> 0%
where the time goes in v2:
time: 279 us; the launch traced here: 277 us
  waiting for transfers between devices  102 us (37%)
  starting transfers between devices  71.1 us (25%)
  other arithmetic  60.2 us (22%)
  local copies, waits for them, and re-layouts  31.1 us (11%)
  matrix products  9.41 us (3%)
    all_to_all x18, waiting for transfers between devices, exchange(): lax.all_to_all(shaped, 'req', split_axis=0, concat_axis=0, tiled=True)  101 us
    all_to_all x18, starting transfers between devices, exchange(): lax.all_to_all(shaped, 'req', split_axis=0, concat_axis=0, tiled=True)  71 us
    reduce_sum x9, other arithmetic, own_matvec(): return jnp.sum(matrices * vectors[:, :, None, :], axis=3)  40.4 us
    convert_element_type x8, other arithmetic, exchange(): slots.astype(jnp.bfloat16).reshape((peer_count, capacity) + slots.shape[1:])  6.35 us
    gather x9, local copies, waits for them, and re-layouts, pack(): return jnp.take(padded, source, axis=0)  6.32 us
    convert_element_type x9, local copies, waits for them, and re-layouts, exchange(): slots.astype(jnp.bfloat16).reshape((peer_count, capacity) + slots.shape[1:])  6.1 us
    unnamed x19, local copies, waits for them, and re-layouts  6.07 us
    dot_general x9, matrix products, owner_apply(): return jnp.einsum('gshj,ghij->shi', split, states, precision=highest)  5.99 us
  transfers between devices with their start and end apart: 19, of which 19 were waited for; matrix products, arithmetic and copies ran while one was open for 14% of the time, Pallas kernels for 0%

profile of v2, /device:TPU:0, one launch (start us, length us, event | category | flops | bytes accessed | tf_op | source)
XLA Modules:
  0.0 277.2 jit_solution(12975878801151457593)
XLA Ops:
  6.6 6.0 %copy.161 = bf16[1024,4,3,128]{0,3,2,1:T(8,128)(2,1)} copy(bf16[1024,4,3,128]{3,1,2,0:T(4,128)(2,1)} %param.23) | data formatting | bytes 6291456 | tf_op args[2]
  18.1 4.5 %multiply_reduce_fusion.5 = f32[24,4,128]{2,1,0:T(4,128)S(1)} fusion(f32[24,4,128,128]{3,2,1,0:T(8,128)} %param.29, f32[24,4,128]{2,1,0:T(4,128)S(1)} %copy.177), kind=kLoop, calls=%fused_computation.46 | loop fusion | flops 3133440 | bytes 6389760 | tf_op jit(solution)/shard_map/reduce_sum | solution.py:16
  22.6 8.2 %all-to-all-start.2 = ((bf16[16,6,5,128]{3,1,2,0:T(8,128)(2,1)}), bf16[16,6,5,128]{3,1,2,0:T(8,128)(2,1)S(1)}, u32[]{:S(2)}, u32[]{:S(2)}) async-start(bf16[16,6,5,128]{3,1,2,0:T(8,128)(2,1)} %copy.170), calls=%async_computation.2 | async-start | bytes 327680 | tf_op jit(solution)/shard_map/all_to_all | solution.py:103
  31.2 7.8 %all-to-all-done.2 = bf16[16,6,5,128]{3,1,2,0:T(8,128)(2,1)S(1)} async-done(((bf16[16,6,5,128]{3,1,2,0:T(8,128)(2,1)}), bf16[16,6,5,128]{3,1,2,0:T(8,128)(2,1)S(1)}, u32[]{:S(2)}, u32[]{:S(2)}) %all-to-all-start.2) | async-done | bytes 122912 | tf_op jit(solution)/shard_map/all_to_all | solution.py:103
  44.2 7.6 %all-to-all-done.3 = bf16[16,6,4,128]{3,2,1,0:T(4,128)(2,1)S(1)} async-done(((bf16[16,6,4,128]{3,2,1,0:T(4,128)(2,1)}), bf16[16,6,4,128]{3,2,1,0:T(4,128)(2,1)S(1)}, u32[]{:S(2)}, u32[]{:S(2)}) %all-to-all-start.3) | async-done | bytes 98336 | tf_op jit(solution)/shard_map/all_to_all | solution.py:103
  53.2 195.5 %while.16 = (s32[]{:T(128)}, f32[24,4,128]{2,1,0:T(4,128)S(1)}, f32[24,4,128]{2,1,0:T(4,128)S(1)}, f32[24,4,128]{2,1,0:T(4,128)S(1)}, f32[24,4,1]{0,1,2:T(4,128)...) while((s32[]{:T(128)}, f32[24,4,128]{2,1,0:T(4,128)S(1)}, ...), condition=%wide.region_17.20_spmd, body=%wide.region_12.19_spmd.sunk | while | flops 154782992 | bytes 10599719 | solution.py:145
  58.3 4.5 %multiply_reduce_fusion.15 = f32[24,4,128]{2,1,0:T(4,128)S(1)} fusion(f32[24,4,128,128]{3,2,1,0:T(8,128)} %get-tuple-element.435, f32[24,4,128]{2,1,0:T(4,128)S(1)} %get-tuple-element.406), kind=kLoop, calls=%fused_computation.7.clone.1 | loop fusion | flops 3133440 | bytes 6389760 | tf_op jit(solution)/shard_map/while/body/eval_jaxpr/reduce_sum | solution.py:16
  67.4 4.0 %all-to-all-start.1 = ((bf16[16,6,4,128]{3,2,1,0:T(4,128)(2,1)}), bf16[16,6,4,128]{3,2,1,0:T(4,128)(2,1)S(1)}, u32[]{:S(2)}, u32[]{:S(2)}) async-start(bf16[16,6,4,128]{3,2,1,0:T(4,128)(2,1)} %bitcast.201), calls=%async_computation.1 | async-start | bytes 196608 | tf_op jit(solution)/shard_map/while/body/eval_jaxpr/all_to_all | solution.py:103
  71.4 7.7 %all-to-all-done.1 = bf16[16,6,4,128]{3,2,1,0:T(4,128)(2,1)S(1)} async-done(((bf16[16,6,4,128]{3,2,1,0:T(4,128)(2,1)}), bf16[16,6,4,128]{3,2,1,0:T(4,128)(2,1)S(1)}, u32[]{:S(2)}, u32[]{:S(2)}) %all-to-all-start.1) | async-done | bytes 98336 | tf_op jit(solution)/shard_map/while/body/eval_jaxpr/all_to_all | solution.py:103
  86.2 4.5 %multiply_reduce_fusion.15 = f32[24,4,128]{2,1,0:T(4,128)S(1)} fusion(f32[24,4,128,128]{3,2,1,0:T(8,128)} %get-tuple-element.435, f32[24,4,128]{2,1,0:T(4,128)S(1)} %get-tuple-element.406), kind=kLoop, calls=%fused_computation.7.clone.1 | loop fusion | flops 3133440 | bytes 6389760 | tf_op jit(solution)/shard_map/while/body/eval_jaxpr/reduce_sum | solution.py:16
  95.2 4.0 %all-to-all-start.1 = ((bf16[16,6,4,128]{3,2,1,0:T(4,128)(2,1)}), bf16[16,6,4,128]{3,2,1,0:T(4,128)(2,1)S(1)}, u32[]{:S(2)}, u32[]{:S(2)}) async-start(bf16[16,6,4,128]{3,2,1,0:T(4,128)(2,1)} %bitcast.201), calls=%async_computation.1 | async-start | bytes 196608 | tf_op jit(solution)/shard_map/while/body/eval_jaxpr/all_to_all | solution.py:103
  99.3 7.7 %all-to-all-done.1 = bf16[16,6,4,128]{3,2,1,0:T(4,128)(2,1)S(1)} async-done(((bf16[16,6,4,128]{3,2,1,0:T(4,128)(2,1)}), bf16[16,6,4,128]{3,2,1,0:T(4,128)(2,1)S(1)}, u32[]{:S(2)}, u32[]{:S(2)}) %all-to-all-start.1) | async-done | bytes 98336 | tf_op jit(solution)/shard_map/while/body/eval_jaxpr/all_to_all | solution.py:103
  114.0 4.5 %multiply_reduce_fusion.15 = f32[24,4,128]{2,1,0:T(4,128)S(1)} fusion(f32[24,4,128,128]{3,2,1,0:T(8,128)} %get-tuple-element.435, f32[24,4,128]{2,1,0:T(4,128)S(1)} %get-tuple-element.406), kind=kLoop, calls=%fused_computation.7.clone.1 | loop fusion | flops 3133440 | bytes 6389760 | tf_op jit(solution)/shard_map/while/body/eval_jaxpr/reduce_sum | solution.py:16
  123.1 4.0 %all-to-all-start.1 = ((bf16[16,6,4,128]{3,2,1,0:T(4,128)(2,1)}), bf16[16,6,4,128]{3,2,1,0:T(4,128)(2,1)S(1)}, u32[]{:S(2)}, u32[]{:S(2)}) async-start(bf16[16,6,4,128]{3,2,1,0:T(4,128)(2,1)} %bitcast.201), calls=%async_computation.1 | async-start | bytes 196608 | tf_op jit(solution)/shard_map/while/body/eval_jaxpr/all_to_all | solution.py:103
  127.2 7.7 %all-to-all-done.1 = bf16[16,6,4,128]{3,2,1,0:T(4,128)(2,1)S(1)} async-done(((bf16[16,6,4,128]{3,2,1,0:T(4,128)(2,1)}), bf16[16,6,4,128]{3,2,1,0:T(4,128)(2,1)S(1)}, u32[]{:S(2)}, u32[]{:S(2)}) %all-to-all-start.1) | async-done | bytes 98336 | tf_op jit(solution)/shard_map/while/body/eval_jaxpr/all_to_all | solution.py:103
  138.4 3.5 %all-to-all-start = ((bf16[16,6,4,128]{3,2,1,0:T(4,128)(2,1)}), bf16[16,6,4,128]{3,2,1,0:T(4,128)(2,1)S(1)}, u32[]{:S(2)}, u32[]{:S(2)}) async-start(bf16[16,6,4,128]{3,2,1,0:T(4,128)(2,1)} %bitcast.197), calls=%async_computation | async-start | bytes 196608 | tf_op jit(solution)/shard_map/while/body/eval_jaxpr/all_to_all | solution.py:103
  141.9 4.5 %multiply_reduce_fusion.15 = f32[24,4,128]{2,1,0:T(4,128)S(1)} fusion(f32[24,4,128,128]{3,2,1,0:T(8,128)} %get-tuple-element.435, f32[24,4,128]{2,1,0:T(4,128)S(1)} %get-tuple-element.406), kind=kLoop, calls=%fused_computation.7.clone.1 | loop fusion | flops 3133440 | bytes 6389760 | tf_op jit(solution)/shard_map/while/body/eval_jaxpr/reduce_sum | solution.py:16
  151.0 4.0 %all-to-all-start.1 = ((bf16[16,6,4,128]{3,2,1,0:T(4,128)(2,1)}), bf16[16,6,4,128]{3,2,1,0:T(4,128)(2,1)S(1)}, u32[]{:S(2)}, u32[]{:S(2)}) async-start(bf16[16,6,4,128]{3,2,1,0:T(4,128)(2,1)} %bitcast.201), calls=%async_computation.1 | async-start | bytes 196608 | tf_op jit(solution)/shard_map/while/body/eval_jaxpr/all_to_all | solution.py:103
  155.0 7.7 %all-to-all-done.1 = bf16[16,6,4,128]{3,2,1,0:T(4,128)(2,1)S(1)} async-done(((bf16[16,6,4,128]{3,2,1,0:T(4,128)(2,1)}), bf16[16,6,4,128]{3,2,1,0:T(4,128)(2,1)S(1)}, u32[]{:S(2)}, u32[]{:S(2)}) %all-to-all-start.1) | async-done | bytes 98336 | tf_op jit(solution)/shard_map/while/body/eval_jaxpr/all_to_all | solution.py:103
  169.8 4.5 %multiply_reduce_fusion.15 = f32[24,4,128]{2,1,0:T(4,128)S(1)} fusion(f32[24,4,128,128]{3,2,1,0:T(8,128)} %get-tuple-element.435, f32[24,4,128]{2,1,0:T(4,128)S(1)} %get-tuple-element.406), kind=kLoop, calls=%fused_computation.7.clone.1 | loop fusion | flops 3133440 | bytes 6389760 | tf_op jit(solution)/shard_map/while/body/eval_jaxpr/reduce_sum | solution.py:16
  178.9 4.0 %all-to-all-start.1 = ((bf16[16,6,4,128]{3,2,1,0:T(4,128)(2,1)}), bf16[16,6,4,128]{3,2,1,0:T(4,128)(2,1)S(1)}, u32[]{:S(2)}, u32[]{:S(2)}) async-start(bf16[16,6,4,128]{3,2,1,0:T(4,128)(2,1)} %bitcast.201), calls=%async_computation.1 | async-start | bytes 196608 | tf_op jit(solution)/shard_map/while/body/eval_jaxpr/all_to_all | solution.py:103
  182.9 7.7 %all-to-all-done.1 = bf16[16,6,4,128]{3,2,1,0:T(4,128)(2,1)S(1)} async-done(((bf16[16,6,4,128]{3,2,1,0:T(4,128)(2,1)}), bf16[16,6,4,128]{3,2,1,0:T(4,128)(2,1)S(1)}, u32[]{:S(2)}, u32[]{:S(2)}) %all-to-all-start.1) | async-done | bytes 98336 | tf_op jit(solution)/shard_map/while/body/eval_jaxpr/all_to_all | solution.py:103
  194.1 3.5 %all-to-all-start = ((bf16[16,6,4,128]{3,2,1,0:T(4,128)(2,1)}), bf16[16,6,4,128]{3,2,1,0:T(4,128)(2,1)S(1)}, u32[]{:S(2)}, u32[]{:S(2)}) async-start(bf16[16,6,4,128]{3,2,1,0:T(4,128)(2,1)} %bitcast.197), calls=%async_computation | async-start | bytes 196608 | tf_op jit(solution)/shard_map/while/body/eval_jaxpr/all_to_all | solution.py:103
  197.6 4.5 %multiply_reduce_fusion.15 = f32[24,4,128]{2,1,0:T(4,128)S(1)} fusion(f32[24,4,128,128]{3,2,1,0:T(8,128)} %get-tuple-element.435, f32[24,4,128]{2,1,0:T(4,128)S(1)} %get-tuple-element.406), kind=kLoop, calls=%fused_computation.7.clone.1 | loop fusion | flops 3133440 | bytes 6389760 | tf_op jit(solution)/shard_map/while/body/eval_jaxpr/reduce_sum | solution.py:16
  206.8 3.9 %all-to-all-start.1 = ((bf16[16,6,4,128]{3,2,1,0:T(4,128)(2,1)}), bf16[16,6,4,128]{3,2,1,0:T(4,128)(2,1)S(1)}, u32[]{:S(2)}, u32[]{:S(2)}) async-start(bf16[16,6,4,128]{3,2,1,0:T(4,128)(2,1)} %bitcast.201), calls=%async_computation.1 | async-start | bytes 196608 | tf_op jit(solution)/shard_map/while/body/eval_jaxpr/all_to_all | solution.py:103
  210.8 7.7 %all-to-all-done.1 = bf16[16,6,4,128]{3,2,1,0:T(4,128)(2,1)S(1)} async-done(((bf16[16,6,4,128]{3,2,1,0:T(4,128)(2,1)}), bf16[16,6,4,128]{3,2,1,0:T(4,128)(2,1)S(1)}, u32[]{:S(2)}, u32[]{:S(2)}) %all-to-all-start.1) | async-done | bytes 98336 | tf_op jit(solution)/shard_map/while/body/eval_jaxpr/all_to_all | solution.py:103
  225.5 4.5 %multiply_reduce_fusion.15 = f32[24,4,128]{2,1,0:T(4,128)S(1)} fusion(f32[24,4,128,128]{3,2,1,0:T(8,128)} %get-tuple-element.435, f32[24,4,128]{2,1,0:T(4,128)S(1)} %get-tuple-element.406), kind=kLoop, calls=%fused_computation.7.clone.1 | loop fusion | flops 3133440 | bytes 6389760 | tf_op jit(solution)/shard_map/while/body/eval_jaxpr/reduce_sum | solution.py:16
  234.9 3.7 %all-to-all-start.1 = ((bf16[16,6,4,128]{3,2,1,0:T(4,128)(2,1)}), bf16[16,6,4,128]{3,2,1,0:T(4,128)(2,1)S(1)}, u32[]{:S(2)}, u32[]{:S(2)}) async-start(bf16[16,6,4,128]{3,2,1,0:T(4,128)(2,1)} %bitcast.201), calls=%async_computation.1 | async-start | bytes 196608 | tf_op jit(solution)/shard_map/while/body/eval_jaxpr/all_to_all | solution.py:103
  238.7 8.0 %all-to-all-done.1 = bf16[16,6,4,128]{3,2,1,0:T(4,128)(2,1)S(1)} async-done(((bf16[16,6,4,128]{3,2,1,0:T(4,128)(2,1)}), bf16[16,6,4,128]{3,2,1,0:T(4,128)(2,1)S(1)}, u32[]{:S(2)}, u32[]{:S(2)}) %all-to-all-start.1) | async-done | bytes 98336 | tf_op jit(solution)/shard_map/while/body/eval_jaxpr/all_to_all | solution.py:103
  250.2 3.5 %all-to-all-start.4 = ((bf16[16,6,4,128]{3,2,1,0:T(4,128)(2,1)}), bf16[16,6,4,128]{3,2,1,0:T(4,128)(2,1)S(1)}, u32[]{:S(2)}, u32[]{:S(2)}) async-start(bf16[16,6,4,128]{3,2,1,0:T(4,128)(2,1)} %bitcast.49), calls=%async_computation.4 | async-start | bytes 196608 | tf_op jit(solution)/shard_map/all_to_all | solution.py:103
  253.8 7.6 %all-to-all-done.4 = bf16[16,6,4,128]{3,2,1,0:T(4,128)(2,1)S(1)} async-done(((bf16[16,6,4,128]{3,2,1,0:T(4,128)(2,1)}), bf16[16,6,4,128]{3,2,1,0:T(4,128)(2,1)S(1)}, u32[]{:S(2)}, u32[]{:S(2)}) %all-to-all-start.4) | async-done | bytes 98336 | tf_op jit(solution)/shard_map/all_to_all | solution.py:103
  266.4 4.5 %multiply_reduce_fusion.4 = f32[24,4,128]{2,1,0:T(4,128)S(1)} fusion(f32[24,4,128,128]{3,2,1,0:T(8,128)} %param.30, f32[24,4,128]{2,1,0:T(4,128)S(1)} %get-tuple-element.94), kind=kLoop, calls=%fused_computation.45 | loop fusion | flops 3133440 | bytes 6389760 | tf_op jit(solution)/shard_map/reduce_sum | solution.py:16
  (301 shorter events, 106.1 us)
Async XLA Ops:
  0.0 274.9 %copy-start = (bf16[4,128,1024]{2,1,0:T(8,128)(2,1)S(1)}, bf16[4,128,1024]{2,1,0:T(8,128)(2,1)}, u32[]{:S(2)}) copy-start(bf16[4,128,1024]{2,1,0:T(8,128)(2,1)} %param.35) | copy-start | bytes 3145732
  0.0 12.6 %copy-start.6 = (f32[1024]{0:T(1024)S(1)}, f32[1024]{0:T(1024)}, u32[]{:S(2)}) copy-start(f32[1024]{0:T(1024)} %param.22) | copy-start | bytes 12292
  12.6 18.3 %copy-start.5 = (bf16[1024,2,4]{0,2,1:T(4,128)(2,1)S(1)}, bf16[1024,2,4]{0,2,1:T(4,128)(2,1)}, u32[]{:S(2)}) copy-start(bf16[1024,2,4]{0,2,1:T(4,128)(2,1)} %param.26) | copy-start | bytes 49156
  12.6 18.3 %copy-start.1 = (f32[2,4,128,128]{3,2,1,0:T(8,128)S(1)}, f32[2,4,128,128]{3,2,1,0:T(8,128)}, u32[]{:S(2)}) copy-start(f32[2,4,128,128]{3,2,1,0:T(8,128)} %param.31) | copy-start | bytes 1572868
  17.4 35.1 %copy-start.4 = (f32[24,4]{0,1:T(4,128)S(1)}, f32[24,4]{0,1:T(4,128)}, u32[]{:S(2)}) copy-start(f32[24,4]{0,1:T(4,128)} %param.27) | copy-start | bytes 1156
  17.4 35.1 %copy-start.7 = (f32[4]{0:T(128)S(1)}, f32[4]{0:T(128)}, u32[]{:S(2)}) copy-start(f32[4]{0:T(128)} %param.28) | copy-start | bytes 52
  22.6 16.4 %all-to-all-start.2 = ((bf16[16,6,5,128]{3,1,2,0:T(8,128)(2,1)}), bf16[16,6,5,128]{3,1,2,0:T(8,128)(2,1)S(1)}, u32[]{:S(2)}, u32[]{:S(2)}) async-start(bf16[16,6,5,128]{3,1,2,0:T(8,128)(2,1)} %copy.170), calls=%async_computation.2 | async-start | bytes 327680 | tf_op jit(solution)/shard_map/all_to_all | solution.py:103
  40.7 11.1 %all-to-all-start.3 = ((bf16[16,6,4,128]{3,2,1,0:T(4,128)(2,1)}), bf16[16,6,4,128]{3,2,1,0:T(4,128)(2,1)S(1)}, u32[]{:S(2)}, u32[]{:S(2)}) async-start(bf16[16,6,4,128]{3,2,1,0:T(4,128)(2,1)} %bitcast.39), calls=%async_computation.3 | async-start | bytes 196608 | tf_op jit(solution)/shard_map/all_to_all | solution.py:103
  53.2 208.3 %copy-start.2 = (f32[2,4,128,128]{3,2,1,0:T(8,128)S(1)}, f32[2,4,128,128]{3,2,1,0:T(8,128)}, u32[]{:S(2)}) copy-start(f32[2,4,128,128]{3,2,1,0:T(8,128)} %param.32) | copy-start | bytes 1572868
  54.8 11.1 %all-to-all-start = ((bf16[16,6,4,128]{3,2,1,0:T(4,128)(2,1)}), bf16[16,6,4,128]{3,2,1,0:T(4,128)(2,1)S(1)}, u32[]{:S(2)}, u32[]{:S(2)}) async-start(bf16[16,6,4,128]{3,2,1,0:T(4,128)(2,1)} %bitcast.197), calls=%async_computation | async-start | bytes 196608 | tf_op jit(solution)/shard_map/while/body/eval_jaxpr/all_to_all | solution.py:103
  67.4 11.7 %all-to-all-start.1 = ((bf16[16,6,4,128]{3,2,1,0:T(4,128)(2,1)}), bf16[16,6,4,128]{3,2,1,0:T(4,128)(2,1)S(1)}, u32[]{:S(2)}, u32[]{:S(2)}) async-start(bf16[16,6,4,128]{3,2,1,0:T(4,128)(2,1)} %bitcast.201), calls=%async_computation.1 | async-start | bytes 196608 | tf_op jit(solution)/shard_map/while/body/eval_jaxpr/all_to_all | solution.py:103
  82.6 11.1 %all-to-all-start = ((bf16[16,6,4,128]{3,2,1,0:T(4,128)(2,1)}), bf16[16,6,4,128]{3,2,1,0:T(4,128)(2,1)S(1)}, u32[]{:S(2)}, u32[]{:S(2)}) async-start(bf16[16,6,4,128]{3,2,1,0:T(4,128)(2,1)} %bitcast.197), calls=%async_computation | async-start | bytes 196608 | tf_op jit(solution)/shard_map/while/body/eval_jaxpr/all_to_all | solution.py:103
  95.2 11.7 %all-to-all-start.1 = ((bf16[16,6,4,128]{3,2,1,0:T(4,128)(2,1)}), bf16[16,6,4,128]{3,2,1,0:T(4,128)(2,1)S(1)}, u32[]{:S(2)}, u32[]{:S(2)}) async-start(bf16[16,6,4,128]{3,2,1,0:T(4,128)(2,1)} %bitcast.201), calls=%async_computation.1 | async-start | bytes 196608 | tf_op jit(solution)/shard_map/while/body/eval_jaxpr/all_to_all | solution.py:103
  110.5 11.1 %all-to-all-start = ((bf16[16,6,4,128]{3,2,1,0:T(4,128)(2,1)}), bf16[16,6,4,128]{3,2,1,0:T(4,128)(2,1)S(1)}, u32[]{:S(2)}, u32[]{:S(2)}) async-start(bf16[16,6,4,128]{3,2,1,0:T(4,128)(2,1)} %bitcast.197), calls=%async_computation | async-start | bytes 196608 | tf_op jit(solution)/shard_map/while/body/eval_jaxpr/all_to_all | solution.py:103
  123.1 11.7 %all-to-all-start.1 = ((bf16[16,6,4,128]{3,2,1,0:T(4,128)(2,1)}), bf16[16,6,4,128]{3,2,1,0:T(4,128)(2,1)S(1)}, u32[]{:S(2)}, u32[]{:S(2)}) async-start(bf16[16,6,4,128]{3,2,1,0:T(4,128)(2,1)} %bitcast.201), calls=%async_computation.1 | async-start | bytes 196608 | tf_op jit(solution)/shard_map/while/body/eval_jaxpr/all_to_all | solution.py:103
  138.4 11.1 %all-to-all-start = ((bf16[16,6,4,128]{3,2,1,0:T(4,128)(2,1)}), bf16[16,6,4,128]{3,2,1,0:T(4,128)(2,1)S(1)}, u32[]{:S(2)}, u32[]{:S(2)}) async-start(bf16[16,6,4,128]{3,2,1,0:T(4,128)(2,1)} %bitcast.197), calls=%async_computation | async-start | bytes 196608 | tf_op jit(solution)/shard_map/while/body/eval_jaxpr/all_to_all | solution.py:103
  151.0 11.7 %all-to-all-start.1 = ((bf16[16,6,4,128]{3,2,1,0:T(4,128)(2,1)}), bf16[16,6,4,128]{3,2,1,0:T(4,128)(2,1)S(1)}, u32[]{:S(2)}, u32[]{:S(2)}) async-start(bf16[16,6,4,128]{3,2,1,0:T(4,128)(2,1)} %bitcast.201), calls=%async_computation.1 | async-start | bytes 196608 | tf_op jit(solution)/shard_map/while/body/eval_jaxpr/all_to_all | solution.py:103
  166.3 11.2 %all-to-all-start = ((bf16[16,6,4,128]{3,2,1,0:T(4,128)(2,1)}), bf16[16,6,4,128]{3,2,1,0:T(4,128)(2,1)S(1)}, u32[]{:S(2)}, u32[]{:S(2)}) async-start(bf16[16,6,4,128]{3,2,1,0:T(4,128)(2,1)} %bitcast.197), calls=%async_computation | async-start | bytes 196608 | tf_op jit(solution)/shard_map/while/body/eval_jaxpr/all_to_all | solution.py:103
  178.9 11.7 %all-to-all-start.1 = ((bf16[16,6,4,128]{3,2,1,0:T(4,128)(2,1)}), bf16[16,6,4,128]{3,2,1,0:T(4,128)(2,1)S(1)}, u32[]{:S(2)}, u32[]{:S(2)}) async-start(bf16[16,6,4,128]{3,2,1,0:T(4,128)(2,1)} %bitcast.201), calls=%async_computation.1 | async-start | bytes 196608 | tf_op jit(solution)/shard_map/while/body/eval_jaxpr/all_to_all | solution.py:103
  194.1 11.3 %all-to-all-start = ((bf16[16,6,4,128]{3,2,1,0:T(4,128)(2,1)}), bf16[16,6,4,128]{3,2,1,0:T(4,128)(2,1)S(1)}, u32[]{:S(2)}, u32[]{:S(2)}) async-start(bf16[16,6,4,128]{3,2,1,0:T(4,128)(2,1)} %bitcast.197), calls=%async_computation | async-start | bytes 196608 | tf_op jit(solution)/shard_map/while/body/eval_jaxpr/all_to_all | solution.py:103
  206.8 11.6 %all-to-all-start.1 = ((bf16[16,6,4,128]{3,2,1,0:T(4,128)(2,1)}), bf16[16,6,4,128]{3,2,1,0:T(4,128)(2,1)S(1)}, u32[]{:S(2)}, u32[]{:S(2)}) async-start(bf16[16,6,4,128]{3,2,1,0:T(4,128)(2,1)} %bitcast.201), calls=%async_computation.1 | async-start | bytes 196608 | tf_op jit(solution)/shard_map/while/body/eval_jaxpr/all_to_all | solution.py:103
  222.0 11.5 %all-to-all-start = ((bf16[16,6,4,128]{3,2,1,0:T(4,128)(2,1)}), bf16[16,6,4,128]{3,2,1,0:T(4,128)(2,1)S(1)}, u32[]{:S(2)}, u32[]{:S(2)}) async-start(bf16[16,6,4,128]{3,2,1,0:T(4,128)(2,1)} %bitcast.197), calls=%async_computation | async-start | bytes 196608 | tf_op jit(solution)/shard_map/while/body/eval_jaxpr/all_to_all | solution.py:103
  234.9 11.8 %all-to-all-start.1 = ((bf16[16,6,4,128]{3,2,1,0:T(4,128)(2,1)}), bf16[16,6,4,128]{3,2,1,0:T(4,128)(2,1)S(1)}, u32[]{:S(2)}, u32[]{:S(2)}) async-start(bf16[16,6,4,128]{3,2,1,0:T(4,128)(2,1)} %bitcast.201), calls=%async_computation.1 | async-start | bytes 196608 | tf_op jit(solution)/shard_map/while/body/eval_jaxpr/all_to_all | solution.py:103
  248.7 27.9 %copy-start.3 = (bf16[24,512]{1,0:T(8,128)(2,1)S(1)}, bf16[24,512]{1,0:T(8,128)(2,1)}, u32[]{:S(2)}) copy-start(bf16[24,512]{1,0:T(8,128)(2,1)} %param.21) | copy-start | bytes 73732
  250.2 11.1 %all-to-all-start.4 = ((bf16[16,6,4,128]{3,2,1,0:T(4,128)(2,1)}), bf16[16,6,4,128]{3,2,1,0:T(4,128)(2,1)S(1)}, u32[]{:S(2)}, u32[]{:S(2)}) async-start(bf16[16,6,4,128]{3,2,1,0:T(4,128)(2,1)} %bitcast.49), calls=%async_computation.4 | async-start | bytes 196608 | tf_op jit(solution)/shard_map/all_to_all | solution.py:103
  262.9 11.1 %all-to-all-start.5 = ((bf16[16,6,4,128]{3,2,1,0:T(4,128)(2,1)}), bf16[16,6,4,128]{3,2,1,0:T(4,128)(2,1)S(1)}, u32[]{:S(2)}, u32[]{:S(2)}) async-start(bf16[16,6,4,128]{3,2,1,0:T(4,128)(2,1)} %bitcast.55), calls=%async_computation.5 | async-start | bytes 196608 | tf_op jit(solution)/shard_map/all_to_all | solution.py:103
  275.3 1.3 collective-permute-start

commit v3 on v2

--- a/solution.py
+++ b/solution.py
@@ -99,9 +99,9 @@
         return jnp.take(padded, source, axis=0)
 
     def exchange(slots):
-        shaped = slots.astype(jnp.bfloat16).reshape((peer_count, capacity) + slots.shape[1:])
+        shaped = slots.reshape((peer_count, capacity) + slots.shape[1:])
         moved = lax.all_to_all(shaped, "req", split_axis=0, concat_axis=0, tiled=True)
-        return moved.reshape(slots.shape).astype(jnp.float32)
+        return moved.reshape(slots.shape)
 
     def unpack(slots):
         taken = jnp.take(slots, slot_of, axis=0)
@@ -113,9 +113,10 @@
         )
         return jnp.einsum("gshj,ghij->shi", split, states, precision=highest)
 
-    def cg_step(arrived, carry):
-        solution, residual, direction, norm_now = carry
-        shares = unpack(exchange(owner_apply(prompt_keys, arrived, chosen)))
+    def lane_row(values):
+        return jnp.pad(values, ((0, 0), (0, head_size - values.shape[1])))[:, None, :]
+
+    def requester_step(shares, solution, residual, direction, norm_now):
         shared = weight_col * shares + own_matvec(own_keys, direction)
         product = (
             decay_col * shared
@@ -127,26 +128,54 @@
         residual = residual - step_size * product
         norm_next = jnp.sum(residual * residual, axis=2, keepdims=True)
         direction = residual + norm_next / norm_now * direction
-        return solution, residual, direction, norm_next
-
-    label_row = jnp.broadcast_to(
-        slot_label.astype(jnp.float32)[:, None, None], (slot_count, 1, head_size)
-    )
+        return solution, residual, direction, norm_next, step_size
+
+    label_row = lane_row(slot_label.astype(jnp.float32)[:, None])
     first = exchange(jnp.concatenate([pack(queries), label_row], axis=1))
     labels_in = first[:, head_count, 0]
     chosen = [labels_in == float(group + 1) for group in range(group_count)]
-    carry = (
-        jnp.zeros_like(queries),
-        queries,
-        queries,
-        jnp.sum(queries * queries, axis=2, keepdims=True),
-    )
-    carry = cg_step(first[:, :head_count], carry)
-    carry = lax.fori_loop(
-        1, ITERS, lambda _, state: cg_step(exchange(pack(state[2])), state), carry
-    )
-    solution = carry[0]
-    value_sum = unpack(exchange(owner_apply(prompt_values, exchange(pack(solution)), chosen)))
+    slot_used = labels_in > 0.5
+    held = first[:, :head_count]
+    shares = unpack(exchange(owner_apply(prompt_keys, held, chosen)))
+    norm_first = jnp.sum(queries * queries, axis=2, keepdims=True)
+    state = requester_step(shares, jnp.zeros_like(queries), queries, queries, norm_first)
+
+    def middle_step(_, carry):
+        solution, residual, direction, norm_now, step_prev, held, running = carry
+        step_row = lane_row(pack(step_prev[:, :, 0]))
+        arrived = exchange(jnp.concatenate([pack(direction), step_row], axis=1))
+        running = running + arrived[:, head_count, :head_count][:, :, None] * held
+        held = arrived[:, :head_count]
+        shares = unpack(exchange(owner_apply(prompt_keys, held, chosen)))
+        return requester_step(shares, solution, residual, direction, norm_now) + (held, running)
+
+    carry = lax.fori_loop(1, ITERS - 1, middle_step, state + (held, jnp.zeros_like(held)))
+    solution, residual, direction, norm_now, step_prev, held, running = carry
+
+    local_part = (
+        decay_col * own_matvec(own_keys, direction)
+        + write_col * key_now * jnp.sum(key_now * direction, axis=2, keepdims=True)
+        + ridge_col * direction
+    )
+    local_curve = jnp.sum(direction * local_part, axis=2)
+    scalars = jnp.concatenate(
+        [step_prev[:, :, 0], norm_now[:, :, 0], local_curve, (decay_col * weight_col)[:, :, 0]],
+        axis=1,
+    )
+    arrived = exchange(jnp.concatenate([pack(direction), lane_row(pack(scalars))], axis=1))
+    extra = arrived[:, head_count]
+    running = running + extra[:, :head_count][:, :, None] * held
+    held = arrived[:, :head_count]
+    prompt_part = owner_apply(prompt_keys, held, chosen)
+    prompt_curve = jnp.sum(held * prompt_part, axis=2)
+    rr_in = extra[:, head_count : 2 * head_count]
+    curve = extra[:, 2 * head_count : 3 * head_count] + extra[:, 3 * head_count : 4 * head_count] * prompt_curve
+    step_last = jnp.where(slot_used[:, None], rr_in / jnp.where(slot_used[:, None], curve, 1.0), 0.0)
+    running = running + step_last[:, :, None] * held
+    finished = owner_apply(prompt_values, running, chosen)
+    returned = unpack(exchange(jnp.concatenate([finished, lane_row(step_last)], axis=1)))
+    value_sum = returned[:, :head_count]
+    solution = solution + returned[:, head_count, :head_count][:, :, None] * direction
     shared_out = weight_col * value_sum + own_matvec(own_values, solution)
     readout = decay_col * shared_out + write_col * value_now * jnp.sum(
         key_now * solution, axis=2, keepdims=True

time: 279 us -> 298 us (1.068)
  blocking collectives: 2.35 us -> 15.1 us
  starting transfers between devices: 71.1 us -> 59.9 us
  local copies, waits for them, and re-layouts: 31.1 us -> 41.8 us
  other arithmetic: 60.2 us -> 68.6 us
  waiting for transfers between devices: 102 us -> 98.9 us
    all_to_all x0 -> x1, blocking collectives: none -> 12.7 us  [exchange(): lax.all_to_all(shaped, 'req', split_axis=0, concat_axis=0, tiled=True)]
    all_to_all x18 -> x15, starting transfers between devices: 71 us -> 59.8 us  [exchange(): lax.all_to_all(shaped, 'req', split_axis=0, concat_axis=0, tiled=True)]
    convert_element_type x26 -> x1, other arithmetic: 6.76 us -> 0.01 us  [on_device(): label_row = lane_row(slot_label.astype(jnp.float32)[:, None])]
    convert_element_type x11 -> x0, local copies, waits for them, and re-layouts: 6.21 us -> none  [the longest x9 6.1 us: exchange(): slots.astype(jnp.bfloat16).reshape((peer_count, capacity) + slots.shape[1:])]
    mul x22 -> x15, other arithmetic: 4.49 us -> 10.7 us  [the longest x7 9.69 us: requester_step(): write_col * key_now * jnp.sum(key_now * direction, axis=2, keepdims=True)]
    transpose x0 -> x8, local copies, waits for them, and re-layouts: none -> 5.75 us  [owner_apply(): return jnp.einsum('gshj,ghij->shi', split, states, precision=highest)]
    concatenate x0 -> x8, local copies, waits for them, and re-layouts: none -> 5.48 us  [the longest x6 4.64 us: middle_step(): arrived = exchange(jnp.concatenate([pack(direction), step_row], axis=1))]
    gather x9 -> x15, local copies, waits for them, and re-layouts: 6.32 us -> 9.99 us  [pack(): return jnp.take(padded, source, axis=0)]
  transfers between devices with their start and end apart: 19 -> 16, of which waited for: 19 -> 16; matrix products, arithmetic and copies ran while one was open for 14% -> 13% of each run, Pallas kernels for 0% -> 0%
where the time goes in v3:
time: 298 us; the launch traced here: 296 us
  waiting for transfers between devices  98.9 us (33%)
  other arithmetic  68.6 us (23%)
  starting transfers between devices  59.9 us (20%)
  local copies, waits for them, and re-layouts  41.8 us (14%)
  blocking collectives  15.1 us (5%)
  matrix products  9.48 us (3%)
    all_to_all x15, waiting for transfers between devices, exchange(): lax.all_to_all(shaped, 'req', split_axis=0, concat_axis=0, tiled=True)  97.7 us
    all_to_all x15, starting transfers between devices, exchange(): lax.all_to_all(shaped, 'req', split_axis=0, concat_axis=0, tiled=True)  59.8 us
    reduce_sum x9, other arithmetic, own_matvec(): return jnp.sum(matrices * vectors[:, :, None, :], axis=3)  40.5 us
    all_to_all x1, blocking collectives, exchange(): lax.all_to_all(shaped, 'req', split_axis=0, concat_axis=0, tiled=True)  12.7 us
    gather x15, local copies, waits for them, and re-layouts, pack(): return jnp.take(padded, source, axis=0)  9.99 us
    mul x7, other arithmetic, requester_step(): write_col * key_now * jnp.sum(key_now * direction, axis=2, keepdims=True)  9.69 us
    unnamed x35, local copies, waits for them, and re-layouts  7.77 us
    dot_general x9, matrix products, owner_apply(): return jnp.einsum('gshj,ghij->shi', split, states, precision=highest)  6.07 us
  transfers between devices with their start and end apart: 16, of which 16 were waited for; matrix products, arithmetic and copies ran while one was open for 13% of the time, Pallas kernels for 0%

profile of v3, /device:TPU:0, one launch (start us, length us, event | category | flops | bytes accessed | tf_op | source)
XLA Modules:
  0.0 295.9 jit_solution(16804825830760506916)
XLA Ops:
  6.9 6.0 %copy.251 = bf16[1024,4,3,128]{0,3,2,1:T(8,128)(2,1)} copy(bf16[1024,4,3,128]{3,1,2,0:T(4,128)(2,1)} %param.23) | data formatting | bytes 6291456 | tf_op args[2]
  18.2 8.2 %all-to-all-start.2 = ((f32[16,6,5,128]{3,1,2,0:T(8,128)}), f32[16,6,5,128]{3,1,2,0:T(8,128)S(1)}, u32[]{:S(2)}, u32[]{:S(2)}) async-start(f32[16,6,5,128]{3,1,2,0:T(8,128)} %copy.262), calls=%async_computation.2 | async-start | bytes 655360 | tf_op jit(solution)/shard_map/all_to_all | solution.py:103
  26.5 11.5 %all-to-all-done.2 = f32[16,6,5,128]{3,1,2,0:T(8,128)S(1)} async-done(((f32[16,6,5,128]{3,1,2,0:T(8,128)}), f32[16,6,5,128]{3,1,2,0:T(8,128)S(1)}, u32[]{:S(2)}, u32[]{:S(2)}) %all-to-all-start.2) | async-done | bytes 245792 | tf_op jit(solution)/shard_map/all_to_all | solution.py:103
  40.4 3.7 %all-to-all-start.3 = ((f32[16,6,4,128]{3,2,1,0:T(4,128)}), f32[16,6,4,128]{3,2,1,0:T(4,128)S(1)}, u32[]{:S(2)}, u32[]{:S(2)}) async-start(f32[16,6,4,128]{3,2,1,0:T(4,128)} %bitcast.25), calls=%async_computation.3 | async-start | bytes 393216 | tf_op jit(solution)/shard_map/all_to_all | solution.py:103
  44.8 4.5 %multiply_reduce_fusion.6 = f32[24,4,128]{2,1,0:T(4,128)S(1)} fusion(f32[24,4,128,128]{3,2,1,0:T(8,128)} %param.29, f32[24,4,128]{2,1,0:T(4,128)S(1)} %copy.268), kind=kLoop, calls=%fused_computation.52 | loop fusion | flops 3133440 | bytes 6389760 | tf_op jit(solution)/shard_map/reduce_sum | solution.py:16
  53.9 195.0 %while.25 = (s32[]{:T(128)}, f32[24,4,128]{2,1,0:T(4,128)S(1)}, f32[24,4,128]{2,1,0:T(4,128)S(1)}, f32[24,4,128]{2,1,0:T(4,128)S(1)}, f32[24,4,1]{0,1,2:T(4,128)...) while((s32[]{:T(128)}, f32[24,4,128]{2,1,0:T(4,128)S(1)}, ...), condition=%wide.region_17.20_spmd.clone, body=%wide.region_12.19_spmd.clone.sunk | while | flops 154846128 | bytes 14649783 | solution.py:152
  56.6 4.1 %all-to-all-start = ((f32[16,6,5,128]{3,1,2,0:T(8,128)}), f32[16,6,5,128]{3,1,2,0:T(8,128)S(1)}, u32[]{:S(2)}, u32[]{:S(2)}) async-start(f32[16,6,5,128]{3,1,2,0:T(8,128)} %copy.365), calls=%async_computation | async-start | bytes 655360 | tf_op jit(solution)/shard_map/while/body/eval_jaxpr/all_to_all | solution.py:103
  61.3 9.7 %all-to-all-done = f32[16,6,5,128]{3,1,2,0:T(8,128)S(1)} async-done(((f32[16,6,5,128]{3,1,2,0:T(8,128)}), f32[16,6,5,128]{3,1,2,0:T(8,128)S(1)}, u32[]{:S(2)}, u32[]{:S(2)}) %all-to-all-start) | async-done | bytes 245792 | tf_op jit(solution)/shard_map/while/body/eval_jaxpr/all_to_all | solution.py:103
  76.7 4.5 %multiply_reduce_fusion.17 = f32[24,4,128]{2,1,0:T(4,128)S(1)} fusion(f32[24,4,128,128]{3,2,1,0:T(8,128)} %get-tuple-element.725, f32[24,4,128]{2,1,0:T(4,128)S(1)} %get-tuple-element.689), kind=kLoop, calls=%fused_computation.9.clone.1 | loop fusion | flops 3133440 | bytes 6389760 | tf_op jit(solution)/shard_map/while/body/eval_jaxpr/reduce_sum | solution.py:16
  90.0 3.6 %all-to-all-start = ((f32[16,6,5,128]{3,1,2,0:T(8,128)}), f32[16,6,5,128]{3,1,2,0:T(8,128)S(1)}, u32[]{:S(2)}, u32[]{:S(2)}) async-start(f32[16,6,5,128]{3,1,2,0:T(8,128)} %copy.365), calls=%async_computation | async-start | bytes 655360 | tf_op jit(solution)/shard_map/while/body/eval_jaxpr/all_to_all | solution.py:103
  94.2 9.0 %all-to-all-done = f32[16,6,5,128]{3,1,2,0:T(8,128)S(1)} async-done(((f32[16,6,5,128]{3,1,2,0:T(8,128)}), f32[16,6,5,128]{3,1,2,0:T(8,128)S(1)}, u32[]{:S(2)}, u32[]{:S(2)}) %all-to-all-start) | async-done | bytes 245792 | tf_op jit(solution)/shard_map/while/body/eval_jaxpr/all_to_all | solution.py:103
  105.2 3.7 %all-to-all-start.1 = ((f32[16,6,4,128]{3,2,1,0:T(4,128)}), f32[16,6,4,128]{3,2,1,0:T(4,128)S(1)}, u32[]{:S(2)}, u32[]{:S(2)}) async-start(f32[16,6,4,128]{3,2,1,0:T(4,128)} %bitcast.222), calls=%async_computation.1 | async-start | bytes 393216 | tf_op jit(solution)/shard_map/while/body/eval_jaxpr/all_to_all | solution.py:103
  109.2 4.5 %multiply_reduce_fusion.17 = f32[24,4,128]{2,1,0:T(4,128)S(1)} fusion(f32[24,4,128,128]{3,2,1,0:T(8,128)} %get-tuple-element.725, f32[24,4,128]{2,1,0:T(4,128)S(1)} %get-tuple-element.689), kind=kLoop, calls=%fused_computation.9.clone.1 | loop fusion | flops 3133440 | bytes 6389760 | tf_op jit(solution)/shard_map/while/body/eval_jaxpr/reduce_sum | solution.py:16
  122.5 3.6 %all-to-all-start = ((f32[16,6,5,128]{3,1,2,0:T(8,128)}), f32[16,6,5,128]{3,1,2,0:T(8,128)S(1)}, u32[]{:S(2)}, u32[]{:S(2)}) async-start(f32[16,6,5,128]{3,1,2,0:T(8,128)} %copy.365), calls=%async_computation | async-start | bytes 655360 | tf_op jit(solution)/shard_map/while/body/eval_jaxpr/all_to_all | solution.py:103
  126.8 8.8 %all-to-all-done = f32[16,6,5,128]{3,1,2,0:T(8,128)S(1)} async-done(((f32[16,6,5,128]{3,1,2,0:T(8,128)}), f32[16,6,5,128]{3,1,2,0:T(8,128)S(1)}, u32[]{:S(2)}, u32[]{:S(2)}) %all-to-all-start) | async-done | bytes 245792 | tf_op jit(solution)/shard_map/while/body/eval_jaxpr/all_to_all | solution.py:103
  137.5 3.7 %all-to-all-start.1 = ((f32[16,6,4,128]{3,2,1,0:T(4,128)}), f32[16,6,4,128]{3,2,1,0:T(4,128)S(1)}, u32[]{:S(2)}, u32[]{:S(2)}) async-start(f32[16,6,4,128]{3,2,1,0:T(4,128)} %bitcast.222), calls=%async_computation.1 | async-start | bytes 393216 | tf_op jit(solution)/shard_map/while/body/eval_jaxpr/all_to_all | solution.py:103
  141.5 4.5 %multiply_reduce_fusion.17 = f32[24,4,128]{2,1,0:T(4,128)S(1)} fusion(f32[24,4,128,128]{3,2,1,0:T(8,128)} %get-tuple-element.725, f32[24,4,128]{2,1,0:T(4,128)S(1)} %get-tuple-element.689), kind=kLoop, calls=%fused_computation.9.clone.1 | loop fusion | flops 3133440 | bytes 6389760 | tf_op jit(solution)/shard_map/while/body/eval_jaxpr/reduce_sum | solution.py:16
  159.1 8.7 %all-to-all-done = f32[16,6,5,128]{3,1,2,0:T(8,128)S(1)} async-done(((f32[16,6,5,128]{3,1,2,0:T(8,128)}), f32[16,6,5,128]{3,1,2,0:T(8,128)S(1)}, u32[]{:S(2)}, u32[]{:S(2)}) %all-to-all-start) | async-done | bytes 245792 | tf_op jit(solution)/shard_map/while/body/eval_jaxpr/all_to_all | solution.py:103
  169.8 3.7 %all-to-all-start.1 = ((f32[16,6,4,128]{3,2,1,0:T(4,128)}), f32[16,6,4,128]{3,2,1,0:T(4,128)S(1)}, u32[]{:S(2)}, u32[]{:S(2)}) async-start(f32[16,6,4,128]{3,2,1,0:T(4,128)} %bitcast.222), calls=%async_computation.1 | async-start | bytes 393216 | tf_op jit(solution)/shard_map/while/body/eval_jaxpr/all_to_all | solution.py:103
  173.8 4.5 %multiply_reduce_fusion.17 = f32[24,4,128]{2,1,0:T(4,128)S(1)} fusion(f32[24,4,128,128]{3,2,1,0:T(8,128)} %get-tuple-element.725, f32[24,4,128]{2,1,0:T(4,128)S(1)} %get-tuple-element.689), kind=kLoop, calls=%fused_computation.9.clone.1 | loop fusion | flops 3133440 | bytes 6389760 | tf_op jit(solution)/shard_map/while/body/eval_jaxpr/reduce_sum | solution.py:16
  191.3 8.7 %all-to-all-done = f32[16,6,5,128]{3,1,2,0:T(8,128)S(1)} async-done(((f32[16,6,5,128]{3,1,2,0:T(8,128)}), f32[16,6,5,128]{3,1,2,0:T(8,128)S(1)}, u32[]{:S(2)}, u32[]{:S(2)}) %all-to-all-start) | async-done | bytes 245792 | tf_op jit(solution)/shard_map/while/body/eval_jaxpr/all_to_all | solution.py:103
  202.0 3.7 %all-to-all-start.1 = ((f32[16,6,4,128]{3,2,1,0:T(4,128)}), f32[16,6,4,128]{3,2,1,0:T(4,128)S(1)}, u32[]{:S(2)}, u32[]{:S(2)}) async-start(f32[16,6,4,128]{3,2,1,0:T(4,128)} %bitcast.222), calls=%async_computation.1 | async-start | bytes 393216 | tf_op jit(solution)/shard_map/while/body/eval_jaxpr/all_to_all | solution.py:103
  206.0 4.5 %multiply_reduce_fusion.17 = f32[24,4,128]{2,1,0:T(4,128)S(1)} fusion(f32[24,4,128,128]{3,2,1,0:T(8,128)} %get-tuple-element.725, f32[24,4,128]{2,1,0:T(4,128)S(1)} %get-tuple-element.689), kind=kLoop, calls=%fused_computation.9.clone.1 | loop fusion | flops 3133440 | bytes 6389760 | tf_op jit(solution)/shard_map/while/body/eval_jaxpr/reduce_sum | solution.py:16
  219.4 3.6 %all-to-all-start = ((f32[16,6,5,128]{3,1,2,0:T(8,128)}), f32[16,6,5,128]{3,1,2,0:T(8,128)S(1)}, u32[]{:S(2)}, u32[]{:S(2)}) async-start(f32[16,6,5,128]{3,1,2,0:T(8,128)} %copy.365), calls=%async_computation | async-start | bytes 655360 | tf_op jit(solution)/shard_map/while/body/eval_jaxpr/all_to_all | solution.py:103
  223.6 8.7 %all-to-all-done = f32[16,6,5,128]{3,1,2,0:T(8,128)S(1)} async-done(((f32[16,6,5,128]{3,1,2,0:T(8,128)}), f32[16,6,5,128]{3,1,2,0:T(8,128)S(1)}, u32[]{:S(2)}, u32[]{:S(2)}) %all-to-all-start) | async-done | bytes 245792 | tf_op jit(solution)/shard_map/while/body/eval_jaxpr/all_to_all | solution.py:103
  234.3 3.7 %all-to-all-start.1 = ((f32[16,6,4,128]{3,2,1,0:T(4,128)}), f32[16,6,4,128]{3,2,1,0:T(4,128)S(1)}, u32[]{:S(2)}, u32[]{:S(2)}) async-start(f32[16,6,4,128]{3,2,1,0:T(4,128)} %bitcast.222), calls=%async_computation.1 | async-start | bytes 393216 | tf_op jit(solution)/shard_map/while/body/eval_jaxpr/all_to_all | solution.py:103
  238.3 4.5 %multiply_reduce_fusion.17 = f32[24,4,128]{2,1,0:T(4,128)S(1)} fusion(f32[24,4,128,128]{3,2,1,0:T(8,128)} %get-tuple-element.725, f32[24,4,128]{2,1,0:T(4,128)S(1)} %get-tuple-element.689), kind=kLoop, calls=%fused_computation.9.clone.1 | loop fusion | flops 3133440 | bytes 6389760 | tf_op jit(solution)/shard_map/while/body/eval_jaxpr/reduce_sum | solution.py:16
  249.0 4.5 %multiply_reduce_fusion.5 = f32[24,4,128]{2,1,0:T(4,128)S(1)} fusion(f32[24,4,128,128]{3,2,1,0:T(8,128)} %get-tuple-element.732, f32[24,4,128]{2,1,0:T(4,128)S(1)} %get-tuple-element.258), kind=kLoop, calls=%fused_computation.51 | loop fusion | flops 3133440 | bytes 6389760 | tf_op jit(solution)/shard_map/reduce_sum | solution.py:16
  256.3 12.7 %all_to_all.40 = f32[16,6,5,128]{3,1,2,0:T(8,128)S(1)} all-to-all(f32[16,6,5,128]{3,1,2,0:T(8,128)S(1)} %copy.282), channel_id=1, replica_groups=mesh['req'=16,'head'=2] {'req'}, dimensions={0} | all-to-all | bytes 491520 | tf_op jit(solution)/shard_map/all_to_all | solution.py:103
  273.6 3.7 %all-to-all-start.5 = ((f32[16,6,5,128]{3,1,2,0:T(8,128)}), f32[16,6,5,128]{3,1,2,0:T(8,128)S(1)}, u32[]{:S(2)}, u32[]{:S(2)}) async-start(f32[16,6,5,128]{3,1,2,0:T(8,128)} %copy.288), calls=%async_computation.5 | async-start | bytes 655360 | tf_op jit(solution)/shard_map/all_to_all | solution.py:103
  277.4 10.1 %all-to-all-done.5 = f32[16,6,5,128]{3,1,2,0:T(8,128)S(1)} async-done(((f32[16,6,5,128]{3,1,2,0:T(8,128)}), f32[16,6,5,128]{3,1,2,0:T(8,128)S(1)}, u32[]{:S(2)}, u32[]{:S(2)}) %all-to-all-start.5) | async-done | bytes 245792 | tf_op jit(solution)/shard_map/all_to_all | solution.py:103
  288.4 4.5 %multiply_reduce_fusion.4 = f32[24,4,128]{2,1,0:T(4,128)S(1)} fusion(f32[24,4,128,128]{3,2,1,0:T(8,128)} %param.30, f32[24,4,128]{2,1,0:T(4,128)S(1)} %copy.295), kind=kLoop, calls=%fused_computation.50 | loop fusion | flops 3133440 | bytes 6389760 | tf_op jit(solution)/shard_map/reduce_sum | solution.py:16
  (435 shorter events, 110.4 us)
Async XLA Ops:
  0.0 293.6 %copy-start = (bf16[4,128,1024]{2,1,0:T(8,128)(2,1)S(1)}, bf16[4,128,1024]{2,1,0:T(8,128)(2,1)}, u32[]{:S(2)}) copy-start(bf16[4,128,1024]{2,1,0:T(8,128)(2,1)} %param.35) | copy-start | bytes 3145732
  2.3 50.3 %copy-start.7 = (pred[24]{0:T(512)(128)(4,1)}, pred[24]{0:T(512)(128)(4,1)S(1)}, u32[]{:S(2)}) copy-start(pred[24]{0:T(512)(128)(4,1)S(1)} %get-tuple-element.485) | copy-start | bytes 76
  6.9 19.6 %copy-start.3 = (f32[24,4]{0,1:T(4,128)S(1)}, f32[24,4]{0,1:T(4,128)}, u32[]{:S(2)}) copy-start(f32[24,4]{0,1:T(4,128)} %param.27) | copy-start | bytes 1156
  12.9 26.0 %copy-start.1 = (f32[2,4,128,128]{3,2,1,0:T(8,128)S(1)}, f32[2,4,128,128]{3,2,1,0:T(8,128)}, u32[]{:S(2)}) copy-start(f32[2,4,128,128]{3,2,1,0:T(8,128)} %param.31) | copy-start | bytes 1572868
  18.2 19.9 %all-to-all-start.2 = ((f32[16,6,5,128]{3,1,2,0:T(8,128)}), f32[16,6,5,128]{3,1,2,0:T(8,128)S(1)}, u32[]{:S(2)}, u32[]{:S(2)}) async-start(f32[16,6,5,128]{3,1,2,0:T(8,128)} %copy.262), calls=%async_computation.2 | async-start | bytes 655360 | tf_op jit(solution)/shard_map/all_to_all | solution.py:103
  40.4 11.6 %all-to-all-start.3 = ((f32[16,6,4,128]{3,2,1,0:T(4,128)}), f32[16,6,4,128]{3,2,1,0:T(4,128)S(1)}, u32[]{:S(2)}, u32[]{:S(2)}) async-start(f32[16,6,4,128]{3,2,1,0:T(4,128)} %bitcast.25), calls=%async_computation.3 | async-start | bytes 393216 | tf_op jit(solution)/shard_map/all_to_all | solution.py:103
  56.6 14.3 %all-to-all-start = ((f32[16,6,5,128]{3,1,2,0:T(8,128)}), f32[16,6,5,128]{3,1,2,0:T(8,128)S(1)}, u32[]{:S(2)}, u32[]{:S(2)}) async-start(f32[16,6,5,128]{3,1,2,0:T(8,128)} %copy.365), calls=%async_computation | async-start | bytes 655360 | tf_op jit(solution)/shard_map/while/body/eval_jaxpr/all_to_all | solution.py:103
  72.9 11.6 %all-to-all-start.1 = ((f32[16,6,4,128]{3,2,1,0:T(4,128)}), f32[16,6,4,128]{3,2,1,0:T(4,128)S(1)}, u32[]{:S(2)}, u32[]{:S(2)}) async-start(f32[16,6,4,128]{3,2,1,0:T(4,128)} %bitcast.222), calls=%async_computation.1 | async-start | bytes 393216 | tf_op jit(solution)/shard_map/while/body/eval_jaxpr/all_to_all | solution.py:103
  90.0 13.2 %all-to-all-start = ((f32[16,6,5,128]{3,1,2,0:T(8,128)}), f32[16,6,5,128]{3,1,2,0:T(8,128)S(1)}, u32[]{:S(2)}, u32[]{:S(2)}) async-start(f32[16,6,5,128]{3,1,2,0:T(8,128)} %copy.365), calls=%async_computation | async-start | bytes 655360 | tf_op jit(solution)/shard_map/while/body/eval_jaxpr/all_to_all | solution.py:103
  103.3 16.5 %copy-start.12 = (s32[24]{0:T(128)S(1)}, s32[24]{0:T(128)}, u32[]{:S(2)}) copy-start(s32[24]{0:T(128)} %copy-done.11) | copy-start | bytes 292 | tf_op jit(solution)/shard_map/while
  103.3 16.5 %copy-start.15 = (s32[96]{0:T(128)S(1)}, s32[96]{0:T(128)}, u32[]{:S(2)}) copy-start(s32[96]{0:T(128)} %copy-done.14) | copy-start | bytes 1156 | tf_op jit(solution)/shard_map/while
  105.2 11.8 %all-to-all-start.1 = ((f32[16,6,4,128]{3,2,1,0:T(4,128)}), f32[16,6,4,128]{3,2,1,0:T(4,128)S(1)}, u32[]{:S(2)}, u32[]{:S(2)}) async-start(f32[16,6,4,128]{3,2,1,0:T(4,128)} %bitcast.222), calls=%async_computation.1 | async-start | bytes 393216 | tf_op jit(solution)/shard_map/while/body/eval_jaxpr/all_to_all | solution.py:103
  122.5 13.0 %all-to-all-start = ((f32[16,6,5,128]{3,1,2,0:T(8,128)}), f32[16,6,5,128]{3,1,2,0:T(8,128)S(1)}, u32[]{:S(2)}, u32[]{:S(2)}) async-start(f32[16,6,5,128]{3,1,2,0:T(8,128)} %copy.365), calls=%async_computation | async-start | bytes 655360 | tf_op jit(solution)/shard_map/while/body/eval_jaxpr/all_to_all | solution.py:103
  135.6 16.5 %copy-start.12 = (s32[24]{0:T(128)S(1)}, s32[24]{0:T(128)}, u32[]{:S(2)}) copy-start(s32[24]{0:T(128)} %copy-done.11) | copy-start | bytes 292 | tf_op jit(solution)/shard_map/while
  135.7 16.5 %copy-start.15 = (s32[96]{0:T(128)S(1)}, s32[96]{0:T(128)}, u32[]{:S(2)}) copy-start(s32[96]{0:T(128)} %copy-done.14) | copy-start | bytes 1156 | tf_op jit(solution)/shard_map/while
  137.5 11.8 %all-to-all-start.1 = ((f32[16,6,4,128]{3,2,1,0:T(4,128)}), f32[16,6,4,128]{3,2,1,0:T(4,128)S(1)}, u32[]{:S(2)}, u32[]{:S(2)}) async-start(f32[16,6,4,128]{3,2,1,0:T(4,128)} %bitcast.222), calls=%async_computation.1 | async-start | bytes 393216 | tf_op jit(solution)/shard_map/while/body/eval_jaxpr/all_to_all | solution.py:103
  154.9 12.9 %all-to-all-start = ((f32[16,6,5,128]{3,1,2,0:T(8,128)}), f32[16,6,5,128]{3,1,2,0:T(8,128)S(1)}, u32[]{:S(2)}, u32[]{:S(2)}) async-start(f32[16,6,5,128]{3,1,2,0:T(8,128)} %copy.365), calls=%async_computation | async-start | bytes 655360 | tf_op jit(solution)/shard_map/while/body/eval_jaxpr/all_to_all | solution.py:103
  167.9 16.5 %copy-start.12 = (s32[24]{0:T(128)S(1)}, s32[24]{0:T(128)}, u32[]{:S(2)}) copy-start(s32[24]{0:T(128)} %copy-done.11) | copy-start | bytes 292 | tf_op jit(solution)/shard_map/while
  169.8 11.8 %all-to-all-start.1 = ((f32[16,6,4,128]{3,2,1,0:T(4,128)}), f32[16,6,4,128]{3,2,1,0:T(4,128)S(1)}, u32[]{:S(2)}, u32[]{:S(2)}) async-start(f32[16,6,4,128]{3,2,1,0:T(4,128)} %bitcast.222), calls=%async_computation.1 | async-start | bytes 393216 | tf_op jit(solution)/shard_map/while/body/eval_jaxpr/all_to_all | solution.py:103
  187.1 12.9 %all-to-all-start = ((f32[16,6,5,128]{3,1,2,0:T(8,128)}), f32[16,6,5,128]{3,1,2,0:T(8,128)S(1)}, u32[]{:S(2)}, u32[]{:S(2)}) async-start(f32[16,6,5,128]{3,1,2,0:T(8,128)} %copy.365), calls=%async_computation | async-start | bytes 655360 | tf_op jit(solution)/shard_map/while/body/eval_jaxpr/all_to_all | solution.py:103
  200.1 16.5 %copy-start.12 = (s32[24]{0:T(128)S(1)}, s32[24]{0:T(128)}, u32[]{:S(2)}) copy-start(s32[24]{0:T(128)} %copy-done.11) | copy-start | bytes 292 | tf_op jit(solution)/shard_map/while
  200.1 16.5 %copy-start.15 = (s32[96]{0:T(128)S(1)}, s32[96]{0:T(128)}, u32[]{:S(2)}) copy-start(s32[96]{0:T(128)} %copy-done.14) | copy-start | bytes 1156 | tf_op jit(solution)/shard_map/while
  202.0 11.8 %all-to-all-start.1 = ((f32[16,6,4,128]{3,2,1,0:T(4,128)}), f32[16,6,4,128]{3,2,1,0:T(4,128)S(1)}, u32[]{:S(2)}, u32[]{:S(2)}) async-start(f32[16,6,4,128]{3,2,1,0:T(4,128)} %bitcast.222), calls=%async_computation.1 | async-start | bytes 393216 | tf_op jit(solution)/shard_map/while/body/eval_jaxpr/all_to_all | solution.py:103
  219.4 12.9 %all-to-all-start = ((f32[16,6,5,128]{3,1,2,0:T(8,128)}), f32[16,6,5,128]{3,1,2,0:T(8,128)S(1)}, u32[]{:S(2)}, u32[]{:S(2)}) async-start(f32[16,6,5,128]{3,1,2,0:T(8,128)} %copy.365), calls=%async_computation | async-start | bytes 655360 | tf_op jit(solution)/shard_map/while/body/eval_jaxpr/all_to_all | solution.py:103
  234.3 11.8 %all-to-all-start.1 = ((f32[16,6,4,128]{3,2,1,0:T(4,128)}), f32[16,6,4,128]{3,2,1,0:T(4,128)S(1)}, u32[]{:S(2)}, u32[]{:S(2)}) async-start(f32[16,6,4,128]{3,2,1,0:T(4,128)} %bitcast.222), calls=%async_computation.1 | async-start | bytes 393216 | tf_op jit(solution)/shard_map/while/body/eval_jaxpr/all_to_all | solution.py:103
  249.0 21.8 %copy-start.13 = (pred[96]{0:T(512)(128)(4,1)S(1)}, pred[96]{0:T(512)(128)(4,1)}, u32[]{:S(2)}) copy-start(pred[96]{0:T(512)(128)(4,1)} %get-tuple-element.426) | copy-start | bytes 292
  249.0 22.9 %copy-start.2 = (f32[2,4,128,128]{3,2,1,0:T(8,128)S(1)}, f32[2,4,128,128]{3,2,1,0:T(8,128)}, u32[]{:S(2)}) copy-start(f32[2,4,128,128]{3,2,1,0:T(8,128)} %param.32) | copy-start | bytes 1572868
  254.2 33.9 %copy-start.8 = (pred[24]{0:T(512)(128)(4,1)S(1)}, pred[24]{0:T(512)(128)(4,1)}, u32[]{:S(2)}) copy-start(pred[24]{0:T(512)(128)(4,1)} %copy-done.7) | copy-start | bytes 76
  271.9 23.3 %copy-start.4 = (bf16[24,512]{1,0:T(8,128)(2,1)S(1)}, bf16[24,512]{1,0:T(8,128)(2,1)}, u32[]{:S(2)}) copy-start(bf16[24,512]{1,0:T(8,128)(2,1)} %param.21) | copy-start | bytes 73732
  271.9 23.3 %copy-start.10 = (pred[24]{0:T(512)(128)(4,1)S(1)}, pred[24]{0:T(512)(128)(4,1)}, u32[]{:S(2)}) copy-start(pred[24]{0:T(512)(128)(4,1)} %copy-done.9) | copy-start | bytes 76
  273.6 13.9 %all-to-all-start.5 = ((f32[16,6,5,128]{3,1,2,0:T(8,128)}), f32[16,6,5,128]{3,1,2,0:T(8,128)S(1)}, u32[]{:S(2)}, u32[]{:S(2)}) async-start(f32[16,6,5,128]{3,1,2,0:T(8,128)} %copy.288), calls=%async_computation.5 | async-start | bytes 655360 | tf_op jit(solution)/shard_map/all_to_all | solution.py:103
  294.0 1.3 collective-permute-start
  (26 other events, 279.0 us)

commit v4 on v3

--- a/solution.py
+++ b/solution.py
@@ -72,31 +72,29 @@
     peer_count = lax.axis_size("req")
     group_count = prompt_keys.shape[0]
     capacity = CAP
+    run_count = row_count // capacity
     slot_count = peer_count * capacity
     mask_of_live = lengths > 0
     owner_of = group_ids // group_count
     local_group = group_ids % group_count
-    order_ids = jnp.arange(row_count)
-    earlier = (
-        (order_ids[None, :] < order_ids[:, None])
-        & (owner_of[None, :] == owner_of[:, None])
-        & mask_of_live[None, :]
-    )
-    rank_of = jnp.sum(earlier.astype(jnp.int32), axis=1)
-    routed = mask_of_live & (rank_of < capacity)
-    slot_of = jnp.where(routed, owner_of * capacity + rank_of, 0)
-    hits = (slot_of[:, None] == jnp.arange(slot_count)[None, :]) & routed[:, None]
-    filled = jnp.any(hits, axis=0)
-    source = jnp.sum(jnp.where(hits, order_ids[:, None], 0), axis=0) + jnp.where(
-        filled, 0, row_count
-    )
-    slot_label = jnp.sum(jnp.where(hits, (local_group + 1)[:, None], 0), axis=0)
+    run_live = jnp.any(mask_of_live.reshape(run_count, capacity), axis=1)
+    run_owner = jnp.max(
+        jnp.where(mask_of_live, owner_of, -1).reshape(run_count, capacity), axis=1
+    )
+    claims = (run_owner[:, None] == jnp.arange(peer_count)[None, :]) & run_live[:, None]
+    run_ids = jnp.arange(run_count)
+    run_of_peer = jnp.sum(jnp.where(claims, run_ids[:, None], 0), axis=0) + jnp.where(
+        jnp.any(claims, axis=0), 0, run_count
+    )
+    peer_of_run = jnp.where(run_live, run_owner, 0)
+    slot_label = jnp.where(mask_of_live, local_group + 1, 0)
+    live_col = mask_of_live[:, None, None]
 
     def pack(vectors):
-        padded = jnp.concatenate(
-            [vectors, jnp.zeros((1,) + vectors.shape[1:], vectors.dtype)], axis=0
-        )
-        return jnp.take(padded, source, axis=0)
+        runs = vectors.reshape((run_count, capacity) + vectors.shape[1:])
+        padded = jnp.concatenate([runs, jnp.zeros((1,) + runs.shape[1:], runs.dtype)], axis=0)
+        taken = jnp.take(padded, run_of_peer, axis=0, mode="clip")
+        return taken.reshape((slot_count,) + vectors.shape[1:])
 
     def exchange(slots):
         shaped = slots.reshape((peer_count, capacity) + slots.shape[1:])
@@ -104,8 +102,9 @@
         return moved.reshape(slots.shape)
 
     def unpack(slots):
-        taken = jnp.take(slots, slot_of, axis=0)
-        return jnp.where(routed[:, None, None], taken, 0.0)
+        shaped = slots.reshape((peer_count, capacity) + slots.shape[1:])
+        taken = jnp.take(shaped, peer_of_run, axis=0, mode="clip")
+        return jnp.where(live_col, taken.reshape((row_count,) + slots.shape[1:]), 0.0)
 
     def owner_apply(states, incoming, chosen):
         split = jnp.stack(
@@ -130,7 +129,7 @@
         direction = residual + norm_next / norm_now * direction
         return solution, residual, direction, norm_next, step_size
 
-    label_row = lane_row(slot_label.astype(jnp.float32)[:, None])
+    label_row = lane_row(pack(slot_label.astype(jnp.float32)[:, None]))
     first = exchange(jnp.concatenate([pack(queries), label_row], axis=1))
     labels_in = first[:, head_count, 0]
     chosen = [labels_in == float(group + 1) for group in range(group_count)]
@@ -138,19 +137,28 @@
     held = first[:, :head_count]
     shares = unpack(exchange(owner_apply(prompt_keys, held, chosen)))
     norm_first = jnp.sum(queries * queries, axis=2, keepdims=True)
-    state = requester_step(shares, jnp.zeros_like(queries), queries, queries, norm_first)
-
-    def middle_step(_, carry):
-        solution, residual, direction, norm_now, step_prev, held, running = carry
-        step_row = lane_row(pack(step_prev[:, :, 0]))
-        arrived = exchange(jnp.concatenate([pack(direction), step_row], axis=1))
-        running = running + arrived[:, head_count, :head_count][:, :, None] * held
-        held = arrived[:, :head_count]
-        shares = unpack(exchange(owner_apply(prompt_keys, held, chosen)))
-        return requester_step(shares, solution, residual, direction, norm_now) + (held, running)
-
-    carry = lax.fori_loop(1, ITERS - 1, middle_step, state + (held, jnp.zeros_like(held)))
-    solution, residual, direction, norm_now, step_prev, held, running = carry
+    solution, residual, direction, norm_now, step_size = requester_step(
+        shares, jnp.zeros_like(queries), queries, queries, norm_first
+    )
+    kept = jnp.zeros((ITERS - 1,) + held.shape, held.dtype).at[0].set(held)
+    steps = jnp.zeros((ITERS - 1,) + step_size.shape[:2], step_size.dtype).at[0].set(
+        step_size[:, :, 0]
+    )
+
+    def middle_step(index, carry):
+        solution, residual, direction, norm_now, kept, steps = carry
+        arrived = exchange(pack(direction))
+        kept = lax.dynamic_update_index_in_dim(kept, arrived, index, 0)
+        shares = unpack(exchange(owner_apply(prompt_keys, arrived, chosen)))
+        solution, residual, direction, norm_now, step_size = requester_step(
+            shares, solution, residual, direction, norm_now
+        )
+        steps = lax.dynamic_update_index_in_dim(steps, step_size[:, :, 0], index, 0)
+        return solution, residual, direction, norm_now, kept, steps
+
+    solution, residual, direction, norm_now, kept, steps = lax.fori_loop(
+        1, ITERS - 1, middle_step, (solution, residual, direction, norm_now, kept, steps)
+    )
 
     local_part = (
         decay_col * own_matvec(own_keys, direction)
@@ -159,17 +167,22 @@
     )
     local_curve = jnp.sum(direction * local_part, axis=2)
     scalars = jnp.concatenate(
-        [step_prev[:, :, 0], norm_now[:, :, 0], local_curve, (decay_col * weight_col)[:, :, 0]],
+        [jnp.transpose(steps, (1, 0, 2)).reshape(row_count, -1), norm_now[:, :, 0], local_curve,
+         (decay_col * weight_col)[:, :, 0]],
         axis=1,
     )
     arrived = exchange(jnp.concatenate([pack(direction), lane_row(pack(scalars))], axis=1))
     extra = arrived[:, head_count]
-    running = running + extra[:, :head_count][:, :, None] * held
     held = arrived[:, :head_count]
+    known = (ITERS - 1) * head_count
+    steps_in = jnp.transpose(extra[:, :known].reshape(slot_count, ITERS - 1, head_count), (1, 0, 2))
+    running = jnp.sum(steps_in[:, :, :, None] * kept, axis=0)
     prompt_part = owner_apply(prompt_keys, held, chosen)
     prompt_curve = jnp.sum(held * prompt_part, axis=2)
-    rr_in = extra[:, head_count : 2 * head_count]
-    curve = extra[:, 2 * head_count : 3 * head_count] + extra[:, 3 * head_count : 4 * head_count] * prompt_curve
+    rr_in = extra[:, known : known + head_count]
+    curve = extra[:, known + head_count : known + 2 * head_count] + extra[
+        :, known + 2 * head_count : known + 3 * head_count
+    ] * prompt_curve
     step_last = jnp.where(slot_used[:, None], rr_in / jnp.where(slot_used[:, None], curve, 1.0), 0.0)
     running = running + step_last[:, :, None] * held
     finished = owner_apply(prompt_values, running, chosen)

time: 298 us -> 310 us (1.040)
  waiting for transfers between devices: 98.9 us -> 64.6 us
  local copies, waits for them, and re-layouts: 41.8 us -> 65 us
  other arithmetic: 68.6 us -> 89.4 us
    all_to_all x15, waiting for transfers between devices: 97.7 us -> 63.4 us  [exchange(): lax.all_to_all(shaped, 'req', split_axis=0, concat_axis=0, tiled=True)]
    gather x21 -> x14, other arithmetic: 0.12 us -> 11.7 us  [the longest x7 7.4 us: unpack(): taken = jnp.take(shaped, peer_of_run, axis=0, mode='clip')]
    mul x6, local copies, waits for them, and re-layouts: 0.51 us -> 8.04 us  [requester_step(): decay_col * shared]
    mul x6, local copies, waits for them, and re-layouts: 0.51 us -> 8.01 us  [requester_step(): write_col * key_now * jnp.sum(key_now * direction, axis=2, keepdims=True)]
    mul x0 -> x13, other arithmetic: none -> 5.25 us  [the longest x6 5.12 us: requester_step(): decay_col * shared]
    and x14 -> x0, other arithmetic: 4.32 us -> none  [the longest x7 4.26 us: unpack(): taken = jnp.take(slots, slot_of, axis=0)]
    mul x6, local copies, waits for them, and re-layouts: 0.51 us -> 4.58 us  [requester_step(): shared = weight_col * shares + own_matvec(own_keys, direction)]
    dynamic_update_slice x0 -> x6, other arithmetic: none -> 3.6 us  [middle_step(): steps = lax.dynamic_update_index_in_dim(steps, step_size[:, :, 0], index, 0)]
  transfers between devices with their start and end apart: 16 -> 16, of which waited for: 16 -> 16; matrix products, arithmetic and copies ran while one was open for 13% -> 20% of each run, Pallas kernels for 0% -> 0%
where the time goes in v4:
time: 310 us; the launch traced here: 306 us
  other arithmetic  89.4 us (29%)
  local copies, waits for them, and re-layouts  65 us (21%)
  waiting for transfers between devices  64.6 us (21%)
  starting transfers between devices  59.6 us (19%)
  blocking collectives  14.5 us (5%)
  matrix products  11.4 us (4%)
    all_to_all x15, waiting for transfers between devices, exchange(): lax.all_to_all(shaped, 'req', split_axis=0, concat_axis=0, tiled=True)  63.4 us
    all_to_all x15, starting transfers between devices, exchange(): lax.all_to_all(shaped, 'req', split_axis=0, concat_axis=0, tiled=True)  59.6 us
    reduce_sum x9, other arithmetic, own_matvec(): return jnp.sum(matrices * vectors[:, :, None, :], axis=3)  40.4 us
    all_to_all x1, blocking collectives, exchange(): lax.all_to_all(shaped, 'req', split_axis=0, concat_axis=0, tiled=True)  12.2 us
    gather x10, local copies, waits for them, and re-layouts, pack(): taken = jnp.take(padded, run_of_peer, axis=0, mode='clip')  11.3 us
    mul x7, other arithmetic, requester_step(): write_col * key_now * jnp.sum(key_now * direction, axis=2, keepdims=True)  9.18 us
    mul x6, local copies, waits for them, and re-layouts, requester_step(): decay_col * shared  8.04 us
    dot_general x9, matrix products, owner_apply(): return jnp.einsum('gshj,ghij->shi', split, states, precision=highest)  8.03 us
  transfers between devices with their start and end apart: 16, of which 16 were waited for; matrix products, arithmetic and copies ran while one was open for 20% of the time, Pallas kernels for 0%

profile of v4, /device:TPU:0, one launch (start us, length us, event | category | flops | bytes accessed | tf_op | source)
XLA Modules:
  0.0 306.0 jit_solution(7025720203629372330)
XLA Ops:
  5.6 6.0 %copy.187 = bf16[1024,4,3,128]{0,3,2,1:T(8,128)(2,1)} copy(bf16[1024,4,3,128]{3,1,2,0:T(4,128)(2,1)} %param.23) | data formatting | bytes 6291456 | tf_op args[2]
  20.6 8.2 %all-to-all-start.2 = ((f32[16,6,5,128]{3,1,2,0:T(8,128)}), f32[16,6,5,128]{3,1,2,0:T(8,128)S(1)}, u32[]{:S(2)}, u32[]{:S(2)}) async-start(f32[16,6,5,128]{3,1,2,0:T(8,128)} %copy.199), calls=%async_computation.2 | async-start | bytes 655360 | tf_op jit(solution)/shard_map/all_to_all | solution.py:101
  29.0 11.5 %all-to-all-done.2 = f32[16,6,5,128]{3,1,2,0:T(8,128)S(1)} async-done(((f32[16,6,5,128]{3,1,2,0:T(8,128)}), f32[16,6,5,128]{3,1,2,0:T(8,128)S(1)}, u32[]{:S(2)}, u32[]{:S(2)}) %all-to-all-start.2) | async-done | bytes 245792 | tf_op jit(solution)/shard_map/all_to_all | solution.py:101
  42.8 3.7 %all-to-all-start.3 = ((f32[16,6,4,128]{3,2,1,0:T(4,128)}), f32[16,6,4,128]{3,2,1,0:T(4,128)S(1)}, u32[]{:S(2)}, u32[]{:S(2)}) async-start(f32[16,6,4,128]{3,2,1,0:T(4,128)} %bitcast.42), calls=%async_computation.3 | async-start | bytes 393216 | tf_op jit(solution)/shard_map/all_to_all | solution.py:101
  48.0 4.5 %multiply_reduce_fusion.6 = f32[24,4,128]{2,1,0:T(4,128)S(1)} fusion(f32[24,4,128,128]{3,2,1,0:T(8,128)} %param.29, f32[24,4,128]{2,1,0:T(4,128)S(1)} %copy.205), kind=kLoop, calls=%fused_computation.43 | loop fusion | flops 3133440 | bytes 6389760 | tf_op jit(solution)/shard_map/reduce_sum | solution.py:16
  57.2 191.1 %while.27 = (s32[]{:T(128)}, f32[24,4,128]{2,1,0:T(4,128)S(1)}, f32[24,4,128]{2,1,0:T(4,128)S(1)}, f32[24,4,128]{2,1,0:T(4,128)S(1)}, f32[24,4,1]{0,1,2:T(4,128)...) while((s32[]{:T(128)}, f32[24,4,128]{2,1,0:T(4,128)S(1)}, ...), condition=%wide.region_17.18_spmd, body=%wide.region_12.17_spmd.sunk | while | flops 154573120 | bytes 11422411 | solution.py:159
  59.2 5.2 %all-to-all-start = ((f32[16,6,4,128]{3,2,1,0:T(4,128)}), f32[16,6,4,128]{3,2,1,0:T(4,128)S(1)}, u32[]{:S(2)}, u32[]{:S(2)}) async-start(f32[16,6,4,128]{3,2,1,0:T(4,128)} %gather_fusion), calls=%async_computation | async-start | bytes 393216 | tf_op jit(solution)/shard_map/while/body/eval_jaxpr/all_to_all | solution.py:101
  74.7 3.5 %all-to-all-start.1 = ((f32[16,6,4,128]{3,2,1,0:T(4,128)}), f32[16,6,4,128]{3,2,1,0:T(4,128)S(1)}, u32[]{:S(2)}, u32[]{:S(2)}) async-start(f32[16,6,4,128]{3,2,1,0:T(4,128)} %bitcast.253), calls=%async_computation.1 | async-start | bytes 393216 | tf_op jit(solution)/shard_map/while/body/eval_jaxpr/all_to_all | solution.py:101
  78.2 4.5 %multiply_reduce_fusion.18 = f32[24,4,128]{2,1,0:T(4,128)S(1)} fusion(f32[24,4,128,128]{3,2,1,0:T(8,128)} %get-tuple-element.830, f32[24,4,128]{2,1,0:T(4,128)S(1)} %get-tuple-element.795), kind=kLoop, calls=%fused_computation.9.clone.1 | loop fusion | flops 3133440 | bytes 6389760 | tf_op jit(solution)/shard_map/while/body/eval_jaxpr/reduce_sum | solution.py:16
  82.7 3.5 %all-to-all-done.1 = f32[16,6,4,128]{3,2,1,0:T(4,128)S(1)} async-done(((f32[16,6,4,128]{3,2,1,0:T(4,128)}), f32[16,6,4,128]{3,2,1,0:T(4,128)S(1)}, u32[]{:S(2)}, u32[]{:S(2)}) %all-to-all-start.1) | async-done | bytes 196640 | tf_op jit(solution)/shard_map/while/body/eval_jaxpr/all_to_all | solution.py:101
  92.5 3.5 %all-to-all-start = ((f32[16,6,4,128]{3,2,1,0:T(4,128)}), f32[16,6,4,128]{3,2,1,0:T(4,128)S(1)}, u32[]{:S(2)}, u32[]{:S(2)}) async-start(f32[16,6,4,128]{3,2,1,0:T(4,128)} %gather_fusion), calls=%async_computation | async-start | bytes 393216 | tf_op jit(solution)/shard_map/while/body/eval_jaxpr/all_to_all | solution.py:101
  106.2 3.5 %all-to-all-start.1 = ((f32[16,6,4,128]{3,2,1,0:T(4,128)}), f32[16,6,4,128]{3,2,1,0:T(4,128)S(1)}, u32[]{:S(2)}, u32[]{:S(2)}) async-start(f32[16,6,4,128]{3,2,1,0:T(4,128)} %bitcast.253), calls=%async_computation.1 | async-start | bytes 393216 | tf_op jit(solution)/shard_map/while/body/eval_jaxpr/all_to_all | solution.py:101
  109.8 4.5 %multiply_reduce_fusion.18 = f32[24,4,128]{2,1,0:T(4,128)S(1)} fusion(f32[24,4,128,128]{3,2,1,0:T(8,128)} %get-tuple-element.830, f32[24,4,128]{2,1,0:T(4,128)S(1)} %get-tuple-element.795), kind=kLoop, calls=%fused_computation.9.clone.1 | loop fusion | flops 3133440 | bytes 6389760 | tf_op jit(solution)/shard_map/while/body/eval_jaxpr/reduce_sum | solution.py:16
  114.3 3.5 %all-to-all-done.1 = f32[16,6,4,128]{3,2,1,0:T(4,128)S(1)} async-done(((f32[16,6,4,128]{3,2,1,0:T(4,128)}), f32[16,6,4,128]{3,2,1,0:T(4,128)S(1)}, u32[]{:S(2)}, u32[]{:S(2)}) %all-to-all-start.1) | async-done | bytes 196640 | tf_op jit(solution)/shard_map/while/body/eval_jaxpr/all_to_all | solution.py:101
  124.0 3.5 %all-to-all-start = ((f32[16,6,4,128]{3,2,1,0:T(4,128)}), f32[16,6,4,128]{3,2,1,0:T(4,128)S(1)}, u32[]{:S(2)}, u32[]{:S(2)}) async-start(f32[16,6,4,128]{3,2,1,0:T(4,128)} %gather_fusion), calls=%async_computation | async-start | bytes 393216 | tf_op jit(solution)/shard_map/while/body/eval_jaxpr/all_to_all | solution.py:101
  137.8 3.5 %all-to-all-start.1 = ((f32[16,6,4,128]{3,2,1,0:T(4,128)}), f32[16,6,4,128]{3,2,1,0:T(4,128)S(1)}, u32[]{:S(2)}, u32[]{:S(2)}) async-start(f32[16,6,4,128]{3,2,1,0:T(4,128)} %bitcast.253), calls=%async_computation.1 | async-start | bytes 393216 | tf_op jit(solution)/shard_map/while/body/eval_jaxpr/all_to_all | solution.py:101
  141.3 4.5 %multiply_reduce_fusion.18 = f32[24,4,128]{2,1,0:T(4,128)S(1)} fusion(f32[24,4,128,128]{3,2,1,0:T(8,128)} %get-tuple-element.830, f32[24,4,128]{2,1,0:T(4,128)S(1)} %get-tuple-element.795), kind=kLoop, calls=%fused_computation.9.clone.1 | loop fusion | flops 3133440 | bytes 6389760 | tf_op jit(solution)/shard_map/while/body/eval_jaxpr/reduce_sum | solution.py:16
  145.8 3.5 %all-to-all-done.1 = f32[16,6,4,128]{3,2,1,0:T(4,128)S(1)} async-done(((f32[16,6,4,128]{3,2,1,0:T(4,128)}), f32[16,6,4,128]{3,2,1,0:T(4,128)S(1)}, u32[]{:S(2)}, u32[]{:S(2)}) %all-to-all-start.1) | async-done | bytes 196640 | tf_op jit(solution)/shard_map/while/body/eval_jaxpr/all_to_all | solution.py:101
  169.3 3.5 %all-to-all-start.1 = ((f32[16,6,4,128]{3,2,1,0:T(4,128)}), f32[16,6,4,128]{3,2,1,0:T(4,128)S(1)}, u32[]{:S(2)}, u32[]{:S(2)}) async-start(f32[16,6,4,128]{3,2,1,0:T(4,128)} %bitcast.253), calls=%async_computation.1 | async-start | bytes 393216 | tf_op jit(solution)/shard_map/while/body/eval_jaxpr/all_to_all | solution.py:101
  172.9 4.5 %multiply_reduce_fusion.18 = f32[24,4,128]{2,1,0:T(4,128)S(1)} fusion(f32[24,4,128,128]{3,2,1,0:T(8,128)} %get-tuple-element.830, f32[24,4,128]{2,1,0:T(4,128)S(1)} %get-tuple-element.795), kind=kLoop, calls=%fused_computation.9.clone.1 | loop fusion | flops 3133440 | bytes 6389760 | tf_op jit(solution)/shard_map/while/body/eval_jaxpr/reduce_sum | solution.py:16
  177.4 3.5 %all-to-all-done.1 = f32[16,6,4,128]{3,2,1,0:T(4,128)S(1)} async-done(((f32[16,6,4,128]{3,2,1,0:T(4,128)}), f32[16,6,4,128]{3,2,1,0:T(4,128)S(1)}, u32[]{:S(2)}, u32[]{:S(2)}) %all-to-all-start.1) | async-done | bytes 196640 | tf_op jit(solution)/shard_map/while/body/eval_jaxpr/all_to_all | solution.py:101
  200.9 3.5 %all-to-all-start.1 = ((f32[16,6,4,128]{3,2,1,0:T(4,128)}), f32[16,6,4,128]{3,2,1,0:T(4,128)S(1)}, u32[]{:S(2)}, u32[]{:S(2)}) async-start(f32[16,6,4,128]{3,2,1,0:T(4,128)} %bitcast.253), calls=%async_computation.1 | async-start | bytes 393216 | tf_op jit(solution)/shard_map/while/body/eval_jaxpr/all_to_all | solution.py:101
  204.5 4.5 %multiply_reduce_fusion.18 = f32[24,4,128]{2,1,0:T(4,128)S(1)} fusion(f32[24,4,128,128]{3,2,1,0:T(8,128)} %get-tuple-element.830, f32[24,4,128]{2,1,0:T(4,128)S(1)} %get-tuple-element.795), kind=kLoop, calls=%fused_computation.9.clone.1 | loop fusion | flops 3133440 | bytes 6389760 | tf_op jit(solution)/shard_map/while/body/eval_jaxpr/reduce_sum | solution.py:16
  209.0 3.5 %all-to-all-done.1 = f32[16,6,4,128]{3,2,1,0:T(4,128)S(1)} async-done(((f32[16,6,4,128]{3,2,1,0:T(4,128)}), f32[16,6,4,128]{3,2,1,0:T(4,128)S(1)}, u32[]{:S(2)}, u32[]{:S(2)}) %all-to-all-start.1) | async-done | bytes 196640 | tf_op jit(solution)/shard_map/while/body/eval_jaxpr/all_to_all | solution.py:101
  232.5 3.5 %all-to-all-start.1 = ((f32[16,6,4,128]{3,2,1,0:T(4,128)}), f32[16,6,4,128]{3,2,1,0:T(4,128)S(1)}, u32[]{:S(2)}, u32[]{:S(2)}) async-start(f32[16,6,4,128]{3,2,1,0:T(4,128)} %bitcast.253), calls=%async_computation.1 | async-start | bytes 393216 | tf_op jit(solution)/shard_map/while/body/eval_jaxpr/all_to_all | solution.py:101
  236.0 4.5 %multiply_reduce_fusion.18 = f32[24,4,128]{2,1,0:T(4,128)S(1)} fusion(f32[24,4,128,128]{3,2,1,0:T(8,128)} %get-tuple-element.830, f32[24,4,128]{2,1,0:T(4,128)S(1)} %get-tuple-element.795), kind=kLoop, calls=%fused_computation.9.clone.1 | loop fusion | flops 3133440 | bytes 6389760 | tf_op jit(solution)/shard_map/while/body/eval_jaxpr/reduce_sum | solution.py:16
  240.6 3.5 %all-to-all-done.1 = f32[16,6,4,128]{3,2,1,0:T(4,128)S(1)} async-done(((f32[16,6,4,128]{3,2,1,0:T(4,128)}), f32[16,6,4,128]{3,2,1,0:T(4,128)S(1)}, u32[]{:S(2)}, u32[]{:S(2)}) %all-to-all-start.1) | async-done | bytes 196640 | tf_op jit(solution)/shard_map/while/body/eval_jaxpr/all_to_all | solution.py:101
  248.4 4.5 %multiply_reduce_fusion.5 = f32[24,4,128]{2,1,0:T(4,128)S(1)} fusion(f32[24,4,128,128]{3,2,1,0:T(8,128)} %get-tuple-element.838, f32[24,4,128]{2,1,0:T(4,128)S(1)} %get-tuple-element.473), kind=kLoop, calls=%fused_computation.42 | loop fusion | flops 3133440 | bytes 6389760 | tf_op jit(solution)/shard_map/reduce_sum | solution.py:16
  257.3 12.2 %all_to_all.46 = f32[16,6,5,128]{3,1,2,0:T(8,128)S(1)} all-to-all(f32[16,6,5,128]{3,1,2,0:T(8,128)S(1)} %copy.223), channel_id=1, replica_groups=mesh['req'=16,'head'=2] {'req'}, dimensions={0} | all-to-all | bytes 491520 | tf_op jit(solution)/shard_map/all_to_all | solution.py:101
  284.3 3.7 %all-to-all-start.5 = ((f32[16,6,5,128]{3,1,2,0:T(8,128)}), f32[16,6,5,128]{3,1,2,0:T(8,128)S(1)}, u32[]{:S(2)}, u32[]{:S(2)}) async-start(f32[16,6,5,128]{3,1,2,0:T(8,128)} %pad_maximum_fusion.2), calls=%async_computation.5 | async-start | bytes 655360 | tf_op jit(solution)/shard_map/all_to_all | solution.py:101
  288.0 9.0 %all-to-all-done.5 = f32[16,6,5,128]{3,1,2,0:T(8,128)S(1)} async-done(((f32[16,6,5,128]{3,1,2,0:T(8,128)}), f32[16,6,5,128]{3,1,2,0:T(8,128)S(1)}, u32[]{:S(2)}, u32[]{:S(2)}) %all-to-all-start.5) | async-done | bytes 245792 | tf_op jit(solution)/shard_map/all_to_all | solution.py:101
  298.1 4.5 %multiply_reduce_fusion.4 = f32[24,4,128]{2,1,0:T(4,128)S(1)} fusion(f32[24,4,128,128]{3,2,1,0:T(8,128)} %param.30, f32[24,4,128]{2,1,0:T(4,128)S(1)} %copy.236), kind=kLoop, calls=%fused_computation.41 | loop fusion | flops 3133440 | bytes 6389760 | tf_op jit(solution)/shard_map/reduce_sum | solution.py:16
  (336 shorter events, 155.5 us)
Async XLA Ops:
  0.0 303.7 %copy-start = (bf16[4,128,1024]{2,1,0:T(8,128)(2,1)S(1)}, bf16[4,128,1024]{2,1,0:T(8,128)(2,1)}, u32[]{:S(2)}) copy-start(bf16[4,128,1024]{2,1,0:T(8,128)(2,1)} %param.35) | copy-start | bytes 3145732
  1.3 53.7 %copy-start.25 = (pred[24]{0:T(512)(128)(4,1)}, pred[24]{0:T(512)(128)(4,1)S(1)}, u32[]{:S(2)}) copy-start(pred[24]{0:T(512)(128)(4,1)S(1)} %get-tuple-element.632) | copy-start | bytes 76
  11.6 7.4 %copy-start.16 = (bf16[1024,2,4]{0,2,1:T(4,128)(2,1)S(1)}, bf16[1024,2,4]{0,2,1:T(4,128)(2,1)}, u32[]{:S(2)}) copy-start(bf16[1024,2,4]{0,2,1:T(4,128)(2,1)} %param.26) | copy-start | bytes 49156
  14.5 42.0 %copy-start.3 = (f32[24,4,3,128]{3,0,2,1:T(8,128)}, f32[24,4,3,128]{3,0,2,1:T(8,128)S(1)}, u32[]{:S(2)}) copy-start(f32[24,4,3,128]{3,0,2,1:T(8,128)S(1)} %divide_multiply_fusion) | copy-start | bytes 442372
  14.5 26.8 %copy-start.1 = (f32[2,4,128,128]{3,2,1,0:T(8,128)S(1)}, f32[2,4,128,128]{3,2,1,0:T(8,128)}, u32[]{:S(2)}) copy-start(f32[2,4,128,128]{3,2,1,0:T(8,128)} %param.31) | copy-start | bytes 1572868
  19.9 35.1 %copy-start.18 = (f32[24,4]{0,1:T(4,128)}, f32[24,4]{0,1:T(4,128)S(1)}, u32[]{:S(2)}) copy-start(f32[24,4]{0,1:T(4,128)S(1)} %get-tuple-element.626) | copy-start | bytes 1156
  19.9 35.1 %copy-start.21 = (f32[24,4]{0,1:T(4,128)}, f32[24,4]{0,1:T(4,128)S(1)}, u32[]{:S(2)}) copy-start(f32[24,4]{0,1:T(4,128)S(1)} %get-tuple-element.627) | copy-start | bytes 1156
  20.6 19.9 %all-to-all-start.2 = ((f32[16,6,5,128]{3,1,2,0:T(8,128)}), f32[16,6,5,128]{3,1,2,0:T(8,128)S(1)}, u32[]{:S(2)}, u32[]{:S(2)}) async-start(f32[16,6,5,128]{3,1,2,0:T(8,128)} %copy.199), calls=%async_computation.2 | async-start | bytes 655360 | tf_op jit(solution)/shard_map/all_to_all | solution.py:101
  28.8 23.7 %copy-start.15 = (s32[4]{0:T(128)}, s32[4]{0:T(128)S(1)}, u32[]{:S(2)}) copy-start(s32[4]{0:T(128)S(1)} %broadcast_select_fusion.1) | copy-start | bytes 52
  29.0 26.0 %copy-start.4 = (f32[24,4,128]{2,0,1:T(8,128)}, f32[24,4,128]{2,0,1:T(8,128)S(1)}, u32[]{:S(2)}) copy-start(f32[24,4,128]{2,0,1:T(8,128)S(1)} %fusion.68) | copy-start | bytes 147460
  42.8 11.6 %all-to-all-start.3 = ((f32[16,6,4,128]{3,2,1,0:T(4,128)}), f32[16,6,4,128]{3,2,1,0:T(4,128)S(1)}, u32[]{:S(2)}, u32[]{:S(2)}) async-start(f32[16,6,4,128]{3,2,1,0:T(4,128)} %bitcast.42), calls=%async_computation.3 | async-start | bytes 393216 | tf_op jit(solution)/shard_map/all_to_all | solution.py:101
  46.5 7.9 %copy-start.24 = (s32[1024]{0:T(1024)}, s32[1024]{0:T(1024)S(1)}, u32[]{:S(2)}) copy-start(s32[1024]{0:T(1024)S(1)} %pad_clamp_fusion.2) | copy-start | bytes 12292
  48.0 7.0 %copy-start.30 = (f32[4]{0:T(128)S(1)}, f32[4]{0:T(128)}, u32[]{:S(2)}) copy-start(f32[4]{0:T(128)} %param.28) | copy-start | bytes 52
  59.2 13.3 %all-to-all-start = ((f32[16,6,4,128]{3,2,1,0:T(4,128)}), f32[16,6,4,128]{3,2,1,0:T(4,128)S(1)}, u32[]{:S(2)}, u32[]{:S(2)}) async-start(f32[16,6,4,128]{3,2,1,0:T(4,128)} %gather_fusion), calls=%async_computation | async-start | bytes 393216 | tf_op jit(solution)/shard_map/while/body/eval_jaxpr/all_to_all | solution.py:101
  74.7 11.6 %all-to-all-start.1 = ((f32[16,6,4,128]{3,2,1,0:T(4,128)}), f32[16,6,4,128]{3,2,1,0:T(4,128)S(1)}, u32[]{:S(2)}, u32[]{:S(2)}) async-start(f32[16,6,4,128]{3,2,1,0:T(4,128)} %bitcast.253), calls=%async_computation.1 | async-start | bytes 393216 | tf_op jit(solution)/shard_map/while/body/eval_jaxpr/all_to_all | solution.py:101
  92.5 11.6 %all-to-all-start = ((f32[16,6,4,128]{3,2,1,0:T(4,128)}), f32[16,6,4,128]{3,2,1,0:T(4,128)S(1)}, u32[]{:S(2)}, u32[]{:S(2)}) async-start(f32[16,6,4,128]{3,2,1,0:T(4,128)} %gather_fusion), calls=%async_computation | async-start | bytes 393216 | tf_op jit(solution)/shard_map/while/body/eval_jaxpr/all_to_all | solution.py:101
  106.2 11.6 %all-to-all-start.1 = ((f32[16,6,4,128]{3,2,1,0:T(4,128)}), f32[16,6,4,128]{3,2,1,0:T(4,128)S(1)}, u32[]{:S(2)}, u32[]{:S(2)}) async-start(f32[16,6,4,128]{3,2,1,0:T(4,128)} %bitcast.253), calls=%async_computation.1 | async-start | bytes 393216 | tf_op jit(solution)/shard_map/while/body/eval_jaxpr/all_to_all | solution.py:101
  124.0 11.6 %all-to-all-start = ((f32[16,6,4,128]{3,2,1,0:T(4,128)}), f32[16,6,4,128]{3,2,1,0:T(4,128)S(1)}, u32[]{:S(2)}, u32[]{:S(2)}) async-start(f32[16,6,4,128]{3,2,1,0:T(4,128)} %gather_fusion), calls=%async_computation | async-start | bytes 393216 | tf_op jit(solution)/shard_map/while/body/eval_jaxpr/all_to_all | solution.py:101
  137.8 11.6 %all-to-all-start.1 = ((f32[16,6,4,128]{3,2,1,0:T(4,128)}), f32[16,6,4,128]{3,2,1,0:T(4,128)S(1)}, u32[]{:S(2)}, u32[]{:S(2)}) async-start(f32[16,6,4,128]{3,2,1,0:T(4,128)} %bitcast.253), calls=%async_computation.1 | async-start | bytes 393216 | tf_op jit(solution)/shard_map/while/body/eval_jaxpr/all_to_all | solution.py:101
  155.6 11.6 %all-to-all-start = ((f32[16,6,4,128]{3,2,1,0:T(4,128)}), f32[16,6,4,128]{3,2,1,0:T(4,128)S(1)}, u32[]{:S(2)}, u32[]{:S(2)}) async-start(f32[16,6,4,128]{3,2,1,0:T(4,128)} %gather_fusion), calls=%async_computation | async-start | bytes 393216 | tf_op jit(solution)/shard_map/while/body/eval_jaxpr/all_to_all | solution.py:101
  169.3 11.6 %all-to-all-start.1 = ((f32[16,6,4,128]{3,2,1,0:T(4,128)}), f32[16,6,4,128]{3,2,1,0:T(4,128)S(1)}, u32[]{:S(2)}, u32[]{:S(2)}) async-start(f32[16,6,4,128]{3,2,1,0:T(4,128)} %bitcast.253), calls=%async_computation.1 | async-start | bytes 393216 | tf_op jit(solution)/shard_map/while/body/eval_jaxpr/all_to_all | solution.py:101
  187.2 11.6 %all-to-all-start = ((f32[16,6,4,128]{3,2,1,0:T(4,128)}), f32[16,6,4,128]{3,2,1,0:T(4,128)S(1)}, u32[]{:S(2)}, u32[]{:S(2)}) async-start(f32[16,6,4,128]{3,2,1,0:T(4,128)} %gather_fusion), calls=%async_computation | async-start | bytes 393216 | tf_op jit(solution)/shard_map/while/body/eval_jaxpr/all_to_all | solution.py:101
  200.9 11.6 %all-to-all-start.1 = ((f32[16,6,4,128]{3,2,1,0:T(4,128)}), f32[16,6,4,128]{3,2,1,0:T(4,128)S(1)}, u32[]{:S(2)}, u32[]{:S(2)}) async-start(f32[16,6,4,128]{3,2,1,0:T(4,128)} %bitcast.253), calls=%async_computation.1 | async-start | bytes 393216 | tf_op jit(solution)/shard_map/while/body/eval_jaxpr/all_to_all | solution.py:101
  218.7 11.6 %all-to-all-start = ((f32[16,6,4,128]{3,2,1,0:T(4,128)}), f32[16,6,4,128]{3,2,1,0:T(4,128)S(1)}, u32[]{:S(2)}, u32[]{:S(2)}) async-start(f32[16,6,4,128]{3,2,1,0:T(4,128)} %gather_fusion), calls=%async_computation | async-start | bytes 393216 | tf_op jit(solution)/shard_map/while/body/eval_jaxpr/all_to_all | solution.py:101
  232.5 11.6 %all-to-all-start.1 = ((f32[16,6,4,128]{3,2,1,0:T(4,128)}), f32[16,6,4,128]{3,2,1,0:T(4,128)S(1)}, u32[]{:S(2)}, u32[]{:S(2)}) async-start(f32[16,6,4,128]{3,2,1,0:T(4,128)} %bitcast.253), calls=%async_computation.1 | async-start | bytes 393216 | tf_op jit(solution)/shard_map/while/body/eval_jaxpr/all_to_all | solution.py:101
  253.0 18.8 %copy-start.10 = (pred[96]{0:T(512)(128)(4,1)S(1)}, pred[96]{0:T(512)(128)(4,1)}, u32[]{:S(2)}) copy-start(pred[96]{0:T(512)(128)(4,1)} %get-tuple-element.846) | copy-start | bytes 292
  253.0 18.8 %copy-start.13 = (pred[96]{0:T(512)(128)(4,1)S(1)}, pred[96]{0:T(512)(128)(4,1)}, u32[]{:S(2)}) copy-start(pred[96]{0:T(512)(128)(4,1)} %get-tuple-element.847) | copy-start | bytes 292
  253.0 24.0 %copy-start.2 = (f32[2,4,128,128]{3,2,1,0:T(8,128)S(1)}, f32[2,4,128,128]{3,2,1,0:T(8,128)}, u32[]{:S(2)}) copy-start(f32[2,4,128,128]{3,2,1,0:T(8,128)} %param.31) | copy-start | bytes 1572868
  279.6 18.1 %copy-start.26 = (pred[24]{0:T(512)(128)(4,1)S(1)}, pred[24]{0:T(512)(128)(4,1)}, u32[]{:S(2)}) copy-start(pred[24]{0:T(512)(128)(4,1)} %copy-done.25) | copy-start | bytes 76
  284.3 12.7 %all-to-all-start.5 = ((f32[16,6,5,128]{3,1,2,0:T(8,128)}), f32[16,6,5,128]{3,1,2,0:T(8,128)S(1)}, u32[]{:S(2)}, u32[]{:S(2)}) async-start(f32[16,6,5,128]{3,1,2,0:T(8,128)} %pad_maximum_fusion.2), calls=%async_computation.5 | async-start | bytes 655360 | tf_op jit(solution)/shard_map/all_to_all | solution.py:101
  298.0 7.2 %copy-start.6 = (bf16[24,512]{1,0:T(8,128)(2,1)S(1)}, bf16[24,512]{1,0:T(8,128)(2,1)}, u32[]{:S(2)}) copy-start(bf16[24,512]{1,0:T(8,128)(2,1)} %param.21) | copy-start | bytes 73732
  304.0 1.3 collective-permute-start
  (16 other events, 66.9 us)

commit v5 on v2

--- a/solution.py
+++ b/solution.py
@@ -99,9 +99,9 @@
         return jnp.take(padded, source, axis=0)
 
     def exchange(slots):
-        shaped = slots.astype(jnp.bfloat16).reshape((peer_count, capacity) + slots.shape[1:])
+        shaped = slots.reshape((peer_count, capacity) + slots.shape[1:])
         moved = lax.all_to_all(shaped, "req", split_axis=0, concat_axis=0, tiled=True)
-        return moved.reshape(slots.shape).astype(jnp.float32)
+        return moved.reshape(slots.shape)
 
     def unpack(slots):
         taken = jnp.take(slots, slot_of, axis=0)
@@ -143,10 +143,35 @@
     )
     carry = cg_step(first[:, :head_count], carry)
     carry = lax.fori_loop(
-        1, ITERS, lambda _, state: cg_step(exchange(pack(state[2])), state), carry
-    )
-    solution = carry[0]
-    value_sum = unpack(exchange(owner_apply(prompt_values, exchange(pack(solution)), chosen)))
+        1, ITERS - 1, lambda _, state: cg_step(exchange(pack(state[2])), state), carry
+    )
+    solution, residual, direction, norm_now = carry
+
+    local_part = (
+        decay_col * own_matvec(own_keys, direction)
+        + write_col * key_now * jnp.sum(key_now * direction, axis=2, keepdims=True)
+        + ridge_col * direction
+    )
+    scalars = jnp.concatenate(
+        [norm_now[:, :, 0], jnp.sum(direction * local_part, axis=2), (decay_col * weight_col)[:, :, 0]],
+        axis=1,
+    )
+    scalar_row = jnp.pad(scalars, ((0, 0), (0, head_size - scalars.shape[1])))[:, None, :]
+    arrived = exchange(jnp.concatenate([pack(direction), pack(solution), pack(scalar_row)], axis=1))
+    held = arrived[:, :head_count]
+    partial = arrived[:, head_count : 2 * head_count]
+    extra = arrived[:, 2 * head_count]
+    prompt_curve = jnp.sum(held * owner_apply(prompt_keys, held, chosen), axis=2)
+    curve = extra[:, head_count : 2 * head_count] + extra[:, 2 * head_count : 3 * head_count] * prompt_curve
+    slot_used = labels_in > 0.5
+    step_last = jnp.where(
+        slot_used[:, None], extra[:, :head_count] / jnp.where(slot_used[:, None], curve, 1.0), 0.0
+    )
+    finished = owner_apply(prompt_values, partial + step_last[:, :, None] * held, chosen)
+    step_row = jnp.pad(step_last, ((0, 0), (0, head_size - head_count)))[:, None, :]
+    returned = unpack(exchange(jnp.concatenate([finished, step_row], axis=1)))
+    value_sum = returned[:, :head_count]
+    solution = solution + returned[:, head_count, :head_count][:, :, None] * direction
     shared_out = weight_col * value_sum + own_matvec(own_values, solution)
     readout = decay_col * shared_out + write_col * value_now * jnp.sum(
         key_now * solution, axis=2, keepdims=True

time: 279 us -> 274 us (0.982)
  blocking collectives: 2.35 us -> 18.3 us
  starting transfers between devices: 71.1 us -> 58.2 us
  waiting for transfers between devices: 102 us -> 93 us
    all_to_all x0 -> x1, blocking collectives: none -> 16 us  [exchange(): lax.all_to_all(shaped, 'req', split_axis=0, concat_axis=0, tiled=True)]
    all_to_all x18 -> x15, starting transfers between devices: 71 us -> 58.1 us  [exchange(): lax.all_to_all(shaped, 'req', split_axis=0, concat_axis=0, tiled=True)]
    all_to_all x18 -> x15, waiting for transfers between devices: 101 us -> 91.8 us  [exchange(): lax.all_to_all(shaped, 'req', split_axis=0, concat_axis=0, tiled=True)]
    convert_element_type x26 -> x1, other arithmetic: 6.76 us -> 0.01 us  [on_device(): slot_label.astype(jnp.float32)[:, None, None]]
    convert_element_type x11 -> x0, local copies, waits for them, and re-layouts: 6.21 us -> none  [the longest x9 6.1 us: exchange(): slots.astype(jnp.bfloat16).reshape((peer_count, capacity) + slots.shape[1:])]
    transpose x0 -> x8, local copies, waits for them, and re-layouts: none -> 5.75 us  [owner_apply(): return jnp.einsum('gshj,ghij->shi', split, states, precision=highest)]
    select_n x8 -> x17, other arithmetic: 0.03 us -> 5.61 us  [pack(): return jnp.take(padded, source, axis=0)]
    gather x9 -> x10, local copies, waits for them, and re-layouts: 6.32 us -> 6.96 us  [pack(): return jnp.take(padded, source, axis=0)]
  transfers between devices with their start and end apart: 19 -> 16, of which waited for: 19 -> 16; matrix products, arithmetic and copies ran while one was open for 14% -> 12% of each run, Pallas kernels for 0% -> 0%
where the time goes in v5:
time: 274 us; the launch traced here: 272 us
  waiting for transfers between devices  93 us (34%)
  other arithmetic  59 us (22%)
  starting transfers between devices  58.2 us (21%)
  local copies, waits for them, and re-layouts  31.7 us (12%)
  blocking collectives  18.3 us (7%)
  matrix products  10.5 us (4%)
    all_to_all x15, waiting for transfers between devices, exchange(): lax.all_to_all(shaped, 'req', split_axis=0, concat_axis=0, tiled=True)  91.8 us
    all_to_all x15, starting transfers between devices, exchange(): lax.all_to_all(shaped, 'req', split_axis=0, concat_axis=0, tiled=True)  58.1 us
    reduce_sum x9, other arithmetic, own_matvec(): return jnp.sum(matrices * vectors[:, :, None, :], axis=3)  40.4 us
    all_to_all x1, blocking collectives, exchange(): lax.all_to_all(shaped, 'req', split_axis=0, concat_axis=0, tiled=True)  16 us
    dot_general x9, matrix products, owner_apply(): return jnp.einsum('gshj,ghij->shi', split, states, precision=highest)  7.13 us
    gather x10, local copies, waits for them, and re-layouts, pack(): return jnp.take(padded, source, axis=0)  6.96 us
    unnamed x19, local copies, waits for them, and re-layouts  6.32 us
    transpose x8, local copies, waits for them, and re-layouts, owner_apply(): return jnp.einsum('gshj,ghij->shi', split, states, precision=highest)  5.75 us
  transfers between devices with their start and end apart: 16, of which 16 were waited for; matrix products, arithmetic and copies ran while one was open for 12% of the time, Pallas kernels for 0%

profile of v5, /device:TPU:0, one launch (start us, length us, event | category | flops | bytes accessed | tf_op | source)
XLA Modules:
  0.0 271.9 jit_solution(13270832038447367234)
XLA Ops:
  6.9 6.0 %copy.222 = bf16[1024,4,3,128]{0,3,2,1:T(8,128)(2,1)} copy(bf16[1024,4,3,128]{3,1,2,0:T(4,128)(2,1)} %param.23) | data formatting | bytes 6291456 | tf_op args[2]
  18.3 8.2 %all-to-all-start.2 = ((f32[16,6,5,128]{3,1,2,0:T(8,128)}), f32[16,6,5,128]{3,1,2,0:T(8,128)S(1)}, u32[]{:S(2)}, u32[]{:S(2)}) async-start(f32[16,6,5,128]{3,1,2,0:T(8,128)} %copy.232), calls=%async_computation.2 | async-start | bytes 655360 | tf_op jit(solution)/shard_map/all_to_all | solution.py:103
  26.7 11.5 %all-to-all-done.2 = f32[16,6,5,128]{3,1,2,0:T(8,128)S(1)} async-done(((f32[16,6,5,128]{3,1,2,0:T(8,128)}), f32[16,6,5,128]{3,1,2,0:T(8,128)S(1)}, u32[]{:S(2)}, u32[]{:S(2)}) %all-to-all-start.2) | async-done | bytes 245792 | tf_op jit(solution)/shard_map/all_to_all | solution.py:103
  39.9 3.7 %all-to-all-start.3 = ((f32[16,6,4,128]{3,2,1,0:T(4,128)}), f32[16,6,4,128]{3,2,1,0:T(4,128)S(1)}, u32[]{:S(2)}, u32[]{:S(2)}) async-start(f32[16,6,4,128]{3,2,1,0:T(4,128)} %bitcast.38), calls=%async_computation.3 | async-start | bytes 393216 | tf_op jit(solution)/shard_map/all_to_all | solution.py:103
  43.7 4.5 %multiply_reduce_fusion.6 = f32[24,4,128]{2,1,0:T(4,128)S(1)} fusion(f32[24,4,128,128]{3,2,1,0:T(8,128)} %param.29, f32[24,4,128]{2,1,0:T(4,128)S(1)} %copy.238), kind=kLoop, calls=%fused_computation.46 | loop fusion | flops 3133440 | bytes 6389760 | tf_op jit(solution)/shard_map/reduce_sum | solution.py:16
  52.8 170.5 %while.16 = (s32[]{:T(128)}, f32[24,4,128]{2,1,0:T(4,128)S(1)}, f32[24,4,128]{2,1,0:T(4,128)S(1)}, f32[24,4,128]{2,1,0:T(4,128)S(1)}, f32[24,4,1]{0,1,2:T(4,128)...) while((s32[]{:T(128)}, f32[24,4,128]{2,1,0:T(4,128)S(1)}, ...), condition=%wide.region_17.20_spmd, body=%wide.region_12.19_spmd.sunk | while | flops 154635536 | bytes 11313449 | solution.py:145
  54.4 3.5 %all-to-all-start = ((f32[16,6,4,128]{3,2,1,0:T(4,128)}), f32[16,6,4,128]{3,2,1,0:T(4,128)S(1)}, u32[]{:S(2)}, u32[]{:S(2)}) async-start(f32[16,6,4,128]{3,2,1,0:T(4,128)} %bitcast.197), calls=%async_computation | async-start | bytes 393216 | tf_op jit(solution)/shard_map/while/body/eval_jaxpr/all_to_all | solution.py:103
  58.0 8.0 %all-to-all-done = f32[16,6,4,128]{3,2,1,0:T(4,128)S(1)} async-done(((f32[16,6,4,128]{3,2,1,0:T(4,128)}), f32[16,6,4,128]{3,2,1,0:T(4,128)S(1)}, u32[]{:S(2)}, u32[]{:S(2)}) %all-to-all-start) | async-done | bytes 196640 | tf_op jit(solution)/shard_map/while/body/eval_jaxpr/all_to_all | solution.py:103
  67.6 3.5 %all-to-all-start.1 = ((f32[16,6,4,128]{3,2,1,0:T(4,128)}), f32[16,6,4,128]{3,2,1,0:T(4,128)S(1)}, u32[]{:S(2)}, u32[]{:S(2)}) async-start(f32[16,6,4,128]{3,2,1,0:T(4,128)} %bitcast.199), calls=%async_computation.1 | async-start | bytes 393216 | tf_op jit(solution)/shard_map/while/body/eval_jaxpr/all_to_all | solution.py:103
  71.4 4.5 %multiply_reduce_fusion.17 = f32[24,4,128]{2,1,0:T(4,128)S(1)} fusion(f32[24,4,128,128]{3,2,1,0:T(8,128)} %get-tuple-element.444, f32[24,4,128]{2,1,0:T(4,128)S(1)} %get-tuple-element.415), kind=kLoop, calls=%fused_computation.9.clone.1 | loop fusion | flops 3133440 | bytes 6389760 | tf_op jit(solution)/shard_map/while/body/eval_jaxpr/reduce_sum | solution.py:16
  82.7 3.6 %all-to-all-start = ((f32[16,6,4,128]{3,2,1,0:T(4,128)}), f32[16,6,4,128]{3,2,1,0:T(4,128)S(1)}, u32[]{:S(2)}, u32[]{:S(2)}) async-start(f32[16,6,4,128]{3,2,1,0:T(4,128)} %bitcast.197), calls=%async_computation | async-start | bytes 393216 | tf_op jit(solution)/shard_map/while/body/eval_jaxpr/all_to_all | solution.py:103
  86.4 8.1 %all-to-all-done = f32[16,6,4,128]{3,2,1,0:T(4,128)S(1)} async-done(((f32[16,6,4,128]{3,2,1,0:T(4,128)}), f32[16,6,4,128]{3,2,1,0:T(4,128)S(1)}, u32[]{:S(2)}, u32[]{:S(2)}) %all-to-all-start) | async-done | bytes 196640 | tf_op jit(solution)/shard_map/while/body/eval_jaxpr/all_to_all | solution.py:103
  99.8 4.5 %multiply_reduce_fusion.17 = f32[24,4,128]{2,1,0:T(4,128)S(1)} fusion(f32[24,4,128,128]{3,2,1,0:T(8,128)} %get-tuple-element.444, f32[24,4,128]{2,1,0:T(4,128)S(1)} %get-tuple-element.415), kind=kLoop, calls=%fused_computation.9.clone.1 | loop fusion | flops 3133440 | bytes 6389760 | tf_op jit(solution)/shard_map/while/body/eval_jaxpr/reduce_sum | solution.py:16
  111.1 3.6 %all-to-all-start = ((f32[16,6,4,128]{3,2,1,0:T(4,128)}), f32[16,6,4,128]{3,2,1,0:T(4,128)S(1)}, u32[]{:S(2)}, u32[]{:S(2)}) async-start(f32[16,6,4,128]{3,2,1,0:T(4,128)} %bitcast.197), calls=%async_computation | async-start | bytes 393216 | tf_op jit(solution)/shard_map/while/body/eval_jaxpr/all_to_all | solution.py:103
  114.8 8.1 %all-to-all-done = f32[16,6,4,128]{3,2,1,0:T(4,128)S(1)} async-done(((f32[16,6,4,128]{3,2,1,0:T(4,128)}), f32[16,6,4,128]{3,2,1,0:T(4,128)S(1)}, u32[]{:S(2)}, u32[]{:S(2)}) %all-to-all-start) | async-done | bytes 196640 | tf_op jit(solution)/shard_map/while/body/eval_jaxpr/all_to_all | solution.py:103
  124.4 3.5 %all-to-all-start.1 = ((f32[16,6,4,128]{3,2,1,0:T(4,128)}), f32[16,6,4,128]{3,2,1,0:T(4,128)S(1)}, u32[]{:S(2)}, u32[]{:S(2)}) async-start(f32[16,6,4,128]{3,2,1,0:T(4,128)} %bitcast.199), calls=%async_computation.1 | async-start | bytes 393216 | tf_op jit(solution)/shard_map/while/body/eval_jaxpr/all_to_all | solution.py:103
  128.2 4.5 %multiply_reduce_fusion.17 = f32[24,4,128]{2,1,0:T(4,128)S(1)} fusion(f32[24,4,128,128]{3,2,1,0:T(8,128)} %get-tuple-element.444, f32[24,4,128]{2,1,0:T(4,128)S(1)} %get-tuple-element.415), kind=kLoop, calls=%fused_computation.9.clone.1 | loop fusion | flops 3133440 | bytes 6389760 | tf_op jit(solution)/shard_map/while/body/eval_jaxpr/reduce_sum | solution.py:16
  139.6 3.6 %all-to-all-start = ((f32[16,6,4,128]{3,2,1,0:T(4,128)}), f32[16,6,4,128]{3,2,1,0:T(4,128)S(1)}, u32[]{:S(2)}, u32[]{:S(2)}) async-start(f32[16,6,4,128]{3,2,1,0:T(4,128)} %bitcast.197), calls=%async_computation | async-start | bytes 393216 | tf_op jit(solution)/shard_map/while/body/eval_jaxpr/all_to_all | solution.py:103
  143.2 8.1 %all-to-all-done = f32[16,6,4,128]{3,2,1,0:T(4,128)S(1)} async-done(((f32[16,6,4,128]{3,2,1,0:T(4,128)}), f32[16,6,4,128]{3,2,1,0:T(4,128)S(1)}, u32[]{:S(2)}, u32[]{:S(2)}) %all-to-all-start) | async-done | bytes 196640 | tf_op jit(solution)/shard_map/while/body/eval_jaxpr/all_to_all | solution.py:103
  156.6 4.5 %multiply_reduce_fusion.17 = f32[24,4,128]{2,1,0:T(4,128)S(1)} fusion(f32[24,4,128,128]{3,2,1,0:T(8,128)} %get-tuple-element.444, f32[24,4,128]{2,1,0:T(4,128)S(1)} %get-tuple-element.415), kind=kLoop, calls=%fused_computation.9.clone.1 | loop fusion | flops 3133440 | bytes 6389760 | tf_op jit(solution)/shard_map/while/body/eval_jaxpr/reduce_sum | solution.py:16
  168.0 3.6 %all-to-all-start = ((f32[16,6,4,128]{3,2,1,0:T(4,128)}), f32[16,6,4,128]{3,2,1,0:T(4,128)S(1)}, u32[]{:S(2)}, u32[]{:S(2)}) async-start(f32[16,6,4,128]{3,2,1,0:T(4,128)} %bitcast.197), calls=%async_computation | async-start | bytes 393216 | tf_op jit(solution)/shard_map/while/body/eval_jaxpr/all_to_all | solution.py:103
  171.6 8.1 %all-to-all-done = f32[16,6,4,128]{3,2,1,0:T(4,128)S(1)} async-done(((f32[16,6,4,128]{3,2,1,0:T(4,128)}), f32[16,6,4,128]{3,2,1,0:T(4,128)S(1)}, u32[]{:S(2)}, u32[]{:S(2)}) %all-to-all-start) | async-done | bytes 196640 | tf_op jit(solution)/shard_map/while/body/eval_jaxpr/all_to_all | solution.py:103
  181.2 3.5 %all-to-all-start.1 = ((f32[16,6,4,128]{3,2,1,0:T(4,128)}), f32[16,6,4,128]{3,2,1,0:T(4,128)S(1)}, u32[]{:S(2)}, u32[]{:S(2)}) async-start(f32[16,6,4,128]{3,2,1,0:T(4,128)} %bitcast.199), calls=%async_computation.1 | async-start | bytes 393216 | tf_op jit(solution)/shard_map/while/body/eval_jaxpr/all_to_all | solution.py:103
  185.0 4.5 %multiply_reduce_fusion.17 = f32[24,4,128]{2,1,0:T(4,128)S(1)} fusion(f32[24,4,128,128]{3,2,1,0:T(8,128)} %get-tuple-element.444, f32[24,4,128]{2,1,0:T(4,128)S(1)} %get-tuple-element.415), kind=kLoop, calls=%fused_computation.9.clone.1 | loop fusion | flops 3133440 | bytes 6389760 | tf_op jit(solution)/shard_map/while/body/eval_jaxpr/reduce_sum | solution.py:16
  196.4 3.6 %all-to-all-start = ((f32[16,6,4,128]{3,2,1,0:T(4,128)}), f32[16,6,4,128]{3,2,1,0:T(4,128)S(1)}, u32[]{:S(2)}, u32[]{:S(2)}) async-start(f32[16,6,4,128]{3,2,1,0:T(4,128)} %bitcast.197), calls=%async_computation | async-start | bytes 393216 | tf_op jit(solution)/shard_map/while/body/eval_jaxpr/all_to_all | solution.py:103
  200.0 8.2 %all-to-all-done = f32[16,6,4,128]{3,2,1,0:T(4,128)S(1)} async-done(((f32[16,6,4,128]{3,2,1,0:T(4,128)}), f32[16,6,4,128]{3,2,1,0:T(4,128)S(1)}, u32[]{:S(2)}, u32[]{:S(2)}) %all-to-all-start) | async-done | bytes 196640 | tf_op jit(solution)/shard_map/while/body/eval_jaxpr/all_to_all | solution.py:103
  213.6 4.5 %multiply_reduce_fusion.17 = f32[24,4,128]{2,1,0:T(4,128)S(1)} fusion(f32[24,4,128,128]{3,2,1,0:T(8,128)} %get-tuple-element.444, f32[24,4,128]{2,1,0:T(4,128)S(1)} %get-tuple-element.415), kind=kLoop, calls=%fused_computation.9.clone.1 | loop fusion | flops 3133440 | bytes 6389760 | tf_op jit(solution)/shard_map/while/body/eval_jaxpr/reduce_sum | solution.py:16
  223.3 4.5 %multiply_reduce_fusion.5 = f32[24,4,128]{2,1,0:T(4,128)S(1)} fusion(f32[24,4,128,128]{3,2,1,0:T(8,128)} %get-tuple-element.450, f32[24,4,128]{2,1,0:T(4,128)S(1)} %get-tuple-element.96), kind=kLoop, calls=%fused_computation.45 | loop fusion | flops 3133440 | bytes 6389760 | tf_op jit(solution)/shard_map/reduce_sum | solution.py:16
  230.9 16.0 %all_to_all.32 = f32[16,6,9,128]{3,1,2,0:T(8,128)S(1)} all-to-all(f32[16,6,9,128]{3,1,2,0:T(8,128)S(1)} %copy.252), channel_id=1, replica_groups=mesh['req'=16,'head'=2] {'req'}, dimensions={0} | all-to-all | bytes 884736 | tf_op jit(solution)/shard_map/all_to_all | solution.py:103
  251.0 3.5 %all-to-all-start.5 = ((f32[16,6,5,128]{3,1,2,0:T(8,128)}), f32[16,6,5,128]{3,1,2,0:T(8,128)S(1)}, u32[]{:S(2)}, u32[]{:S(2)}) async-start(f32[16,6,5,128]{3,1,2,0:T(8,128)} %copy.258), calls=%async_computation.5 | async-start | bytes 655360 | tf_op jit(solution)/shard_map/all_to_all | solution.py:103
  254.5 9.0 %all-to-all-done.5 = f32[16,6,5,128]{3,1,2,0:T(8,128)S(1)} async-done(((f32[16,6,5,128]{3,1,2,0:T(8,128)}), f32[16,6,5,128]{3,1,2,0:T(8,128)S(1)}, u32[]{:S(2)}, u32[]{:S(2)}) %all-to-all-start.5) | async-done | bytes 245792 | tf_op jit(solution)/shard_map/all_to_all | solution.py:103
  264.4 4.5 %multiply_reduce_fusion.4 = f32[24,4,128]{2,1,0:T(4,128)S(1)} fusion(f32[24,4,128,128]{3,2,1,0:T(8,128)} %param.30, f32[24,4,128]{2,1,0:T(4,128)S(1)} %copy.265), kind=kLoop, calls=%fused_computation.44 | loop fusion | flops 3133440 | bytes 6389760 | tf_op jit(solution)/shard_map/reduce_sum | solution.py:16
  (281 shorter events, 91.8 us)
Async XLA Ops:
  0.0 269.6 %copy-start = (bf16[4,128,1024]{2,1,0:T(8,128)(2,1)S(1)}, bf16[4,128,1024]{2,1,0:T(8,128)(2,1)}, u32[]{:S(2)}) copy-start(bf16[4,128,1024]{2,1,0:T(8,128)(2,1)} %param.35) | copy-start | bytes 3145732
  0.0 12.9 %copy-start.5 = (f32[1024]{0:T(1024)S(1)}, f32[1024]{0:T(1024)}, u32[]{:S(2)}) copy-start(f32[1024]{0:T(1024)} %param.22) | copy-start | bytes 12292
  6.8 11.1 %copy-start.4 = (bf16[1024,2,4]{0,2,1:T(4,128)(2,1)S(1)}, bf16[1024,2,4]{0,2,1:T(4,128)(2,1)}, u32[]{:S(2)}) copy-start(bf16[1024,2,4]{0,2,1:T(4,128)(2,1)} %param.26) | copy-start | bytes 49156
  6.9 11.4 %copy-start.2 = (f32[24,4]{0,1:T(4,128)S(1)}, f32[24,4]{0,1:T(4,128)}, u32[]{:S(2)}) copy-start(f32[24,4]{0,1:T(4,128)} %param.27) | copy-start | bytes 1156
  6.9 31.6 %copy-start.1 = (f32[2,4,128,128]{3,2,1,0:T(8,128)S(1)}, f32[2,4,128,128]{3,2,1,0:T(8,128)}, u32[]{:S(2)}) copy-start(f32[2,4,128,128]{3,2,1,0:T(8,128)} %param.31) | copy-start | bytes 1572868
  18.0 34.1 %copy-start.6 = (f32[4]{0:T(128)S(1)}, f32[4]{0:T(128)}, u32[]{:S(2)}) copy-start(f32[4]{0:T(128)} %param.28) | copy-start | bytes 52
  18.3 19.9 %all-to-all-start.2 = ((f32[16,6,5,128]{3,1,2,0:T(8,128)}), f32[16,6,5,128]{3,1,2,0:T(8,128)S(1)}, u32[]{:S(2)}, u32[]{:S(2)}) async-start(f32[16,6,5,128]{3,1,2,0:T(8,128)} %copy.232), calls=%async_computation.2 | async-start | bytes 655360 | tf_op jit(solution)/shard_map/all_to_all | solution.py:103
  39.9 11.6 %all-to-all-start.3 = ((f32[16,6,4,128]{3,2,1,0:T(4,128)}), f32[16,6,4,128]{3,2,1,0:T(4,128)S(1)}, u32[]{:S(2)}, u32[]{:S(2)}) async-start(f32[16,6,4,128]{3,2,1,0:T(4,128)} %bitcast.38), calls=%async_computation.3 | async-start | bytes 393216 | tf_op jit(solution)/shard_map/all_to_all | solution.py:103
  54.4 11.6 %all-to-all-start = ((f32[16,6,4,128]{3,2,1,0:T(4,128)}), f32[16,6,4,128]{3,2,1,0:T(4,128)S(1)}, u32[]{:S(2)}, u32[]{:S(2)}) async-start(f32[16,6,4,128]{3,2,1,0:T(4,128)} %bitcast.197), calls=%async_computation | async-start | bytes 393216 | tf_op jit(solution)/shard_map/while/body/eval_jaxpr/all_to_all | solution.py:103
  67.6 11.6 %all-to-all-start.1 = ((f32[16,6,4,128]{3,2,1,0:T(4,128)}), f32[16,6,4,128]{3,2,1,0:T(4,128)S(1)}, u32[]{:S(2)}, u32[]{:S(2)}) async-start(f32[16,6,4,128]{3,2,1,0:T(4,128)} %bitcast.199), calls=%async_computation.1 | async-start | bytes 393216 | tf_op jit(solution)/shard_map/while/body/eval_jaxpr/all_to_all | solution.py:103
  82.7 11.7 %all-to-all-start = ((f32[16,6,4,128]{3,2,1,0:T(4,128)}), f32[16,6,4,128]{3,2,1,0:T(4,128)S(1)}, u32[]{:S(2)}, u32[]{:S(2)}) async-start(f32[16,6,4,128]{3,2,1,0:T(4,128)} %bitcast.197), calls=%async_computation | async-start | bytes 393216 | tf_op jit(solution)/shard_map/while/body/eval_jaxpr/all_to_all | solution.py:103
  96.0 11.6 %all-to-all-start.1 = ((f32[16,6,4,128]{3,2,1,0:T(4,128)}), f32[16,6,4,128]{3,2,1,0:T(4,128)S(1)}, u32[]{:S(2)}, u32[]{:S(2)}) async-start(f32[16,6,4,128]{3,2,1,0:T(4,128)} %bitcast.199), calls=%async_computation.1 | async-start | bytes 393216 | tf_op jit(solution)/shard_map/while/body/eval_jaxpr/all_to_all | solution.py:103
  111.1 11.7 %all-to-all-start = ((f32[16,6,4,128]{3,2,1,0:T(4,128)}), f32[16,6,4,128]{3,2,1,0:T(4,128)S(1)}, u32[]{:S(2)}, u32[]{:S(2)}) async-start(f32[16,6,4,128]{3,2,1,0:T(4,128)} %bitcast.197), calls=%async_computation | async-start | bytes 393216 | tf_op jit(solution)/shard_map/while/body/eval_jaxpr/all_to_all | solution.py:103
  124.4 11.6 %all-to-all-start.1 = ((f32[16,6,4,128]{3,2,1,0:T(4,128)}), f32[16,6,4,128]{3,2,1,0:T(4,128)S(1)}, u32[]{:S(2)}, u32[]{:S(2)}) async-start(f32[16,6,4,128]{3,2,1,0:T(4,128)} %bitcast.199), calls=%async_computation.1 | async-start | bytes 393216 | tf_op jit(solution)/shard_map/while/body/eval_jaxpr/all_to_all | solution.py:103
  139.6 11.7 %all-to-all-start = ((f32[16,6,4,128]{3,2,1,0:T(4,128)}), f32[16,6,4,128]{3,2,1,0:T(4,128)S(1)}, u32[]{:S(2)}, u32[]{:S(2)}) async-start(f32[16,6,4,128]{3,2,1,0:T(4,128)} %bitcast.197), calls=%async_computation | async-start | bytes 393216 | tf_op jit(solution)/shard_map/while/body/eval_jaxpr/all_to_all | solution.py:103
  152.8 11.6 %all-to-all-start.1 = ((f32[16,6,4,128]{3,2,1,0:T(4,128)}), f32[16,6,4,128]{3,2,1,0:T(4,128)S(1)}, u32[]{:S(2)}, u32[]{:S(2)}) async-start(f32[16,6,4,128]{3,2,1,0:T(4,128)} %bitcast.199), calls=%async_computation.1 | async-start | bytes 393216 | tf_op jit(solution)/shard_map/while/body/eval_jaxpr/all_to_all | solution.py:103
  168.0 11.7 %all-to-all-start = ((f32[16,6,4,128]{3,2,1,0:T(4,128)}), f32[16,6,4,128]{3,2,1,0:T(4,128)S(1)}, u32[]{:S(2)}, u32[]{:S(2)}) async-start(f32[16,6,4,128]{3,2,1,0:T(4,128)} %bitcast.197), calls=%async_computation | async-start | bytes 393216 | tf_op jit(solution)/shard_map/while/body/eval_jaxpr/all_to_all | solution.py:103
  181.2 11.6 %all-to-all-start.1 = ((f32[16,6,4,128]{3,2,1,0:T(4,128)}), f32[16,6,4,128]{3,2,1,0:T(4,128)S(1)}, u32[]{:S(2)}, u32[]{:S(2)}) async-start(f32[16,6,4,128]{3,2,1,0:T(4,128)} %bitcast.199), calls=%async_computation.1 | async-start | bytes 393216 | tf_op jit(solution)/shard_map/while/body/eval_jaxpr/all_to_all | solution.py:103
  196.4 11.8 %all-to-all-start = ((f32[16,6,4,128]{3,2,1,0:T(4,128)}), f32[16,6,4,128]{3,2,1,0:T(4,128)S(1)}, u32[]{:S(2)}, u32[]{:S(2)}) async-start(f32[16,6,4,128]{3,2,1,0:T(4,128)} %bitcast.197), calls=%async_computation | async-start | bytes 393216 | tf_op jit(solution)/shard_map/while/body/eval_jaxpr/all_to_all | solution.py:103
  209.8 11.6 %all-to-all-start.1 = ((f32[16,6,4,128]{3,2,1,0:T(4,128)}), f32[16,6,4,128]{3,2,1,0:T(4,128)S(1)}, u32[]{:S(2)}, u32[]{:S(2)}) async-start(f32[16,6,4,128]{3,2,1,0:T(4,128)} %bitcast.199), calls=%async_computation.1 | async-start | bytes 393216 | tf_op jit(solution)/shard_map/while/body/eval_jaxpr/all_to_all | solution.py:103
  248.2 23.0 %copy-start.3 = (bf16[24,512]{1,0:T(8,128)(2,1)S(1)}, bf16[24,512]{1,0:T(8,128)(2,1)}, u32[]{:S(2)}) copy-start(bf16[24,512]{1,0:T(8,128)(2,1)} %param.21) | copy-start | bytes 73732
  251.0 12.5 %all-to-all-start.5 = ((f32[16,6,5,128]{3,1,2,0:T(8,128)}), f32[16,6,5,128]{3,1,2,0:T(8,128)S(1)}, u32[]{:S(2)}, u32[]{:S(2)}) async-start(f32[16,6,5,128]{3,1,2,0:T(8,128)} %copy.258), calls=%async_computation.5 | async-start | bytes 655360 | tf_op jit(solution)/shard_map/all_to_all | solution.py:103
  270.0 1.3 collective-permute-start

commit v6 on v5

--- a/solution.py
+++ b/solution.py
@@ -44,23 +44,24 @@
     row_count, model_width = gathered.shape
     head_count = qkv_weight.shape[1]
     head_size = qkv_weight.shape[3]
-    projected = jnp.dot(
-        normed,
-        qkv_weight.reshape(model_width, head_count * 3 * head_size),
-        preferred_element_type=jnp.float32,
-    ).reshape(row_count, head_count, 3, head_size)
-    mixing = conv_weight[0] * projected
-    for offset in range(1, KW):
-        usable = (lengths >= offset).astype(jnp.float32)[:, None, None, None]
-        mixing = (
-            mixing + conv_weight[offset] * conv_state[:, offset - 1].astype(jnp.float32) * usable
-        )
-    active = jax.nn.silu(mixing)
-    queries = active[:, :, 0]
+    live_rows = [(lengths >= offset).astype(jnp.float32)[:, None, None] for offset in range(KW)]
+
+    def project(part):
+        weights = qkv_weight[:, :, part, :].reshape(model_width, head_count * head_size)
+        mixing = conv_weight[0, :, part] * jnp.dot(
+            normed, weights, preferred_element_type=jnp.float32
+        ).reshape(row_count, head_count, head_size)
+        for offset in range(1, KW):
+            mixing = mixing + conv_weight[offset, :, part] * conv_state[
+                :, offset - 1, :, part
+            ].astype(jnp.float32) * live_rows[offset]
+        return jax.nn.silu(mixing)
+
+    queries = project(0)
     queries = queries * lax.rsqrt(jnp.sum(queries * queries, axis=2, keepdims=True) + epsilon)
-    key_now = active[:, :, 1]
+    key_now = project(1)
     key_now = key_now * lax.rsqrt(jnp.sum(key_now * key_now, axis=2, keepdims=True) + epsilon)
-    value_now = active[:, :, 2]
+    value_now = project(2)
     gate_logit = jnp.dot(
         normed, gate_weight.reshape(model_width, 2 * head_count), preferred_element_type=jnp.float32
     ).reshape(row_count, 2, head_count)

time: 274 us -> 340 us (1.24)
  other arithmetic: 59 us -> 100 us
  waiting for transfers between devices: 93 us -> 57.7 us
  local copies, waits for them, and re-layouts: 31.7 us -> 65.1 us
  starting transfers between devices: 58.2 us -> 77.3 us
    all_to_all x15, waiting for transfers between devices: 91.8 us -> 56.5 us  [exchange(): lax.all_to_all(shaped, 'req', split_axis=0, concat_axis=0, tiled=True)]
    all_to_all x15, starting transfers between devices: 58.1 us -> 77.2 us  [exchange(): lax.all_to_all(shaped, 'req', split_axis=0, concat_axis=0, tiled=True)]
    select_n x17, other arithmetic: 5.61 us -> 13.8 us  [pack(): return jnp.take(padded, source, axis=0)]
    and x7, other arithmetic: 0.72 us -> 8.44 us  [unpack(): taken = jnp.take(slots, slot_of, axis=0)]
    and x8, other arithmetic: 0.07 us -> 7.69 us  [pack(): return jnp.take(padded, source, axis=0)]
    mul x6, local copies, waits for them, and re-layouts: 0.51 us -> 8.07 us  [cg_step(): write_col * key_now * jnp.sum(key_now * direction, axis=2, keepdims=True)]
    mul x6, local copies, waits for them, and re-layouts: 0.51 us -> 8.02 us  [cg_step(): decay_col * shared]
    another operation x0 -> x3, local copies, waits for them, and re-layouts: none -> 6.5 us  [project(): qkv_weight[:, :, part, :].reshape(model_width, head_count * head_size)]
  transfers between devices with their start and end apart: 16 -> 16, of which waited for: 16 -> 16; matrix products, arithmetic and copies ran while one was open for 12% -> 20% of each run, Pallas kernels for 0% -> 0%
where the time goes in v6:
time: 340 us; the launch traced here: 337 us
  other arithmetic  100 us (29%)
  starting transfers between devices  77.3 us (23%)
  local copies, waits for them, and re-layouts  65.1 us (19%)
  waiting for transfers between devices  57.7 us (17%)
  blocking collectives  21.1 us (6%)
  matrix products  13.7 us (4%)
    all_to_all x15, starting transfers between devices, exchange(): lax.all_to_all(shaped, 'req', split_axis=0, concat_axis=0, tiled=True)  77.2 us
    all_to_all x15, waiting for transfers between devices, exchange(): lax.all_to_all(shaped, 'req', split_axis=0, concat_axis=0, tiled=True)  56.5 us
    reduce_sum x9, other arithmetic, own_matvec(): return jnp.sum(matrices * vectors[:, :, None, :], axis=3)  40.4 us
    all_to_all x1, blocking collectives, exchange(): lax.all_to_all(shaped, 'req', split_axis=0, concat_axis=0, tiled=True)  19.2 us
    select_n x17, other arithmetic, pack(): return jnp.take(padded, source, axis=0)  13.8 us
    mul x7, other arithmetic, cg_step(): write_col * key_now * jnp.sum(key_now * direction, axis=2, keepdims=True)  9.8 us
    gather x8, local copies, waits for them, and re-layouts, unpack(): taken = jnp.take(slots, slot_of, axis=0)  9.47 us
    and x7, other arithmetic, unpack(): taken = jnp.take(slots, slot_of, axis=0)  8.44 us
  transfers between devices with their start and end apart: 16, of which 16 were waited for; matrix products, arithmetic and copies ran while one was open for 20% of the time, Pallas kernels for 0%

profile of v6, /device:TPU:0, one launch (start us, length us, event | category | flops | bytes accessed | tf_op | source)
XLA Modules:
  0.0 336.6 jit_solution(16876064892678125791)
XLA Ops:
  7.2 4.3 %fusion.106 = (bf16[1024,4,1,128]{3,1,2,0:T(4,128)(2,1)S(1)}, bf16[1024,4,1,128]{3,1,2,0:T(4,128)(2,1)}, bf16[1024,4,1,128]{3,1,2,0:T(4,128)(2,1)}) fusion(bf16[1024,4,3,128]{3,1,2,0:T(4,128)(2,1)} %param.23), kind=kLoop, calls=%fused_computation.249 | loop fusion | bytes 6291456 | tf_op jit(solution)/shard_map/slice | solution.py:50
  25.6 8.2 %all-to-all-start.2 = ((f32[16,6,5,128]{3,1,2,0:T(8,128)}), f32[16,6,5,128]{3,1,2,0:T(8,128)S(1)}, u32[]{:S(2)}, u32[]{:S(2)}) async-start(f32[16,6,5,128]{3,1,2,0:T(8,128)} %copy.236), calls=%async_computation.2 | async-start | bytes 655360 | tf_op jit(solution)/shard_map/all_to_all | solution.py:104
  34.6 10.9 %all-to-all-done.2 = f32[16,6,5,128]{3,1,2,0:T(8,128)S(1)} async-done(((f32[16,6,5,128]{3,1,2,0:T(8,128)}), f32[16,6,5,128]{3,1,2,0:T(8,128)S(1)}, u32[]{:S(2)}, u32[]{:S(2)}) %all-to-all-start.2) | async-done | bytes 245792 | tf_op jit(solution)/shard_map/all_to_all | solution.py:104
  47.8 4.4 %all-to-all-start.3 = ((f32[16,6,4,128]{3,2,1,0:T(4,128)}), f32[16,6,4,128]{3,2,1,0:T(4,128)}, u32[]{:S(2)}, u32[]{:S(2)}) async-start(f32[16,6,4,128]{3,2,1,0:T(4,128)} %bitcast.35), calls=%async_computation.3 | async-start | bytes 393216 | tf_op jit(solution)/shard_map/all_to_all | solution.py:104
  54.1 4.5 %multiply_reduce_fusion.6 = f32[24,4,128]{2,1,0:T(4,128)S(1)} fusion(f32[24,4,128,128]{3,2,1,0:T(8,128)} %param.29, f32[24,4,128]{2,1,0:T(4,128)S(1)} %copy.297), kind=kLoop, calls=%fused_computation.46 | loop fusion | flops 3133440 | bytes 6389760 | tf_op jit(solution)/shard_map/reduce_sum | solution.py:16
  63.0 216.1 %while.16 = (s32[]{:T(128)}, f32[24,4,128]{2,1,0:T(4,128)S(1)}, f32[24,4,128]{2,1,0:T(4,128)S(1)}, f32[24,4,128]{2,1,0:T(4,128)S(1)}, f32[24,4,1]{0,1,2:T(4,128)...) while((s32[]{:T(128)}, f32[24,4,128]{2,1,0:T(4,128)S(1)}, ...), condition=%wide.region_17.20_spmd, body=%wide.region_12.19_spmd.sunk | while | flops 154635536 | bytes 11313573 | solution.py:146
  67.0 5.2 %all-to-all-start = ((f32[16,6,4,128]{3,2,1,0:T(4,128)}), f32[16,6,4,128]{3,2,1,0:T(4,128)S(1)}, u32[]{:S(2)}, u32[]{:S(2)}) async-start(f32[16,6,4,128]{3,2,1,0:T(4,128)} %bitcast.231), calls=%async_computation | async-start | bytes 393216 | tf_op jit(solution)/shard_map/while/body/eval_jaxpr/all_to_all | solution.py:104
  74.1 6.2 %all-to-all-done = f32[16,6,4,128]{3,2,1,0:T(4,128)S(1)} async-done(((f32[16,6,4,128]{3,2,1,0:T(4,128)}), f32[16,6,4,128]{3,2,1,0:T(4,128)S(1)}, u32[]{:S(2)}, u32[]{:S(2)}) %all-to-all-start) | async-done | bytes 196640 | tf_op jit(solution)/shard_map/while/body/eval_jaxpr/all_to_all | solution.py:104
  89.4 4.5 %multiply_reduce_fusion.18 = f32[24,4,128]{2,1,0:T(4,128)S(1)} fusion(f32[24,4,128,128]{3,2,1,0:T(8,128)} %get-tuple-element.459, f32[24,4,128]{2,1,0:T(4,128)S(1)} %get-tuple-element.430), kind=kLoop, calls=%fused_computation.9.clone.1 | loop fusion | flops 3133440 | bytes 6389760 | tf_op jit(solution)/shard_map/while/body/eval_jaxpr/reduce_sum | solution.py:16
  101.6 6.7 %all-to-all-start = ((f32[16,6,4,128]{3,2,1,0:T(4,128)}), f32[16,6,4,128]{3,2,1,0:T(4,128)S(1)}, u32[]{:S(2)}, u32[]{:S(2)}) async-start(f32[16,6,4,128]{3,2,1,0:T(4,128)} %bitcast.231), calls=%async_computation | async-start | bytes 393216 | tf_op jit(solution)/shard_map/while/body/eval_jaxpr/all_to_all | solution.py:104
  110.2 6.2 %all-to-all-done = f32[16,6,4,128]{3,2,1,0:T(4,128)S(1)} async-done(((f32[16,6,4,128]{3,2,1,0:T(4,128)}), f32[16,6,4,128]{3,2,1,0:T(4,128)S(1)}, u32[]{:S(2)}, u32[]{:S(2)}) %all-to-all-start) | async-done | bytes 196640 | tf_op jit(solution)/shard_map/while/body/eval_jaxpr/all_to_all | solution.py:104
  118.6 3.5 %all-to-all-start.1 = ((f32[16,6,4,128]{3,2,1,0:T(4,128)}), f32[16,6,4,128]{3,2,1,0:T(4,128)S(1)}, u32[]{:S(2)}, u32[]{:S(2)}) async-start(f32[16,6,4,128]{3,2,1,0:T(4,128)} %bitcast.233), calls=%async_computation.1 | async-start | bytes 393216 | tf_op jit(solution)/shard_map/while/body/eval_jaxpr/all_to_all | solution.py:104
  125.5 4.5 %multiply_reduce_fusion.18 = f32[24,4,128]{2,1,0:T(4,128)S(1)} fusion(f32[24,4,128,128]{3,2,1,0:T(8,128)} %get-tuple-element.459, f32[24,4,128]{2,1,0:T(4,128)S(1)} %get-tuple-element.430), kind=kLoop, calls=%fused_computation.9.clone.1 | loop fusion | flops 3133440 | bytes 6389760 | tf_op jit(solution)/shard_map/while/body/eval_jaxpr/reduce_sum | solution.py:16
  137.6 6.7 %all-to-all-start = ((f32[16,6,4,128]{3,2,1,0:T(4,128)}), f32[16,6,4,128]{3,2,1,0:T(4,128)S(1)}, u32[]{:S(2)}, u32[]{:S(2)}) async-start(f32[16,6,4,128]{3,2,1,0:T(4,128)} %bitcast.231), calls=%async_computation | async-start | bytes 393216 | tf_op jit(solution)/shard_map/while/body/eval_jaxpr/all_to_all | solution.py:104
  146.2 6.2 %all-to-all-done = f32[16,6,4,128]{3,2,1,0:T(4,128)S(1)} async-done(((f32[16,6,4,128]{3,2,1,0:T(4,128)}), f32[16,6,4,128]{3,2,1,0:T(4,128)S(1)}, u32[]{:S(2)}, u32[]{:S(2)}) %all-to-all-start) | async-done | bytes 196640 | tf_op jit(solution)/shard_map/while/body/eval_jaxpr/all_to_all | solution.py:104
  154.6 3.5 %all-to-all-start.1 = ((f32[16,6,4,128]{3,2,1,0:T(4,128)}), f32[16,6,4,128]{3,2,1,0:T(4,128)S(1)}, u32[]{:S(2)}, u32[]{:S(2)}) async-start(f32[16,6,4,128]{3,2,1,0:T(4,128)} %bitcast.233), calls=%async_computation.1 | async-start | bytes 393216 | tf_op jit(solution)/shard_map/while/body/eval_jaxpr/all_to_all | solution.py:104
  161.5 4.5 %multiply_reduce_fusion.18 = f32[24,4,128]{2,1,0:T(4,128)S(1)} fusion(f32[24,4,128,128]{3,2,1,0:T(8,128)} %get-tuple-element.459, f32[24,4,128]{2,1,0:T(4,128)S(1)} %get-tuple-element.430), kind=kLoop, calls=%fused_computation.9.clone.1 | loop fusion | flops 3133440 | bytes 6389760 | tf_op jit(solution)/shard_map/while/body/eval_jaxpr/reduce_sum | solution.py:16
  173.7 6.7 %all-to-all-start = ((f32[16,6,4,128]{3,2,1,0:T(4,128)}), f32[16,6,4,128]{3,2,1,0:T(4,128)S(1)}, u32[]{:S(2)}, u32[]{:S(2)}) async-start(f32[16,6,4,128]{3,2,1,0:T(4,128)} %bitcast.231), calls=%async_computation | async-start | bytes 393216 | tf_op jit(solution)/shard_map/while/body/eval_jaxpr/all_to_all | solution.py:104
  182.3 6.2 %all-to-all-done = f32[16,6,4,128]{3,2,1,0:T(4,128)S(1)} async-done(((f32[16,6,4,128]{3,2,1,0:T(4,128)}), f32[16,6,4,128]{3,2,1,0:T(4,128)S(1)}, u32[]{:S(2)}, u32[]{:S(2)}) %all-to-all-start) | async-done | bytes 196640 | tf_op jit(solution)/shard_map/while/body/eval_jaxpr/all_to_all | solution.py:104
  197.6 4.5 %multiply_reduce_fusion.18 = f32[24,4,128]{2,1,0:T(4,128)S(1)} fusion(f32[24,4,128,128]{3,2,1,0:T(8,128)} %get-tuple-element.459, f32[24,4,128]{2,1,0:T(4,128)S(1)} %get-tuple-element.430), kind=kLoop, calls=%fused_computation.9.clone.1 | loop fusion | flops 3133440 | bytes 6389760 | tf_op jit(solution)/shard_map/while/body/eval_jaxpr/reduce_sum | solution.py:16
  209.7 6.7 %all-to-all-start = ((f32[16,6,4,128]{3,2,1,0:T(4,128)}), f32[16,6,4,128]{3,2,1,0:T(4,128)S(1)}, u32[]{:S(2)}, u32[]{:S(2)}) async-start(f32[16,6,4,128]{3,2,1,0:T(4,128)} %bitcast.231), calls=%async_computation | async-start | bytes 393216 | tf_op jit(solution)/shard_map/while/body/eval_jaxpr/all_to_all | solution.py:104
  218.3 6.3 %all-to-all-done = f32[16,6,4,128]{3,2,1,0:T(4,128)S(1)} async-done(((f32[16,6,4,128]{3,2,1,0:T(4,128)}), f32[16,6,4,128]{3,2,1,0:T(4,128)S(1)}, u32[]{:S(2)}, u32[]{:S(2)}) %all-to-all-start) | async-done | bytes 196640 | tf_op jit(solution)/shard_map/while/body/eval_jaxpr/all_to_all | solution.py:104
  233.6 4.5 %multiply_reduce_fusion.18 = f32[24,4,128]{2,1,0:T(4,128)S(1)} fusion(f32[24,4,128,128]{3,2,1,0:T(8,128)} %get-tuple-element.459, f32[24,4,128]{2,1,0:T(4,128)S(1)} %get-tuple-element.430), kind=kLoop, calls=%fused_computation.9.clone.1 | loop fusion | flops 3133440 | bytes 6389760 | tf_op jit(solution)/shard_map/while/body/eval_jaxpr/reduce_sum | solution.py:16
  245.8 6.7 %all-to-all-start = ((f32[16,6,4,128]{3,2,1,0:T(4,128)}), f32[16,6,4,128]{3,2,1,0:T(4,128)S(1)}, u32[]{:S(2)}, u32[]{:S(2)}) async-start(f32[16,6,4,128]{3,2,1,0:T(4,128)} %bitcast.231), calls=%async_computation | async-start | bytes 393216 | tf_op jit(solution)/shard_map/while/body/eval_jaxpr/all_to_all | solution.py:104
  254.4 6.6 %all-to-all-done = f32[16,6,4,128]{3,2,1,0:T(4,128)S(1)} async-done(((f32[16,6,4,128]{3,2,1,0:T(4,128)}), f32[16,6,4,128]{3,2,1,0:T(4,128)S(1)}, u32[]{:S(2)}, u32[]{:S(2)}) %all-to-all-start) | async-done | bytes 196640 | tf_op jit(solution)/shard_map/while/body/eval_jaxpr/all_to_all | solution.py:104
  263.1 4.5 %all-to-all-start.1 = ((f32[16,6,4,128]{3,2,1,0:T(4,128)}), f32[16,6,4,128]{3,2,1,0:T(4,128)S(1)}, u32[]{:S(2)}, u32[]{:S(2)}) async-start(f32[16,6,4,128]{3,2,1,0:T(4,128)} %bitcast.233), calls=%async_computation.1 | async-start | bytes 393216 | tf_op jit(solution)/shard_map/while/body/eval_jaxpr/all_to_all | solution.py:104
  271.0 4.5 %multiply_reduce_fusion.18 = f32[24,4,128]{2,1,0:T(4,128)S(1)} fusion(f32[24,4,128,128]{3,2,1,0:T(8,128)} %get-tuple-element.459, f32[24,4,128]{2,1,0:T(4,128)S(1)} %get-tuple-element.430), kind=kLoop, calls=%fused_computation.9.clone.1 | loop fusion | flops 3133440 | bytes 6389760 | tf_op jit(solution)/shard_map/while/body/eval_jaxpr/reduce_sum | solution.py:16
  279.3 4.5 %multiply_reduce_fusion.5 = f32[24,4,128]{2,1,0:T(4,128)S(1)} fusion(f32[24,4,128,128]{3,2,1,0:T(8,128)} %get-tuple-element.465, f32[24,4,128]{2,1,0:T(4,128)S(1)} %get-tuple-element.96), kind=kLoop, calls=%fused_computation.45 | loop fusion | flops 3133440 | bytes 6389760 | tf_op jit(solution)/shard_map/reduce_sum | solution.py:16
  287.3 19.2 %all_to_all.32 = f32[16,6,9,128]{3,1,2,0:T(8,128)S(1)} all-to-all(f32[16,6,9,128]{3,1,2,0:T(8,128)S(1)} %copy.259), channel_id=1, replica_groups=mesh['req'=16,'head'=2] {'req'}, dimensions={0} | all-to-all | bytes 884736 | tf_op jit(solution)/shard_map/all_to_all | solution.py:104
  315.5 3.8 %all-to-all-start.5 = ((f32[16,6,5,128]{3,1,2,0:T(8,128)}), f32[16,6,5,128]{3,1,2,0:T(8,128)S(1)}, u32[]{:S(2)}, u32[]{:S(2)}) async-start(f32[16,6,5,128]{3,1,2,0:T(8,128)} %copy.265), calls=%async_computation.5 | async-start | bytes 655360 | tf_op jit(solution)/shard_map/all_to_all | solution.py:104
  322.5 5.5 %all-to-all-done.5 = f32[16,6,5,128]{3,1,2,0:T(8,128)S(1)} async-done(((f32[16,6,5,128]{3,1,2,0:T(8,128)}), f32[16,6,5,128]{3,1,2,0:T(8,128)S(1)}, u32[]{:S(2)}, u32[]{:S(2)}) %all-to-all-start.5) | async-done | bytes 245792 | tf_op jit(solution)/shard_map/all_to_all | solution.py:104
  329.1 4.5 %multiply_reduce_fusion.4 = f32[24,4,128]{2,1,0:T(4,128)S(1)} fusion(f32[24,4,128,128]{3,2,1,0:T(8,128)} %param.30, f32[24,4,128]{2,1,0:T(4,128)S(1)} %copy.272), kind=kLoop, calls=%fused_computation.44 | loop fusion | flops 3133440 | bytes 6389760 | tf_op jit(solution)/shard_map/reduce_sum | solution.py:16
  (357 shorter events, 150.7 us)
Async XLA Ops:
  0.0 334.3 %copy-start = (bf16[4,128,1024]{2,1,0:T(8,128)(2,1)S(1)}, bf16[4,128,1024]{2,1,0:T(8,128)(2,1)}, u32[]{:S(2)}) copy-start(bf16[4,128,1024]{2,1,0:T(8,128)(2,1)} %param.35) | copy-start | bytes 3145732
  4.1 29.7 %copy-start.27 = (s32[96]{0:T(128)}, s32[96]{0:T(128)S(1)}, u32[]{:S(2)}) copy-start(s32[96]{0:T(128)S(1)} %get-tuple-element.417) | copy-start | bytes 1156
  4.1 19.7 %copy-start.32 = (pred[96]{0:T(512)(128)(4,1)}, pred[96]{0:T(512)(128)(4,1)S(1)}, u32[]{:S(2)}) copy-start(pred[96]{0:T(512)(128)(4,1)S(1)} %compare_and_fusion.3) | copy-start | bytes 292
  11.4 34.9 %copy-start.1 = (f32[2,4,128,128]{3,2,1,0:T(8,128)S(1)}, f32[2,4,128,128]{3,2,1,0:T(8,128)}, u32[]{:S(2)}) copy-start(f32[2,4,128,128]{3,2,1,0:T(8,128)} %param.31) | copy-start | bytes 1572868
  23.1 35.5 %copy-start.16 = (s32[1024]{0:T(1024)}, s32[1024]{0:T(1024)S(1)}, u32[]{:S(2)}) copy-start(s32[1024]{0:T(1024)S(1)} %pad_clamp_fusion.4) | copy-start | bytes 12292
  24.3 37.3 %copy-start.19 = (pred[24]{0:T(512)(128)(4,1)S(1)}, pred[24]{0:T(512)(128)(4,1)}, u32[]{:S(2)}) copy-start(pred[24]{0:T(512)(128)(4,1)} %copy-done.18) | copy-start | bytes 76
  25.6 19.9 %all-to-all-start.2 = ((f32[16,6,5,128]{3,1,2,0:T(8,128)}), f32[16,6,5,128]{3,1,2,0:T(8,128)S(1)}, u32[]{:S(2)}, u32[]{:S(2)}) async-start(f32[16,6,5,128]{3,1,2,0:T(8,128)} %copy.236), calls=%async_computation.2 | async-start | bytes 655360 | tf_op jit(solution)/shard_map/all_to_all | solution.py:104
  33.9 29.0 %copy-start.17 = (s32[1024]{0:T(1024)}, s32[1024]{0:T(1024)S(1)}, u32[]{:S(2)}) copy-start(s32[1024]{0:T(1024)S(1)} %pad_clamp_fusion.3) | copy-start | bytes 12292
  34.6 28.4 %copy-start.4 = (f32[24,4,128]{2,0,1:T(8,128)}, f32[24,4,128]{2,0,1:T(8,128)S(1)}, u32[]{:S(2)}) copy-start(f32[24,4,128]{2,0,1:T(8,128)S(1)} %broadcast_multiply_fusion.1) | copy-start | bytes 147460
  47.8 12.3 %all-to-all-start.3 = ((f32[16,6,4,128]{3,2,1,0:T(4,128)}), f32[16,6,4,128]{3,2,1,0:T(4,128)}, u32[]{:S(2)}, u32[]{:S(2)}) async-start(f32[16,6,4,128]{3,2,1,0:T(4,128)} %bitcast.35), calls=%async_computation.3 | async-start | bytes 393216 | tf_op jit(solution)/shard_map/all_to_all | solution.py:104
  67.0 13.3 %all-to-all-start = ((f32[16,6,4,128]{3,2,1,0:T(4,128)}), f32[16,6,4,128]{3,2,1,0:T(4,128)S(1)}, u32[]{:S(2)}, u32[]{:S(2)}) async-start(f32[16,6,4,128]{3,2,1,0:T(4,128)} %bitcast.231), calls=%async_computation | async-start | bytes 393216 | tf_op jit(solution)/shard_map/while/body/eval_jaxpr/all_to_all | solution.py:104
  82.5 11.6 %all-to-all-start.1 = ((f32[16,6,4,128]{3,2,1,0:T(4,128)}), f32[16,6,4,128]{3,2,1,0:T(4,128)S(1)}, u32[]{:S(2)}, u32[]{:S(2)}) async-start(f32[16,6,4,128]{3,2,1,0:T(4,128)} %bitcast.233), calls=%async_computation.1 | async-start | bytes 393216 | tf_op jit(solution)/shard_map/while/body/eval_jaxpr/all_to_all | solution.py:104
  101.6 14.8 %all-to-all-start = ((f32[16,6,4,128]{3,2,1,0:T(4,128)}), f32[16,6,4,128]{3,2,1,0:T(4,128)S(1)}, u32[]{:S(2)}, u32[]{:S(2)}) async-start(f32[16,6,4,128]{3,2,1,0:T(4,128)} %bitcast.231), calls=%async_computation | async-start | bytes 393216 | tf_op jit(solution)/shard_map/while/body/eval_jaxpr/all_to_all | solution.py:104
  118.6 11.6 %all-to-all-start.1 = ((f32[16,6,4,128]{3,2,1,0:T(4,128)}), f32[16,6,4,128]{3,2,1,0:T(4,128)S(1)}, u32[]{:S(2)}, u32[]{:S(2)}) async-start(f32[16,6,4,128]{3,2,1,0:T(4,128)} %bitcast.233), calls=%async_computation.1 | async-start | bytes 393216 | tf_op jit(solution)/shard_map/while/body/eval_jaxpr/all_to_all | solution.py:104
  137.6 14.8 %all-to-all-start = ((f32[16,6,4,128]{3,2,1,0:T(4,128)}), f32[16,6,4,128]{3,2,1,0:T(4,128)S(1)}, u32[]{:S(2)}, u32[]{:S(2)}) async-start(f32[16,6,4,128]{3,2,1,0:T(4,128)} %bitcast.231), calls=%async_computation | async-start | bytes 393216 | tf_op jit(solution)/shard_map/while/body/eval_jaxpr/all_to_all | solution.py:104
  154.6 11.6 %all-to-all-start.1 = ((f32[16,6,4,128]{3,2,1,0:T(4,128)}), f32[16,6,4,128]{3,2,1,0:T(4,128)S(1)}, u32[]{:S(2)}, u32[]{:S(2)}) async-start(f32[16,6,4,128]{3,2,1,0:T(4,128)} %bitcast.233), calls=%async_computation.1 | async-start | bytes 393216 | tf_op jit(solution)/shard_map/while/body/eval_jaxpr/all_to_all | solution.py:104
  173.7 14.8 %all-to-all-start = ((f32[16,6,4,128]{3,2,1,0:T(4,128)}), f32[16,6,4,128]{3,2,1,0:T(4,128)S(1)}, u32[]{:S(2)}, u32[]{:S(2)}) async-start(f32[16,6,4,128]{3,2,1,0:T(4,128)} %bitcast.231), calls=%async_computation | async-start | bytes 393216 | tf_op jit(solution)/shard_map/while/body/eval_jaxpr/all_to_all | solution.py:104
  190.6 11.6 %all-to-all-start.1 = ((f32[16,6,4,128]{3,2,1,0:T(4,128)}), f32[16,6,4,128]{3,2,1,0:T(4,128)S(1)}, u32[]{:S(2)}, u32[]{:S(2)}) async-start(f32[16,6,4,128]{3,2,1,0:T(4,128)} %bitcast.233), calls=%async_computation.1 | async-start | bytes 393216 | tf_op jit(solution)/shard_map/while/body/eval_jaxpr/all_to_all | solution.py:104
  209.7 14.8 %all-to-all-start = ((f32[16,6,4,128]{3,2,1,0:T(4,128)}), f32[16,6,4,128]{3,2,1,0:T(4,128)S(1)}, u32[]{:S(2)}, u32[]{:S(2)}) async-start(f32[16,6,4,128]{3,2,1,0:T(4,128)} %bitcast.231), calls=%async_computation | async-start | bytes 393216 | tf_op jit(solution)/shard_map/while/body/eval_jaxpr/all_to_all | solution.py:104
  226.7 11.6 %all-to-all-start.1 = ((f32[16,6,4,128]{3,2,1,0:T(4,128)}), f32[16,6,4,128]{3,2,1,0:T(4,128)S(1)}, u32[]{:S(2)}, u32[]{:S(2)}) async-start(f32[16,6,4,128]{3,2,1,0:T(4,128)} %bitcast.233), calls=%async_computation.1 | async-start | bytes 393216 | tf_op jit(solution)/shard_map/while/body/eval_jaxpr/all_to_all | solution.py:104
  245.8 15.2 %all-to-all-start = ((f32[16,6,4,128]{3,2,1,0:T(4,128)}), f32[16,6,4,128]{3,2,1,0:T(4,128)S(1)}, u32[]{:S(2)}, u32[]{:S(2)}) async-start(f32[16,6,4,128]{3,2,1,0:T(4,128)} %bitcast.231), calls=%async_computation | async-start | bytes 393216 | tf_op jit(solution)/shard_map/while/body/eval_jaxpr/all_to_all | solution.py:104
  263.1 12.6 %all-to-all-start.1 = ((f32[16,6,4,128]{3,2,1,0:T(4,128)}), f32[16,6,4,128]{3,2,1,0:T(4,128)S(1)}, u32[]{:S(2)}, u32[]{:S(2)}) async-start(f32[16,6,4,128]{3,2,1,0:T(4,128)} %bitcast.233), calls=%async_computation.1 | async-start | bytes 393216 | tf_op jit(solution)/shard_map/while/body/eval_jaxpr/all_to_all | solution.py:104
  279.2 29.3 %copy-start.10 = (pred[96]{0:T(512)(128)(4,1)S(1)}, pred[96]{0:T(512)(128)(4,1)}, u32[]{:S(2)}) copy-start(pred[96]{0:T(512)(128)(4,1)} %get-tuple-element.473) | copy-start | bytes 292
  279.2 29.3 %copy-start.12 = (pred[96]{0:T(512)(128)(4,1)S(1)}, pred[96]{0:T(512)(128)(4,1)}, u32[]{:S(2)}) copy-start(pred[96]{0:T(512)(128)(4,1)} %get-tuple-element.474) | copy-start | bytes 292
  283.8 27.9 %copy-start.25 = (pred[96]{0:T(512)(128)(4,1)S(1)}, pred[96]{0:T(512)(128)(4,1)}, u32[]{:S(2)}) copy-start(pred[96]{0:T(512)(128)(4,1)} %get-tuple-element.184) | copy-start | bytes 292
  287.3 33.5 %copy-start.3 = (bf16[24,1024]{1,0:T(8,128)(2,1)S(1)}, bf16[24,1024]{1,0:T(8,128)(2,1)}, u32[]{:S(2)}) copy-start(bf16[24,1024]{1,0:T(8,128)(2,1)} %copy-done.2) | copy-start | bytes 147460
  306.5 22.3 %copy-start.21 = (pred[24]{0:T(512)(128)(4,1)S(1)}, pred[24]{0:T(512)(128)(4,1)}, u32[]{:S(2)}) copy-start(pred[24]{0:T(512)(128)(4,1)} %get-tuple-element.475) | copy-start | bytes 76
  306.5 22.3 %copy-start.22 = (pred[24]{0:T(512)(128)(4,1)S(1)}, pred[24]{0:T(512)(128)(4,1)}, u32[]{:S(2)}) copy-start(pred[24]{0:T(512)(128)(4,1)} %get-tuple-element.231) | copy-start | bytes 76
  314.7 18.9 %copy-start.29 = (f32[24,4]{0,1:T(4,128)S(1)}, f32[24,4]{0,1:T(4,128)}, u32[]{:S(2)}) copy-start(f32[24,4]{0,1:T(4,128)} %get-tuple-element.272) | copy-start | bytes 1156
  314.7 18.9 %copy-start.31 = (f32[24,4]{0,1:T(4,128)S(1)}, f32[24,4]{0,1:T(4,128)}, u32[]{:S(2)}) copy-start(f32[24,4]{0,1:T(4,128)} %get-tuple-element.273) | copy-start | bytes 1156
  315.5 12.5 %all-to-all-start.5 = ((f32[16,6,5,128]{3,1,2,0:T(8,128)}), f32[16,6,5,128]{3,1,2,0:T(8,128)S(1)}, u32[]{:S(2)}, u32[]{:S(2)}) async-start(f32[16,6,5,128]{3,1,2,0:T(8,128)} %copy.265), calls=%async_computation.5 | async-start | bytes 655360 | tf_op jit(solution)/shard_map/all_to_all | solution.py:104
  334.6 1.3 collective-permute-start
  (29 other events, 275.8 us)

commit v7 on v2

--- a/solution.py
+++ b/solution.py
@@ -99,19 +99,20 @@
         return jnp.take(padded, source, axis=0)
 
     def exchange(slots):
-        shaped = slots.astype(jnp.bfloat16).reshape((peer_count, capacity) + slots.shape[1:])
+        shaped = slots.reshape((peer_count, capacity) + slots.shape[1:])
         moved = lax.all_to_all(shaped, "req", split_axis=0, concat_axis=0, tiled=True)
-        return moved.reshape(slots.shape).astype(jnp.float32)
+        return moved.reshape(slots.shape)
 
     def unpack(slots):
         taken = jnp.take(slots, slot_of, axis=0)
         return jnp.where(routed[:, None, None], taken, 0.0)
 
     def owner_apply(states, incoming, chosen):
-        split = jnp.stack(
-            [jnp.where(chosen[group][:, None, None], incoming, 0.0) for group in range(group_count)]
-        )
-        return jnp.einsum("gshj,ghij->shi", split, states, precision=highest)
+        products = jnp.einsum("shj,ghij->gshi", incoming, states, precision=highest)
+        total = jnp.where(chosen[0][:, None, None], products[0], 0.0)
+        for group in range(1, group_count):
+            total = total + jnp.where(chosen[group][:, None, None], products[group], 0.0)
+        return total
 
     def cg_step(arrived, carry):
         solution, residual, direction, norm_now = carry
@@ -143,11 +144,36 @@
     )
     carry = cg_step(first[:, :head_count], carry)
     carry = lax.fori_loop(
-        1, ITERS, lambda _, state: cg_step(exchange(pack(state[2])), state), carry
-    )
-    solution = carry[0]
-    value_sum = unpack(exchange(owner_apply(prompt_values, exchange(pack(solution)), chosen)))
-    shared_out = weight_col * value_sum + own_matvec(own_values, solution)
+        1, ITERS - 1, lambda _, state: cg_step(exchange(pack(state[2])), state), carry
+    )
+    solution, residual, direction, norm_now = carry
+
+    both = exchange(jnp.concatenate([pack(direction), pack(solution)], axis=1))
+    held = both[:, :head_count]
+    owner_out = jnp.concatenate(
+        [
+            owner_apply(prompt_keys, held, chosen),
+            owner_apply(prompt_values, both[:, head_count:], chosen),
+            owner_apply(prompt_values, held, chosen),
+        ],
+        axis=1,
+    )
+    returned = unpack(exchange(owner_out))
+    own_out_partial = own_matvec(own_values, solution)
+    own_out_direction = own_matvec(own_values, direction)
+    partial = solution
+    shares = returned[:, :head_count]
+    shared = weight_col * shares + own_matvec(own_keys, direction)
+    product = (
+        decay_col * shared
+        + write_col * key_now * jnp.sum(key_now * direction, axis=2, keepdims=True)
+        + ridge_col * direction
+    )
+    step_last = norm_now / jnp.sum(direction * product, axis=2, keepdims=True)
+    solution = partial + step_last * direction
+    value_sum = returned[:, head_count : 2 * head_count] + step_last * returned[:, 2 * head_count :]
+    own_out = own_out_partial + step_last * own_out_direction
+    shared_out = weight_col * value_sum + own_out
     readout = decay_col * shared_out + write_col * value_now * jnp.sum(
         key_now * solution, axis=2, keepdims=True
     )

time: 279 us -> 268 us (0.961)
  waiting for transfers between devices: 102 us -> 88.4 us
  blocking collectives: 2.35 us -> 15.7 us
  starting transfers between devices: 71.1 us -> 58.1 us
  other arithmetic: 60.2 us -> 64.7 us
  local copies, waits for them, and re-layouts: 31.1 us -> 28 us
    all_to_all x18 -> x15, waiting for transfers between devices: 101 us -> 87.2 us  [exchange(): lax.all_to_all(shaped, 'req', split_axis=0, concat_axis=0, tiled=True)]
    all_to_all x0 -> x1, blocking collectives: none -> 13.4 us  [exchange(): lax.all_to_all(shaped, 'req', split_axis=0, concat_axis=0, tiled=True)]
    all_to_all x18 -> x15, starting transfers between devices: 71 us -> 58 us  [exchange(): lax.all_to_all(shaped, 'req', split_axis=0, concat_axis=0, tiled=True)]
    add x0 -> x8, other arithmetic: none -> 6.94 us  [owner_apply(): total + jnp.where(chosen[group][:, None, None], products[group], 0.0)]
    convert_element_type x26 -> x1, other arithmetic: 6.76 us -> 0.01 us  [on_device(): slot_label.astype(jnp.float32)[:, None, None]]
    convert_element_type x11 -> x0, local copies, waits for them, and re-layouts: 6.21 us -> none  [the longest x9 6.1 us: exchange(): slots.astype(jnp.bfloat16).reshape((peer_count, capacity) + slots.shape[1:])]
    select_n x8 -> x15, other arithmetic: 0.03 us -> 5.41 us  [pack(): return jnp.take(padded, source, axis=0)]
    slice x0 -> x31, local copies, waits for them, and re-layouts: none -> 2.94 us  [the longest x20 1.58 us: owner_apply(): total = jnp.where(chosen[0][:, None, None], products[0], 0.0)]
  transfers between devices with their start and end apart: 19 -> 16, of which waited for: 19 -> 16; matrix products, arithmetic and copies ran while one was open for 14% -> 16% of each run, Pallas kernels for 0% -> 0%
where the time goes in v7:
time: 268 us; the launch traced here: 266 us
  waiting for transfers between devices  88.4 us (33%)
  other arithmetic  64.7 us (24%)
  starting transfers between devices  58.1 us (22%)
  local copies, waits for them, and re-layouts  28 us (10%)
  blocking collectives  15.7 us (6%)
  matrix products  9.68 us (4%)
    all_to_all x15, waiting for transfers between devices, exchange(): lax.all_to_all(shaped, 'req', split_axis=0, concat_axis=0, tiled=True)  87.2 us
    all_to_all x15, starting transfers between devices, exchange(): lax.all_to_all(shaped, 'req', split_axis=0, concat_axis=0, tiled=True)  58 us
    reduce_sum x8, other arithmetic, own_matvec(): return jnp.sum(matrices * vectors[:, :, None, :], axis=3)  39.3 us
    all_to_all x1, blocking collectives, exchange(): lax.all_to_all(shaped, 'req', split_axis=0, concat_axis=0, tiled=True)  13.4 us
    add x8, other arithmetic, owner_apply(): total + jnp.where(chosen[group][:, None, None], products[group], 0.0)  6.94 us
    gather x9, local copies, waits for them, and re-layouts, pack(): return jnp.take(padded, source, axis=0)  6.34 us
    dot_general x10, matrix products, owner_apply(): products = jnp.einsum('shj,ghij->gshi', incoming, states, precision=highest)  6.33 us
    unnamed x19, local copies, waits for them, and re-layouts  6.13 us
  transfers between devices with their start and end apart: 16, of which 16 were waited for; matrix products, arithmetic and copies ran while one was open for 16% of the time, Pallas kernels for 0%

profile of v7, /device:TPU:0, one launch (start us, length us, event | category | flops | bytes accessed | tf_op | source)
XLA Modules:
  0.0 266.0 jit_solution(632343748867445318)
XLA Ops:
  6.6 6.0 %copy.151 = bf16[1024,4,3,128]{0,3,2,1:T(8,128)(2,1)} copy(bf16[1024,4,3,128]{3,1,2,0:T(4,128)(2,1)} %param.23) | data formatting | bytes 6291456 | tf_op args[2]
  18.2 8.2 %all-to-all-start.2 = ((f32[16,6,5,128]{3,1,2,0:T(8,128)}), f32[16,6,5,128]{3,1,2,0:T(8,128)S(1)}, u32[]{:S(2)}, u32[]{:S(2)}) async-start(f32[16,6,5,128]{3,1,2,0:T(8,128)} %copy.161), calls=%async_computation.2 | async-start | bytes 655360 | tf_op jit(solution)/shard_map/all_to_all | solution.py:103
  26.5 11.5 %all-to-all-done.2 = f32[16,6,5,128]{3,1,2,0:T(8,128)S(1)} async-done(((f32[16,6,5,128]{3,1,2,0:T(8,128)}), f32[16,6,5,128]{3,1,2,0:T(8,128)S(1)}, u32[]{:S(2)}, u32[]{:S(2)}) %all-to-all-start.2) | async-done | bytes 245792 | tf_op jit(solution)/shard_map/all_to_all | solution.py:103
  40.3 3.5 %all-to-all-start.3 = ((f32[16,6,4,128]{3,2,1,0:T(4,128)}), f32[16,6,4,128]{3,2,1,0:T(4,128)S(1)}, u32[]{:S(2)}, u32[]{:S(2)}) async-start(f32[16,6,4,128]{3,2,1,0:T(4,128)} %select_add_fusion.4), calls=%async_computation.3 | async-start | bytes 393216 | tf_op jit(solution)/shard_map/all_to_all | solution.py:103
  44.0 4.5 %multiply_reduce_fusion.7 = f32[24,4,128]{2,1,0:T(4,128)S(1)} fusion(f32[24,4,128,128]{3,2,1,0:T(8,128)} %param.29, f32[24,4,128]{2,1,0:T(4,128)S(1)} %copy.167), kind=kLoop, calls=%fused_computation.42 | loop fusion | flops 3133440 | bytes 6389760 | tf_op jit(solution)/shard_map/reduce_sum | solution.py:16
  53.2 172.4 %while.16 = (s32[]{:T(128)}, f32[24,4,128]{2,1,0:T(4,128)S(1)}, f32[24,4,128]{2,1,0:T(4,128)S(1)}, f32[24,4,128]{2,1,0:T(4,128)S(1)}, f32[24,4,1]{0,1,2:T(4,128)...) while((s32[]{:T(128)}, f32[24,4,128]{2,1,0:T(4,128)S(1)}, ...), condition=%wide.region_17.20_spmd, body=%wide.region_12.19_spmd.sunk | while | flops 154586384 | bytes 12493481 | solution.py:146
  54.8 3.5 %all-to-all-start = ((f32[16,6,4,128]{3,2,1,0:T(4,128)}), f32[16,6,4,128]{3,2,1,0:T(4,128)S(1)}, u32[]{:S(2)}, u32[]{:S(2)}) async-start(f32[16,6,4,128]{3,2,1,0:T(4,128)} %bitcast.185), calls=%async_computation | async-start | bytes 393216 | tf_op jit(solution)/shard_map/while/body/eval_jaxpr/all_to_all | solution.py:103
  58.6 7.8 %all-to-all-done = f32[16,6,4,128]{3,2,1,0:T(4,128)S(1)} async-done(((f32[16,6,4,128]{3,2,1,0:T(4,128)}), f32[16,6,4,128]{3,2,1,0:T(4,128)S(1)}, u32[]{:S(2)}, u32[]{:S(2)}) %all-to-all-start) | async-done | bytes 196640 | tf_op jit(solution)/shard_map/while/body/eval_jaxpr/all_to_all | solution.py:103
  72.1 4.5 %multiply_reduce_fusion.17 = f32[24,4,128]{2,1,0:T(4,128)S(1)} fusion(f32[24,4,128,128]{3,2,1,0:T(8,128)} %get-tuple-element.436, f32[24,4,128]{2,1,0:T(4,128)S(1)} %get-tuple-element.407), kind=kLoop, calls=%fused_computation.8.clone.1 | loop fusion | flops 3133440 | bytes 6389760 | tf_op jit(solution)/shard_map/while/body/eval_jaxpr/reduce_sum | solution.py:16
  83.4 3.6 %all-to-all-start = ((f32[16,6,4,128]{3,2,1,0:T(4,128)}), f32[16,6,4,128]{3,2,1,0:T(4,128)S(1)}, u32[]{:S(2)}, u32[]{:S(2)}) async-start(f32[16,6,4,128]{3,2,1,0:T(4,128)} %bitcast.185), calls=%async_computation | async-start | bytes 393216 | tf_op jit(solution)/shard_map/while/body/eval_jaxpr/all_to_all | solution.py:103
  87.3 7.9 %all-to-all-done = f32[16,6,4,128]{3,2,1,0:T(4,128)S(1)} async-done(((f32[16,6,4,128]{3,2,1,0:T(4,128)}), f32[16,6,4,128]{3,2,1,0:T(4,128)S(1)}, u32[]{:S(2)}, u32[]{:S(2)}) %all-to-all-start) | async-done | bytes 196640 | tf_op jit(solution)/shard_map/while/body/eval_jaxpr/all_to_all | solution.py:103
  97.0 3.5 %all-to-all-start.1 = ((f32[16,6,4,128]{3,2,1,0:T(4,128)}), f32[16,6,4,128]{3,2,1,0:T(4,128)S(1)}, u32[]{:S(2)}, u32[]{:S(2)}) async-start(f32[16,6,4,128]{3,2,1,0:T(4,128)} %select_add_fusion.8), calls=%async_computation.1 | async-start | bytes 393216 | tf_op jit(solution)/shard_map/while/body/eval_jaxpr/all_to_all | solution.py:103
  100.8 4.5 %multiply_reduce_fusion.17 = f32[24,4,128]{2,1,0:T(4,128)S(1)} fusion(f32[24,4,128,128]{3,2,1,0:T(8,128)} %get-tuple-element.436, f32[24,4,128]{2,1,0:T(4,128)S(1)} %get-tuple-element.407), kind=kLoop, calls=%fused_computation.8.clone.1 | loop fusion | flops 3133440 | bytes 6389760 | tf_op jit(solution)/shard_map/while/body/eval_jaxpr/reduce_sum | solution.py:16
  112.2 3.6 %all-to-all-start = ((f32[16,6,4,128]{3,2,1,0:T(4,128)}), f32[16,6,4,128]{3,2,1,0:T(4,128)S(1)}, u32[]{:S(2)}, u32[]{:S(2)}) async-start(f32[16,6,4,128]{3,2,1,0:T(4,128)} %bitcast.185), calls=%async_computation | async-start | bytes 393216 | tf_op jit(solution)/shard_map/while/body/eval_jaxpr/all_to_all | solution.py:103
  116.0 7.9 %all-to-all-done = f32[16,6,4,128]{3,2,1,0:T(4,128)S(1)} async-done(((f32[16,6,4,128]{3,2,1,0:T(4,128)}), f32[16,6,4,128]{3,2,1,0:T(4,128)S(1)}, u32[]{:S(2)}, u32[]{:S(2)}) %all-to-all-start) | async-done | bytes 196640 | tf_op jit(solution)/shard_map/while/body/eval_jaxpr/all_to_all | solution.py:103
  125.8 3.5 %all-to-all-start.1 = ((f32[16,6,4,128]{3,2,1,0:T(4,128)}), f32[16,6,4,128]{3,2,1,0:T(4,128)S(1)}, u32[]{:S(2)}, u32[]{:S(2)}) async-start(f32[16,6,4,128]{3,2,1,0:T(4,128)} %select_add_fusion.8), calls=%async_computation.1 | async-start | bytes 393216 | tf_op jit(solution)/shard_map/while/body/eval_jaxpr/all_to_all | solution.py:103
  129.6 4.5 %multiply_reduce_fusion.17 = f32[24,4,128]{2,1,0:T(4,128)S(1)} fusion(f32[24,4,128,128]{3,2,1,0:T(8,128)} %get-tuple-element.436, f32[24,4,128]{2,1,0:T(4,128)S(1)} %get-tuple-element.407), kind=kLoop, calls=%fused_computation.8.clone.1 | loop fusion | flops 3133440 | bytes 6389760 | tf_op jit(solution)/shard_map/while/body/eval_jaxpr/reduce_sum | solution.py:16
  140.9 3.6 %all-to-all-start = ((f32[16,6,4,128]{3,2,1,0:T(4,128)}), f32[16,6,4,128]{3,2,1,0:T(4,128)S(1)}, u32[]{:S(2)}, u32[]{:S(2)}) async-start(f32[16,6,4,128]{3,2,1,0:T(4,128)} %bitcast.185), calls=%async_computation | async-start | bytes 393216 | tf_op jit(solution)/shard_map/while/body/eval_jaxpr/all_to_all | solution.py:103
  144.7 7.9 %all-to-all-done = f32[16,6,4,128]{3,2,1,0:T(4,128)S(1)} async-done(((f32[16,6,4,128]{3,2,1,0:T(4,128)}), f32[16,6,4,128]{3,2,1,0:T(4,128)S(1)}, u32[]{:S(2)}, u32[]{:S(2)}) %all-to-all-start) | async-done | bytes 196640 | tf_op jit(solution)/shard_map/while/body/eval_jaxpr/all_to_all | solution.py:103
  158.3 4.5 %multiply_reduce_fusion.17 = f32[24,4,128]{2,1,0:T(4,128)S(1)} fusion(f32[24,4,128,128]{3,2,1,0:T(8,128)} %get-tuple-element.436, f32[24,4,128]{2,1,0:T(4,128)S(1)} %get-tuple-element.407), kind=kLoop, calls=%fused_computation.8.clone.1 | loop fusion | flops 3133440 | bytes 6389760 | tf_op jit(solution)/shard_map/while/body/eval_jaxpr/reduce_sum | solution.py:16
  169.6 3.6 %all-to-all-start = ((f32[16,6,4,128]{3,2,1,0:T(4,128)}), f32[16,6,4,128]{3,2,1,0:T(4,128)S(1)}, u32[]{:S(2)}, u32[]{:S(2)}) async-start(f32[16,6,4,128]{3,2,1,0:T(4,128)} %bitcast.185), calls=%async_computation | async-start | bytes 393216 | tf_op jit(solution)/shard_map/while/body/eval_jaxpr/all_to_all | solution.py:103
  173.5 7.9 %all-to-all-done = f32[16,6,4,128]{3,2,1,0:T(4,128)S(1)} async-done(((f32[16,6,4,128]{3,2,1,0:T(4,128)}), f32[16,6,4,128]{3,2,1,0:T(4,128)S(1)}, u32[]{:S(2)}, u32[]{:S(2)}) %all-to-all-start) | async-done | bytes 196640 | tf_op jit(solution)/shard_map/while/body/eval_jaxpr/all_to_all | solution.py:103
  183.2 3.5 %all-to-all-start.1 = ((f32[16,6,4,128]{3,2,1,0:T(4,128)}), f32[16,6,4,128]{3,2,1,0:T(4,128)S(1)}, u32[]{:S(2)}, u32[]{:S(2)}) async-start(f32[16,6,4,128]{3,2,1,0:T(4,128)} %select_add_fusion.8), calls=%async_computation.1 | async-start | bytes 393216 | tf_op jit(solution)/shard_map/while/body/eval_jaxpr/all_to_all | solution.py:103
  187.0 4.5 %multiply_reduce_fusion.17 = f32[24,4,128]{2,1,0:T(4,128)S(1)} fusion(f32[24,4,128,128]{3,2,1,0:T(8,128)} %get-tuple-element.436, f32[24,4,128]{2,1,0:T(4,128)S(1)} %get-tuple-element.407), kind=kLoop, calls=%fused_computation.8.clone.1 | loop fusion | flops 3133440 | bytes 6389760 | tf_op jit(solution)/shard_map/while/body/eval_jaxpr/reduce_sum | solution.py:16
  198.4 3.6 %all-to-all-start = ((f32[16,6,4,128]{3,2,1,0:T(4,128)}), f32[16,6,4,128]{3,2,1,0:T(4,128)S(1)}, u32[]{:S(2)}, u32[]{:S(2)}) async-start(f32[16,6,4,128]{3,2,1,0:T(4,128)} %bitcast.185), calls=%async_computation | async-start | bytes 393216 | tf_op jit(solution)/shard_map/while/body/eval_jaxpr/all_to_all | solution.py:103
  202.2 7.9 %all-to-all-done = f32[16,6,4,128]{3,2,1,0:T(4,128)S(1)} async-done(((f32[16,6,4,128]{3,2,1,0:T(4,128)}), f32[16,6,4,128]{3,2,1,0:T(4,128)S(1)}, u32[]{:S(2)}, u32[]{:S(2)}) %all-to-all-start) | async-done | bytes 196640 | tf_op jit(solution)/shard_map/while/body/eval_jaxpr/all_to_all | solution.py:103
  212.0 3.5 %all-to-all-start.1 = ((f32[16,6,4,128]{3,2,1,0:T(4,128)}), f32[16,6,4,128]{3,2,1,0:T(4,128)S(1)}, u32[]{:S(2)}, u32[]{:S(2)}) async-start(f32[16,6,4,128]{3,2,1,0:T(4,128)} %select_add_fusion.8), calls=%async_computation.1 | async-start | bytes 393216 | tf_op jit(solution)/shard_map/while/body/eval_jaxpr/all_to_all | solution.py:103
  215.8 4.5 %multiply_reduce_fusion.17 = f32[24,4,128]{2,1,0:T(4,128)S(1)} fusion(f32[24,4,128,128]{3,2,1,0:T(8,128)} %get-tuple-element.436, f32[24,4,128]{2,1,0:T(4,128)S(1)} %get-tuple-element.407), kind=kLoop, calls=%fused_computation.8.clone.1 | loop fusion | flops 3133440 | bytes 6389760 | tf_op jit(solution)/shard_map/while/body/eval_jaxpr/reduce_sum | solution.py:16
  227.3 13.4 %all_to_all.32 = f32[16,6,8,128]{3,2,1,0:T(8,128)S(1)} all-to-all(f32[16,6,8,128]{3,2,1,0:T(8,128)S(1)} %bitcast.198), channel_id=1, replica_groups=mesh['req'=16,'head'=2] {'req'}, dimensions={0} | all-to-all | bytes 786432 | tf_op jit(solution)/shard_map/all_to_all | solution.py:103
  244.9 3.6 %all-to-all-start.5 = ((f32[16,6,12,128]{3,2,1,0:T(8,128)}), f32[16,6,12,128]{3,2,1,0:T(8,128)S(1)}, u32[]{:S(2)}, u32[]{:S(2)}) async-start(f32[16,6,12,128]{3,2,1,0:T(8,128)} %pad_maximum_fusion), calls=%async_computation.5 | async-start | bytes 1572864 | tf_op jit(solution)/shard_map/all_to_all | solution.py:103
  248.6 7.9 %multiply_reduce_fusion.4 = (f32[24,4,128]{2,1,0:T(4,128)S(1)}, f32[24,4,128]{2,1,0:T(4,128)S(1)}, f32[24,4,128]{2,1,0:T(4,128)S(1)}) fusion(f32[24,4,128,128]{3,2,1,0:T(8,128)} %param.30, f32[24,4,128]{2,1,0:T(4,128)S(1)} %get-tuple-element.96, f32[24,4,128]{2,1,0:T(4,128)S(1)} %get-tuple-element.97, f32[24,4,128,128]{3,2,1,0:T(8,128)} %get-tuple-element.442), kind=kLoop, calls=%fused_computation.39 | loop fusion | flops 9400320 | bytes 12828672 | tf_op jit(solution)/shard_map/reduce_sum | solution.py:16
  256.5 5.3 %all-to-all-done.5 = f32[16,6,12,128]{3,2,1,0:T(8,128)S(1)} async-done(((f32[16,6,12,128]{3,2,1,0:T(8,128)}), f32[16,6,12,128]{3,2,1,0:T(8,128)S(1)}, u32[]{:S(2)}, u32[]{:S(2)}) %all-to-all-start.5) | async-done | bytes 589856 | tf_op jit(solution)/shard_map/all_to_all | solution.py:103
  (296 shorter events, 90.8 us)
Async XLA Ops:
  0.0 263.7 %copy-start = (bf16[4,128,1024]{2,1,0:T(8,128)(2,1)S(1)}, bf16[4,128,1024]{2,1,0:T(8,128)(2,1)}, u32[]{:S(2)}) copy-start(bf16[4,128,1024]{2,1,0:T(8,128)(2,1)} %param.35) | copy-start | bytes 3145732
  0.0 12.7 %copy-start.6 = (f32[1024]{0:T(1024)S(1)}, f32[1024]{0:T(1024)}, u32[]{:S(2)}) copy-start(f32[1024]{0:T(1024)} %param.22) | copy-start | bytes 12292
  6.6 11.3 %copy-start.5 = (bf16[1024,2,4]{0,2,1:T(4,128)(2,1)S(1)}, bf16[1024,2,4]{0,2,1:T(4,128)(2,1)}, u32[]{:S(2)}) copy-start(bf16[1024,2,4]{0,2,1:T(4,128)(2,1)} %param.26) | copy-start | bytes 49156
  6.6 31.6 %copy-start.1 = (f32[2,4,128,128]{3,2,1,0:T(8,128)S(1)}, f32[2,4,128,128]{3,2,1,0:T(8,128)}, u32[]{:S(2)}) copy-start(f32[2,4,128,128]{3,2,1,0:T(8,128)} %param.31) | copy-start | bytes 1572868
  18.2 19.9 %all-to-all-start.2 = ((f32[16,6,5,128]{3,1,2,0:T(8,128)}), f32[16,6,5,128]{3,1,2,0:T(8,128)S(1)}, u32[]{:S(2)}, u32[]{:S(2)}) async-start(f32[16,6,5,128]{3,1,2,0:T(8,128)} %copy.161), calls=%async_computation.2 | async-start | bytes 655360 | tf_op jit(solution)/shard_map/all_to_all | solution.py:103
  26.5 26.0 %copy-start.4 = (f32[24,4]{0,1:T(4,128)S(1)}, f32[24,4]{0,1:T(4,128)}, u32[]{:S(2)}) copy-start(f32[24,4]{0,1:T(4,128)} %param.27) | copy-start | bytes 1156
  26.5 26.0 %copy-start.7 = (f32[4]{0:T(128)S(1)}, f32[4]{0:T(128)}, u32[]{:S(2)}) copy-start(f32[4]{0:T(128)} %param.28) | copy-start | bytes 52
  40.3 11.6 %all-to-all-start.3 = ((f32[16,6,4,128]{3,2,1,0:T(4,128)}), f32[16,6,4,128]{3,2,1,0:T(4,128)S(1)}, u32[]{:S(2)}, u32[]{:S(2)}) async-start(f32[16,6,4,128]{3,2,1,0:T(4,128)} %select_add_fusion.4), calls=%async_computation.3 | async-start | bytes 393216 | tf_op jit(solution)/shard_map/all_to_all | solution.py:103
  54.8 11.6 %all-to-all-start = ((f32[16,6,4,128]{3,2,1,0:T(4,128)}), f32[16,6,4,128]{3,2,1,0:T(4,128)S(1)}, u32[]{:S(2)}, u32[]{:S(2)}) async-start(f32[16,6,4,128]{3,2,1,0:T(4,128)} %bitcast.185), calls=%async_computation | async-start | bytes 393216 | tf_op jit(solution)/shard_map/while/body/eval_jaxpr/all_to_all | solution.py:103
  68.3 11.6 %all-to-all-start.1 = ((f32[16,6,4,128]{3,2,1,0:T(4,128)}), f32[16,6,4,128]{3,2,1,0:T(4,128)S(1)}, u32[]{:S(2)}, u32[]{:S(2)}) async-start(f32[16,6,4,128]{3,2,1,0:T(4,128)} %select_add_fusion.8), calls=%async_computation.1 | async-start | bytes 393216 | tf_op jit(solution)/shard_map/while/body/eval_jaxpr/all_to_all | solution.py:103
  83.4 11.7 %all-to-all-start = ((f32[16,6,4,128]{3,2,1,0:T(4,128)}), f32[16,6,4,128]{3,2,1,0:T(4,128)S(1)}, u32[]{:S(2)}, u32[]{:S(2)}) async-start(f32[16,6,4,128]{3,2,1,0:T(4,128)} %bitcast.185), calls=%async_computation | async-start | bytes 393216 | tf_op jit(solution)/shard_map/while/body/eval_jaxpr/all_to_all | solution.py:103
  97.0 11.6 %all-to-all-start.1 = ((f32[16,6,4,128]{3,2,1,0:T(4,128)}), f32[16,6,4,128]{3,2,1,0:T(4,128)S(1)}, u32[]{:S(2)}, u32[]{:S(2)}) async-start(f32[16,6,4,128]{3,2,1,0:T(4,128)} %select_add_fusion.8), calls=%async_computation.1 | async-start | bytes 393216 | tf_op jit(solution)/shard_map/while/body/eval_jaxpr/all_to_all | solution.py:103
  112.2 11.7 %all-to-all-start = ((f32[16,6,4,128]{3,2,1,0:T(4,128)}), f32[16,6,4,128]{3,2,1,0:T(4,128)S(1)}, u32[]{:S(2)}, u32[]{:S(2)}) async-start(f32[16,6,4,128]{3,2,1,0:T(4,128)} %bitcast.185), calls=%async_computation | async-start | bytes 393216 | tf_op jit(solution)/shard_map/while/body/eval_jaxpr/all_to_all | solution.py:103
  125.8 11.6 %all-to-all-start.1 = ((f32[16,6,4,128]{3,2,1,0:T(4,128)}), f32[16,6,4,128]{3,2,1,0:T(4,128)S(1)}, u32[]{:S(2)}, u32[]{:S(2)}) async-start(f32[16,6,4,128]{3,2,1,0:T(4,128)} %select_add_fusion.8), calls=%async_computation.1 | async-start | bytes 393216 | tf_op jit(solution)/shard_map/while/body/eval_jaxpr/all_to_all | solution.py:103
  140.9 11.7 %all-to-all-start = ((f32[16,6,4,128]{3,2,1,0:T(4,128)}), f32[16,6,4,128]{3,2,1,0:T(4,128)S(1)}, u32[]{:S(2)}, u32[]{:S(2)}) async-start(f32[16,6,4,128]{3,2,1,0:T(4,128)} %bitcast.185), calls=%async_computation | async-start | bytes 393216 | tf_op jit(solution)/shard_map/while/body/eval_jaxpr/all_to_all | solution.py:103
  154.5 11.6 %all-to-all-start.1 = ((f32[16,6,4,128]{3,2,1,0:T(4,128)}), f32[16,6,4,128]{3,2,1,0:T(4,128)S(1)}, u32[]{:S(2)}, u32[]{:S(2)}) async-start(f32[16,6,4,128]{3,2,1,0:T(4,128)} %select_add_fusion.8), calls=%async_computation.1 | async-start | bytes 393216 | tf_op jit(solution)/shard_map/while/body/eval_jaxpr/all_to_all | solution.py:103
  169.6 11.7 %all-to-all-start = ((f32[16,6,4,128]{3,2,1,0:T(4,128)}), f32[16,6,4,128]{3,2,1,0:T(4,128)S(1)}, u32[]{:S(2)}, u32[]{:S(2)}) async-start(f32[16,6,4,128]{3,2,1,0:T(4,128)} %bitcast.185), calls=%async_computation | async-start | bytes 393216 | tf_op jit(solution)/shard_map/while/body/eval_jaxpr/all_to_all | solution.py:103
  183.2 11.6 %all-to-all-start.1 = ((f32[16,6,4,128]{3,2,1,0:T(4,128)}), f32[16,6,4,128]{3,2,1,0:T(4,128)S(1)}, u32[]{:S(2)}, u32[]{:S(2)}) async-start(f32[16,6,4,128]{3,2,1,0:T(4,128)} %select_add_fusion.8), calls=%async_computation.1 | async-start | bytes 393216 | tf_op jit(solution)/shard_map/while/body/eval_jaxpr/all_to_all | solution.py:103
  198.4 11.8 %all-to-all-start = ((f32[16,6,4,128]{3,2,1,0:T(4,128)}), f32[16,6,4,128]{3,2,1,0:T(4,128)S(1)}, u32[]{:S(2)}, u32[]{:S(2)}) async-start(f32[16,6,4,128]{3,2,1,0:T(4,128)} %bitcast.185), calls=%async_computation | async-start | bytes 393216 | tf_op jit(solution)/shard_map/while/body/eval_jaxpr/all_to_all | solution.py:103
  212.0 11.6 %all-to-all-start.1 = ((f32[16,6,4,128]{3,2,1,0:T(4,128)}), f32[16,6,4,128]{3,2,1,0:T(4,128)S(1)}, u32[]{:S(2)}, u32[]{:S(2)}) async-start(f32[16,6,4,128]{3,2,1,0:T(4,128)} %select_add_fusion.8), calls=%async_computation.1 | async-start | bytes 393216 | tf_op jit(solution)/shard_map/while/body/eval_jaxpr/all_to_all | solution.py:103
  225.6 16.1 %copy-start.2 = (f32[2,4,128,128]{3,2,1,0:T(8,128)S(1)}, f32[2,4,128,128]{3,2,1,0:T(8,128)}, u32[]{:S(2)}) copy-start(f32[2,4,128,128]{3,2,1,0:T(8,128)} %param.32) | copy-start | bytes 1572868
  244.9 16.8 %all-to-all-start.5 = ((f32[16,6,12,128]{3,2,1,0:T(8,128)}), f32[16,6,12,128]{3,2,1,0:T(8,128)S(1)}, u32[]{:S(2)}, u32[]{:S(2)}) async-start(f32[16,6,12,128]{3,2,1,0:T(8,128)} %pad_maximum_fusion), calls=%async_computation.5 | async-start | bytes 1572864 | tf_op jit(solution)/shard_map/all_to_all | solution.py:103
  248.6 16.8 %copy-start.3 = (bf16[24,512]{1,0:T(8,128)(2,1)S(1)}, bf16[24,512]{1,0:T(8,128)(2,1)}, u32[]{:S(2)}) copy-start(bf16[24,512]{1,0:T(8,128)(2,1)} %param.21) | copy-start | bytes 73732
  264.0 1.3 collective-permute-start

commit v8 on v7

--- a/solution.py
+++ b/solution.py
@@ -96,7 +96,7 @@
         padded = jnp.concatenate(
             [vectors, jnp.zeros((1,) + vectors.shape[1:], vectors.dtype)], axis=0
         )
-        return jnp.take(padded, source, axis=0)
+        return jnp.take(padded, source, axis=0, mode="clip")
 
     def exchange(slots):
         shaped = slots.reshape((peer_count, capacity) + slots.shape[1:])
@@ -104,7 +104,7 @@
         return moved.reshape(slots.shape)
 
     def unpack(slots):
-        taken = jnp.take(slots, slot_of, axis=0)
+        taken = jnp.take(slots, slot_of, axis=0, mode="clip")
         return jnp.where(routed[:, None, None], taken, 0.0)
 
     def owner_apply(states, incoming, chosen):

time: 268 us -> 266 us (level)
  other arithmetic: 64.7 us -> 59.2 us
  local copies, waits for them, and re-layouts: 28 us -> 32 us
    select_n x22 -> x1, other arithmetic: 5.44 us -> 0.66 us  [on_device(): slot_of = jnp.where(routed, owner_of * capacity + rank_of, 0)]
    gather x17, local copies, waits for them, and re-layouts: 11.1 us -> 15.1 us  [the longest x9 10.3 us: pack(): return jnp.take(padded, source, axis=0, mode='clip')]
where the time goes in v8:
time: 266 us; the launch traced here: 264 us
  waiting for transfers between devices  88.6 us (33%)
  other arithmetic  59.2 us (22%)
  starting transfers between devices  58.1 us (22%)
  local copies, waits for them, and re-layouts  32 us (12%)
  blocking collectives  15.4 us (6%)
  matrix products  9.68 us (4%)
    all_to_all x15, waiting for transfers between devices, exchange(): lax.all_to_all(shaped, 'req', split_axis=0, concat_axis=0, tiled=True)  87.4 us
    all_to_all x15, starting transfers between devices, exchange(): lax.all_to_all(shaped, 'req', split_axis=0, concat_axis=0, tiled=True)  58 us
    reduce_sum x8, other arithmetic, own_matvec(): return jnp.sum(matrices * vectors[:, :, None, :], axis=3)  39.3 us
    all_to_all x1, blocking collectives, exchange(): lax.all_to_all(shaped, 'req', split_axis=0, concat_axis=0, tiled=True)  13.1 us
    gather x9, local copies, waits for them, and re-layouts, pack(): return jnp.take(padded, source, axis=0, mode='clip')  10.3 us
    add x8, other arithmetic, owner_apply(): total + jnp.where(chosen[group][:, None, None], products[group], 0.0)  6.94 us
    dot_general x10, matrix products, owner_apply(): products = jnp.einsum('shj,ghij->gshi', incoming, states, precision=highest)  6.33 us
    unnamed x19, local copies, waits for them, and re-layouts  6.13 us
  transfers between devices with their start and end apart: 16, of which 16 were waited for; matrix products, arithmetic and copies ran while one was open for 16% of the time, Pallas kernels for 0%

profile of v8, /device:TPU:0, one launch (start us, length us, event | category | flops | bytes accessed | tf_op | source)
XLA Modules:
  0.0 264.3 jit_solution(6764256447097308238)
XLA Ops:
  7.3 6.0 %copy.151 = bf16[1024,4,3,128]{0,3,2,1:T(8,128)(2,1)} copy(bf16[1024,4,3,128]{3,1,2,0:T(4,128)(2,1)} %param.19) | data formatting | bytes 6291456 | tf_op args[2]
  18.4 8.2 %all-to-all-start.2 = ((f32[16,6,5,128]{3,1,2,0:T(8,128)}), f32[16,6,5,128]{3,1,2,0:T(8,128)S(1)}, u32[]{:S(2)}, u32[]{:S(2)}) async-start(f32[16,6,5,128]{3,1,2,0:T(8,128)} %copy.161), calls=%async_computation.2 | async-start | bytes 655360 | tf_op jit(solution)/shard_map/all_to_all | solution.py:103
  27.0 11.3 %all-to-all-done.2 = f32[16,6,5,128]{3,1,2,0:T(8,128)S(1)} async-done(((f32[16,6,5,128]{3,1,2,0:T(8,128)}), f32[16,6,5,128]{3,1,2,0:T(8,128)S(1)}, u32[]{:S(2)}, u32[]{:S(2)}) %all-to-all-start.2) | async-done | bytes 245792 | tf_op jit(solution)/shard_map/all_to_all | solution.py:103
  40.6 3.5 %all-to-all-start.3 = ((f32[16,6,4,128]{3,2,1,0:T(4,128)}), f32[16,6,4,128]{3,2,1,0:T(4,128)S(1)}, u32[]{:S(2)}, u32[]{:S(2)}) async-start(f32[16,6,4,128]{3,2,1,0:T(4,128)} %select_add_fusion.4), calls=%async_computation.3 | async-start | bytes 393216 | tf_op jit(solution)/shard_map/all_to_all | solution.py:103
  44.2 4.5 %multiply_reduce_fusion.7 = f32[24,4,128]{2,1,0:T(4,128)S(1)} fusion(f32[24,4,128,128]{3,2,1,0:T(8,128)} %param.25, f32[24,4,128]{2,1,0:T(4,128)S(1)} %copy.167), kind=kLoop, calls=%fused_computation.33 | loop fusion | flops 3133440 | bytes 6389760 | tf_op jit(solution)/shard_map/reduce_sum | solution.py:16
  53.5 170.9 %while.16 = (s32[]{:T(128)}, f32[24,4,128]{2,1,0:T(4,128)S(1)}, f32[24,4,128]{2,1,0:T(4,128)S(1)}, f32[24,4,128]{2,1,0:T(4,128)S(1)}, f32[24,4,1]{0,1,2:T(4,128)...) while((s32[]{:T(128)}, f32[24,4,128]{2,1,0:T(4,128)S(1)}, ...), condition=%wide.region_17.18_spmd, body=%wide.region_12.17_spmd.sunk | while | flops 154523872 | bytes 12098585 | solution.py:146
  54.9 3.5 %all-to-all-start = ((f32[16,6,4,128]{3,2,1,0:T(4,128)}), f32[16,6,4,128]{3,2,1,0:T(4,128)S(1)}, u32[]{:S(2)}, u32[]{:S(2)}) async-start(f32[16,6,4,128]{3,2,1,0:T(4,128)} %bitcast.185), calls=%async_computation | async-start | bytes 393216 | tf_op jit(solution)/shard_map/while/body/eval_jaxpr/all_to_all | solution.py:103
  58.6 7.9 %all-to-all-done = f32[16,6,4,128]{3,2,1,0:T(4,128)S(1)} async-done(((f32[16,6,4,128]{3,2,1,0:T(4,128)}), f32[16,6,4,128]{3,2,1,0:T(4,128)S(1)}, u32[]{:S(2)}, u32[]{:S(2)}) %all-to-all-start) | async-done | bytes 196640 | tf_op jit(solution)/shard_map/while/body/eval_jaxpr/all_to_all | solution.py:103
  68.3 3.5 %all-to-all-start.1 = ((f32[16,6,4,128]{3,2,1,0:T(4,128)}), f32[16,6,4,128]{3,2,1,0:T(4,128)S(1)}, u32[]{:S(2)}, u32[]{:S(2)}) async-start(f32[16,6,4,128]{3,2,1,0:T(4,128)} %select_add_fusion.7), calls=%async_computation.1 | async-start | bytes 393216 | tf_op jit(solution)/shard_map/while/body/eval_jaxpr/all_to_all | solution.py:103
  72.1 4.5 %multiply_reduce_fusion.17 = f32[24,4,128]{2,1,0:T(4,128)S(1)} fusion(f32[24,4,128,128]{3,2,1,0:T(8,128)} %get-tuple-element.428, f32[24,4,128]{2,1,0:T(4,128)S(1)} %get-tuple-element.399), kind=kLoop, calls=%fused_computation.8.clone.1 | loop fusion | flops 3133440 | bytes 6389760 | tf_op jit(solution)/shard_map/while/body/eval_jaxpr/reduce_sum | solution.py:16
  83.2 3.6 %all-to-all-start = ((f32[16,6,4,128]{3,2,1,0:T(4,128)}), f32[16,6,4,128]{3,2,1,0:T(4,128)S(1)}, u32[]{:S(2)}, u32[]{:S(2)}) async-start(f32[16,6,4,128]{3,2,1,0:T(4,128)} %bitcast.185), calls=%async_computation | async-start | bytes 393216 | tf_op jit(solution)/shard_map/while/body/eval_jaxpr/all_to_all | solution.py:103
  87.0 7.9 %all-to-all-done = f32[16,6,4,128]{3,2,1,0:T(4,128)S(1)} async-done(((f32[16,6,4,128]{3,2,1,0:T(4,128)}), f32[16,6,4,128]{3,2,1,0:T(4,128)S(1)}, u32[]{:S(2)}, u32[]{:S(2)}) %all-to-all-start) | async-done | bytes 196640 | tf_op jit(solution)/shard_map/while/body/eval_jaxpr/all_to_all | solution.py:103
  96.8 3.5 %all-to-all-start.1 = ((f32[16,6,4,128]{3,2,1,0:T(4,128)}), f32[16,6,4,128]{3,2,1,0:T(4,128)S(1)}, u32[]{:S(2)}, u32[]{:S(2)}) async-start(f32[16,6,4,128]{3,2,1,0:T(4,128)} %select_add_fusion.7), calls=%async_computation.1 | async-start | bytes 393216 | tf_op jit(solution)/shard_map/while/body/eval_jaxpr/all_to_all | solution.py:103
  100.6 4.5 %multiply_reduce_fusion.17 = f32[24,4,128]{2,1,0:T(4,128)S(1)} fusion(f32[24,4,128,128]{3,2,1,0:T(8,128)} %get-tuple-element.428, f32[24,4,128]{2,1,0:T(4,128)S(1)} %get-tuple-element.399), kind=kLoop, calls=%fused_computation.8.clone.1 | loop fusion | flops 3133440 | bytes 6389760 | tf_op jit(solution)/shard_map/while/body/eval_jaxpr/reduce_sum | solution.py:16
  111.6 3.6 %all-to-all-start = ((f32[16,6,4,128]{3,2,1,0:T(4,128)}), f32[16,6,4,128]{3,2,1,0:T(4,128)S(1)}, u32[]{:S(2)}, u32[]{:S(2)}) async-start(f32[16,6,4,128]{3,2,1,0:T(4,128)} %bitcast.185), calls=%async_computation | async-start | bytes 393216 | tf_op jit(solution)/shard_map/while/body/eval_jaxpr/all_to_all | solution.py:103
  115.4 7.9 %all-to-all-done = f32[16,6,4,128]{3,2,1,0:T(4,128)S(1)} async-done(((f32[16,6,4,128]{3,2,1,0:T(4,128)}), f32[16,6,4,128]{3,2,1,0:T(4,128)S(1)}, u32[]{:S(2)}, u32[]{:S(2)}) %all-to-all-start) | async-done | bytes 196640 | tf_op jit(solution)/shard_map/while/body/eval_jaxpr/all_to_all | solution.py:103
  129.0 4.5 %multiply_reduce_fusion.17 = f32[24,4,128]{2,1,0:T(4,128)S(1)} fusion(f32[24,4,128,128]{3,2,1,0:T(8,128)} %get-tuple-element.428, f32[24,4,128]{2,1,0:T(4,128)S(1)} %get-tuple-element.399), kind=kLoop, calls=%fused_computation.8.clone.1 | loop fusion | flops 3133440 | bytes 6389760 | tf_op jit(solution)/shard_map/while/body/eval_jaxpr/reduce_sum | solution.py:16
  140.1 3.6 %all-to-all-start = ((f32[16,6,4,128]{3,2,1,0:T(4,128)}), f32[16,6,4,128]{3,2,1,0:T(4,128)S(1)}, u32[]{:S(2)}, u32[]{:S(2)}) async-start(f32[16,6,4,128]{3,2,1,0:T(4,128)} %bitcast.185), calls=%async_computation | async-start | bytes 393216 | tf_op jit(solution)/shard_map/while/body/eval_jaxpr/all_to_all | solution.py:103
  143.9 7.9 %all-to-all-done = f32[16,6,4,128]{3,2,1,0:T(4,128)S(1)} async-done(((f32[16,6,4,128]{3,2,1,0:T(4,128)}), f32[16,6,4,128]{3,2,1,0:T(4,128)S(1)}, u32[]{:S(2)}, u32[]{:S(2)}) %all-to-all-start) | async-done | bytes 196640 | tf_op jit(solution)/shard_map/while/body/eval_jaxpr/all_to_all | solution.py:103
  157.4 4.5 %multiply_reduce_fusion.17 = f32[24,4,128]{2,1,0:T(4,128)S(1)} fusion(f32[24,4,128,128]{3,2,1,0:T(8,128)} %get-tuple-element.428, f32[24,4,128]{2,1,0:T(4,128)S(1)} %get-tuple-element.399), kind=kLoop, calls=%fused_computation.8.clone.1 | loop fusion | flops 3133440 | bytes 6389760 | tf_op jit(solution)/shard_map/while/body/eval_jaxpr/reduce_sum | solution.py:16
  168.5 3.6 %all-to-all-start = ((f32[16,6,4,128]{3,2,1,0:T(4,128)}), f32[16,6,4,128]{3,2,1,0:T(4,128)S(1)}, u32[]{:S(2)}, u32[]{:S(2)}) async-start(f32[16,6,4,128]{3,2,1,0:T(4,128)} %bitcast.185), calls=%async_computation | async-start | bytes 393216 | tf_op jit(solution)/shard_map/while/body/eval_jaxpr/all_to_all | solution.py:103
  172.3 7.9 %all-to-all-done = f32[16,6,4,128]{3,2,1,0:T(4,128)S(1)} async-done(((f32[16,6,4,128]{3,2,1,0:T(4,128)}), f32[16,6,4,128]{3,2,1,0:T(4,128)S(1)}, u32[]{:S(2)}, u32[]{:S(2)}) %all-to-all-start) | async-done | bytes 196640 | tf_op jit(solution)/shard_map/while/body/eval_jaxpr/all_to_all | solution.py:103
  185.9 4.5 %multiply_reduce_fusion.17 = f32[24,4,128]{2,1,0:T(4,128)S(1)} fusion(f32[24,4,128,128]{3,2,1,0:T(8,128)} %get-tuple-element.428, f32[24,4,128]{2,1,0:T(4,128)S(1)} %get-tuple-element.399), kind=kLoop, calls=%fused_computation.8.clone.1 | loop fusion | flops 3133440 | bytes 6389760 | tf_op jit(solution)/shard_map/while/body/eval_jaxpr/reduce_sum | solution.py:16
  196.9 3.6 %all-to-all-start = ((f32[16,6,4,128]{3,2,1,0:T(4,128)}), f32[16,6,4,128]{3,2,1,0:T(4,128)S(1)}, u32[]{:S(2)}, u32[]{:S(2)}) async-start(f32[16,6,4,128]{3,2,1,0:T(4,128)} %bitcast.185), calls=%async_computation | async-start | bytes 393216 | tf_op jit(solution)/shard_map/while/body/eval_jaxpr/all_to_all | solution.py:103
  200.7 8.0 %all-to-all-done = f32[16,6,4,128]{3,2,1,0:T(4,128)S(1)} async-done(((f32[16,6,4,128]{3,2,1,0:T(4,128)}), f32[16,6,4,128]{3,2,1,0:T(4,128)S(1)}, u32[]{:S(2)}, u32[]{:S(2)}) %all-to-all-start) | async-done | bytes 196640 | tf_op jit(solution)/shard_map/while/body/eval_jaxpr/all_to_all | solution.py:103
  210.6 3.5 %all-to-all-start.1 = ((f32[16,6,4,128]{3,2,1,0:T(4,128)}), f32[16,6,4,128]{3,2,1,0:T(4,128)S(1)}, u32[]{:S(2)}, u32[]{:S(2)}) async-start(f32[16,6,4,128]{3,2,1,0:T(4,128)} %select_add_fusion.7), calls=%async_computation.1 | async-start | bytes 393216 | tf_op jit(solution)/shard_map/while/body/eval_jaxpr/all_to_all | solution.py:103
  214.4 4.5 %multiply_reduce_fusion.17 = f32[24,4,128]{2,1,0:T(4,128)S(1)} fusion(f32[24,4,128,128]{3,2,1,0:T(8,128)} %get-tuple-element.428, f32[24,4,128]{2,1,0:T(4,128)S(1)} %get-tuple-element.399), kind=kLoop, calls=%fused_computation.8.clone.1 | loop fusion | flops 3133440 | bytes 6389760 | tf_op jit(solution)/shard_map/while/body/eval_jaxpr/reduce_sum | solution.py:16
  218.9 3.6 %all-to-all-done.1 = f32[16,6,4,128]{3,2,1,0:T(4,128)S(1)} async-done(((f32[16,6,4,128]{3,2,1,0:T(4,128)}), f32[16,6,4,128]{3,2,1,0:T(4,128)S(1)}, u32[]{:S(2)}, u32[]{:S(2)}) %all-to-all-start.1) | async-done | bytes 196640 | tf_op jit(solution)/shard_map/while/body/eval_jaxpr/all_to_all | solution.py:103
  225.9 13.1 %all_to_all.32 = f32[16,6,8,128]{3,2,1,0:T(8,128)S(1)} all-to-all(f32[16,6,8,128]{3,2,1,0:T(8,128)S(1)} %bitcast.198), channel_id=1, replica_groups=mesh['req'=16,'head'=2] {'req'}, dimensions={0} | all-to-all | bytes 786432 | tf_op jit(solution)/shard_map/all_to_all | solution.py:103
  243.2 3.6 %all-to-all-start.5 = ((f32[16,6,12,128]{3,2,1,0:T(8,128)}), f32[16,6,12,128]{3,2,1,0:T(8,128)S(1)}, u32[]{:S(2)}, u32[]{:S(2)}) async-start(f32[16,6,12,128]{3,2,1,0:T(8,128)} %pad_maximum_fusion), calls=%async_computation.5 | async-start | bytes 1572864 | tf_op jit(solution)/shard_map/all_to_all | solution.py:103
  246.9 7.9 %multiply_reduce_fusion.4 = (f32[24,4,128]{2,1,0:T(4,128)S(1)}, f32[24,4,128]{2,1,0:T(4,128)S(1)}, f32[24,4,128]{2,1,0:T(4,128)S(1)}) fusion(f32[24,4,128,128]{3,2,1,0:T(8,128)} %param.26, f32[24,4,128]{2,1,0:T(4,128)S(1)} %get-tuple-element.94, f32[24,4,128]{2,1,0:T(4,128)S(1)} %get-tuple-element.95, f32[24,4,128,128]{3,2,1,0:T(8,128)} %get-tuple-element.434), kind=kLoop, calls=%fused_computation.30 | loop fusion | flops 9400320 | bytes 12828672 | tf_op jit(solution)/shard_map/reduce_sum | solution.py:16
  254.8 5.3 %all-to-all-done.5 = f32[16,6,12,128]{3,2,1,0:T(8,128)S(1)} async-done(((f32[16,6,12,128]{3,2,1,0:T(8,128)}), f32[16,6,12,128]{3,2,1,0:T(8,128)S(1)}, u32[]{:S(2)}, u32[]{:S(2)}) %all-to-all-start.5) | async-done | bytes 589856 | tf_op jit(solution)/shard_map/all_to_all | solution.py:103
  (263 shorter events, 89.6 us)
Async XLA Ops:
  0.0 262.0 %copy-start = (bf16[4,128,1024]{2,1,0:T(8,128)(2,1)S(1)}, bf16[4,128,1024]{2,1,0:T(8,128)(2,1)}, u32[]{:S(2)}) copy-start(bf16[4,128,1024]{2,1,0:T(8,128)(2,1)} %param.31) | copy-start | bytes 3145732
  0.0 13.3 %copy-start.6 = (f32[1024]{0:T(1024)S(1)}, f32[1024]{0:T(1024)}, u32[]{:S(2)}) copy-start(f32[1024]{0:T(1024)} %param.18) | copy-start | bytes 12292
  6.2 12.2 %copy-start.5 = (bf16[1024,2,4]{0,2,1:T(4,128)(2,1)S(1)}, bf16[1024,2,4]{0,2,1:T(4,128)(2,1)}, u32[]{:S(2)}) copy-start(bf16[1024,2,4]{0,2,1:T(4,128)(2,1)} %param.22) | copy-start | bytes 49156
  7.3 31.2 %copy-start.1 = (f32[2,4,128,128]{3,2,1,0:T(8,128)S(1)}, f32[2,4,128,128]{3,2,1,0:T(8,128)}, u32[]{:S(2)}) copy-start(f32[2,4,128,128]{3,2,1,0:T(8,128)} %param.27) | copy-start | bytes 1572868
  18.4 19.9 %all-to-all-start.2 = ((f32[16,6,5,128]{3,1,2,0:T(8,128)}), f32[16,6,5,128]{3,1,2,0:T(8,128)S(1)}, u32[]{:S(2)}, u32[]{:S(2)}) async-start(f32[16,6,5,128]{3,1,2,0:T(8,128)} %copy.161), calls=%async_computation.2 | async-start | bytes 655360 | tf_op jit(solution)/shard_map/all_to_all | solution.py:103
  27.0 25.8 %copy-start.4 = (f32[24,4]{0,1:T(4,128)S(1)}, f32[24,4]{0,1:T(4,128)}, u32[]{:S(2)}) copy-start(f32[24,4]{0,1:T(4,128)} %param.23) | copy-start | bytes 1156
  27.0 25.8 %copy-start.7 = (f32[4]{0:T(128)S(1)}, f32[4]{0:T(128)}, u32[]{:S(2)}) copy-start(f32[4]{0:T(128)} %param.24) | copy-start | bytes 52
  40.6 11.6 %all-to-all-start.3 = ((f32[16,6,4,128]{3,2,1,0:T(4,128)}), f32[16,6,4,128]{3,2,1,0:T(4,128)S(1)}, u32[]{:S(2)}, u32[]{:S(2)}) async-start(f32[16,6,4,128]{3,2,1,0:T(4,128)} %select_add_fusion.4), calls=%async_computation.3 | async-start | bytes 393216 | tf_op jit(solution)/shard_map/all_to_all | solution.py:103
  54.9 11.6 %all-to-all-start = ((f32[16,6,4,128]{3,2,1,0:T(4,128)}), f32[16,6,4,128]{3,2,1,0:T(4,128)S(1)}, u32[]{:S(2)}, u32[]{:S(2)}) async-start(f32[16,6,4,128]{3,2,1,0:T(4,128)} %bitcast.185), calls=%async_computation | async-start | bytes 393216 | tf_op jit(solution)/shard_map/while/body/eval_jaxpr/all_to_all | solution.py:103
  68.3 11.6 %all-to-all-start.1 = ((f32[16,6,4,128]{3,2,1,0:T(4,128)}), f32[16,6,4,128]{3,2,1,0:T(4,128)S(1)}, u32[]{:S(2)}, u32[]{:S(2)}) async-start(f32[16,6,4,128]{3,2,1,0:T(4,128)} %select_add_fusion.7), calls=%async_computation.1 | async-start | bytes 393216 | tf_op jit(solution)/shard_map/while/body/eval_jaxpr/all_to_all | solution.py:103
  83.2 11.7 %all-to-all-start = ((f32[16,6,4,128]{3,2,1,0:T(4,128)}), f32[16,6,4,128]{3,2,1,0:T(4,128)S(1)}, u32[]{:S(2)}, u32[]{:S(2)}) async-start(f32[16,6,4,128]{3,2,1,0:T(4,128)} %bitcast.185), calls=%async_computation | async-start | bytes 393216 | tf_op jit(solution)/shard_map/while/body/eval_jaxpr/all_to_all | solution.py:103
  96.8 11.6 %all-to-all-start.1 = ((f32[16,6,4,128]{3,2,1,0:T(4,128)}), f32[16,6,4,128]{3,2,1,0:T(4,128)S(1)}, u32[]{:S(2)}, u32[]{:S(2)}) async-start(f32[16,6,4,128]{3,2,1,0:T(4,128)} %select_add_fusion.7), calls=%async_computation.1 | async-start | bytes 393216 | tf_op jit(solution)/shard_map/while/body/eval_jaxpr/all_to_all | solution.py:103
  111.6 11.7 %all-to-all-start = ((f32[16,6,4,128]{3,2,1,0:T(4,128)}), f32[16,6,4,128]{3,2,1,0:T(4,128)S(1)}, u32[]{:S(2)}, u32[]{:S(2)}) async-start(f32[16,6,4,128]{3,2,1,0:T(4,128)} %bitcast.185), calls=%async_computation | async-start | bytes 393216 | tf_op jit(solution)/shard_map/while/body/eval_jaxpr/all_to_all | solution.py:103
  125.2 11.6 %all-to-all-start.1 = ((f32[16,6,4,128]{3,2,1,0:T(4,128)}), f32[16,6,4,128]{3,2,1,0:T(4,128)S(1)}, u32[]{:S(2)}, u32[]{:S(2)}) async-start(f32[16,6,4,128]{3,2,1,0:T(4,128)} %select_add_fusion.7), calls=%async_computation.1 | async-start | bytes 393216 | tf_op jit(solution)/shard_map/while/body/eval_jaxpr/all_to_all | solution.py:103
  140.1 11.7 %all-to-all-start = ((f32[16,6,4,128]{3,2,1,0:T(4,128)}), f32[16,6,4,128]{3,2,1,0:T(4,128)S(1)}, u32[]{:S(2)}, u32[]{:S(2)}) async-start(f32[16,6,4,128]{3,2,1,0:T(4,128)} %bitcast.185), calls=%async_computation | async-start | bytes 393216 | tf_op jit(solution)/shard_map/while/body/eval_jaxpr/all_to_all | solution.py:103
  153.6 11.6 %all-to-all-start.1 = ((f32[16,6,4,128]{3,2,1,0:T(4,128)}), f32[16,6,4,128]{3,2,1,0:T(4,128)S(1)}, u32[]{:S(2)}, u32[]{:S(2)}) async-start(f32[16,6,4,128]{3,2,1,0:T(4,128)} %select_add_fusion.7), calls=%async_computation.1 | async-start | bytes 393216 | tf_op jit(solution)/shard_map/while/body/eval_jaxpr/all_to_all | solution.py:103
  168.5 11.7 %all-to-all-start = ((f32[16,6,4,128]{3,2,1,0:T(4,128)}), f32[16,6,4,128]{3,2,1,0:T(4,128)S(1)}, u32[]{:S(2)}, u32[]{:S(2)}) async-start(f32[16,6,4,128]{3,2,1,0:T(4,128)} %bitcast.185), calls=%async_computation | async-start | bytes 393216 | tf_op jit(solution)/shard_map/while/body/eval_jaxpr/all_to_all | solution.py:103
  182.1 11.6 %all-to-all-start.1 = ((f32[16,6,4,128]{3,2,1,0:T(4,128)}), f32[16,6,4,128]{3,2,1,0:T(4,128)S(1)}, u32[]{:S(2)}, u32[]{:S(2)}) async-start(f32[16,6,4,128]{3,2,1,0:T(4,128)} %select_add_fusion.7), calls=%async_computation.1 | async-start | bytes 393216 | tf_op jit(solution)/shard_map/while/body/eval_jaxpr/all_to_all | solution.py:103
  196.9 11.8 %all-to-all-start = ((f32[16,6,4,128]{3,2,1,0:T(4,128)}), f32[16,6,4,128]{3,2,1,0:T(4,128)S(1)}, u32[]{:S(2)}, u32[]{:S(2)}) async-start(f32[16,6,4,128]{3,2,1,0:T(4,128)} %bitcast.185), calls=%async_computation | async-start | bytes 393216 | tf_op jit(solution)/shard_map/while/body/eval_jaxpr/all_to_all | solution.py:103
  210.6 11.9 %all-to-all-start.1 = ((f32[16,6,4,128]{3,2,1,0:T(4,128)}), f32[16,6,4,128]{3,2,1,0:T(4,128)S(1)}, u32[]{:S(2)}, u32[]{:S(2)}) async-start(f32[16,6,4,128]{3,2,1,0:T(4,128)} %select_add_fusion.7), calls=%async_computation.1 | async-start | bytes 393216 | tf_op jit(solution)/shard_map/while/body/eval_jaxpr/all_to_all | solution.py:103
  224.3 15.7 %copy-start.2 = (f32[2,4,128,128]{3,2,1,0:T(8,128)S(1)}, f32[2,4,128,128]{3,2,1,0:T(8,128)}, u32[]{:S(2)}) copy-start(f32[2,4,128,128]{3,2,1,0:T(8,128)} %param.28) | copy-start | bytes 1572868
  243.2 16.8 %all-to-all-start.5 = ((f32[16,6,12,128]{3,2,1,0:T(8,128)}), f32[16,6,12,128]{3,2,1,0:T(8,128)S(1)}, u32[]{:S(2)}, u32[]{:S(2)}) async-start(f32[16,6,12,128]{3,2,1,0:T(8,128)} %pad_maximum_fusion), calls=%async_computation.5 | async-start | bytes 1572864 | tf_op jit(solution)/shard_map/all_to_all | solution.py:103
  246.8 16.8 %copy-start.3 = (bf16[24,512]{1,0:T(8,128)(2,1)S(1)}, bf16[24,512]{1,0:T(8,128)(2,1)}, u32[]{:S(2)}) copy-start(bf16[24,512]{1,0:T(8,128)(2,1)} %param.17) | copy-start | bytes 73732
  262.3 1.3 collective-permute-start

commit v9 on v8

--- a/solution.py
+++ b/solution.py
@@ -114,41 +114,55 @@
             total = total + jnp.where(chosen[group][:, None, None], products[group], 0.0)
         return total
 
-    def cg_step(arrived, carry):
-        solution, residual, direction, norm_now = carry
-        shares = unpack(exchange(owner_apply(prompt_keys, arrived, chosen)))
-        shared = weight_col * shares + own_matvec(own_keys, direction)
+    filled_col = filled[:, None, None]
+    queries_s = pack(queries)
+    key_s = pack(key_now)
+    decay_s = pack(decay_col)
+    write_s = pack(write_col)
+    weight_s = pack(weight_col)
+
+    def own_in_slots(states, vectors):
+        return pack(own_matvec(states, jnp.take(vectors, slot_of, axis=0, mode="clip")))
+
+    def requester_step(shares, own, solution, residual, direction, norm_now):
         product = (
-            decay_col * shared
-            + write_col * key_now * jnp.sum(key_now * direction, axis=2, keepdims=True)
+            decay_s * (weight_s * shares + own)
+            + write_s * key_s * jnp.sum(key_s * direction, axis=2, keepdims=True)
             + ridge_col * direction
         )
-        step_size = norm_now / jnp.sum(direction * product, axis=2, keepdims=True)
+        curve = jnp.sum(direction * product, axis=2, keepdims=True)
+        step_size = jnp.where(filled_col, norm_now / jnp.where(filled_col, curve, 1.0), 0.0)
         solution = solution + step_size * direction
         residual = residual - step_size * product
         norm_next = jnp.sum(residual * residual, axis=2, keepdims=True)
-        direction = residual + norm_next / norm_now * direction
+        ratio = jnp.where(filled_col, norm_next / jnp.where(filled_col, norm_now, 1.0), 0.0)
+        direction = residual + ratio * direction
         return solution, residual, direction, norm_next
 
     label_row = jnp.broadcast_to(
         slot_label.astype(jnp.float32)[:, None, None], (slot_count, 1, head_size)
     )
-    first = exchange(jnp.concatenate([pack(queries), label_row], axis=1))
+    first = exchange(jnp.concatenate([queries_s, label_row], axis=1))
+    own_first = own_in_slots(own_keys, queries_s)
     labels_in = first[:, head_count, 0]
     chosen = [labels_in == float(group + 1) for group in range(group_count)]
-    carry = (
-        jnp.zeros_like(queries),
-        queries,
-        queries,
-        jnp.sum(queries * queries, axis=2, keepdims=True),
-    )
-    carry = cg_step(first[:, :head_count], carry)
-    carry = lax.fori_loop(
-        1, ITERS - 1, lambda _, state: cg_step(exchange(pack(state[2])), state), carry
-    )
-    solution, residual, direction, norm_now = carry
-
-    both = exchange(jnp.concatenate([pack(direction), pack(solution)], axis=1))
+    shares = exchange(owner_apply(prompt_keys, first[:, :head_count], chosen))
+    norm_first = jnp.sum(queries_s * queries_s, axis=2, keepdims=True)
+    carry = requester_step(
+        shares, own_first, jnp.zeros_like(queries_s), queries_s, queries_s, norm_first
+    )
+
+    def middle_step(_, carry):
+        solution, residual, direction, norm_now = carry
+        arrived = exchange(direction)
+        own = own_in_slots(own_keys, direction)
+        shares = exchange(owner_apply(prompt_keys, arrived, chosen))
+        return requester_step(shares, own, solution, residual, direction, norm_now)
+
+    solution, residual, direction, norm_now = lax.fori_loop(1, ITERS - 1, middle_step, carry)
+
+    both = exchange(jnp.concatenate([direction, solution], axis=1))
+    own = own_in_slots(own_keys, direction)
     held = both[:, :head_count]
     owner_out = jnp.concatenate(
         [
@@ -158,21 +172,22 @@
         ],
         axis=1,
     )
-    returned = unpack(exchange(owner_out))
-    own_out_partial = own_matvec(own_values, solution)
-    own_out_direction = own_matvec(own_values, direction)
-    partial = solution
+    returned = exchange(owner_out)
+    own_out_partial = own_matvec(own_values, unpack(solution))
+    own_out_direction = own_matvec(own_values, unpack(direction))
     shares = returned[:, :head_count]
-    shared = weight_col * shares + own_matvec(own_keys, direction)
     product = (
-        decay_col * shared
-        + write_col * key_now * jnp.sum(key_now * direction, axis=2, keepdims=True)
+        decay_s * (weight_s * shares + own)
+        + write_s * key_s * jnp.sum(key_s * direction, axis=2, keepdims=True)
         + ridge_col * direction
     )
-    step_last = norm_now / jnp.sum(direction * product, axis=2, keepdims=True)
-    solution = partial + step_last * direction
-    value_sum = returned[:, head_count : 2 * head_count] + step_last * returned[:, 2 * head_count :]
-    own_out = own_out_partial + step_last * own_out_direction
+    curve = jnp.sum(direction * product, axis=2, keepdims=True)
+    step_last = jnp.where(filled_col, norm_now / jnp.where(filled_col, curve, 1.0), 0.0)
+    solution = unpack(solution + step_last * direction)
+    value_sum = unpack(
+        returned[:, head_count : 2 * head_count] + step_last * returned[:, 2 * head_count :]
+    )
+    own_out = own_out_partial + unpack(step_last) * own_out_direction
     shared_out = weight_col * value_sum + own_out
     readout = decay_col * shared_out + write_col * value_now * jnp.sum(
         key_now * solution, axis=2, keepdims=True

time: 266 us -> 318 us (1.20)
  other arithmetic: 59.2 us -> 102 us
  waiting for transfers between devices: 88.6 us -> 63.9 us
  starting transfers between devices: 58.1 us -> 75.4 us
  local copies, waits for them, and re-layouts: 32 us -> 43.1 us
    all_to_all x15, waiting for transfers between devices: 87.4 us -> 62.7 us  [exchange(): lax.all_to_all(shaped, 'req', split_axis=0, concat_axis=0, tiled=True)]
    all_to_all x15, starting transfers between devices: 58 us -> 75.4 us  [exchange(): lax.all_to_all(shaped, 'req', split_axis=0, concat_axis=0, tiled=True)]
    mul x21 -> x25, other arithmetic: 3.68 us -> 20.6 us  [the longest x6 15.2 us: requester_step(): write_s * key_s * jnp.sum(key_s * direction, axis=2, keepdims=True)]
    add x8, other arithmetic: 2.06 us -> 16.2 us  [the longest x7 15.1 us: requester_step(): direction = residual + ratio * direction]
    gather x0 -> x8, local copies, waits for them, and re-layouts: none -> 11.3 us  [own_in_slots(): jnp.take(vectors, slot_of, axis=0, mode='clip')]
    reduce_sum x8 -> x10, other arithmetic: 1.52 us -> 6.2 us  [the longest x7 3.72 us: requester_step(): norm_next = jnp.sum(residual * residual, axis=2, keepdims=True)]
    reduce_sum x8 -> x9, other arithmetic: 39.3 us -> 42.1 us  [own_matvec(): return jnp.sum(matrices * vectors[:, :, None, :], axis=3)]
    gather x9 -> x13, local copies, waits for them, and re-layouts: 10.3 us -> 9.41 us  [pack(): return jnp.take(padded, source, axis=0, mode='clip')]
  transfers between devices with their start and end apart: 16 -> 16, of which waited for: 16 -> 15; matrix products, arithmetic and copies ran while one was open for 16% -> 21% of each run, Pallas kernels for 0% -> 0%
where the time goes in v9:
time: 318 us; the launch traced here: 315 us
  other arithmetic  102 us (32%)
  starting transfers between devices  75.4 us (24%)
  waiting for transfers between devices  63.9 us (20%)
  local copies, waits for them, and re-layouts  43.1 us (14%)
  blocking collectives  17.7 us (6%)
  matrix products  11.6 us (4%)
    all_to_all x15, starting transfers between devices, exchange(): lax.all_to_all(shaped, 'req', split_axis=0, concat_axis=0, tiled=True)  75.4 us
    all_to_all x15, waiting for transfers between devices, exchange(): lax.all_to_all(shaped, 'req', split_axis=0, concat_axis=0, tiled=True)  62.7 us
    reduce_sum x9, other arithmetic, own_matvec(): return jnp.sum(matrices * vectors[:, :, None, :], axis=3)  42.1 us
    all_to_all x1, blocking collectives, exchange(): lax.all_to_all(shaped, 'req', split_axis=0, concat_axis=0, tiled=True)  15.4 us
    mul x6, other arithmetic, requester_step(): write_s * key_s * jnp.sum(key_s * direction, axis=2, keepdims=True)  15.2 us
    add x7, other arithmetic, requester_step(): direction = residual + ratio * direction  15.1 us
    gather x8, local copies, waits for them, and re-layouts, own_in_slots(): jnp.take(vectors, slot_of, axis=0, mode='clip')  11.3 us
    gather x13, local copies, waits for them, and re-layouts, pack(): return jnp.take(padded, source, axis=0, mode='clip')  9.41 us
  transfers between devices with their start and end apart: 16, of which 15 were waited for; matrix products, arithmetic and copies ran while one was open for 21% of the time, Pallas kernels for 0%

profile of v9, /device:TPU:0, one launch (start us, length us, event | category | flops | bytes accessed | tf_op | source)
XLA Modules:
  0.0 315.4 jit_solution(8102512388931788648)
XLA Ops:
  7.2 6.0 %copy.173 = bf16[1024,4,3,128]{0,3,2,1:T(8,128)(2,1)} copy(bf16[1024,4,3,128]{3,1,2,0:T(4,128)(2,1)} %param.19) | data formatting | bytes 6291456 | tf_op args[2]
  22.5 8.2 %all-to-all-start.2 = ((f32[16,6,5,128]{3,1,2,0:T(8,128)}), f32[16,6,5,128]{3,1,2,0:T(8,128)S(1)}, u32[]{:S(2)}, u32[]{:S(2)}) async-start(f32[16,6,5,128]{3,1,2,0:T(8,128)} %copy.182), calls=%async_computation.2 | async-start | bytes 655360 | tf_op jit(solution)/shard_map/all_to_all | solution.py:103
  30.7 4.5 %multiply_reduce_fusion.7 = f32[24,4,128]{2,1,0:T(4,128)S(1)} fusion(f32[24,4,128,128]{3,2,1,0:T(8,128)} %param.25, f32[24,4,128]{2,1,0:T(4,128)S(1)} %gather_fusion.5), kind=kLoop, calls=%fused_computation.45 | loop fusion | flops 3133440 | bytes 6389760 | tf_op jit(solution)/shard_map/reduce_sum | solution.py:16
  36.9 5.4 %all-to-all-done.2 = f32[16,6,5,128]{3,1,2,0:T(8,128)S(1)} async-done(((f32[16,6,5,128]{3,1,2,0:T(8,128)}), f32[16,6,5,128]{3,1,2,0:T(8,128)S(1)}, u32[]{:S(2)}, u32[]{:S(2)}) %all-to-all-start.2) | async-done | bytes 245792 | tf_op jit(solution)/shard_map/all_to_all | solution.py:103
  46.3 3.7 %all-to-all-start.3 = ((f32[16,6,4,128]{3,2,1,0:T(4,128)}), f32[16,6,4,128]{3,2,1,0:T(4,128)S(1)}, u32[]{:S(2)}, u32[]{:S(2)}) async-start(f32[16,6,4,128]{3,2,1,0:T(4,128)} %select_add_fusion.4), calls=%async_computation.3 | async-start | bytes 393216 | tf_op jit(solution)/shard_map/all_to_all | solution.py:103
  64.3 198.5 %while.16 = (s32[]{:T(128)}, f32[96,4,128]{2,1,0:T(4,128)S(1)}, f32[96,4,128]{2,1,0:T(4,128)S(1)}, f32[96,4,128]{2,1,0:T(4,128)}, f32[96,4,1]{1,0,2:T(8,128)S(1)...) while((s32[]{:T(128)}, f32[96,4,128]{2,1,0:T(4,128)S(1)}, ...), condition=%wide.region_17.18_spmd, body=%wide.region_12.17_spmd.sunk | while | flops 155213824 | bytes 14422045 | solution.py:162
  64.3 4.8 %all-to-all-start = ((f32[16,6,4,128]{3,2,1,0:T(4,128)}), f32[16,6,4,128]{3,2,1,0:T(4,128)S(1)}, u32[]{:S(2)}, u32[]{:S(2)}) async-start(f32[16,6,4,128]{3,2,1,0:T(4,128)} %bitcast.220), calls=%async_computation | async-start | bytes 393216 | tf_op jit(solution)/shard_map/while/body/eval_jaxpr/all_to_all | solution.py:103
  69.4 7.9 %all-to-all-done = f32[16,6,4,128]{3,2,1,0:T(4,128)S(1)} async-done(((f32[16,6,4,128]{3,2,1,0:T(4,128)}), f32[16,6,4,128]{3,2,1,0:T(4,128)S(1)}, u32[]{:S(2)}, u32[]{:S(2)}) %all-to-all-start) | async-done | bytes 196640 | tf_op jit(solution)/shard_map/while/body/eval_jaxpr/all_to_all | solution.py:103
  79.2 3.5 %all-to-all-start.1 = ((f32[16,6,4,128]{3,2,1,0:T(4,128)}), f32[16,6,4,128]{3,2,1,0:T(4,128)S(1)}, u32[]{:S(2)}, u32[]{:S(2)}) async-start(f32[16,6,4,128]{3,2,1,0:T(4,128)} %select_add_fusion.7), calls=%async_computation.1 | async-start | bytes 393216 | tf_op jit(solution)/shard_map/while/body/eval_jaxpr/all_to_all | solution.py:103
  84.3 4.5 %multiply_reduce_fusion.19 = f32[24,4,128]{2,1,0:T(4,128)S(1)} fusion(f32[24,4,128,128]{3,2,1,0:T(8,128)} %get-tuple-element.441, f32[24,4,128]{2,1,0:T(4,128)S(1)} %gather_fusion), kind=kLoop, calls=%fused_computation.16.clone.1 | loop fusion | flops 3133440 | bytes 6389760 | tf_op jit(solution)/shard_map/while/body/eval_jaxpr/reduce_sum | solution.py:16
  96.4 5.7 %all-to-all-start = ((f32[16,6,4,128]{3,2,1,0:T(4,128)}), f32[16,6,4,128]{3,2,1,0:T(4,128)S(1)}, u32[]{:S(2)}, u32[]{:S(2)}) async-start(f32[16,6,4,128]{3,2,1,0:T(4,128)} %bitcast.220), calls=%async_computation | async-start | bytes 393216 | tf_op jit(solution)/shard_map/while/body/eval_jaxpr/all_to_all | solution.py:103
  102.4 7.9 %all-to-all-done = f32[16,6,4,128]{3,2,1,0:T(4,128)S(1)} async-done(((f32[16,6,4,128]{3,2,1,0:T(4,128)}), f32[16,6,4,128]{3,2,1,0:T(4,128)S(1)}, u32[]{:S(2)}, u32[]{:S(2)}) %all-to-all-start) | async-done | bytes 196640 | tf_op jit(solution)/shard_map/while/body/eval_jaxpr/all_to_all | solution.py:103
  112.2 3.5 %all-to-all-start.1 = ((f32[16,6,4,128]{3,2,1,0:T(4,128)}), f32[16,6,4,128]{3,2,1,0:T(4,128)S(1)}, u32[]{:S(2)}, u32[]{:S(2)}) async-start(f32[16,6,4,128]{3,2,1,0:T(4,128)} %select_add_fusion.7), calls=%async_computation.1 | async-start | bytes 393216 | tf_op jit(solution)/shard_map/while/body/eval_jaxpr/all_to_all | solution.py:103
  117.3 4.5 %multiply_reduce_fusion.19 = f32[24,4,128]{2,1,0:T(4,128)S(1)} fusion(f32[24,4,128,128]{3,2,1,0:T(8,128)} %get-tuple-element.441, f32[24,4,128]{2,1,0:T(4,128)S(1)} %gather_fusion), kind=kLoop, calls=%fused_computation.16.clone.1 | loop fusion | flops 3133440 | bytes 6389760 | tf_op jit(solution)/shard_map/while/body/eval_jaxpr/reduce_sum | solution.py:16
  129.4 5.7 %all-to-all-start = ((f32[16,6,4,128]{3,2,1,0:T(4,128)}), f32[16,6,4,128]{3,2,1,0:T(4,128)S(1)}, u32[]{:S(2)}, u32[]{:S(2)}) async-start(f32[16,6,4,128]{3,2,1,0:T(4,128)} %bitcast.220), calls=%async_computation | async-start | bytes 393216 | tf_op jit(solution)/shard_map/while/body/eval_jaxpr/all_to_all | solution.py:103
  135.4 7.9 %all-to-all-done = f32[16,6,4,128]{3,2,1,0:T(4,128)S(1)} async-done(((f32[16,6,4,128]{3,2,1,0:T(4,128)}), f32[16,6,4,128]{3,2,1,0:T(4,128)S(1)}, u32[]{:S(2)}, u32[]{:S(2)}) %all-to-all-start) | async-done | bytes 196640 | tf_op jit(solution)/shard_map/while/body/eval_jaxpr/all_to_all | solution.py:103
  145.2 3.5 %all-to-all-start.1 = ((f32[16,6,4,128]{3,2,1,0:T(4,128)}), f32[16,6,4,128]{3,2,1,0:T(4,128)S(1)}, u32[]{:S(2)}, u32[]{:S(2)}) async-start(f32[16,6,4,128]{3,2,1,0:T(4,128)} %select_add_fusion.7), calls=%async_computation.1 | async-start | bytes 393216 | tf_op jit(solution)/shard_map/while/body/eval_jaxpr/all_to_all | solution.py:103
  150.2 4.5 %multiply_reduce_fusion.19 = f32[24,4,128]{2,1,0:T(4,128)S(1)} fusion(f32[24,4,128,128]{3,2,1,0:T(8,128)} %get-tuple-element.441, f32[24,4,128]{2,1,0:T(4,128)S(1)} %gather_fusion), kind=kLoop, calls=%fused_computation.16.clone.1 | loop fusion | flops 3133440 | bytes 6389760 | tf_op jit(solution)/shard_map/while/body/eval_jaxpr/reduce_sum | solution.py:16
  162.4 5.7 %all-to-all-start = ((f32[16,6,4,128]{3,2,1,0:T(4,128)}), f32[16,6,4,128]{3,2,1,0:T(4,128)S(1)}, u32[]{:S(2)}, u32[]{:S(2)}) async-start(f32[16,6,4,128]{3,2,1,0:T(4,128)} %bitcast.220), calls=%async_computation | async-start | bytes 393216 | tf_op jit(solution)/shard_map/while/body/eval_jaxpr/all_to_all | solution.py:103
  168.3 7.9 %all-to-all-done = f32[16,6,4,128]{3,2,1,0:T(4,128)S(1)} async-done(((f32[16,6,4,128]{3,2,1,0:T(4,128)}), f32[16,6,4,128]{3,2,1,0:T(4,128)S(1)}, u32[]{:S(2)}, u32[]{:S(2)}) %all-to-all-start) | async-done | bytes 196640 | tf_op jit(solution)/shard_map/while/body/eval_jaxpr/all_to_all | solution.py:103
  183.2 4.5 %multiply_reduce_fusion.19 = f32[24,4,128]{2,1,0:T(4,128)S(1)} fusion(f32[24,4,128,128]{3,2,1,0:T(8,128)} %get-tuple-element.441, f32[24,4,128]{2,1,0:T(4,128)S(1)} %gather_fusion), kind=kLoop, calls=%fused_computation.16.clone.1 | loop fusion | flops 3133440 | bytes 6389760 | tf_op jit(solution)/shard_map/while/body/eval_jaxpr/reduce_sum | solution.py:16
  195.4 5.7 %all-to-all-start = ((f32[16,6,4,128]{3,2,1,0:T(4,128)}), f32[16,6,4,128]{3,2,1,0:T(4,128)S(1)}, u32[]{:S(2)}, u32[]{:S(2)}) async-start(f32[16,6,4,128]{3,2,1,0:T(4,128)} %bitcast.220), calls=%async_computation | async-start | bytes 393216 | tf_op jit(solution)/shard_map/while/body/eval_jaxpr/all_to_all | solution.py:103
  201.3 8.0 %all-to-all-done = f32[16,6,4,128]{3,2,1,0:T(4,128)S(1)} async-done(((f32[16,6,4,128]{3,2,1,0:T(4,128)}), f32[16,6,4,128]{3,2,1,0:T(4,128)S(1)}, u32[]{:S(2)}, u32[]{:S(2)}) %all-to-all-start) | async-done | bytes 196640 | tf_op jit(solution)/shard_map/while/body/eval_jaxpr/all_to_all | solution.py:103
  216.4 4.5 %multiply_reduce_fusion.19 = f32[24,4,128]{2,1,0:T(4,128)S(1)} fusion(f32[24,4,128,128]{3,2,1,0:T(8,128)} %get-tuple-element.441, f32[24,4,128]{2,1,0:T(4,128)S(1)} %gather_fusion), kind=kLoop, calls=%fused_computation.16.clone.1 | loop fusion | flops 3133440 | bytes 6389760 | tf_op jit(solution)/shard_map/while/body/eval_jaxpr/reduce_sum | solution.py:16
  228.5 5.7 %all-to-all-start = ((f32[16,6,4,128]{3,2,1,0:T(4,128)}), f32[16,6,4,128]{3,2,1,0:T(4,128)S(1)}, u32[]{:S(2)}, u32[]{:S(2)}) async-start(f32[16,6,4,128]{3,2,1,0:T(4,128)} %bitcast.220), calls=%async_computation | async-start | bytes 393216 | tf_op jit(solution)/shard_map/while/body/eval_jaxpr/all_to_all | solution.py:103
  234.5 8.0 %all-to-all-done = f32[16,6,4,128]{3,2,1,0:T(4,128)S(1)} async-done(((f32[16,6,4,128]{3,2,1,0:T(4,128)}), f32[16,6,4,128]{3,2,1,0:T(4,128)S(1)}, u32[]{:S(2)}, u32[]{:S(2)}) %all-to-all-start) | async-done | bytes 196640 | tf_op jit(solution)/shard_map/while/body/eval_jaxpr/all_to_all | solution.py:103
  244.4 4.7 %all-to-all-start.1 = ((f32[16,6,4,128]{3,2,1,0:T(4,128)}), f32[16,6,4,128]{3,2,1,0:T(4,128)S(1)}, u32[]{:S(2)}, u32[]{:S(2)}) async-start(f32[16,6,4,128]{3,2,1,0:T(4,128)} %select_add_fusion.7), calls=%async_computation.1 | async-start | bytes 393216 | tf_op jit(solution)/shard_map/while/body/eval_jaxpr/all_to_all | solution.py:103
  250.6 4.5 %multiply_reduce_fusion.19 = f32[24,4,128]{2,1,0:T(4,128)S(1)} fusion(f32[24,4,128,128]{3,2,1,0:T(8,128)} %get-tuple-element.441, f32[24,4,128]{2,1,0:T(4,128)S(1)} %gather_fusion), kind=kLoop, calls=%fused_computation.16.clone.1 | loop fusion | flops 3133440 | bytes 6389760 | tf_op jit(solution)/shard_map/while/body/eval_jaxpr/reduce_sum | solution.py:16
  263.9 15.4 %all_to_all.32 = f32[16,6,8,128]{3,2,1,0:T(8,128)S(1)} all-to-all(f32[16,6,8,128]{3,2,1,0:T(8,128)S(1)} %bitcast.246), channel_id=1, replica_groups=mesh['req'=16,'head'=2] {'req'}, dimensions={0} | all-to-all | bytes 786432 | tf_op jit(solution)/shard_map/all_to_all | solution.py:103
  284.5 7.6 %all-to-all-start.5 = ((f32[16,6,12,128]{3,2,1,0:T(8,128)}), f32[16,6,12,128]{3,2,1,0:T(8,128)S(1)}, u32[]{:S(2)}, u32[]{:S(2)}) async-start(f32[16,6,12,128]{3,2,1,0:T(8,128)} %pad_maximum_fusion), calls=%async_computation.5 | async-start | bytes 1572864 | tf_op jit(solution)/shard_map/all_to_all | solution.py:103
  294.5 4.5 %multiply_reduce_fusion.6 = f32[24,4,128]{2,1,0:T(4,128)S(1)} fusion(f32[24,4,128,128]{3,2,1,0:T(8,128)} %get-tuple-element.448, f32[24,4,128]{2,1,0:T(4,128)S(1)} %gather_fusion.9), kind=kLoop, calls=%fused_computation.44 | loop fusion | flops 3133440 | bytes 6389760 | tf_op jit(solution)/shard_map/reduce_sum | solution.py:16
  299.9 6.1 %multiply_reduce_fusion.4 = (f32[24,4,128]{2,1,0:T(4,128)S(1)}, f32[24,4,128]{2,1,0:T(4,128)S(1)}) fusion(f32[24,4,128,128]{3,2,1,0:T(8,128)} %param.26, f32[24,4,128]{2,1,0:T(4,128)S(1)} %copy.229, f32[24,4,128]{2,1,0:T(4,128)S(1)} %copy.226), kind=kLoop, calls=%fused_computation.42 | loop fusion | flops 6266880 | bytes 6488064 | tf_op jit(solution)/shard_map/reduce_sum | solution.py:16
  (290 shorter events, 129.2 us)
Async XLA Ops:
  0.0 313.1 %copy-start = (bf16[4,128,1024]{2,1,0:T(8,128)(2,1)S(1)}, bf16[4,128,1024]{2,1,0:T(8,128)(2,1)}, u32[]{:S(2)}) copy-start(bf16[4,128,1024]{2,1,0:T(8,128)(2,1)} %param.31) | copy-start | bytes 3145732
  2.3 17.3 %copy-start.13 = (pred[24]{0:T(512)(128)(4,1)}, pred[24]{0:T(512)(128)(4,1)S(1)}, u32[]{:S(2)}) copy-start(pred[24]{0:T(512)(128)(4,1)S(1)} %get-tuple-element.256) | copy-start | bytes 76
  16.1 19.8 %copy-start.9 = (bf16[1024,2,4]{0,2,1:T(4,128)(2,1)S(1)}, bf16[1024,2,4]{0,2,1:T(4,128)(2,1)}, u32[]{:S(2)}) copy-start(bf16[1024,2,4]{0,2,1:T(4,128)(2,1)} %param.22) | copy-start | bytes 49156
  16.1 19.9 %copy-start.1 = (f32[2,4,128,128]{3,2,1,0:T(8,128)S(1)}, f32[2,4,128,128]{3,2,1,0:T(8,128)}, u32[]{:S(2)}) copy-start(f32[2,4,128,128]{3,2,1,0:T(8,128)} %param.27) | copy-start | bytes 1572868
  16.9 18.3 %copy-start.11 = (s32[1024]{0:T(1024)}, s32[1024]{0:T(1024)S(1)}, u32[]{:S(2)}) copy-start(s32[1024]{0:T(1024)S(1)} %pad_clamp_fusion.2) | copy-start | bytes 12292
  17.8 17.4 %copy-start.10 = (s32[1024]{0:T(1024)}, s32[1024]{0:T(1024)S(1)}, u32[]{:S(2)}) copy-start(s32[1024]{0:T(1024)S(1)} %pad_clamp_fusion.3) | copy-start | bytes 12292
  19.6 16.5 %copy-start.24 = (f32[24]{0:T(128)S(1)}, f32[24]{0:T(128)}, u32[]{:S(2)}) copy-start(f32[24]{0:T(128)} %copy-done.23) | copy-start | bytes 292
  21.2 23.6 %copy-start.4 = (f32[96,4]{1,0:T(8,128)}, f32[96,4]{1,0:T(8,128)S(1)}, u32[]{:S(2)}) copy-start(f32[96,4]{1,0:T(8,128)S(1)} %get-tuple-element.169) | copy-start | bytes 4612
  22.5 19.9 %all-to-all-start.2 = ((f32[16,6,5,128]{3,1,2,0:T(8,128)}), f32[16,6,5,128]{3,1,2,0:T(8,128)S(1)}, u32[]{:S(2)}, u32[]{:S(2)}) async-start(f32[16,6,5,128]{3,1,2,0:T(8,128)} %copy.182), calls=%async_computation.2 | async-start | bytes 655360 | tf_op jit(solution)/shard_map/all_to_all | solution.py:103
  44.9 17.4 %copy-start.5 = (f32[96,4]{1,0:T(8,128)S(1)}, f32[96,4]{1,0:T(8,128)}, u32[]{:S(2)}) copy-start(f32[96,4]{1,0:T(8,128)} %copy-done.4) | copy-start | bytes 4612
  46.3 11.6 %all-to-all-start.3 = ((f32[16,6,4,128]{3,2,1,0:T(4,128)}), f32[16,6,4,128]{3,2,1,0:T(4,128)S(1)}, u32[]{:S(2)}, u32[]{:S(2)}) async-start(f32[16,6,4,128]{3,2,1,0:T(4,128)} %select_add_fusion.4), calls=%async_computation.3 | async-start | bytes 393216 | tf_op jit(solution)/shard_map/all_to_all | solution.py:103
  64.3 26.7 %copy-start.15 = (f32[1,4,1]{1,2,0:T(1,128)S(1)}, f32[1,4,1]{1,2,0:T(1,128)}, u32[]{:S(2)}) copy-start(f32[1,4,1]{1,2,0:T(1,128)} %get-tuple-element.445) | copy-start | bytes 52 | tf_op jit(solution)/shard_map/while
  64.3 12.9 %all-to-all-start = ((f32[16,6,4,128]{3,2,1,0:T(4,128)}), f32[16,6,4,128]{3,2,1,0:T(4,128)S(1)}, u32[]{:S(2)}, u32[]{:S(2)}) async-start(f32[16,6,4,128]{3,2,1,0:T(4,128)} %bitcast.220), calls=%async_computation | async-start | bytes 393216 | tf_op jit(solution)/shard_map/while/body/eval_jaxpr/all_to_all | solution.py:103
  79.2 11.6 %all-to-all-start.1 = ((f32[16,6,4,128]{3,2,1,0:T(4,128)}), f32[16,6,4,128]{3,2,1,0:T(4,128)S(1)}, u32[]{:S(2)}, u32[]{:S(2)}) async-start(f32[16,6,4,128]{3,2,1,0:T(4,128)} %select_add_fusion.7), calls=%async_computation.1 | async-start | bytes 393216 | tf_op jit(solution)/shard_map/while/body/eval_jaxpr/all_to_all | solution.py:103
  96.4 27.6 %copy-start.15 = (f32[1,4,1]{1,2,0:T(1,128)S(1)}, f32[1,4,1]{1,2,0:T(1,128)}, u32[]{:S(2)}) copy-start(f32[1,4,1]{1,2,0:T(1,128)} %get-tuple-element.445) | copy-start | bytes 52 | tf_op jit(solution)/shard_map/while
  96.4 13.8 %all-to-all-start = ((f32[16,6,4,128]{3,2,1,0:T(4,128)}), f32[16,6,4,128]{3,2,1,0:T(4,128)S(1)}, u32[]{:S(2)}, u32[]{:S(2)}) async-start(f32[16,6,4,128]{3,2,1,0:T(4,128)} %bitcast.220), calls=%async_computation | async-start | bytes 393216 | tf_op jit(solution)/shard_map/while/body/eval_jaxpr/all_to_all | solution.py:103
  112.2 11.6 %all-to-all-start.1 = ((f32[16,6,4,128]{3,2,1,0:T(4,128)}), f32[16,6,4,128]{3,2,1,0:T(4,128)S(1)}, u32[]{:S(2)}, u32[]{:S(2)}) async-start(f32[16,6,4,128]{3,2,1,0:T(4,128)} %select_add_fusion.7), calls=%async_computation.1 | async-start | bytes 393216 | tf_op jit(solution)/shard_map/while/body/eval_jaxpr/all_to_all | solution.py:103
  129.4 27.6 %copy-start.15 = (f32[1,4,1]{1,2,0:T(1,128)S(1)}, f32[1,4,1]{1,2,0:T(1,128)}, u32[]{:S(2)}) copy-start(f32[1,4,1]{1,2,0:T(1,128)} %get-tuple-element.445) | copy-start | bytes 52 | tf_op jit(solution)/shard_map/while
  129.4 13.8 %all-to-all-start = ((f32[16,6,4,128]{3,2,1,0:T(4,128)}), f32[16,6,4,128]{3,2,1,0:T(4,128)S(1)}, u32[]{:S(2)}, u32[]{:S(2)}) async-start(f32[16,6,4,128]{3,2,1,0:T(4,128)} %bitcast.220), calls=%async_computation | async-start | bytes 393216 | tf_op jit(solution)/shard_map/while/body/eval_jaxpr/all_to_all | solution.py:103
  145.2 11.6 %all-to-all-start.1 = ((f32[16,6,4,128]{3,2,1,0:T(4,128)}), f32[16,6,4,128]{3,2,1,0:T(4,128)S(1)}, u32[]{:S(2)}, u32[]{:S(2)}) async-start(f32[16,6,4,128]{3,2,1,0:T(4,128)} %select_add_fusion.7), calls=%async_computation.1 | async-start | bytes 393216 | tf_op jit(solution)/shard_map/while/body/eval_jaxpr/all_to_all | solution.py:103
  162.4 27.6 %copy-start.15 = (f32[1,4,1]{1,2,0:T(1,128)S(1)}, f32[1,4,1]{1,2,0:T(1,128)}, u32[]{:S(2)}) copy-start(f32[1,4,1]{1,2,0:T(1,128)} %get-tuple-element.445) | copy-start | bytes 52 | tf_op jit(solution)/shard_map/while
  162.4 13.8 %all-to-all-start = ((f32[16,6,4,128]{3,2,1,0:T(4,128)}), f32[16,6,4,128]{3,2,1,0:T(4,128)S(1)}, u32[]{:S(2)}, u32[]{:S(2)}) async-start(f32[16,6,4,128]{3,2,1,0:T(4,128)} %bitcast.220), calls=%async_computation | async-start | bytes 393216 | tf_op jit(solution)/shard_map/while/body/eval_jaxpr/all_to_all | solution.py:103
  178.2 11.6 %all-to-all-start.1 = ((f32[16,6,4,128]{3,2,1,0:T(4,128)}), f32[16,6,4,128]{3,2,1,0:T(4,128)S(1)}, u32[]{:S(2)}, u32[]{:S(2)}) async-start(f32[16,6,4,128]{3,2,1,0:T(4,128)} %select_add_fusion.7), calls=%async_computation.1 | async-start | bytes 393216 | tf_op jit(solution)/shard_map/while/body/eval_jaxpr/all_to_all | solution.py:103
  195.4 27.7 %copy-start.15 = (f32[1,4,1]{1,2,0:T(1,128)S(1)}, f32[1,4,1]{1,2,0:T(1,128)}, u32[]{:S(2)}) copy-start(f32[1,4,1]{1,2,0:T(1,128)} %get-tuple-element.445) | copy-start | bytes 52 | tf_op jit(solution)/shard_map/while
  195.4 14.0 %all-to-all-start = ((f32[16,6,4,128]{3,2,1,0:T(4,128)}), f32[16,6,4,128]{3,2,1,0:T(4,128)S(1)}, u32[]{:S(2)}, u32[]{:S(2)}) async-start(f32[16,6,4,128]{3,2,1,0:T(4,128)} %bitcast.220), calls=%async_computation | async-start | bytes 393216 | tf_op jit(solution)/shard_map/while/body/eval_jaxpr/all_to_all | solution.py:103
  211.3 11.6 %all-to-all-start.1 = ((f32[16,6,4,128]{3,2,1,0:T(4,128)}), f32[16,6,4,128]{3,2,1,0:T(4,128)S(1)}, u32[]{:S(2)}, u32[]{:S(2)}) async-start(f32[16,6,4,128]{3,2,1,0:T(4,128)} %select_add_fusion.7), calls=%async_computation.1 | async-start | bytes 393216 | tf_op jit(solution)/shard_map/while/body/eval_jaxpr/all_to_all | solution.py:103
  228.5 28.9 %copy-start.15 = (f32[1,4,1]{1,2,0:T(1,128)S(1)}, f32[1,4,1]{1,2,0:T(1,128)}, u32[]{:S(2)}) copy-start(f32[1,4,1]{1,2,0:T(1,128)} %get-tuple-element.445) | copy-start | bytes 52 | tf_op jit(solution)/shard_map/while
  228.5 13.9 %all-to-all-start = ((f32[16,6,4,128]{3,2,1,0:T(4,128)}), f32[16,6,4,128]{3,2,1,0:T(4,128)S(1)}, u32[]{:S(2)}, u32[]{:S(2)}) async-start(f32[16,6,4,128]{3,2,1,0:T(4,128)} %bitcast.220), calls=%async_computation | async-start | bytes 393216 | tf_op jit(solution)/shard_map/while/body/eval_jaxpr/all_to_all | solution.py:103
  244.4 12.8 %all-to-all-start.1 = ((f32[16,6,4,128]{3,2,1,0:T(4,128)}), f32[16,6,4,128]{3,2,1,0:T(4,128)S(1)}, u32[]{:S(2)}, u32[]{:S(2)}) async-start(f32[16,6,4,128]{3,2,1,0:T(4,128)} %select_add_fusion.7), calls=%async_computation.1 | async-start | bytes 393216 | tf_op jit(solution)/shard_map/while/body/eval_jaxpr/all_to_all | solution.py:103
  262.8 19.1 %copy-start.2 = (f32[2,4,128,128]{3,2,1,0:T(8,128)S(1)}, f32[2,4,128,128]{3,2,1,0:T(8,128)}, u32[]{:S(2)}) copy-start(f32[2,4,128,128]{3,2,1,0:T(8,128)} %param.28) | copy-start | bytes 1572868
  284.5 21.5 %all-to-all-start.5 = ((f32[16,6,12,128]{3,2,1,0:T(8,128)}), f32[16,6,12,128]{3,2,1,0:T(8,128)S(1)}, u32[]{:S(2)}, u32[]{:S(2)}) async-start(f32[16,6,12,128]{3,2,1,0:T(8,128)} %pad_maximum_fusion), calls=%async_computation.5 | async-start | bytes 1572864 | tf_op jit(solution)/shard_map/all_to_all | solution.py:103
  313.4 1.3 collective-permute-start
  (14 other events, 159.0 us)

commit v10 on v8

--- a/solution.py
+++ b/solution.py
@@ -44,23 +44,24 @@
     row_count, model_width = gathered.shape
     head_count = qkv_weight.shape[1]
     head_size = qkv_weight.shape[3]
-    projected = jnp.dot(
-        normed,
-        qkv_weight.reshape(model_width, head_count * 3 * head_size),
-        preferred_element_type=jnp.float32,
-    ).reshape(row_count, head_count, 3, head_size)
-    mixing = conv_weight[0] * projected
-    for offset in range(1, KW):
-        usable = (lengths >= offset).astype(jnp.float32)[:, None, None, None]
-        mixing = (
-            mixing + conv_weight[offset] * conv_state[:, offset - 1].astype(jnp.float32) * usable
-        )
-    active = jax.nn.silu(mixing)
-    queries = active[:, :, 0]
+    live_rows = [(lengths >= offset).astype(jnp.float32)[:, None, None] for offset in range(KW)]
+
+    def project(part):
+        weights = qkv_weight[:, :, part, :].reshape(model_width, head_count * head_size)
+        mixing = conv_weight[0, :, part] * jnp.dot(
+            normed, weights, preferred_element_type=jnp.float32
+        ).reshape(row_count, head_count, head_size)
+        for offset in range(1, KW):
+            mixing = mixing + conv_weight[offset, :, part] * conv_state[
+                :, offset - 1, :, part
+            ].astype(jnp.float32) * live_rows[offset]
+        return jax.nn.silu(mixing)
+
+    queries = project(0)
     queries = queries * lax.rsqrt(jnp.sum(queries * queries, axis=2, keepdims=True) + epsilon)
-    key_now = active[:, :, 1]
+    key_now = project(1)
     key_now = key_now * lax.rsqrt(jnp.sum(key_now * key_now, axis=2, keepdims=True) + epsilon)
-    value_now = active[:, :, 2]
+    value_now = project(2)
     gate_logit = jnp.dot(
         normed, gate_weight.reshape(model_width, 2 * head_count), preferred_element_type=jnp.float32
     ).reshape(row_count, 2, head_count)
@@ -91,6 +92,9 @@
         filled, 0, row_count
     )
     slot_label = jnp.sum(jnp.where(hits, (local_group + 1)[:, None], 0), axis=0)
+    source, slot_of, routed, slot_label = lax.optimization_barrier(
+        (source, slot_of, routed, slot_label)
+    )
 
     def pack(vectors):
         padded = jnp.concatenate(
@@ -136,6 +140,7 @@
     first = exchange(jnp.concatenate([pack(queries), label_row], axis=1))
     labels_in = first[:, head_count, 0]
     chosen = [labels_in == float(group + 1) for group in range(group_count)]
+    chosen = list(lax.optimization_barrier(tuple(chosen)))
     carry = (
         jnp.zeros_like(queries),
         queries,

time: 266 us -> 333 us (1.25)
  local copies, waits for them, and re-layouts: 32 us -> 74.8 us
  waiting for transfers between devices: 88.6 us -> 57.3 us
  other arithmetic: 59.2 us -> 82.9 us
  starting transfers between devices: 58.1 us -> 81.8 us
  blocking collectives: 15.4 us -> 19.1 us
    all_to_all x15, waiting for transfers between devices: 87.4 us -> 56.1 us  [exchange(): lax.all_to_all(shaped, 'req', split_axis=0, concat_axis=0, tiled=True)]
    all_to_all x15, starting transfers between devices: 58 us -> 81.8 us  [exchange(): lax.all_to_all(shaped, 'req', split_axis=0, concat_axis=0, tiled=True)]
    gather x7, other arithmetic: 0.04 us -> 7.79 us  [unpack(): taken = jnp.take(slots, slot_of, axis=0, mode='clip')]
    mul x6, local copies, waits for them, and re-layouts: 0.51 us -> 8.14 us  [cg_step(): shared = weight_col * shares + own_matvec(own_keys, direction)]
    mul x6, local copies, waits for them, and re-layouts: 0.51 us -> 8.09 us  [cg_step(): decay_col * shared]
    gather x8, local copies, waits for them, and re-layouts: 4.73 us -> 11.3 us  [unpack(): taken = jnp.take(slots, slot_of, axis=0, mode='clip')]
    another operation x0 -> x3, local copies, waits for them, and re-layouts: none -> 6.44 us  [project(): qkv_weight[:, :, part, :].reshape(model_width, head_count * head_size)]
    mul x7, other arithmetic: 3.23 us -> 9.2 us  [cg_step(): write_col * key_now * jnp.sum(key_now * direction, axis=2, keepdims=True)]
  transfers between devices with their start and end apart: 16 -> 16, of which waited for: 16 -> 10; matrix products, arithmetic and copies ran while one was open for 16% -> 25% of each run, Pallas kernels for 0% -> 0%
where the time goes in v10:
time: 333 us; the launch traced here: 329 us
  other arithmetic  82.9 us (25%)
  starting transfers between devices  81.8 us (25%)
  local copies, waits for them, and re-layouts  74.8 us (22%)
  waiting for transfers between devices  57.3 us (17%)
  blocking collectives  19.1 us (6%)
  matrix products  11.9 us (4%)
    all_to_all x15, starting transfers between devices, exchange(): lax.all_to_all(shaped, 'req', split_axis=0, concat_axis=0, tiled=True)  81.8 us
    all_to_all x15, waiting for transfers between devices, exchange(): lax.all_to_all(shaped, 'req', split_axis=0, concat_axis=0, tiled=True)  56.1 us
    reduce_sum x8, other arithmetic, own_matvec(): return jnp.sum(matrices * vectors[:, :, None, :], axis=3)  39.3 us
    all_to_all x1, blocking collectives, exchange(): lax.all_to_all(shaped, 'req', split_axis=0, concat_axis=0, tiled=True)  17.1 us
    gather x9, local copies, waits for them, and re-layouts, pack(): return jnp.take(padded, source, axis=0, mode='clip')  12 us
    gather x8, local copies, waits for them, and re-layouts, unpack(): taken = jnp.take(slots, slot_of, axis=0, mode='clip')  11.3 us
    mul x7, other arithmetic, cg_step(): write_col * key_now * jnp.sum(key_now * direction, axis=2, keepdims=True)  9.2 us
    mul x6, local copies, waits for them, and re-layouts, cg_step(): shared = weight_col * shares + own_matvec(own_keys, direction)  8.14 us
  transfers between devices with their start and end apart: 16, of which 10 were waited for; matrix products, arithmetic and copies ran while one was open for 25% of the time, Pallas kernels for 0%

profile of v10, /device:TPU:0, one launch (start us, length us, event | category | flops | bytes accessed | tf_op | source)
XLA Modules:
  0.0 329.2 jit_solution(14314086221424325615)
XLA Ops:
  6.5 4.3 %fusion.89 = (bf16[1024,4,1,128]{3,1,2,0:T(4,128)(2,1)S(1)}, bf16[1024,4,1,128]{3,1,2,0:T(4,128)(2,1)}, bf16[1024,4,1,128]{3,1,2,0:T(4,128)(2,1)}) fusion(bf16[1024,4,3,128]{3,1,2,0:T(4,128)(2,1)} %param.19), kind=kLoop, calls=%fused_computation.208 | loop fusion | bytes 6291456 | tf_op jit(solution)/shard_map/slice | solution.py:50
  25.9 8.2 %all-to-all-start.2 = ((f32[16,6,5,128]{3,1,2,0:T(8,128)}), f32[16,6,5,128]{3,1,2,0:T(8,128)S(1)}, u32[]{:S(2)}, u32[]{:S(2)}) async-start(f32[16,6,5,128]{3,1,2,0:T(8,128)} %copy.163), calls=%async_computation.2 | async-start | bytes 655360 | tf_op jit(solution)/shard_map/all_to_all | solution.py:107
  34.9 10.9 %all-to-all-done.2 = f32[16,6,5,128]{3,1,2,0:T(8,128)S(1)} async-done(((f32[16,6,5,128]{3,1,2,0:T(8,128)}), f32[16,6,5,128]{3,1,2,0:T(8,128)S(1)}, u32[]{:S(2)}, u32[]{:S(2)}) %all-to-all-start.2) | async-done | bytes 245792 | tf_op jit(solution)/shard_map/all_to_all | solution.py:107
  49.9 4.2 %all-to-all-start.3 = ((f32[16,6,4,128]{3,2,1,0:T(4,128)}), f32[16,6,4,128]{3,2,1,0:T(4,128)}, u32[]{:S(2)}, u32[]{:S(2)}) async-start(f32[16,6,4,128]{3,2,1,0:T(4,128)} %select_add_fusion.4), calls=%async_computation.3 | async-start | bytes 393216 | tf_op jit(solution)/shard_map/all_to_all | solution.py:107
  55.4 4.5 %multiply_reduce_fusion.7 = f32[24,4,128]{2,1,0:T(4,128)S(1)} fusion(f32[24,4,128,128]{3,2,1,0:T(8,128)} %param.25, f32[24,4,128]{2,1,0:T(4,128)S(1)} %copy.229), kind=kLoop, calls=%fused_computation.33 | loop fusion | flops 3133440 | bytes 6389760 | tf_op jit(solution)/shard_map/reduce_sum | solution.py:16
  65.2 209.3 %while.16 = (s32[]{:T(128)}, f32[24,4,128]{2,1,0:T(4,128)S(1)}, f32[24,4,128]{2,1,0:T(4,128)S(1)}, f32[24,4,128]{2,1,0:T(4,128)S(1)}, f32[24,4,1]{0,1,2:T(4,128)...) while((s32[]{:T(128)}, f32[24,4,128]{2,1,0:T(4,128)S(1)}, ...), condition=%wide.region_17.18_spmd, body=%wide.region_12.17_spmd.sunk | while | flops 154523872 | bytes 12098585 | solution.py:151
  67.2 4.5 %all-to-all-start = ((f32[16,6,4,128]{3,2,1,0:T(4,128)}), f32[16,6,4,128]{3,2,1,0:T(4,128)S(1)}, u32[]{:S(2)}, u32[]{:S(2)}) async-start(f32[16,6,4,128]{3,2,1,0:T(4,128)} %bitcast.219), calls=%async_computation | async-start | bytes 393216 | tf_op jit(solution)/shard_map/while/body/eval_jaxpr/all_to_all | solution.py:107
  73.2 6.6 %all-to-all-done = f32[16,6,4,128]{3,2,1,0:T(4,128)S(1)} async-done(((f32[16,6,4,128]{3,2,1,0:T(4,128)}), f32[16,6,4,128]{3,2,1,0:T(4,128)S(1)}, u32[]{:S(2)}, u32[]{:S(2)}) %all-to-all-start) | async-done | bytes 196640 | tf_op jit(solution)/shard_map/while/body/eval_jaxpr/all_to_all | solution.py:107
  81.7 3.5 %all-to-all-start.1 = ((f32[16,6,4,128]{3,2,1,0:T(4,128)}), f32[16,6,4,128]{3,2,1,0:T(4,128)S(1)}, u32[]{:S(2)}, u32[]{:S(2)}) async-start(f32[16,6,4,128]{3,2,1,0:T(4,128)} %select_add_fusion.7), calls=%async_computation.1 | async-start | bytes 393216 | tf_op jit(solution)/shard_map/while/body/eval_jaxpr/all_to_all | solution.py:107
  89.9 4.5 %multiply_reduce_fusion.18 = f32[24,4,128]{2,1,0:T(4,128)S(1)} fusion(f32[24,4,128,128]{3,2,1,0:T(8,128)} %get-tuple-element.455, f32[24,4,128]{2,1,0:T(4,128)S(1)} %get-tuple-element.426), kind=kLoop, calls=%fused_computation.8.clone.1 | loop fusion | flops 3133440 | bytes 6389760 | tf_op jit(solution)/shard_map/while/body/eval_jaxpr/reduce_sum | solution.py:16
  99.8 6.9 %all-to-all-start = ((f32[16,6,4,128]{3,2,1,0:T(4,128)}), f32[16,6,4,128]{3,2,1,0:T(4,128)S(1)}, u32[]{:S(2)}, u32[]{:S(2)}) async-start(f32[16,6,4,128]{3,2,1,0:T(4,128)} %bitcast.219), calls=%async_computation | async-start | bytes 393216 | tf_op jit(solution)/shard_map/while/body/eval_jaxpr/all_to_all | solution.py:107
  108.2 6.6 %all-to-all-done = f32[16,6,4,128]{3,2,1,0:T(4,128)S(1)} async-done(((f32[16,6,4,128]{3,2,1,0:T(4,128)}), f32[16,6,4,128]{3,2,1,0:T(4,128)S(1)}, u32[]{:S(2)}, u32[]{:S(2)}) %all-to-all-start) | async-done | bytes 196640 | tf_op jit(solution)/shard_map/while/body/eval_jaxpr/all_to_all | solution.py:107
  116.7 3.5 %all-to-all-start.1 = ((f32[16,6,4,128]{3,2,1,0:T(4,128)}), f32[16,6,4,128]{3,2,1,0:T(4,128)S(1)}, u32[]{:S(2)}, u32[]{:S(2)}) async-start(f32[16,6,4,128]{3,2,1,0:T(4,128)} %select_add_fusion.7), calls=%async_computation.1 | async-start | bytes 393216 | tf_op jit(solution)/shard_map/while/body/eval_jaxpr/all_to_all | solution.py:107
  124.9 4.5 %multiply_reduce_fusion.18 = f32[24,4,128]{2,1,0:T(4,128)S(1)} fusion(f32[24,4,128,128]{3,2,1,0:T(8,128)} %get-tuple-element.455, f32[24,4,128]{2,1,0:T(4,128)S(1)} %get-tuple-element.426), kind=kLoop, calls=%fused_computation.8.clone.1 | loop fusion | flops 3133440 | bytes 6389760 | tf_op jit(solution)/shard_map/while/body/eval_jaxpr/reduce_sum | solution.py:16
  134.8 6.9 %all-to-all-start = ((f32[16,6,4,128]{3,2,1,0:T(4,128)}), f32[16,6,4,128]{3,2,1,0:T(4,128)S(1)}, u32[]{:S(2)}, u32[]{:S(2)}) async-start(f32[16,6,4,128]{3,2,1,0:T(4,128)} %bitcast.219), calls=%async_computation | async-start | bytes 393216 | tf_op jit(solution)/shard_map/while/body/eval_jaxpr/all_to_all | solution.py:107
  143.2 6.6 %all-to-all-done = f32[16,6,4,128]{3,2,1,0:T(4,128)S(1)} async-done(((f32[16,6,4,128]{3,2,1,0:T(4,128)}), f32[16,6,4,128]{3,2,1,0:T(4,128)S(1)}, u32[]{:S(2)}, u32[]{:S(2)}) %all-to-all-start) | async-done | bytes 196640 | tf_op jit(solution)/shard_map/while/body/eval_jaxpr/all_to_all | solution.py:107
  159.8 4.5 %multiply_reduce_fusion.18 = f32[24,4,128]{2,1,0:T(4,128)S(1)} fusion(f32[24,4,128,128]{3,2,1,0:T(8,128)} %get-tuple-element.455, f32[24,4,128]{2,1,0:T(4,128)S(1)} %get-tuple-element.426), kind=kLoop, calls=%fused_computation.8.clone.1 | loop fusion | flops 3133440 | bytes 6389760 | tf_op jit(solution)/shard_map/while/body/eval_jaxpr/reduce_sum | solution.py:16
  169.8 6.9 %all-to-all-start = ((f32[16,6,4,128]{3,2,1,0:T(4,128)}), f32[16,6,4,128]{3,2,1,0:T(4,128)S(1)}, u32[]{:S(2)}, u32[]{:S(2)}) async-start(f32[16,6,4,128]{3,2,1,0:T(4,128)} %bitcast.219), calls=%async_computation | async-start | bytes 393216 | tf_op jit(solution)/shard_map/while/body/eval_jaxpr/all_to_all | solution.py:107
  178.2 6.6 %all-to-all-done = f32[16,6,4,128]{3,2,1,0:T(4,128)S(1)} async-done(((f32[16,6,4,128]{3,2,1,0:T(4,128)}), f32[16,6,4,128]{3,2,1,0:T(4,128)S(1)}, u32[]{:S(2)}, u32[]{:S(2)}) %all-to-all-start) | async-done | bytes 196640 | tf_op jit(solution)/shard_map/while/body/eval_jaxpr/all_to_all | solution.py:107
  186.7 3.5 %all-to-all-start.1 = ((f32[16,6,4,128]{3,2,1,0:T(4,128)}), f32[16,6,4,128]{3,2,1,0:T(4,128)S(1)}, u32[]{:S(2)}, u32[]{:S(2)}) async-start(f32[16,6,4,128]{3,2,1,0:T(4,128)} %select_add_fusion.7), calls=%async_computation.1 | async-start | bytes 393216 | tf_op jit(solution)/shard_map/while/body/eval_jaxpr/all_to_all | solution.py:107
  194.9 4.5 %multiply_reduce_fusion.18 = f32[24,4,128]{2,1,0:T(4,128)S(1)} fusion(f32[24,4,128,128]{3,2,1,0:T(8,128)} %get-tuple-element.455, f32[24,4,128]{2,1,0:T(4,128)S(1)} %get-tuple-element.426), kind=kLoop, calls=%fused_computation.8.clone.1 | loop fusion | flops 3133440 | bytes 6389760 | tf_op jit(solution)/shard_map/while/body/eval_jaxpr/reduce_sum | solution.py:16
  204.8 6.9 %all-to-all-start = ((f32[16,6,4,128]{3,2,1,0:T(4,128)}), f32[16,6,4,128]{3,2,1,0:T(4,128)S(1)}, u32[]{:S(2)}, u32[]{:S(2)}) async-start(f32[16,6,4,128]{3,2,1,0:T(4,128)} %bitcast.219), calls=%async_computation | async-start | bytes 393216 | tf_op jit(solution)/shard_map/while/body/eval_jaxpr/all_to_all | solution.py:107
  213.2 6.8 %all-to-all-done = f32[16,6,4,128]{3,2,1,0:T(4,128)S(1)} async-done(((f32[16,6,4,128]{3,2,1,0:T(4,128)}), f32[16,6,4,128]{3,2,1,0:T(4,128)S(1)}, u32[]{:S(2)}, u32[]{:S(2)}) %all-to-all-start) | async-done | bytes 196640 | tf_op jit(solution)/shard_map/while/body/eval_jaxpr/all_to_all | solution.py:107
  221.8 3.5 %all-to-all-start.1 = ((f32[16,6,4,128]{3,2,1,0:T(4,128)}), f32[16,6,4,128]{3,2,1,0:T(4,128)S(1)}, u32[]{:S(2)}, u32[]{:S(2)}) async-start(f32[16,6,4,128]{3,2,1,0:T(4,128)} %select_add_fusion.7), calls=%async_computation.1 | async-start | bytes 393216 | tf_op jit(solution)/shard_map/while/body/eval_jaxpr/all_to_all | solution.py:107
  230.0 4.5 %multiply_reduce_fusion.18 = f32[24,4,128]{2,1,0:T(4,128)S(1)} fusion(f32[24,4,128,128]{3,2,1,0:T(8,128)} %get-tuple-element.455, f32[24,4,128]{2,1,0:T(4,128)S(1)} %get-tuple-element.426), kind=kLoop, calls=%fused_computation.8.clone.1 | loop fusion | flops 3133440 | bytes 6389760 | tf_op jit(solution)/shard_map/while/body/eval_jaxpr/reduce_sum | solution.py:16
  240.0 6.9 %all-to-all-start = ((f32[16,6,4,128]{3,2,1,0:T(4,128)}), f32[16,6,4,128]{3,2,1,0:T(4,128)S(1)}, u32[]{:S(2)}, u32[]{:S(2)}) async-start(f32[16,6,4,128]{3,2,1,0:T(4,128)} %bitcast.219), calls=%async_computation | async-start | bytes 393216 | tf_op jit(solution)/shard_map/while/body/eval_jaxpr/all_to_all | solution.py:107
  248.3 7.5 %all-to-all-done = f32[16,6,4,128]{3,2,1,0:T(4,128)S(1)} async-done(((f32[16,6,4,128]{3,2,1,0:T(4,128)}), f32[16,6,4,128]{3,2,1,0:T(4,128)S(1)}, u32[]{:S(2)}, u32[]{:S(2)}) %all-to-all-start) | async-done | bytes 196640 | tf_op jit(solution)/shard_map/while/body/eval_jaxpr/all_to_all | solution.py:107
  257.7 4.2 %all-to-all-start.1 = ((f32[16,6,4,128]{3,2,1,0:T(4,128)}), f32[16,6,4,128]{3,2,1,0:T(4,128)S(1)}, u32[]{:S(2)}, u32[]{:S(2)}) async-start(f32[16,6,4,128]{3,2,1,0:T(4,128)} %select_add_fusion.7), calls=%async_computation.1 | async-start | bytes 393216 | tf_op jit(solution)/shard_map/while/body/eval_jaxpr/all_to_all | solution.py:107
  266.5 4.5 %multiply_reduce_fusion.18 = f32[24,4,128]{2,1,0:T(4,128)S(1)} fusion(f32[24,4,128,128]{3,2,1,0:T(8,128)} %get-tuple-element.455, f32[24,4,128]{2,1,0:T(4,128)S(1)} %get-tuple-element.426), kind=kLoop, calls=%fused_computation.8.clone.1 | loop fusion | flops 3133440 | bytes 6389760 | tf_op jit(solution)/shard_map/while/body/eval_jaxpr/reduce_sum | solution.py:16
  278.8 17.1 %all_to_all.32 = f32[16,6,8,128]{3,2,1,0:T(8,128)S(1)} all-to-all(f32[16,6,8,128]{3,2,1,0:T(8,128)S(1)} %bitcast.232), channel_id=1, replica_groups=mesh['req'=16,'head'=2] {'req'}, dimensions={0} | all-to-all | bytes 786432 | tf_op jit(solution)/shard_map/all_to_all | solution.py:107
  300.3 8.7 %all-to-all-start.5 = ((f32[16,6,12,128]{3,2,1,0:T(8,128)}), f32[16,6,12,128]{3,2,1,0:T(8,128)}, u32[]{:S(2)}, u32[]{:S(2)}) async-start(f32[16,6,12,128]{3,2,1,0:T(8,128)} %pad_maximum_fusion), calls=%async_computation.5 | async-start | bytes 1572864 | tf_op jit(solution)/shard_map/all_to_all | solution.py:107
  312.3 7.9 %multiply_reduce_fusion.4 = (f32[24,4,128]{2,1,0:T(4,128)S(1)}, f32[24,4,128]{2,1,0:T(4,128)S(1)}, f32[24,4,128]{2,1,0:T(4,128)S(1)}) fusion(f32[24,4,128,128]{3,2,1,0:T(8,128)} %param.26, f32[24,4,128]{2,1,0:T(4,128)S(1)} %get-tuple-element.106, f32[24,4,128]{2,1,0:T(4,128)S(1)} %get-tuple-element.107, f32[24,4,128,128]{3,2,1,0:T(8,128)} %get-tuple-element.461), kind=kLoop, calls=%fused_computation.30 | loop fusion | flops 9400320 | bytes 12828672 | tf_op jit(solution)/shard_map/reduce_sum | solution.py:16
  (329 shorter events, 137.2 us)
Async XLA Ops:
  0.0 326.9 %copy-start = (bf16[4,128,1024]{2,1,0:T(8,128)(2,1)S(1)}, bf16[4,128,1024]{2,1,0:T(8,128)(2,1)}, u32[]{:S(2)}) copy-start(bf16[4,128,1024]{2,1,0:T(8,128)(2,1)} %param.31) | copy-start | bytes 3145732
  0.0 17.8 %copy-start.37 = (f32[1024]{0:T(1024)S(1)}, f32[1024]{0:T(1024)}, u32[]{:S(2)}) copy-start(f32[1024]{0:T(1024)} %param.18) | copy-start | bytes 12292
  0.0 19.5 %copy-start.16 = (bf16[1024,2,4]{0,2,1:T(4,128)(2,1)S(1)}, bf16[1024,2,4]{0,2,1:T(4,128)(2,1)}, u32[]{:S(2)}) copy-start(bf16[1024,2,4]{0,2,1:T(4,128)(2,1)} %param.22) | copy-start | bytes 49156
  2.3 21.9 %copy-start.31 = (f32[24]{0:T(128)}, f32[24]{0:T(128)S(1)}, u32[]{:S(2)}) copy-start(f32[24]{0:T(128)S(1)} %get-tuple-element.273) | copy-start | bytes 292
  2.3 21.9 %copy-start.33 = (f32[24]{0:T(128)}, f32[24]{0:T(128)S(1)}, u32[]{:S(2)}) copy-start(f32[24]{0:T(128)S(1)} %get-tuple-element.274) | copy-start | bytes 292
  2.3 21.9 %copy-start.35 = (f32[24]{0:T(128)}, f32[24]{0:T(128)S(1)}, u32[]{:S(2)}) copy-start(f32[24]{0:T(128)S(1)} %get-tuple-element.275) | copy-start | bytes 292
  2.3 61.4 %copy-start.19 = (pred[24]{0:T(512)(128)(4,1)}, pred[24]{0:T(512)(128)(4,1)S(1)}, u32[]{:S(2)}) copy-start(pred[24]{0:T(512)(128)(4,1)S(1)} %get-tuple-element.411) | copy-start | bytes 76
  10.7 35.8 %copy-start.1 = (f32[2,4,128,128]{3,2,1,0:T(8,128)S(1)}, f32[2,4,128,128]{3,2,1,0:T(8,128)}, u32[]{:S(2)}) copy-start(f32[2,4,128,128]{3,2,1,0:T(8,128)} %param.27) | copy-start | bytes 1572868
  15.3 19.5 %copy-start.39 = (f32[24]{0:T(128)}, f32[24]{0:T(128)S(1)}, u32[]{:S(2)}) copy-start(f32[24]{0:T(128)S(1)} %add_rsqrt_fusion.3) | copy-start | bytes 292
  22.4 37.5 %copy-start.17 = (s32[1024]{0:T(1024)}, s32[1024]{0:T(1024)S(1)}, u32[]{:S(2)}) copy-start(s32[1024]{0:T(1024)S(1)} %pad_clamp_fusion.3) | copy-start | bytes 12292
  25.9 19.9 %all-to-all-start.2 = ((f32[16,6,5,128]{3,1,2,0:T(8,128)}), f32[16,6,5,128]{3,1,2,0:T(8,128)S(1)}, u32[]{:S(2)}, u32[]{:S(2)}) async-start(f32[16,6,5,128]{3,1,2,0:T(8,128)} %copy.163), calls=%async_computation.2 | async-start | bytes 655360 | tf_op jit(solution)/shard_map/all_to_all | solution.py:107
  34.8 29.0 %copy-start.27 = (f32[24,4]{0,1:T(4,128)}, f32[24,4]{0,1:T(4,128)S(1)}, u32[]{:S(2)}) copy-start(f32[24,4]{0,1:T(4,128)S(1)} %get-tuple-element.270) | copy-start | bytes 1156
  34.8 29.0 %copy-start.29 = (f32[24,4]{0,1:T(4,128)}, f32[24,4]{0,1:T(4,128)S(1)}, u32[]{:S(2)}) copy-start(f32[24,4]{0,1:T(4,128)S(1)} %get-tuple-element.271) | copy-start | bytes 1156
  34.9 28.9 %copy-start.5 = (f32[24,4,128]{2,0,1:T(8,128)}, f32[24,4,128]{2,0,1:T(8,128)S(1)}, u32[]{:S(2)}) copy-start(f32[24,4,128]{2,0,1:T(8,128)S(1)} %broadcast_multiply_fusion.1) | copy-start | bytes 147460
  49.9 12.3 %all-to-all-start.3 = ((f32[16,6,4,128]{3,2,1,0:T(4,128)}), f32[16,6,4,128]{3,2,1,0:T(4,128)}, u32[]{:S(2)}, u32[]{:S(2)}) async-start(f32[16,6,4,128]{3,2,1,0:T(4,128)} %select_add_fusion.4), calls=%async_computation.3 | async-start | bytes 393216 | tf_op jit(solution)/shard_map/all_to_all | solution.py:107
  67.2 12.6 %all-to-all-start = ((f32[16,6,4,128]{3,2,1,0:T(4,128)}), f32[16,6,4,128]{3,2,1,0:T(4,128)S(1)}, u32[]{:S(2)}, u32[]{:S(2)}) async-start(f32[16,6,4,128]{3,2,1,0:T(4,128)} %bitcast.219), calls=%async_computation | async-start | bytes 393216 | tf_op jit(solution)/shard_map/while/body/eval_jaxpr/all_to_all | solution.py:107
  81.7 12.7 %all-to-all-start.1 = ((f32[16,6,4,128]{3,2,1,0:T(4,128)}), f32[16,6,4,128]{3,2,1,0:T(4,128)S(1)}, u32[]{:S(2)}, u32[]{:S(2)}) async-start(f32[16,6,4,128]{3,2,1,0:T(4,128)} %select_add_fusion.7), calls=%async_computation.1 | async-start | bytes 393216 | tf_op jit(solution)/shard_map/while/body/eval_jaxpr/all_to_all | solution.py:107
  99.8 15.0 %all-to-all-start = ((f32[16,6,4,128]{3,2,1,0:T(4,128)}), f32[16,6,4,128]{3,2,1,0:T(4,128)S(1)}, u32[]{:S(2)}, u32[]{:S(2)}) async-start(f32[16,6,4,128]{3,2,1,0:T(4,128)} %bitcast.219), calls=%async_computation | async-start | bytes 393216 | tf_op jit(solution)/shard_map/while/body/eval_jaxpr/all_to_all | solution.py:107
  116.7 12.7 %all-to-all-start.1 = ((f32[16,6,4,128]{3,2,1,0:T(4,128)}), f32[16,6,4,128]{3,2,1,0:T(4,128)S(1)}, u32[]{:S(2)}, u32[]{:S(2)}) async-start(f32[16,6,4,128]{3,2,1,0:T(4,128)} %select_add_fusion.7), calls=%async_computation.1 | async-start | bytes 393216 | tf_op jit(solution)/shard_map/while/body/eval_jaxpr/all_to_all | solution.py:107
  134.8 15.0 %all-to-all-start = ((f32[16,6,4,128]{3,2,1,0:T(4,128)}), f32[16,6,4,128]{3,2,1,0:T(4,128)S(1)}, u32[]{:S(2)}, u32[]{:S(2)}) async-start(f32[16,6,4,128]{3,2,1,0:T(4,128)} %bitcast.219), calls=%async_computation | async-start | bytes 393216 | tf_op jit(solution)/shard_map/while/body/eval_jaxpr/all_to_all | solution.py:107
  151.7 12.7 %all-to-all-start.1 = ((f32[16,6,4,128]{3,2,1,0:T(4,128)}), f32[16,6,4,128]{3,2,1,0:T(4,128)S(1)}, u32[]{:S(2)}, u32[]{:S(2)}) async-start(f32[16,6,4,128]{3,2,1,0:T(4,128)} %select_add_fusion.7), calls=%async_computation.1 | async-start | bytes 393216 | tf_op jit(solution)/shard_map/while/body/eval_jaxpr/all_to_all | solution.py:107
  169.8 15.0 %all-to-all-start = ((f32[16,6,4,128]{3,2,1,0:T(4,128)}), f32[16,6,4,128]{3,2,1,0:T(4,128)S(1)}, u32[]{:S(2)}, u32[]{:S(2)}) async-start(f32[16,6,4,128]{3,2,1,0:T(4,128)} %bitcast.219), calls=%async_computation | async-start | bytes 393216 | tf_op jit(solution)/shard_map/while/body/eval_jaxpr/all_to_all | solution.py:107
  186.7 12.7 %all-to-all-start.1 = ((f32[16,6,4,128]{3,2,1,0:T(4,128)}), f32[16,6,4,128]{3,2,1,0:T(4,128)S(1)}, u32[]{:S(2)}, u32[]{:S(2)}) async-start(f32[16,6,4,128]{3,2,1,0:T(4,128)} %select_add_fusion.7), calls=%async_computation.1 | async-start | bytes 393216 | tf_op jit(solution)/shard_map/while/body/eval_jaxpr/all_to_all | solution.py:107
  204.8 15.1 %all-to-all-start = ((f32[16,6,4,128]{3,2,1,0:T(4,128)}), f32[16,6,4,128]{3,2,1,0:T(4,128)S(1)}, u32[]{:S(2)}, u32[]{:S(2)}) async-start(f32[16,6,4,128]{3,2,1,0:T(4,128)} %bitcast.219), calls=%async_computation | async-start | bytes 393216 | tf_op jit(solution)/shard_map/while/body/eval_jaxpr/all_to_all | solution.py:107
  221.8 12.7 %all-to-all-start.1 = ((f32[16,6,4,128]{3,2,1,0:T(4,128)}), f32[16,6,4,128]{3,2,1,0:T(4,128)S(1)}, u32[]{:S(2)}, u32[]{:S(2)}) async-start(f32[16,6,4,128]{3,2,1,0:T(4,128)} %select_add_fusion.7), calls=%async_computation.1 | async-start | bytes 393216 | tf_op jit(solution)/shard_map/while/body/eval_jaxpr/all_to_all | solution.py:107
  240.0 15.8 %all-to-all-start = ((f32[16,6,4,128]{3,2,1,0:T(4,128)}), f32[16,6,4,128]{3,2,1,0:T(4,128)S(1)}, u32[]{:S(2)}, u32[]{:S(2)}) async-start(f32[16,6,4,128]{3,2,1,0:T(4,128)} %bitcast.219), calls=%async_computation | async-start | bytes 393216 | tf_op jit(solution)/shard_map/while/body/eval_jaxpr/all_to_all | solution.py:107
  257.7 13.3 %all-to-all-start.1 = ((f32[16,6,4,128]{3,2,1,0:T(4,128)}), f32[16,6,4,128]{3,2,1,0:T(4,128)S(1)}, u32[]{:S(2)}, u32[]{:S(2)}) async-start(f32[16,6,4,128]{3,2,1,0:T(4,128)} %select_add_fusion.7), calls=%async_computation.1 | async-start | bytes 393216 | tf_op jit(solution)/shard_map/while/body/eval_jaxpr/all_to_all | solution.py:107
  274.5 22.6 %copy-start.2 = (f32[2,4,128,128]{3,2,1,0:T(8,128)S(1)}, f32[2,4,128,128]{3,2,1,0:T(8,128)}, u32[]{:S(2)}) copy-start(f32[2,4,128,128]{3,2,1,0:T(8,128)} %param.28) | copy-start | bytes 1572868
  274.5 24.5 %copy-start.13 = (pred[16,6]{1,0:T(8,128)(4,1)S(1)}, pred[16,6]{1,0:T(8,128)(4,1)}, u32[]{:S(2)}) copy-start(pred[16,6]{1,0:T(8,128)(4,1)} %copy-done.12) | copy-start | bytes 292
  274.5 24.5 %copy-start.15 = (pred[16,6]{1,0:T(8,128)(4,1)S(1)}, pred[16,6]{1,0:T(8,128)(4,1)}, u32[]{:S(2)}) copy-start(pred[16,6]{1,0:T(8,128)(4,1)} %copy-done.14) | copy-start | bytes 292
  300.3 22.0 %all-to-all-start.5 = ((f32[16,6,12,128]{3,2,1,0:T(8,128)}), f32[16,6,12,128]{3,2,1,0:T(8,128)}, u32[]{:S(2)}, u32[]{:S(2)}) async-start(f32[16,6,12,128]{3,2,1,0:T(8,128)} %pad_maximum_fusion), calls=%async_computation.5 | async-start | bytes 1572864 | tf_op jit(solution)/shard_map/all_to_all | solution.py:107
  327.2 1.3 collective-permute-start
  (25 other events, 326.3 us)

commit v11 on v8

--- a/solution.py
+++ b/solution.py
@@ -84,7 +84,7 @@
     )
     rank_of = jnp.sum(earlier.astype(jnp.int32), axis=1)
     routed = mask_of_live & (rank_of < capacity)
-    slot_of = jnp.where(routed, owner_of * capacity + rank_of, 0)
+    slot_of = jnp.clip(jnp.where(routed, owner_of * capacity + rank_of, 0), 0, slot_count - 1)
     hits = (slot_of[:, None] == jnp.arange(slot_count)[None, :]) & routed[:, None]
     filled = jnp.any(hits, axis=0)
     source = jnp.sum(jnp.where(hits, order_ids[:, None], 0), axis=0) + jnp.where(
@@ -96,7 +96,7 @@
         padded = jnp.concatenate(
             [vectors, jnp.zeros((1,) + vectors.shape[1:], vectors.dtype)], axis=0
         )
-        return jnp.take(padded, source, axis=0, mode="clip")
+        return padded.at[source].get(mode="promise_in_bounds")
 
     def exchange(slots):
         shaped = slots.reshape((peer_count, capacity) + slots.shape[1:])
@@ -104,7 +104,7 @@
         return moved.reshape(slots.shape)
 
     def unpack(slots):
-        taken = jnp.take(slots, slot_of, axis=0, mode="clip")
+        taken = slots.at[slot_of].get(mode="promise_in_bounds")
         return jnp.where(routed[:, None, None], taken, 0.0)
 
     def owner_apply(states, incoming, chosen):

time: 266 us -> 266 us (level)
  no operation moved by 1% of the time
where the time goes in v11:
time: 266 us; the launch traced here: 264 us
  waiting for transfers between devices  88.6 us (33%)
  other arithmetic  59.3 us (22%)
  starting transfers between devices  58.1 us (22%)
  local copies, waits for them, and re-layouts  32 us (12%)
  blocking collectives  15.4 us (6%)
  matrix products  9.68 us (4%)
    all_to_all x15, waiting for transfers between devices, exchange(): lax.all_to_all(shaped, 'req', split_axis=0, concat_axis=0, tiled=True)  87.3 us
    all_to_all x15, starting transfers between devices, exchange(): lax.all_to_all(shaped, 'req', split_axis=0, concat_axis=0, tiled=True)  58 us
    reduce_sum x8, other arithmetic, own_matvec(): return jnp.sum(matrices * vectors[:, :, None, :], axis=3)  39.3 us
    all_to_all x1, blocking collectives, exchange(): lax.all_to_all(shaped, 'req', split_axis=0, concat_axis=0, tiled=True)  13.1 us
    gather x9, local copies, waits for them, and re-layouts, pack(): return padded.at[source].get(mode='promise_in_bounds')  10.3 us
    add x8, other arithmetic, owner_apply(): total + jnp.where(chosen[group][:, None, None], products[group], 0.0)  6.94 us
    dot_general x10, matrix products, owner_apply(): products = jnp.einsum('shj,ghij->gshi', incoming, states, precision=highest)  6.33 us
    unnamed x19, local copies, waits for them, and re-layouts  6.13 us
  transfers between devices with their start and end apart: 16, of which 16 were waited for; matrix products, arithmetic and copies ran while one was open for 16% of the time, Pallas kernels for 0%

profile of v11, /device:TPU:0, one launch (start us, length us, event | category | flops | bytes accessed | tf_op | source)
XLA Modules:
  0.0 264.4 jit_solution(10404790530442884728)
XLA Ops:
  7.3 6.0 %copy.151 = bf16[1024,4,3,128]{0,3,2,1:T(8,128)(2,1)} copy(bf16[1024,4,3,128]{3,1,2,0:T(4,128)(2,1)} %param.19) | data formatting | bytes 6291456 | tf_op args[2]
  18.4 8.2 %all-to-all-start.2 = ((f32[16,6,5,128]{3,1,2,0:T(8,128)}), f32[16,6,5,128]{3,1,2,0:T(8,128)S(1)}, u32[]{:S(2)}, u32[]{:S(2)}) async-start(f32[16,6,5,128]{3,1,2,0:T(8,128)} %copy.161), calls=%async_computation.2 | async-start | bytes 655360 | tf_op jit(solution)/shard_map/all_to_all | solution.py:103
  27.0 11.3 %all-to-all-done.2 = f32[16,6,5,128]{3,1,2,0:T(8,128)S(1)} async-done(((f32[16,6,5,128]{3,1,2,0:T(8,128)}), f32[16,6,5,128]{3,1,2,0:T(8,128)S(1)}, u32[]{:S(2)}, u32[]{:S(2)}) %all-to-all-start.2) | async-done | bytes 245792 | tf_op jit(solution)/shard_map/all_to_all | solution.py:103
  40.6 3.5 %all-to-all-start.3 = ((f32[16,6,4,128]{3,2,1,0:T(4,128)}), f32[16,6,4,128]{3,2,1,0:T(4,128)S(1)}, u32[]{:S(2)}, u32[]{:S(2)}) async-start(f32[16,6,4,128]{3,2,1,0:T(4,128)} %select_add_fusion.4), calls=%async_computation.3 | async-start | bytes 393216 | tf_op jit(solution)/shard_map/all_to_all | solution.py:103
  44.2 4.5 %multiply_reduce_fusion.7 = f32[24,4,128]{2,1,0:T(4,128)S(1)} fusion(f32[24,4,128,128]{3,2,1,0:T(8,128)} %param.25, f32[24,4,128]{2,1,0:T(4,128)S(1)} %copy.167), kind=kLoop, calls=%fused_computation.37 | loop fusion | flops 3133440 | bytes 6389760 | tf_op jit(solution)/shard_map/reduce_sum | solution.py:16
  53.5 170.9 %while.16 = (s32[]{:T(128)}, f32[24,4,128]{2,1,0:T(4,128)S(1)}, f32[24,4,128]{2,1,0:T(4,128)S(1)}, f32[24,4,128]{2,1,0:T(4,128)S(1)}, f32[24,4,1]{0,1,2:T(4,128)...) while((s32[]{:T(128)}, f32[24,4,128]{2,1,0:T(4,128)S(1)}, ...), condition=%wide.region_17.18_spmd, body=%wide.region_12.17_spmd.sunk | while | flops 154524224 | bytes 12099545 | solution.py:146
  58.6 7.8 %all-to-all-done = f32[16,6,4,128]{3,2,1,0:T(4,128)S(1)} async-done(((f32[16,6,4,128]{3,2,1,0:T(4,128)}), f32[16,6,4,128]{3,2,1,0:T(4,128)S(1)}, u32[]{:S(2)}, u32[]{:S(2)}) %all-to-all-start) | async-done | bytes 196640 | tf_op jit(solution)/shard_map/while/body/eval_jaxpr/all_to_all | solution.py:103
  68.4 3.5 %all-to-all-start.1 = ((f32[16,6,4,128]{3,2,1,0:T(4,128)}), f32[16,6,4,128]{3,2,1,0:T(4,128)S(1)}, u32[]{:S(2)}, u32[]{:S(2)}) async-start(f32[16,6,4,128]{3,2,1,0:T(4,128)} %select_add_fusion.8), calls=%async_computation.1 | async-start | bytes 393216 | tf_op jit(solution)/shard_map/while/body/eval_jaxpr/all_to_all | solution.py:103
  72.2 4.5 %multiply_reduce_fusion.17 = f32[24,4,128]{2,1,0:T(4,128)S(1)} fusion(f32[24,4,128,128]{3,2,1,0:T(8,128)} %get-tuple-element.432, f32[24,4,128]{2,1,0:T(4,128)S(1)} %get-tuple-element.403), kind=kLoop, calls=%fused_computation.8.clone.1 | loop fusion | flops 3133440 | bytes 6389760 | tf_op jit(solution)/shard_map/while/body/eval_jaxpr/reduce_sum | solution.py:16
  83.2 3.6 %all-to-all-start = ((f32[16,6,4,128]{3,2,1,0:T(4,128)}), f32[16,6,4,128]{3,2,1,0:T(4,128)S(1)}, u32[]{:S(2)}, u32[]{:S(2)}) async-start(f32[16,6,4,128]{3,2,1,0:T(4,128)} %bitcast.205), calls=%async_computation | async-start | bytes 393216 | tf_op jit(solution)/shard_map/while/body/eval_jaxpr/all_to_all | solution.py:103
  87.0 7.9 %all-to-all-done = f32[16,6,4,128]{3,2,1,0:T(4,128)S(1)} async-done(((f32[16,6,4,128]{3,2,1,0:T(4,128)}), f32[16,6,4,128]{3,2,1,0:T(4,128)S(1)}, u32[]{:S(2)}, u32[]{:S(2)}) %all-to-all-start) | async-done | bytes 196640 | tf_op jit(solution)/shard_map/while/body/eval_jaxpr/all_to_all | solution.py:103
  96.8 3.5 %all-to-all-start.1 = ((f32[16,6,4,128]{3,2,1,0:T(4,128)}), f32[16,6,4,128]{3,2,1,0:T(4,128)S(1)}, u32[]{:S(2)}, u32[]{:S(2)}) async-start(f32[16,6,4,128]{3,2,1,0:T(4,128)} %select_add_fusion.8), calls=%async_computation.1 | async-start | bytes 393216 | tf_op jit(solution)/shard_map/while/body/eval_jaxpr/all_to_all | solution.py:103
  100.6 4.5 %multiply_reduce_fusion.17 = f32[24,4,128]{2,1,0:T(4,128)S(1)} fusion(f32[24,4,128,128]{3,2,1,0:T(8,128)} %get-tuple-element.432, f32[24,4,128]{2,1,0:T(4,128)S(1)} %get-tuple-element.403), kind=kLoop, calls=%fused_computation.8.clone.1 | loop fusion | flops 3133440 | bytes 6389760 | tf_op jit(solution)/shard_map/while/body/eval_jaxpr/reduce_sum | solution.py:16
  111.7 3.6 %all-to-all-start = ((f32[16,6,4,128]{3,2,1,0:T(4,128)}), f32[16,6,4,128]{3,2,1,0:T(4,128)S(1)}, u32[]{:S(2)}, u32[]{:S(2)}) async-start(f32[16,6,4,128]{3,2,1,0:T(4,128)} %bitcast.205), calls=%async_computation | async-start | bytes 393216 | tf_op jit(solution)/shard_map/while/body/eval_jaxpr/all_to_all | solution.py:103
  115.5 7.9 %all-to-all-done = f32[16,6,4,128]{3,2,1,0:T(4,128)S(1)} async-done(((f32[16,6,4,128]{3,2,1,0:T(4,128)}), f32[16,6,4,128]{3,2,1,0:T(4,128)S(1)}, u32[]{:S(2)}, u32[]{:S(2)}) %all-to-all-start) | async-done | bytes 196640 | tf_op jit(solution)/shard_map/while/body/eval_jaxpr/all_to_all | solution.py:103
  125.3 3.5 %all-to-all-start.1 = ((f32[16,6,4,128]{3,2,1,0:T(4,128)}), f32[16,6,4,128]{3,2,1,0:T(4,128)S(1)}, u32[]{:S(2)}, u32[]{:S(2)}) async-start(f32[16,6,4,128]{3,2,1,0:T(4,128)} %select_add_fusion.8), calls=%async_computation.1 | async-start | bytes 393216 | tf_op jit(solution)/shard_map/while/body/eval_jaxpr/all_to_all | solution.py:103
  129.1 4.5 %multiply_reduce_fusion.17 = f32[24,4,128]{2,1,0:T(4,128)S(1)} fusion(f32[24,4,128,128]{3,2,1,0:T(8,128)} %get-tuple-element.432, f32[24,4,128]{2,1,0:T(4,128)S(1)} %get-tuple-element.403), kind=kLoop, calls=%fused_computation.8.clone.1 | loop fusion | flops 3133440 | bytes 6389760 | tf_op jit(solution)/shard_map/while/body/eval_jaxpr/reduce_sum | solution.py:16
  140.1 3.6 %all-to-all-start = ((f32[16,6,4,128]{3,2,1,0:T(4,128)}), f32[16,6,4,128]{3,2,1,0:T(4,128)S(1)}, u32[]{:S(2)}, u32[]{:S(2)}) async-start(f32[16,6,4,128]{3,2,1,0:T(4,128)} %bitcast.205), calls=%async_computation | async-start | bytes 393216 | tf_op jit(solution)/shard_map/while/body/eval_jaxpr/all_to_all | solution.py:103
  143.9 7.9 %all-to-all-done = f32[16,6,4,128]{3,2,1,0:T(4,128)S(1)} async-done(((f32[16,6,4,128]{3,2,1,0:T(4,128)}), f32[16,6,4,128]{3,2,1,0:T(4,128)S(1)}, u32[]{:S(2)}, u32[]{:S(2)}) %all-to-all-start) | async-done | bytes 196640 | tf_op jit(solution)/shard_map/while/body/eval_jaxpr/all_to_all | solution.py:103
  157.5 4.5 %multiply_reduce_fusion.17 = f32[24,4,128]{2,1,0:T(4,128)S(1)} fusion(f32[24,4,128,128]{3,2,1,0:T(8,128)} %get-tuple-element.432, f32[24,4,128]{2,1,0:T(4,128)S(1)} %get-tuple-element.403), kind=kLoop, calls=%fused_computation.8.clone.1 | loop fusion | flops 3133440 | bytes 6389760 | tf_op jit(solution)/shard_map/while/body/eval_jaxpr/reduce_sum | solution.py:16
  168.6 3.6 %all-to-all-start = ((f32[16,6,4,128]{3,2,1,0:T(4,128)}), f32[16,6,4,128]{3,2,1,0:T(4,128)S(1)}, u32[]{:S(2)}, u32[]{:S(2)}) async-start(f32[16,6,4,128]{3,2,1,0:T(4,128)} %bitcast.205), calls=%async_computation | async-start | bytes 393216 | tf_op jit(solution)/shard_map/while/body/eval_jaxpr/all_to_all | solution.py:103
  172.4 7.9 %all-to-all-done = f32[16,6,4,128]{3,2,1,0:T(4,128)S(1)} async-done(((f32[16,6,4,128]{3,2,1,0:T(4,128)}), f32[16,6,4,128]{3,2,1,0:T(4,128)S(1)}, u32[]{:S(2)}, u32[]{:S(2)}) %all-to-all-start) | async-done | bytes 196640 | tf_op jit(solution)/shard_map/while/body/eval_jaxpr/all_to_all | solution.py:103
  182.2 3.5 %all-to-all-start.1 = ((f32[16,6,4,128]{3,2,1,0:T(4,128)}), f32[16,6,4,128]{3,2,1,0:T(4,128)S(1)}, u32[]{:S(2)}, u32[]{:S(2)}) async-start(f32[16,6,4,128]{3,2,1,0:T(4,128)} %select_add_fusion.8), calls=%async_computation.1 | async-start | bytes 393216 | tf_op jit(solution)/shard_map/while/body/eval_jaxpr/all_to_all | solution.py:103
  186.0 4.5 %multiply_reduce_fusion.17 = f32[24,4,128]{2,1,0:T(4,128)S(1)} fusion(f32[24,4,128,128]{3,2,1,0:T(8,128)} %get-tuple-element.432, f32[24,4,128]{2,1,0:T(4,128)S(1)} %get-tuple-element.403), kind=kLoop, calls=%fused_computation.8.clone.1 | loop fusion | flops 3133440 | bytes 6389760 | tf_op jit(solution)/shard_map/while/body/eval_jaxpr/reduce_sum | solution.py:16
  197.0 3.6 %all-to-all-start = ((f32[16,6,4,128]{3,2,1,0:T(4,128)}), f32[16,6,4,128]{3,2,1,0:T(4,128)S(1)}, u32[]{:S(2)}, u32[]{:S(2)}) async-start(f32[16,6,4,128]{3,2,1,0:T(4,128)} %bitcast.205), calls=%async_computation | async-start | bytes 393216 | tf_op jit(solution)/shard_map/while/body/eval_jaxpr/all_to_all | solution.py:103
  200.8 8.0 %all-to-all-done = f32[16,6,4,128]{3,2,1,0:T(4,128)S(1)} async-done(((f32[16,6,4,128]{3,2,1,0:T(4,128)}), f32[16,6,4,128]{3,2,1,0:T(4,128)S(1)}, u32[]{:S(2)}, u32[]{:S(2)}) %all-to-all-start) | async-done | bytes 196640 | tf_op jit(solution)/shard_map/while/body/eval_jaxpr/all_to_all | solution.py:103
  214.5 4.5 %multiply_reduce_fusion.17 = f32[24,4,128]{2,1,0:T(4,128)S(1)} fusion(f32[24,4,128,128]{3,2,1,0:T(8,128)} %get-tuple-element.432, f32[24,4,128]{2,1,0:T(4,128)S(1)} %get-tuple-element.403), kind=kLoop, calls=%fused_computation.8.clone.1 | loop fusion | flops 3133440 | bytes 6389760 | tf_op jit(solution)/shard_map/while/body/eval_jaxpr/reduce_sum | solution.py:16
  219.0 3.6 %all-to-all-done.1 = f32[16,6,4,128]{3,2,1,0:T(4,128)S(1)} async-done(((f32[16,6,4,128]{3,2,1,0:T(4,128)}), f32[16,6,4,128]{3,2,1,0:T(4,128)S(1)}, u32[]{:S(2)}, u32[]{:S(2)}) %all-to-all-start.1) | async-done | bytes 196640 | tf_op jit(solution)/shard_map/while/body/eval_jaxpr/all_to_all | solution.py:103
  226.0 13.1 %all_to_all.32 = f32[16,6,8,128]{3,2,1,0:T(8,128)S(1)} all-to-all(f32[16,6,8,128]{3,2,1,0:T(8,128)S(1)} %bitcast.218), channel_id=1, replica_groups=mesh['req'=16,'head'=2] {'req'}, dimensions={0} | all-to-all | bytes 786432 | tf_op jit(solution)/shard_map/all_to_all | solution.py:103
  243.3 3.6 %all-to-all-start.5 = ((f32[16,6,12,128]{3,2,1,0:T(8,128)}), f32[16,6,12,128]{3,2,1,0:T(8,128)S(1)}, u32[]{:S(2)}, u32[]{:S(2)}) async-start(f32[16,6,12,128]{3,2,1,0:T(8,128)} %pad_maximum_fusion), calls=%async_computation.5 | async-start | bytes 1572864 | tf_op jit(solution)/shard_map/all_to_all | solution.py:103
  246.9 7.9 %multiply_reduce_fusion.4 = (f32[24,4,128]{2,1,0:T(4,128)S(1)}, f32[24,4,128]{2,1,0:T(4,128)S(1)}, f32[24,4,128]{2,1,0:T(4,128)S(1)}) fusion(f32[24,4,128,128]{3,2,1,0:T(8,128)} %param.26, f32[24,4,128]{2,1,0:T(4,128)S(1)} %get-tuple-element.94, f32[24,4,128]{2,1,0:T(4,128)S(1)} %get-tuple-element.95, f32[24,4,128,128]{3,2,1,0:T(8,128)} %get-tuple-element.438), kind=kLoop, calls=%fused_computation.34 | loop fusion | flops 9400320 | bytes 12828672 | tf_op jit(solution)/shard_map/reduce_sum | solution.py:16
  254.9 5.3 %all-to-all-done.5 = f32[16,6,12,128]{3,2,1,0:T(8,128)S(1)} async-done(((f32[16,6,12,128]{3,2,1,0:T(8,128)}), f32[16,6,12,128]{3,2,1,0:T(8,128)S(1)}, u32[]{:S(2)}, u32[]{:S(2)}) %all-to-all-start.5) | async-done | bytes 589856 | tf_op jit(solution)/shard_map/all_to_all | solution.py:103
  (276 shorter events, 89.7 us)
Async XLA Ops:
  0.0 262.1 %copy-start = (bf16[4,128,1024]{2,1,0:T(8,128)(2,1)S(1)}, bf16[4,128,1024]{2,1,0:T(8,128)(2,1)}, u32[]{:S(2)}) copy-start(bf16[4,128,1024]{2,1,0:T(8,128)(2,1)} %param.31) | copy-start | bytes 3145732
  0.0 13.3 %copy-start.6 = (f32[1024]{0:T(1024)S(1)}, f32[1024]{0:T(1024)}, u32[]{:S(2)}) copy-start(f32[1024]{0:T(1024)} %param.18) | copy-start | bytes 12292
  6.2 12.2 %copy-start.5 = (bf16[1024,2,4]{0,2,1:T(4,128)(2,1)S(1)}, bf16[1024,2,4]{0,2,1:T(4,128)(2,1)}, u32[]{:S(2)}) copy-start(bf16[1024,2,4]{0,2,1:T(4,128)(2,1)} %param.22) | copy-start | bytes 49156
  7.3 31.2 %copy-start.1 = (f32[2,4,128,128]{3,2,1,0:T(8,128)S(1)}, f32[2,4,128,128]{3,2,1,0:T(8,128)}, u32[]{:S(2)}) copy-start(f32[2,4,128,128]{3,2,1,0:T(8,128)} %param.27) | copy-start | bytes 1572868
  18.4 19.9 %all-to-all-start.2 = ((f32[16,6,5,128]{3,1,2,0:T(8,128)}), f32[16,6,5,128]{3,1,2,0:T(8,128)S(1)}, u32[]{:S(2)}, u32[]{:S(2)}) async-start(f32[16,6,5,128]{3,1,2,0:T(8,128)} %copy.161), calls=%async_computation.2 | async-start | bytes 655360 | tf_op jit(solution)/shard_map/all_to_all | solution.py:103
  27.0 25.8 %copy-start.4 = (f32[24,4]{0,1:T(4,128)S(1)}, f32[24,4]{0,1:T(4,128)}, u32[]{:S(2)}) copy-start(f32[24,4]{0,1:T(4,128)} %param.23) | copy-start | bytes 1156
  27.0 25.8 %copy-start.7 = (f32[4]{0:T(128)S(1)}, f32[4]{0:T(128)}, u32[]{:S(2)}) copy-start(f32[4]{0:T(128)} %param.24) | copy-start | bytes 52
  40.6 11.6 %all-to-all-start.3 = ((f32[16,6,4,128]{3,2,1,0:T(4,128)}), f32[16,6,4,128]{3,2,1,0:T(4,128)S(1)}, u32[]{:S(2)}, u32[]{:S(2)}) async-start(f32[16,6,4,128]{3,2,1,0:T(4,128)} %select_add_fusion.4), calls=%async_computation.3 | async-start | bytes 393216 | tf_op jit(solution)/shard_map/all_to_all | solution.py:103
  54.9 11.6 %all-to-all-start = ((f32[16,6,4,128]{3,2,1,0:T(4,128)}), f32[16,6,4,128]{3,2,1,0:T(4,128)S(1)}, u32[]{:S(2)}, u32[]{:S(2)}) async-start(f32[16,6,4,128]{3,2,1,0:T(4,128)} %bitcast.205), calls=%async_computation | async-start | bytes 393216 | tf_op jit(solution)/shard_map/while/body/eval_jaxpr/all_to_all | solution.py:103
  68.4 11.6 %all-to-all-start.1 = ((f32[16,6,4,128]{3,2,1,0:T(4,128)}), f32[16,6,4,128]{3,2,1,0:T(4,128)S(1)}, u32[]{:S(2)}, u32[]{:S(2)}) async-start(f32[16,6,4,128]{3,2,1,0:T(4,128)} %select_add_fusion.8), calls=%async_computation.1 | async-start | bytes 393216 | tf_op jit(solution)/shard_map/while/body/eval_jaxpr/all_to_all | solution.py:103
  83.2 11.7 %all-to-all-start = ((f32[16,6,4,128]{3,2,1,0:T(4,128)}), f32[16,6,4,128]{3,2,1,0:T(4,128)S(1)}, u32[]{:S(2)}, u32[]{:S(2)}) async-start(f32[16,6,4,128]{3,2,1,0:T(4,128)} %bitcast.205), calls=%async_computation | async-start | bytes 393216 | tf_op jit(solution)/shard_map/while/body/eval_jaxpr/all_to_all | solution.py:103
  96.8 11.6 %all-to-all-start.1 = ((f32[16,6,4,128]{3,2,1,0:T(4,128)}), f32[16,6,4,128]{3,2,1,0:T(4,128)S(1)}, u32[]{:S(2)}, u32[]{:S(2)}) async-start(f32[16,6,4,128]{3,2,1,0:T(4,128)} %select_add_fusion.8), calls=%async_computation.1 | async-start | bytes 393216 | tf_op jit(solution)/shard_map/while/body/eval_jaxpr/all_to_all | solution.py:103
  111.7 11.7 %all-to-all-start = ((f32[16,6,4,128]{3,2,1,0:T(4,128)}), f32[16,6,4,128]{3,2,1,0:T(4,128)S(1)}, u32[]{:S(2)}, u32[]{:S(2)}) async-start(f32[16,6,4,128]{3,2,1,0:T(4,128)} %bitcast.205), calls=%async_computation | async-start | bytes 393216 | tf_op jit(solution)/shard_map/while/body/eval_jaxpr/all_to_all | solution.py:103
  125.3 11.6 %all-to-all-start.1 = ((f32[16,6,4,128]{3,2,1,0:T(4,128)}), f32[16,6,4,128]{3,2,1,0:T(4,128)S(1)}, u32[]{:S(2)}, u32[]{:S(2)}) async-start(f32[16,6,4,128]{3,2,1,0:T(4,128)} %select_add_fusion.8), calls=%async_computation.1 | async-start | bytes 393216 | tf_op jit(solution)/shard_map/while/body/eval_jaxpr/all_to_all | solution.py:103
  140.1 11.7 %all-to-all-start = ((f32[16,6,4,128]{3,2,1,0:T(4,128)}), f32[16,6,4,128]{3,2,1,0:T(4,128)S(1)}, u32[]{:S(2)}, u32[]{:S(2)}) async-start(f32[16,6,4,128]{3,2,1,0:T(4,128)} %bitcast.205), calls=%async_computation | async-start | bytes 393216 | tf_op jit(solution)/shard_map/while/body/eval_jaxpr/all_to_all | solution.py:103
  153.7 11.6 %all-to-all-start.1 = ((f32[16,6,4,128]{3,2,1,0:T(4,128)}), f32[16,6,4,128]{3,2,1,0:T(4,128)S(1)}, u32[]{:S(2)}, u32[]{:S(2)}) async-start(f32[16,6,4,128]{3,2,1,0:T(4,128)} %select_add_fusion.8), calls=%async_computation.1 | async-start | bytes 393216 | tf_op jit(solution)/shard_map/while/body/eval_jaxpr/all_to_all | solution.py:103
  168.6 11.7 %all-to-all-start = ((f32[16,6,4,128]{3,2,1,0:T(4,128)}), f32[16,6,4,128]{3,2,1,0:T(4,128)S(1)}, u32[]{:S(2)}, u32[]{:S(2)}) async-start(f32[16,6,4,128]{3,2,1,0:T(4,128)} %bitcast.205), calls=%async_computation | async-start | bytes 393216 | tf_op jit(solution)/shard_map/while/body/eval_jaxpr/all_to_all | solution.py:103
  182.2 11.6 %all-to-all-start.1 = ((f32[16,6,4,128]{3,2,1,0:T(4,128)}), f32[16,6,4,128]{3,2,1,0:T(4,128)S(1)}, u32[]{:S(2)}, u32[]{:S(2)}) async-start(f32[16,6,4,128]{3,2,1,0:T(4,128)} %select_add_fusion.8), calls=%async_computation.1 | async-start | bytes 393216 | tf_op jit(solution)/shard_map/while/body/eval_jaxpr/all_to_all | solution.py:103
  197.0 11.8 %all-to-all-start = ((f32[16,6,4,128]{3,2,1,0:T(4,128)}), f32[16,6,4,128]{3,2,1,0:T(4,128)S(1)}, u32[]{:S(2)}, u32[]{:S(2)}) async-start(f32[16,6,4,128]{3,2,1,0:T(4,128)} %bitcast.205), calls=%async_computation | async-start | bytes 393216 | tf_op jit(solution)/shard_map/while/body/eval_jaxpr/all_to_all | solution.py:103
  210.7 11.9 %all-to-all-start.1 = ((f32[16,6,4,128]{3,2,1,0:T(4,128)}), f32[16,6,4,128]{3,2,1,0:T(4,128)S(1)}, u32[]{:S(2)}, u32[]{:S(2)}) async-start(f32[16,6,4,128]{3,2,1,0:T(4,128)} %select_add_fusion.8), calls=%async_computation.1 | async-start | bytes 393216 | tf_op jit(solution)/shard_map/while/body/eval_jaxpr/all_to_all | solution.py:103
  224.4 15.6 %copy-start.2 = (f32[2,4,128,128]{3,2,1,0:T(8,128)S(1)}, f32[2,4,128,128]{3,2,1,0:T(8,128)}, u32[]{:S(2)}) copy-start(f32[2,4,128,128]{3,2,1,0:T(8,128)} %param.28) | copy-start | bytes 1572868
  243.3 16.8 %all-to-all-start.5 = ((f32[16,6,12,128]{3,2,1,0:T(8,128)}), f32[16,6,12,128]{3,2,1,0:T(8,128)S(1)}, u32[]{:S(2)}, u32[]{:S(2)}) async-start(f32[16,6,12,128]{3,2,1,0:T(8,128)} %pad_maximum_fusion), calls=%async_computation.5 | async-start | bytes 1572864 | tf_op jit(solution)/shard_map/all_to_all | solution.py:103
  246.9 16.8 %copy-start.3 = (bf16[24,512]{1,0:T(8,128)(2,1)S(1)}, bf16[24,512]{1,0:T(8,128)(2,1)}, u32[]{:S(2)}) copy-start(bf16[24,512]{1,0:T(8,128)(2,1)} %param.17) | copy-start | bytes 73732
  262.4 1.3 collective-permute-start

commit v12 on v8

--- a/solution.py
+++ b/solution.py
@@ -33,7 +33,16 @@
     lengths,
     out_weight,
 ):
-    gathered = lax.all_gather(hidden, "head", axis=1, tiled=True)
+    if lax.axis_size("head") == 2:
+        other_half = lax.ppermute(hidden, "head", [(0, 1), (1, 0)])
+        first_core = lax.axis_index("head") == 0
+        gathered = jnp.where(
+            first_core,
+            jnp.concatenate([hidden, other_half], axis=1),
+            jnp.concatenate([other_half, hidden], axis=1),
+        )
+    else:
+        gathered = lax.all_gather(hidden, "head", axis=1, tiled=True)
     widened = gathered.astype(jnp.float32)
     scaled = (
         widened

time: 266 us -> 264 us (level)
  transfers between devices with their start and end apart: 16 -> 17, of which waited for: 16 -> 16; matrix products, arithmetic and copies ran while one was open for 16% -> 20% of each run, Pallas kernels for 0% -> 0%
where the time goes in v12:
time: 264 us; the launch traced here: 262 us
  waiting for transfers between devices  88.8 us (34%)
  other arithmetic  59.1 us (22%)
  starting transfers between devices  58.3 us (22%)
  local copies, waits for them, and re-layouts  32 us (12%)
  blocking collectives  13.1 us (5%)
  matrix products  9.7 us (4%)
    all_to_all x15, waiting for transfers between devices, exchange(): lax.all_to_all(shaped, 'req', split_axis=0, concat_axis=0, tiled=True)  87.6 us
    all_to_all x15, starting transfers between devices, exchange(): lax.all_to_all(shaped, 'req', split_axis=0, concat_axis=0, tiled=True)  57.8 us
    reduce_sum x8, other arithmetic, own_matvec(): return jnp.sum(matrices * vectors[:, :, None, :], axis=3)  39.3 us
    all_to_all x1, blocking collectives, exchange(): lax.all_to_all(shaped, 'req', split_axis=0, concat_axis=0, tiled=True)  13.1 us
    gather x9, local copies, waits for them, and re-layouts, pack(): return jnp.take(padded, source, axis=0, mode='clip')  10.3 us
    add x8, other arithmetic, owner_apply(): total + jnp.where(chosen[group][:, None, None], products[group], 0.0)  6.94 us
    dot_general x10, matrix products, owner_apply(): products = jnp.einsum('shj,ghij->gshi', incoming, states, precision=highest)  6.33 us
    unnamed x19, local copies, waits for them, and re-layouts  6.13 us
  transfers between devices with their start and end apart: 17, of which 16 were waited for; matrix products, arithmetic and copies ran while one was open for 20% of the time, Pallas kernels for 0%

profile of v12, /device:TPU:0, one launch (start us, length us, event | category | flops | bytes accessed | tf_op | source)
XLA Modules:
  0.0 262.3 jit_solution(1842385298943751808)
XLA Ops:
  5.4 6.0 %copy.151 = bf16[1024,4,3,128]{0,3,2,1:T(8,128)(2,1)} copy(bf16[1024,4,3,128]{3,1,2,0:T(4,128)(2,1)} %param.19) | data formatting | bytes 6291456 | tf_op args[2]
  16.5 7.9 %all-to-all-start.2 = ((f32[16,6,5,128]{3,1,2,0:T(8,128)}), f32[16,6,5,128]{3,1,2,0:T(8,128)S(1)}, u32[]{:S(2)}, u32[]{:S(2)}) async-start(f32[16,6,5,128]{3,1,2,0:T(8,128)} %copy.161), calls=%async_computation.2 | async-start | bytes 655360 | tf_op jit(solution)/shard_map/all_to_all | solution.py:112
  24.9 11.5 %all-to-all-done.2 = f32[16,6,5,128]{3,1,2,0:T(8,128)S(1)} async-done(((f32[16,6,5,128]{3,1,2,0:T(8,128)}), f32[16,6,5,128]{3,1,2,0:T(8,128)S(1)}, u32[]{:S(2)}, u32[]{:S(2)}) %all-to-all-start.2) | async-done | bytes 245792 | tf_op jit(solution)/shard_map/all_to_all | solution.py:112
  38.6 3.5 %all-to-all-start.3 = ((f32[16,6,4,128]{3,2,1,0:T(4,128)}), f32[16,6,4,128]{3,2,1,0:T(4,128)S(1)}, u32[]{:S(2)}, u32[]{:S(2)}) async-start(f32[16,6,4,128]{3,2,1,0:T(4,128)} %select_add_fusion.4), calls=%async_computation.3 | async-start | bytes 393216 | tf_op jit(solution)/shard_map/all_to_all | solution.py:112
  42.2 4.5 %multiply_reduce_fusion.7 = f32[24,4,128]{2,1,0:T(4,128)S(1)} fusion(f32[24,4,128,128]{3,2,1,0:T(8,128)} %param.25, f32[24,4,128]{2,1,0:T(4,128)S(1)} %copy.167), kind=kLoop, calls=%fused_computation.33 | loop fusion | flops 3133440 | bytes 6389760 | tf_op jit(solution)/shard_map/reduce_sum | solution.py:16
  51.5 170.9 %while.16 = (s32[]{:T(128)}, f32[24,4,128]{2,1,0:T(4,128)S(1)}, f32[24,4,128]{2,1,0:T(4,128)S(1)}, f32[24,4,128]{2,1,0:T(4,128)S(1)}, f32[24,4,1]{0,1,2:T(4,128)...) while((s32[]{:T(128)}, f32[24,4,128]{2,1,0:T(4,128)S(1)}, ...), condition=%wide.region_17.18_spmd, body=%wide.region_12.17_spmd.sunk | while | flops 154523872 | bytes 12098585 | solution.py:155
  56.7 7.9 %all-to-all-done = f32[16,6,4,128]{3,2,1,0:T(4,128)S(1)} async-done(((f32[16,6,4,128]{3,2,1,0:T(4,128)}), f32[16,6,4,128]{3,2,1,0:T(4,128)S(1)}, u32[]{:S(2)}, u32[]{:S(2)}) %all-to-all-start) | async-done | bytes 196640 | tf_op jit(solution)/shard_map/while/body/eval_jaxpr/all_to_all | solution.py:112
  66.4 3.5 %all-to-all-start.1 = ((f32[16,6,4,128]{3,2,1,0:T(4,128)}), f32[16,6,4,128]{3,2,1,0:T(4,128)S(1)}, u32[]{:S(2)}, u32[]{:S(2)}) async-start(f32[16,6,4,128]{3,2,1,0:T(4,128)} %select_add_fusion.7), calls=%async_computation.1 | async-start | bytes 393216 | tf_op jit(solution)/shard_map/while/body/eval_jaxpr/all_to_all | solution.py:112
  70.2 4.5 %multiply_reduce_fusion.17 = f32[24,4,128]{2,1,0:T(4,128)S(1)} fusion(f32[24,4,128,128]{3,2,1,0:T(8,128)} %get-tuple-element.428, f32[24,4,128]{2,1,0:T(4,128)S(1)} %get-tuple-element.399), kind=kLoop, calls=%fused_computation.8.clone.1 | loop fusion | flops 3133440 | bytes 6389760 | tf_op jit(solution)/shard_map/while/body/eval_jaxpr/reduce_sum | solution.py:16
  81.2 3.6 %all-to-all-start = ((f32[16,6,4,128]{3,2,1,0:T(4,128)}), f32[16,6,4,128]{3,2,1,0:T(4,128)S(1)}, u32[]{:S(2)}, u32[]{:S(2)}) async-start(f32[16,6,4,128]{3,2,1,0:T(4,128)} %bitcast.185), calls=%async_computation | async-start | bytes 393216 | tf_op jit(solution)/shard_map/while/body/eval_jaxpr/all_to_all | solution.py:112
  85.1 7.9 %all-to-all-done = f32[16,6,4,128]{3,2,1,0:T(4,128)S(1)} async-done(((f32[16,6,4,128]{3,2,1,0:T(4,128)}), f32[16,6,4,128]{3,2,1,0:T(4,128)S(1)}, u32[]{:S(2)}, u32[]{:S(2)}) %all-to-all-start) | async-done | bytes 196640 | tf_op jit(solution)/shard_map/while/body/eval_jaxpr/all_to_all | solution.py:112
  98.6 4.5 %multiply_reduce_fusion.17 = f32[24,4,128]{2,1,0:T(4,128)S(1)} fusion(f32[24,4,128,128]{3,2,1,0:T(8,128)} %get-tuple-element.428, f32[24,4,128]{2,1,0:T(4,128)S(1)} %get-tuple-element.399), kind=kLoop, calls=%fused_computation.8.clone.1 | loop fusion | flops 3133440 | bytes 6389760 | tf_op jit(solution)/shard_map/while/body/eval_jaxpr/reduce_sum | solution.py:16
  109.7 3.6 %all-to-all-start = ((f32[16,6,4,128]{3,2,1,0:T(4,128)}), f32[16,6,4,128]{3,2,1,0:T(4,128)S(1)}, u32[]{:S(2)}, u32[]{:S(2)}) async-start(f32[16,6,4,128]{3,2,1,0:T(4,128)} %bitcast.185), calls=%async_computation | async-start | bytes 393216 | tf_op jit(solution)/shard_map/while/body/eval_jaxpr/all_to_all | solution.py:112
  113.5 7.9 %all-to-all-done = f32[16,6,4,128]{3,2,1,0:T(4,128)S(1)} async-done(((f32[16,6,4,128]{3,2,1,0:T(4,128)}), f32[16,6,4,128]{3,2,1,0:T(4,128)S(1)}, u32[]{:S(2)}, u32[]{:S(2)}) %all-to-all-start) | async-done | bytes 196640 | tf_op jit(solution)/shard_map/while/body/eval_jaxpr/all_to_all | solution.py:112
  127.1 4.5 %multiply_reduce_fusion.17 = f32[24,4,128]{2,1,0:T(4,128)S(1)} fusion(f32[24,4,128,128]{3,2,1,0:T(8,128)} %get-tuple-element.428, f32[24,4,128]{2,1,0:T(4,128)S(1)} %get-tuple-element.399), kind=kLoop, calls=%fused_computation.8.clone.1 | loop fusion | flops 3133440 | bytes 6389760 | tf_op jit(solution)/shard_map/while/body/eval_jaxpr/reduce_sum | solution.py:16
  138.1 3.6 %all-to-all-start = ((f32[16,6,4,128]{3,2,1,0:T(4,128)}), f32[16,6,4,128]{3,2,1,0:T(4,128)S(1)}, u32[]{:S(2)}, u32[]{:S(2)}) async-start(f32[16,6,4,128]{3,2,1,0:T(4,128)} %bitcast.185), calls=%async_computation | async-start | bytes 393216 | tf_op jit(solution)/shard_map/while/body/eval_jaxpr/all_to_all | solution.py:112
  141.9 7.9 %all-to-all-done = f32[16,6,4,128]{3,2,1,0:T(4,128)S(1)} async-done(((f32[16,6,4,128]{3,2,1,0:T(4,128)}), f32[16,6,4,128]{3,2,1,0:T(4,128)S(1)}, u32[]{:S(2)}, u32[]{:S(2)}) %all-to-all-start) | async-done | bytes 196640 | tf_op jit(solution)/shard_map/while/body/eval_jaxpr/all_to_all | solution.py:112
  151.7 3.5 %all-to-all-start.1 = ((f32[16,6,4,128]{3,2,1,0:T(4,128)}), f32[16,6,4,128]{3,2,1,0:T(4,128)S(1)}, u32[]{:S(2)}, u32[]{:S(2)}) async-start(f32[16,6,4,128]{3,2,1,0:T(4,128)} %select_add_fusion.7), calls=%async_computation.1 | async-start | bytes 393216 | tf_op jit(solution)/shard_map/while/body/eval_jaxpr/all_to_all | solution.py:112
  155.5 4.5 %multiply_reduce_fusion.17 = f32[24,4,128]{2,1,0:T(4,128)S(1)} fusion(f32[24,4,128,128]{3,2,1,0:T(8,128)} %get-tuple-element.428, f32[24,4,128]{2,1,0:T(4,128)S(1)} %get-tuple-element.399), kind=kLoop, calls=%fused_computation.8.clone.1 | loop fusion | flops 3133440 | bytes 6389760 | tf_op jit(solution)/shard_map/while/body/eval_jaxpr/reduce_sum | solution.py:16
  166.5 3.6 %all-to-all-start = ((f32[16,6,4,128]{3,2,1,0:T(4,128)}), f32[16,6,4,128]{3,2,1,0:T(4,128)S(1)}, u32[]{:S(2)}, u32[]{:S(2)}) async-start(f32[16,6,4,128]{3,2,1,0:T(4,128)} %bitcast.185), calls=%async_computation | async-start | bytes 393216 | tf_op jit(solution)/shard_map/while/body/eval_jaxpr/all_to_all | solution.py:112
  170.3 7.9 %all-to-all-done = f32[16,6,4,128]{3,2,1,0:T(4,128)S(1)} async-done(((f32[16,6,4,128]{3,2,1,0:T(4,128)}), f32[16,6,4,128]{3,2,1,0:T(4,128)S(1)}, u32[]{:S(2)}, u32[]{:S(2)}) %all-to-all-start) | async-done | bytes 196640 | tf_op jit(solution)/shard_map/while/body/eval_jaxpr/all_to_all | solution.py:112
  180.1 3.5 %all-to-all-start.1 = ((f32[16,6,4,128]{3,2,1,0:T(4,128)}), f32[16,6,4,128]{3,2,1,0:T(4,128)S(1)}, u32[]{:S(2)}, u32[]{:S(2)}) async-start(f32[16,6,4,128]{3,2,1,0:T(4,128)} %select_add_fusion.7), calls=%async_computation.1 | async-start | bytes 393216 | tf_op jit(solution)/shard_map/while/body/eval_jaxpr/all_to_all | solution.py:112
  183.9 4.5 %multiply_reduce_fusion.17 = f32[24,4,128]{2,1,0:T(4,128)S(1)} fusion(f32[24,4,128,128]{3,2,1,0:T(8,128)} %get-tuple-element.428, f32[24,4,128]{2,1,0:T(4,128)S(1)} %get-tuple-element.399), kind=kLoop, calls=%fused_computation.8.clone.1 | loop fusion | flops 3133440 | bytes 6389760 | tf_op jit(solution)/shard_map/while/body/eval_jaxpr/reduce_sum | solution.py:16
  195.0 3.6 %all-to-all-start = ((f32[16,6,4,128]{3,2,1,0:T(4,128)}), f32[16,6,4,128]{3,2,1,0:T(4,128)S(1)}, u32[]{:S(2)}, u32[]{:S(2)}) async-start(f32[16,6,4,128]{3,2,1,0:T(4,128)} %bitcast.185), calls=%async_computation | async-start | bytes 393216 | tf_op jit(solution)/shard_map/while/body/eval_jaxpr/all_to_all | solution.py:112
  198.8 8.0 %all-to-all-done = f32[16,6,4,128]{3,2,1,0:T(4,128)S(1)} async-done(((f32[16,6,4,128]{3,2,1,0:T(4,128)}), f32[16,6,4,128]{3,2,1,0:T(4,128)S(1)}, u32[]{:S(2)}, u32[]{:S(2)}) %all-to-all-start) | async-done | bytes 196640 | tf_op jit(solution)/shard_map/while/body/eval_jaxpr/all_to_all | solution.py:112
  208.7 3.5 %all-to-all-start.1 = ((f32[16,6,4,128]{3,2,1,0:T(4,128)}), f32[16,6,4,128]{3,2,1,0:T(4,128)S(1)}, u32[]{:S(2)}, u32[]{:S(2)}) async-start(f32[16,6,4,128]{3,2,1,0:T(4,128)} %select_add_fusion.7), calls=%async_computation.1 | async-start | bytes 393216 | tf_op jit(solution)/shard_map/while/body/eval_jaxpr/all_to_all | solution.py:112
  212.5 4.5 %multiply_reduce_fusion.17 = f32[24,4,128]{2,1,0:T(4,128)S(1)} fusion(f32[24,4,128,128]{3,2,1,0:T(8,128)} %get-tuple-element.428, f32[24,4,128]{2,1,0:T(4,128)S(1)} %get-tuple-element.399), kind=kLoop, calls=%fused_computation.8.clone.1 | loop fusion | flops 3133440 | bytes 6389760 | tf_op jit(solution)/shard_map/while/body/eval_jaxpr/reduce_sum | solution.py:16
  217.0 3.6 %all-to-all-done.1 = f32[16,6,4,128]{3,2,1,0:T(4,128)S(1)} async-done(((f32[16,6,4,128]{3,2,1,0:T(4,128)}), f32[16,6,4,128]{3,2,1,0:T(4,128)S(1)}, u32[]{:S(2)}, u32[]{:S(2)}) %all-to-all-start.1) | async-done | bytes 196640 | tf_op jit(solution)/shard_map/while/body/eval_jaxpr/all_to_all | solution.py:112
  223.9 13.1 %all_to_all.32 = f32[16,6,8,128]{3,2,1,0:T(8,128)S(1)} all-to-all(f32[16,6,8,128]{3,2,1,0:T(8,128)S(1)} %bitcast.198), channel_id=1, replica_groups=mesh['req'=16,'head'=2] {'req'}, dimensions={0} | all-to-all | bytes 786432 | tf_op jit(solution)/shard_map/all_to_all | solution.py:112
  241.3 3.6 %all-to-all-start.5 = ((f32[16,6,12,128]{3,2,1,0:T(8,128)}), f32[16,6,12,128]{3,2,1,0:T(8,128)S(1)}, u32[]{:S(2)}, u32[]{:S(2)}) async-start(f32[16,6,12,128]{3,2,1,0:T(8,128)} %pad_maximum_fusion), calls=%async_computation.5 | async-start | bytes 1572864 | tf_op jit(solution)/shard_map/all_to_all | solution.py:112
  244.9 7.9 %multiply_reduce_fusion.4 = (f32[24,4,128]{2,1,0:T(4,128)S(1)}, f32[24,4,128]{2,1,0:T(4,128)S(1)}, f32[24,4,128]{2,1,0:T(4,128)S(1)}) fusion(f32[24,4,128,128]{3,2,1,0:T(8,128)} %param.26, f32[24,4,128]{2,1,0:T(4,128)S(1)} %get-tuple-element.94, f32[24,4,128]{2,1,0:T(4,128)S(1)} %get-tuple-element.95, f32[24,4,128,128]{3,2,1,0:T(8,128)} %get-tuple-element.434), kind=kLoop, calls=%fused_computation.30 | loop fusion | flops 9400320 | bytes 12828672 | tf_op jit(solution)/shard_map/reduce_sum | solution.py:16
  252.8 5.3 %all-to-all-done.5 = f32[16,6,12,128]{3,2,1,0:T(8,128)S(1)} async-done(((f32[16,6,12,128]{3,2,1,0:T(8,128)}), f32[16,6,12,128]{3,2,1,0:T(8,128)S(1)}, u32[]{:S(2)}, u32[]{:S(2)}) %all-to-all-start.5) | async-done | bytes 589856 | tf_op jit(solution)/shard_map/all_to_all | solution.py:112
  (264 shorter events, 87.7 us)
Async XLA Ops:
  0.0 260.0 %copy-start = (bf16[4,128,1024]{2,1,0:T(8,128)(2,1)S(1)}, bf16[4,128,1024]{2,1,0:T(8,128)(2,1)}, u32[]{:S(2)}) copy-start(bf16[4,128,1024]{2,1,0:T(8,128)(2,1)} %param.31) | copy-start | bytes 3145732
  0.0 11.5 %copy-start.3 = (bf16[24,512]{1,0:T(8,128)(2,1)S(1)}, bf16[24,512]{1,0:T(8,128)(2,1)}, u32[]{:S(2)}) copy-start(bf16[24,512]{1,0:T(8,128)(2,1)} %param.17) | copy-start | bytes 73732
  0.0 11.6 %copy-start.6 = (f32[1024]{0:T(1024)S(1)}, f32[1024]{0:T(1024)}, u32[]{:S(2)}) copy-start(f32[1024]{0:T(1024)} %param.18) | copy-start | bytes 12292
  0.0 11.5 %collective-permute-start = (bf16[24,512]{1,0:T(8,128)(2,1)}, bf16[24,512]{1,0:T(8,128)(2,1)S(1)}, u32[]{:S(2)}, u32[]{:S(2)}) collective-permute-start(bf16[24,512]{1,0:T(8,128)(2,1)} %param.17), channel_id=1, source_target_pairs={{0,1},{1,0},{2,3},{3,2},{4,5},{5,4},{6,7},{7,6},{8,9},{9,8},{10,11... | collective-permute-start | bytes 73736 | tf_op jit(solution)/shard_map/ppermute | solution.py:37
  5.4 19.1 %copy-start.5 = (bf16[1024,2,4]{0,2,1:T(4,128)(2,1)S(1)}, bf16[1024,2,4]{0,2,1:T(4,128)(2,1)}, u32[]{:S(2)}) copy-start(bf16[1024,2,4]{0,2,1:T(4,128)(2,1)} %param.22) | copy-start | bytes 49156
  5.4 19.1 %copy-start.1 = (f32[2,4,128,128]{3,2,1,0:T(8,128)S(1)}, f32[2,4,128,128]{3,2,1,0:T(8,128)}, u32[]{:S(2)}) copy-start(f32[2,4,128,128]{3,2,1,0:T(8,128)} %param.27) | copy-start | bytes 1572868
  16.5 19.9 %all-to-all-start.2 = ((f32[16,6,5,128]{3,1,2,0:T(8,128)}), f32[16,6,5,128]{3,1,2,0:T(8,128)S(1)}, u32[]{:S(2)}, u32[]{:S(2)}) async-start(f32[16,6,5,128]{3,1,2,0:T(8,128)} %copy.161), calls=%async_computation.2 | async-start | bytes 655360 | tf_op jit(solution)/shard_map/all_to_all | solution.py:112
  24.6 26.3 %copy-start.4 = (f32[24,4]{0,1:T(4,128)S(1)}, f32[24,4]{0,1:T(4,128)}, u32[]{:S(2)}) copy-start(f32[24,4]{0,1:T(4,128)} %param.23) | copy-start | bytes 1156
  24.6 26.3 %copy-start.7 = (f32[4]{0:T(128)S(1)}, f32[4]{0:T(128)}, u32[]{:S(2)}) copy-start(f32[4]{0:T(128)} %param.24) | copy-start | bytes 52
  38.6 11.6 %all-to-all-start.3 = ((f32[16,6,4,128]{3,2,1,0:T(4,128)}), f32[16,6,4,128]{3,2,1,0:T(4,128)S(1)}, u32[]{:S(2)}, u32[]{:S(2)}) async-start(f32[16,6,4,128]{3,2,1,0:T(4,128)} %select_add_fusion.4), calls=%async_computation.3 | async-start | bytes 393216 | tf_op jit(solution)/shard_map/all_to_all | solution.py:112
  52.9 11.6 %all-to-all-start = ((f32[16,6,4,128]{3,2,1,0:T(4,128)}), f32[16,6,4,128]{3,2,1,0:T(4,128)S(1)}, u32[]{:S(2)}, u32[]{:S(2)}) async-start(f32[16,6,4,128]{3,2,1,0:T(4,128)} %bitcast.185), calls=%async_computation | async-start | bytes 393216 | tf_op jit(solution)/shard_map/while/body/eval_jaxpr/all_to_all | solution.py:112
  66.4 11.6 %all-to-all-start.1 = ((f32[16,6,4,128]{3,2,1,0:T(4,128)}), f32[16,6,4,128]{3,2,1,0:T(4,128)S(1)}, u32[]{:S(2)}, u32[]{:S(2)}) async-start(f32[16,6,4,128]{3,2,1,0:T(4,128)} %select_add_fusion.7), calls=%async_computation.1 | async-start | bytes 393216 | tf_op jit(solution)/shard_map/while/body/eval_jaxpr/all_to_all | solution.py:112
  81.2 11.7 %all-to-all-start = ((f32[16,6,4,128]{3,2,1,0:T(4,128)}), f32[16,6,4,128]{3,2,1,0:T(4,128)S(1)}, u32[]{:S(2)}, u32[]{:S(2)}) async-start(f32[16,6,4,128]{3,2,1,0:T(4,128)} %bitcast.185), calls=%async_computation | async-start | bytes 393216 | tf_op jit(solution)/shard_map/while/body/eval_jaxpr/all_to_all | solution.py:112
  94.8 11.6 %all-to-all-start.1 = ((f32[16,6,4,128]{3,2,1,0:T(4,128)}), f32[16,6,4,128]{3,2,1,0:T(4,128)S(1)}, u32[]{:S(2)}, u32[]{:S(2)}) async-start(f32[16,6,4,128]{3,2,1,0:T(4,128)} %select_add_fusion.7), calls=%async_computation.1 | async-start | bytes 393216 | tf_op jit(solution)/shard_map/while/body/eval_jaxpr/all_to_all | solution.py:112
  109.7 11.7 %all-to-all-start = ((f32[16,6,4,128]{3,2,1,0:T(4,128)}), f32[16,6,4,128]{3,2,1,0:T(4,128)S(1)}, u32[]{:S(2)}, u32[]{:S(2)}) async-start(f32[16,6,4,128]{3,2,1,0:T(4,128)} %bitcast.185), calls=%async_computation | async-start | bytes 393216 | tf_op jit(solution)/shard_map/while/body/eval_jaxpr/all_to_all | solution.py:112
  123.3 11.6 %all-to-all-start.1 = ((f32[16,6,4,128]{3,2,1,0:T(4,128)}), f32[16,6,4,128]{3,2,1,0:T(4,128)S(1)}, u32[]{:S(2)}, u32[]{:S(2)}) async-start(f32[16,6,4,128]{3,2,1,0:T(4,128)} %select_add_fusion.7), calls=%async_computation.1 | async-start | bytes 393216 | tf_op jit(solution)/shard_map/while/body/eval_jaxpr/all_to_all | solution.py:112
  138.1 11.7 %all-to-all-start = ((f32[16,6,4,128]{3,2,1,0:T(4,128)}), f32[16,6,4,128]{3,2,1,0:T(4,128)S(1)}, u32[]{:S(2)}, u32[]{:S(2)}) async-start(f32[16,6,4,128]{3,2,1,0:T(4,128)} %bitcast.185), calls=%async_computation | async-start | bytes 393216 | tf_op jit(solution)/shard_map/while/body/eval_jaxpr/all_to_all | solution.py:112
  151.7 11.6 %all-to-all-start.1 = ((f32[16,6,4,128]{3,2,1,0:T(4,128)}), f32[16,6,4,128]{3,2,1,0:T(4,128)S(1)}, u32[]{:S(2)}, u32[]{:S(2)}) async-start(f32[16,6,4,128]{3,2,1,0:T(4,128)} %select_add_fusion.7), calls=%async_computation.1 | async-start | bytes 393216 | tf_op jit(solution)/shard_map/while/body/eval_jaxpr/all_to_all | solution.py:112
  166.5 11.7 %all-to-all-start = ((f32[16,6,4,128]{3,2,1,0:T(4,128)}), f32[16,6,4,128]{3,2,1,0:T(4,128)S(1)}, u32[]{:S(2)}, u32[]{:S(2)}) async-start(f32[16,6,4,128]{3,2,1,0:T(4,128)} %bitcast.185), calls=%async_computation | async-start | bytes 393216 | tf_op jit(solution)/shard_map/while/body/eval_jaxpr/all_to_all | solution.py:112
  180.1 11.6 %all-to-all-start.1 = ((f32[16,6,4,128]{3,2,1,0:T(4,128)}), f32[16,6,4,128]{3,2,1,0:T(4,128)S(1)}, u32[]{:S(2)}, u32[]{:S(2)}) async-start(f32[16,6,4,128]{3,2,1,0:T(4,128)} %select_add_fusion.7), calls=%async_computation.1 | async-start | bytes 393216 | tf_op jit(solution)/shard_map/while/body/eval_jaxpr/all_to_all | solution.py:112
  195.0 11.8 %all-to-all-start = ((f32[16,6,4,128]{3,2,1,0:T(4,128)}), f32[16,6,4,128]{3,2,1,0:T(4,128)S(1)}, u32[]{:S(2)}, u32[]{:S(2)}) async-start(f32[16,6,4,128]{3,2,1,0:T(4,128)} %bitcast.185), calls=%async_computation | async-start | bytes 393216 | tf_op jit(solution)/shard_map/while/body/eval_jaxpr/all_to_all | solution.py:112
  208.7 11.9 %all-to-all-start.1 = ((f32[16,6,4,128]{3,2,1,0:T(4,128)}), f32[16,6,4,128]{3,2,1,0:T(4,128)S(1)}, u32[]{:S(2)}, u32[]{:S(2)}) async-start(f32[16,6,4,128]{3,2,1,0:T(4,128)} %select_add_fusion.7), calls=%async_computation.1 | async-start | bytes 393216 | tf_op jit(solution)/shard_map/while/body/eval_jaxpr/all_to_all | solution.py:112
  222.4 15.6 %copy-start.2 = (f32[2,4,128,128]{3,2,1,0:T(8,128)S(1)}, f32[2,4,128,128]{3,2,1,0:T(8,128)}, u32[]{:S(2)}) copy-start(f32[2,4,128,128]{3,2,1,0:T(8,128)} %param.28) | copy-start | bytes 1572868
  241.3 16.8 %all-to-all-start.5 = ((f32[16,6,12,128]{3,2,1,0:T(8,128)}), f32[16,6,12,128]{3,2,1,0:T(8,128)S(1)}, u32[]{:S(2)}, u32[]{:S(2)}) async-start(f32[16,6,12,128]{3,2,1,0:T(8,128)} %pad_maximum_fusion), calls=%async_computation.5 | async-start | bytes 1572864 | tf_op jit(solution)/shard_map/all_to_all | solution.py:112
  260.4 1.3 collective-permute-start.1

commit v13 on v12

--- a/solution.py
+++ b/solution.py
@@ -157,7 +157,9 @@
     )
     solution, residual, direction, norm_now = carry
 
-    both = exchange(jnp.concatenate([pack(direction), pack(solution)], axis=1))
+    both = exchange(
+        jnp.concatenate([pack(direction), pack(solution)], axis=1).astype(jnp.bfloat16)
+    ).astype(jnp.float32)
     held = both[:, :head_count]
     owner_out = jnp.concatenate(
         [
@@ -167,7 +169,7 @@
         ],
         axis=1,
     )
-    returned = unpack(exchange(owner_out))
+    returned = unpack(exchange(owner_out.astype(jnp.bfloat16)).astype(jnp.float32))
     own_out_partial = own_matvec(own_values, solution)
     own_out_direction = own_matvec(own_values, direction)
     partial = solution

time: 264 us -> 259 us (0.981)
  blocking collectives: 13.1 us -> 0 us
  waiting for transfers between devices: 88.8 us -> 93.1 us
  starting transfers between devices: 58.3 us -> 62 us
    all_to_all x1 -> x0, blocking collectives: 13.1 us -> none  [exchange(): lax.all_to_all(shaped, 'req', split_axis=0, concat_axis=0, tiled=True)]
    all_to_all x15 -> x16, waiting for transfers between devices: 87.6 us -> 91.8 us  [exchange(): lax.all_to_all(shaped, 'req', split_axis=0, concat_axis=0, tiled=True)]
    all_to_all x15 -> x16, starting transfers between devices: 57.8 us -> 61.4 us  [exchange(): lax.all_to_all(shaped, 'req', split_axis=0, concat_axis=0, tiled=True)]
    add x8 -> x7, other arithmetic: 6.94 us -> 6.62 us  [owner_apply(): total + jnp.where(chosen[group][:, None, None], products[group], 0.0)]
  transfers between devices with their start and end apart: 17 -> 18, of which waited for: 16 -> 17; matrix products, arithmetic and copies ran while one was open for 20% -> 21% of each run, Pallas kernels for 0% -> 0%
where the time goes in v13:
time: 259 us; the launch traced here: 257 us
  waiting for transfers between devices  93.1 us (36%)
  starting transfers between devices  62 us (24%)
  other arithmetic  59.9 us (23%)
  local copies, waits for them, and re-layouts  32.2 us (12%)
  matrix products  9.03 us (3%)
    all_to_all x16, waiting for transfers between devices, exchange(): lax.all_to_all(shaped, 'req', split_axis=0, concat_axis=0, tiled=True)  91.8 us
    all_to_all x16, starting transfers between devices, exchange(): lax.all_to_all(shaped, 'req', split_axis=0, concat_axis=0, tiled=True)  61.4 us
    reduce_sum x8, other arithmetic, own_matvec(): return jnp.sum(matrices * vectors[:, :, None, :], axis=3)  39.3 us
    gather x9, local copies, waits for them, and re-layouts, pack(): return jnp.take(padded, source, axis=0, mode='clip')  10.3 us
    add x7, other arithmetic, owner_apply(): total + jnp.where(chosen[group][:, None, None], products[group], 0.0)  6.62 us
    unnamed x19, local copies, waits for them, and re-layouts  6.13 us
    dot_general x10, matrix products, owner_apply(): products = jnp.einsum('shj,ghij->gshi', incoming, states, precision=highest)  5.66 us
  transfers between devices with their start and end apart: 18, of which 17 were waited for; matrix products, arithmetic and copies ran while one was open for 21% of the time, Pallas kernels for 0%

profile of v13, /device:TPU:0, one launch (start us, length us, event | category | flops | bytes accessed | tf_op | source)
XLA Modules:
  0.0 257.4 jit_solution(5360642302153621273)
XLA Ops:
  5.4 6.0 %copy.276 = bf16[1024,4,3,128]{0,3,2,1:T(8,128)(2,1)} copy(bf16[1024,4,3,128]{3,1,2,0:T(4,128)(2,1)} %param.19) | data formatting | bytes 6291456 | tf_op args[2]
  16.5 7.9 %all-to-all-start.2 = ((f32[16,6,5,128]{3,1,2,0:T(8,128)}), f32[16,6,5,128]{3,1,2,0:T(8,128)S(1)}, u32[]{:S(2)}, u32[]{:S(2)}) async-start(f32[16,6,5,128]{3,1,2,0:T(8,128)} %copy.286), calls=%async_computation.2 | async-start | bytes 655360 | tf_op jit(solution)/shard_map/all_to_all | solution.py:112
  24.9 11.5 %all-to-all-done.2 = f32[16,6,5,128]{3,1,2,0:T(8,128)S(1)} async-done(((f32[16,6,5,128]{3,1,2,0:T(8,128)}), f32[16,6,5,128]{3,1,2,0:T(8,128)S(1)}, u32[]{:S(2)}, u32[]{:S(2)}) %all-to-all-start.2) | async-done | bytes 245792 | tf_op jit(solution)/shard_map/all_to_all | solution.py:112
  38.6 3.5 %all-to-all-start.3 = ((f32[16,6,4,128]{3,2,1,0:T(4,128)}), f32[16,6,4,128]{3,2,1,0:T(4,128)S(1)}, u32[]{:S(2)}, u32[]{:S(2)}) async-start(f32[16,6,4,128]{3,2,1,0:T(4,128)} %select_add_fusion.1), calls=%async_computation.3 | async-start | bytes 393216 | tf_op jit(solution)/shard_map/all_to_all | solution.py:112
  42.2 4.5 %multiply_reduce_fusion.7 = f32[24,4,128]{2,1,0:T(4,128)S(1)} fusion(f32[24,4,128,128]{3,2,1,0:T(8,128)} %param.25, f32[24,4,128]{2,1,0:T(4,128)S(1)} %copy.292), kind=kLoop, calls=%fused_computation.33 | loop fusion | flops 3133440 | bytes 6389760 | tf_op jit(solution)/shard_map/reduce_sum | solution.py:16
  51.5 170.6 %while.16 = (s32[]{:T(128)}, f32[24,4,128]{2,1,0:T(4,128)S(1)}, f32[24,4,128]{2,1,0:T(4,128)S(1)}, f32[24,4,128]{2,1,0:T(4,128)S(1)}, f32[24,4,1]{0,1,2:T(4,128)...) while((s32[]{:T(128)}, f32[24,4,128]{2,1,0:T(4,128)S(1)}, ...), condition=%wide.region_17.18_spmd, body=%wide.region_12.17_spmd.sunk | while | flops 154523872 | bytes 12098585 | solution.py:155
  53.0 3.5 %all-to-all-start = ((f32[16,6,4,128]{3,2,1,0:T(4,128)}), f32[16,6,4,128]{3,2,1,0:T(4,128)S(1)}, u32[]{:S(2)}, u32[]{:S(2)}) async-start(f32[16,6,4,128]{3,2,1,0:T(4,128)} %bitcast.186), calls=%async_computation | async-start | bytes 393216 | tf_op jit(solution)/shard_map/while/body/eval_jaxpr/all_to_all | solution.py:112
  56.7 7.9 %all-to-all-done = f32[16,6,4,128]{3,2,1,0:T(4,128)S(1)} async-done(((f32[16,6,4,128]{3,2,1,0:T(4,128)}), f32[16,6,4,128]{3,2,1,0:T(4,128)S(1)}, u32[]{:S(2)}, u32[]{:S(2)}) %all-to-all-start) | async-done | bytes 196640 | tf_op jit(solution)/shard_map/while/body/eval_jaxpr/all_to_all | solution.py:112
  66.4 3.5 %all-to-all-start.1 = ((f32[16,6,4,128]{3,2,1,0:T(4,128)}), f32[16,6,4,128]{3,2,1,0:T(4,128)S(1)}, u32[]{:S(2)}, u32[]{:S(2)}) async-start(f32[16,6,4,128]{3,2,1,0:T(4,128)} %select_add_fusion.4), calls=%async_computation.1 | async-start | bytes 393216 | tf_op jit(solution)/shard_map/while/body/eval_jaxpr/all_to_all | solution.py:112
  70.2 4.5 %multiply_reduce_fusion.17 = f32[24,4,128]{2,1,0:T(4,128)S(1)} fusion(f32[24,4,128,128]{3,2,1,0:T(8,128)} %get-tuple-element.462, f32[24,4,128]{2,1,0:T(4,128)S(1)} %get-tuple-element.433), kind=kLoop, calls=%fused_computation.8.clone.1 | loop fusion | flops 3133440 | bytes 6389760 | tf_op jit(solution)/shard_map/while/body/eval_jaxpr/reduce_sum | solution.py:16
  81.3 3.6 %all-to-all-start = ((f32[16,6,4,128]{3,2,1,0:T(4,128)}), f32[16,6,4,128]{3,2,1,0:T(4,128)S(1)}, u32[]{:S(2)}, u32[]{:S(2)}) async-start(f32[16,6,4,128]{3,2,1,0:T(4,128)} %bitcast.186), calls=%async_computation | async-start | bytes 393216 | tf_op jit(solution)/shard_map/while/body/eval_jaxpr/all_to_all | solution.py:112
  85.1 7.9 %all-to-all-done = f32[16,6,4,128]{3,2,1,0:T(4,128)S(1)} async-done(((f32[16,6,4,128]{3,2,1,0:T(4,128)}), f32[16,6,4,128]{3,2,1,0:T(4,128)S(1)}, u32[]{:S(2)}, u32[]{:S(2)}) %all-to-all-start) | async-done | bytes 196640 | tf_op jit(solution)/shard_map/while/body/eval_jaxpr/all_to_all | solution.py:112
  94.8 3.5 %all-to-all-start.1 = ((f32[16,6,4,128]{3,2,1,0:T(4,128)}), f32[16,6,4,128]{3,2,1,0:T(4,128)S(1)}, u32[]{:S(2)}, u32[]{:S(2)}) async-start(f32[16,6,4,128]{3,2,1,0:T(4,128)} %select_add_fusion.4), calls=%async_computation.1 | async-start | bytes 393216 | tf_op jit(solution)/shard_map/while/body/eval_jaxpr/all_to_all | solution.py:112
  98.6 4.5 %multiply_reduce_fusion.17 = f32[24,4,128]{2,1,0:T(4,128)S(1)} fusion(f32[24,4,128,128]{3,2,1,0:T(8,128)} %get-tuple-element.462, f32[24,4,128]{2,1,0:T(4,128)S(1)} %get-tuple-element.433), kind=kLoop, calls=%fused_computation.8.clone.1 | loop fusion | flops 3133440 | bytes 6389760 | tf_op jit(solution)/shard_map/while/body/eval_jaxpr/reduce_sum | solution.py:16
  109.7 3.6 %all-to-all-start = ((f32[16,6,4,128]{3,2,1,0:T(4,128)}), f32[16,6,4,128]{3,2,1,0:T(4,128)S(1)}, u32[]{:S(2)}, u32[]{:S(2)}) async-start(f32[16,6,4,128]{3,2,1,0:T(4,128)} %bitcast.186), calls=%async_computation | async-start | bytes 393216 | tf_op jit(solution)/shard_map/while/body/eval_jaxpr/all_to_all | solution.py:112
  113.5 7.9 %all-to-all-done = f32[16,6,4,128]{3,2,1,0:T(4,128)S(1)} async-done(((f32[16,6,4,128]{3,2,1,0:T(4,128)}), f32[16,6,4,128]{3,2,1,0:T(4,128)S(1)}, u32[]{:S(2)}, u32[]{:S(2)}) %all-to-all-start) | async-done | bytes 196640 | tf_op jit(solution)/shard_map/while/body/eval_jaxpr/all_to_all | solution.py:112
  123.3 3.5 %all-to-all-start.1 = ((f32[16,6,4,128]{3,2,1,0:T(4,128)}), f32[16,6,4,128]{3,2,1,0:T(4,128)S(1)}, u32[]{:S(2)}, u32[]{:S(2)}) async-start(f32[16,6,4,128]{3,2,1,0:T(4,128)} %select_add_fusion.4), calls=%async_computation.1 | async-start | bytes 393216 | tf_op jit(solution)/shard_map/while/body/eval_jaxpr/all_to_all | solution.py:112
  127.1 4.5 %multiply_reduce_fusion.17 = f32[24,4,128]{2,1,0:T(4,128)S(1)} fusion(f32[24,4,128,128]{3,2,1,0:T(8,128)} %get-tuple-element.462, f32[24,4,128]{2,1,0:T(4,128)S(1)} %get-tuple-element.433), kind=kLoop, calls=%fused_computation.8.clone.1 | loop fusion | flops 3133440 | bytes 6389760 | tf_op jit(solution)/shard_map/while/body/eval_jaxpr/reduce_sum | solution.py:16
  138.1 3.6 %all-to-all-start = ((f32[16,6,4,128]{3,2,1,0:T(4,128)}), f32[16,6,4,128]{3,2,1,0:T(4,128)S(1)}, u32[]{:S(2)}, u32[]{:S(2)}) async-start(f32[16,6,4,128]{3,2,1,0:T(4,128)} %bitcast.186), calls=%async_computation | async-start | bytes 393216 | tf_op jit(solution)/shard_map/while/body/eval_jaxpr/all_to_all | solution.py:112
  141.9 7.9 %all-to-all-done = f32[16,6,4,128]{3,2,1,0:T(4,128)S(1)} async-done(((f32[16,6,4,128]{3,2,1,0:T(4,128)}), f32[16,6,4,128]{3,2,1,0:T(4,128)S(1)}, u32[]{:S(2)}, u32[]{:S(2)}) %all-to-all-start) | async-done | bytes 196640 | tf_op jit(solution)/shard_map/while/body/eval_jaxpr/all_to_all | solution.py:112
  155.5 4.5 %multiply_reduce_fusion.17 = f32[24,4,128]{2,1,0:T(4,128)S(1)} fusion(f32[24,4,128,128]{3,2,1,0:T(8,128)} %get-tuple-element.462, f32[24,4,128]{2,1,0:T(4,128)S(1)} %get-tuple-element.433), kind=kLoop, calls=%fused_computation.8.clone.1 | loop fusion | flops 3133440 | bytes 6389760 | tf_op jit(solution)/shard_map/while/body/eval_jaxpr/reduce_sum | solution.py:16
  166.6 3.6 %all-to-all-start = ((f32[16,6,4,128]{3,2,1,0:T(4,128)}), f32[16,6,4,128]{3,2,1,0:T(4,128)S(1)}, u32[]{:S(2)}, u32[]{:S(2)}) async-start(f32[16,6,4,128]{3,2,1,0:T(4,128)} %bitcast.186), calls=%async_computation | async-start | bytes 393216 | tf_op jit(solution)/shard_map/while/body/eval_jaxpr/all_to_all | solution.py:112
  170.4 7.9 %all-to-all-done = f32[16,6,4,128]{3,2,1,0:T(4,128)S(1)} async-done(((f32[16,6,4,128]{3,2,1,0:T(4,128)}), f32[16,6,4,128]{3,2,1,0:T(4,128)S(1)}, u32[]{:S(2)}, u32[]{:S(2)}) %all-to-all-start) | async-done | bytes 196640 | tf_op jit(solution)/shard_map/while/body/eval_jaxpr/all_to_all | solution.py:112
  180.2 3.5 %all-to-all-start.1 = ((f32[16,6,4,128]{3,2,1,0:T(4,128)}), f32[16,6,4,128]{3,2,1,0:T(4,128)S(1)}, u32[]{:S(2)}, u32[]{:S(2)}) async-start(f32[16,6,4,128]{3,2,1,0:T(4,128)} %select_add_fusion.4), calls=%async_computation.1 | async-start | bytes 393216 | tf_op jit(solution)/shard_map/while/body/eval_jaxpr/all_to_all | solution.py:112
  184.0 4.5 %multiply_reduce_fusion.17 = f32[24,4,128]{2,1,0:T(4,128)S(1)} fusion(f32[24,4,128,128]{3,2,1,0:T(8,128)} %get-tuple-element.462, f32[24,4,128]{2,1,0:T(4,128)S(1)} %get-tuple-element.433), kind=kLoop, calls=%fused_computation.8.clone.1 | loop fusion | flops 3133440 | bytes 6389760 | tf_op jit(solution)/shard_map/while/body/eval_jaxpr/reduce_sum | solution.py:16
  195.0 3.6 %all-to-all-start = ((f32[16,6,4,128]{3,2,1,0:T(4,128)}), f32[16,6,4,128]{3,2,1,0:T(4,128)S(1)}, u32[]{:S(2)}, u32[]{:S(2)}) async-start(f32[16,6,4,128]{3,2,1,0:T(4,128)} %bitcast.186), calls=%async_computation | async-start | bytes 393216 | tf_op jit(solution)/shard_map/while/body/eval_jaxpr/all_to_all | solution.py:112
  198.8 8.0 %all-to-all-done = f32[16,6,4,128]{3,2,1,0:T(4,128)S(1)} async-done(((f32[16,6,4,128]{3,2,1,0:T(4,128)}), f32[16,6,4,128]{3,2,1,0:T(4,128)S(1)}, u32[]{:S(2)}, u32[]{:S(2)}) %all-to-all-start) | async-done | bytes 196640 | tf_op jit(solution)/shard_map/while/body/eval_jaxpr/all_to_all | solution.py:112
  212.5 4.5 %multiply_reduce_fusion.17 = f32[24,4,128]{2,1,0:T(4,128)S(1)} fusion(f32[24,4,128,128]{3,2,1,0:T(8,128)} %get-tuple-element.462, f32[24,4,128]{2,1,0:T(4,128)S(1)} %get-tuple-element.433), kind=kLoop, calls=%fused_computation.8.clone.1 | loop fusion | flops 3133440 | bytes 6389760 | tf_op jit(solution)/shard_map/while/body/eval_jaxpr/reduce_sum | solution.py:16
  224.4 3.7 %all-to-all-start.4 = ((bf16[16,6,8,128]{3,2,1,0:T(8,128)(2,1)}), bf16[16,6,8,128]{3,2,1,0:T(8,128)(2,1)S(1)}, u32[]{:S(2)}, u32[]{:S(2)}) async-start(bf16[16,6,8,128]{3,2,1,0:T(8,128)(2,1)} %pad_maximum_fusion.2), calls=%async_computation.4 | async-start | bytes 393216 | tf_op jit(solution)/shard_map/all_to_all | solution.py:112
  228.1 8.1 %all-to-all-done.4 = bf16[16,6,8,128]{3,2,1,0:T(8,128)(2,1)S(1)} async-done(((bf16[16,6,8,128]{3,2,1,0:T(8,128)(2,1)}), bf16[16,6,8,128]{3,2,1,0:T(8,128)(2,1)S(1)}, u32[]{:S(2)}, u32[]{:S(2)}) %all-to-all-start.4) | async-done | bytes 196640 | tf_op jit(solution)/shard_map/all_to_all | solution.py:112
  239.7 3.6 %all-to-all-start.5 = ((bf16[16,6,12,128]{3,2,1,0:T(8,128)(2,1)}), bf16[16,6,12,128]{3,2,1,0:T(8,128)(2,1)S(1)}, u32[]{:S(2)}, u32[]{:S(2)}) async-start(bf16[16,6,12,128]{3,2,1,0:T(8,128)(2,1)} %pad_maximum_fusion.1), calls=%async_computation.5 | async-start | bytes 786432 | tf_op jit(solution)/shard_map/all_to_all | solution.py:112
  243.3 7.9 %multiply_reduce_fusion.4 = (f32[24,4,128]{2,1,0:T(4,128)S(1)}, f32[24,4,128]{2,1,0:T(4,128)S(1)}, f32[24,4,128]{2,1,0:T(4,128)S(1)}) fusion(f32[24,4,128,128]{3,2,1,0:T(8,128)} %param.26, f32[24,4,128]{2,1,0:T(4,128)S(1)} %get-tuple-element.94, f32[24,4,128]{2,1,0:T(4,128)S(1)} %get-tuple-element.95, f32[24,4,128,128]{3,2,1,0:T(8,128)} %get-tuple-element.468), kind=kLoop, calls=%fused_computation.30 | loop fusion | flops 9400320 | bytes 12828672 | tf_op jit(solution)/shard_map/reduce_sum | solution.py:16
  (267 shorter events, 89.4 us)
Async XLA Ops:
  0.0 255.1 %copy-start = (bf16[4,128,1024]{2,1,0:T(8,128)(2,1)S(1)}, bf16[4,128,1024]{2,1,0:T(8,128)(2,1)}, u32[]{:S(2)}) copy-start(bf16[4,128,1024]{2,1,0:T(8,128)(2,1)} %param.31) | copy-start | bytes 3145732
  0.0 11.5 %copy-start.3 = (bf16[24,512]{1,0:T(8,128)(2,1)S(1)}, bf16[24,512]{1,0:T(8,128)(2,1)}, u32[]{:S(2)}) copy-start(bf16[24,512]{1,0:T(8,128)(2,1)} %param.17) | copy-start | bytes 73732
  0.0 11.6 %copy-start.6 = (f32[1024]{0:T(1024)S(1)}, f32[1024]{0:T(1024)}, u32[]{:S(2)}) copy-start(f32[1024]{0:T(1024)} %param.18) | copy-start | bytes 12292
  0.0 11.5 %collective-permute-start = (bf16[24,512]{1,0:T(8,128)(2,1)}, bf16[24,512]{1,0:T(8,128)(2,1)S(1)}, u32[]{:S(2)}, u32[]{:S(2)}) collective-permute-start(bf16[24,512]{1,0:T(8,128)(2,1)} %param.17), channel_id=1, source_target_pairs={{0,1},{1,0},{2,3},{3,2},{4,5},{5,4},{6,7},{7,6},{8,9},{9,8},{10,11... | collective-permute-start | bytes 73736 | tf_op jit(solution)/shard_map/ppermute | solution.py:37
  5.4 19.1 %copy-start.5 = (bf16[1024,2,4]{0,2,1:T(4,128)(2,1)S(1)}, bf16[1024,2,4]{0,2,1:T(4,128)(2,1)}, u32[]{:S(2)}) copy-start(bf16[1024,2,4]{0,2,1:T(4,128)(2,1)} %param.22) | copy-start | bytes 49156
  5.4 19.1 %copy-start.1 = (f32[2,4,128,128]{3,2,1,0:T(8,128)S(1)}, f32[2,4,128,128]{3,2,1,0:T(8,128)}, u32[]{:S(2)}) copy-start(f32[2,4,128,128]{3,2,1,0:T(8,128)} %param.27) | copy-start | bytes 1572868
  16.5 19.9 %all-to-all-start.2 = ((f32[16,6,5,128]{3,1,2,0:T(8,128)}), f32[16,6,5,128]{3,1,2,0:T(8,128)S(1)}, u32[]{:S(2)}, u32[]{:S(2)}) async-start(f32[16,6,5,128]{3,1,2,0:T(8,128)} %copy.286), calls=%async_computation.2 | async-start | bytes 655360 | tf_op jit(solution)/shard_map/all_to_all | solution.py:112
  24.6 26.3 %copy-start.4 = (f32[24,4]{0,1:T(4,128)S(1)}, f32[24,4]{0,1:T(4,128)}, u32[]{:S(2)}) copy-start(f32[24,4]{0,1:T(4,128)} %param.23) | copy-start | bytes 1156
  24.6 26.3 %copy-start.7 = (f32[4]{0:T(128)S(1)}, f32[4]{0:T(128)}, u32[]{:S(2)}) copy-start(f32[4]{0:T(128)} %param.24) | copy-start | bytes 52
  38.6 11.6 %all-to-all-start.3 = ((f32[16,6,4,128]{3,2,1,0:T(4,128)}), f32[16,6,4,128]{3,2,1,0:T(4,128)S(1)}, u32[]{:S(2)}, u32[]{:S(2)}) async-start(f32[16,6,4,128]{3,2,1,0:T(4,128)} %select_add_fusion.1), calls=%async_computation.3 | async-start | bytes 393216 | tf_op jit(solution)/shard_map/all_to_all | solution.py:112
  51.5 185.5 %copy-start.2 = (f32[2,4,128,128]{3,2,1,0:T(8,128)S(1)}, f32[2,4,128,128]{3,2,1,0:T(8,128)}, u32[]{:S(2)}) copy-start(f32[2,4,128,128]{3,2,1,0:T(8,128)} %param.28) | copy-start | bytes 1572868
  53.0 11.6 %all-to-all-start = ((f32[16,6,4,128]{3,2,1,0:T(4,128)}), f32[16,6,4,128]{3,2,1,0:T(4,128)S(1)}, u32[]{:S(2)}, u32[]{:S(2)}) async-start(f32[16,6,4,128]{3,2,1,0:T(4,128)} %bitcast.186), calls=%async_computation | async-start | bytes 393216 | tf_op jit(solution)/shard_map/while/body/eval_jaxpr/all_to_all | solution.py:112
  66.4 11.6 %all-to-all-start.1 = ((f32[16,6,4,128]{3,2,1,0:T(4,128)}), f32[16,6,4,128]{3,2,1,0:T(4,128)S(1)}, u32[]{:S(2)}, u32[]{:S(2)}) async-start(f32[16,6,4,128]{3,2,1,0:T(4,128)} %select_add_fusion.4), calls=%async_computation.1 | async-start | bytes 393216 | tf_op jit(solution)/shard_map/while/body/eval_jaxpr/all_to_all | solution.py:112
  81.3 11.7 %all-to-all-start = ((f32[16,6,4,128]{3,2,1,0:T(4,128)}), f32[16,6,4,128]{3,2,1,0:T(4,128)S(1)}, u32[]{:S(2)}, u32[]{:S(2)}) async-start(f32[16,6,4,128]{3,2,1,0:T(4,128)} %bitcast.186), calls=%async_computation | async-start | bytes 393216 | tf_op jit(solution)/shard_map/while/body/eval_jaxpr/all_to_all | solution.py:112
  94.8 11.6 %all-to-all-start.1 = ((f32[16,6,4,128]{3,2,1,0:T(4,128)}), f32[16,6,4,128]{3,2,1,0:T(4,128)S(1)}, u32[]{:S(2)}, u32[]{:S(2)}) async-start(f32[16,6,4,128]{3,2,1,0:T(4,128)} %select_add_fusion.4), calls=%async_computation.1 | async-start | bytes 393216 | tf_op jit(solution)/shard_map/while/body/eval_jaxpr/all_to_all | solution.py:112
  109.7 11.7 %all-to-all-start = ((f32[16,6,4,128]{3,2,1,0:T(4,128)}), f32[16,6,4,128]{3,2,1,0:T(4,128)S(1)}, u32[]{:S(2)}, u32[]{:S(2)}) async-start(f32[16,6,4,128]{3,2,1,0:T(4,128)} %bitcast.186), calls=%async_computation | async-start | bytes 393216 | tf_op jit(solution)/shard_map/while/body/eval_jaxpr/all_to_all | solution.py:112
  123.3 11.6 %all-to-all-start.1 = ((f32[16,6,4,128]{3,2,1,0:T(4,128)}), f32[16,6,4,128]{3,2,1,0:T(4,128)S(1)}, u32[]{:S(2)}, u32[]{:S(2)}) async-start(f32[16,6,4,128]{3,2,1,0:T(4,128)} %select_add_fusion.4), calls=%async_computation.1 | async-start | bytes 393216 | tf_op jit(solution)/shard_map/while/body/eval_jaxpr/all_to_all | solution.py:112
  138.1 11.7 %all-to-all-start = ((f32[16,6,4,128]{3,2,1,0:T(4,128)}), f32[16,6,4,128]{3,2,1,0:T(4,128)S(1)}, u32[]{:S(2)}, u32[]{:S(2)}) async-start(f32[16,6,4,128]{3,2,1,0:T(4,128)} %bitcast.186), calls=%async_computation | async-start | bytes 393216 | tf_op jit(solution)/shard_map/while/body/eval_jaxpr/all_to_all | solution.py:112
  151.7 11.6 %all-to-all-start.1 = ((f32[16,6,4,128]{3,2,1,0:T(4,128)}), f32[16,6,4,128]{3,2,1,0:T(4,128)S(1)}, u32[]{:S(2)}, u32[]{:S(2)}) async-start(f32[16,6,4,128]{3,2,1,0:T(4,128)} %select_add_fusion.4), calls=%async_computation.1 | async-start | bytes 393216 | tf_op jit(solution)/shard_map/while/body/eval_jaxpr/all_to_all | solution.py:112
  166.6 11.7 %all-to-all-start = ((f32[16,6,4,128]{3,2,1,0:T(4,128)}), f32[16,6,4,128]{3,2,1,0:T(4,128)S(1)}, u32[]{:S(2)}, u32[]{:S(2)}) async-start(f32[16,6,4,128]{3,2,1,0:T(4,128)} %bitcast.186), calls=%async_computation | async-start | bytes 393216 | tf_op jit(solution)/shard_map/while/body/eval_jaxpr/all_to_all | solution.py:112
  180.2 11.6 %all-to-all-start.1 = ((f32[16,6,4,128]{3,2,1,0:T(4,128)}), f32[16,6,4,128]{3,2,1,0:T(4,128)S(1)}, u32[]{:S(2)}, u32[]{:S(2)}) async-start(f32[16,6,4,128]{3,2,1,0:T(4,128)} %select_add_fusion.4), calls=%async_computation.1 | async-start | bytes 393216 | tf_op jit(solution)/shard_map/while/body/eval_jaxpr/all_to_all | solution.py:112
  195.0 11.8 %all-to-all-start = ((f32[16,6,4,128]{3,2,1,0:T(4,128)}), f32[16,6,4,128]{3,2,1,0:T(4,128)S(1)}, u32[]{:S(2)}, u32[]{:S(2)}) async-start(f32[16,6,4,128]{3,2,1,0:T(4,128)} %bitcast.186), calls=%async_computation | async-start | bytes 393216 | tf_op jit(solution)/shard_map/while/body/eval_jaxpr/all_to_all | solution.py:112
  208.7 11.6 %all-to-all-start.1 = ((f32[16,6,4,128]{3,2,1,0:T(4,128)}), f32[16,6,4,128]{3,2,1,0:T(4,128)S(1)}, u32[]{:S(2)}, u32[]{:S(2)}) async-start(f32[16,6,4,128]{3,2,1,0:T(4,128)} %select_add_fusion.4), calls=%async_computation.1 | async-start | bytes 393216 | tf_op jit(solution)/shard_map/while/body/eval_jaxpr/all_to_all | solution.py:112
  224.4 11.8 %all-to-all-start.4 = ((bf16[16,6,8,128]{3,2,1,0:T(8,128)(2,1)}), bf16[16,6,8,128]{3,2,1,0:T(8,128)(2,1)S(1)}, u32[]{:S(2)}, u32[]{:S(2)}) async-start(bf16[16,6,8,128]{3,2,1,0:T(8,128)(2,1)} %pad_maximum_fusion.2), calls=%async_computation.4 | async-start | bytes 393216 | tf_op jit(solution)/shard_map/all_to_all | solution.py:112
  239.7 13.2 %all-to-all-start.5 = ((bf16[16,6,12,128]{3,2,1,0:T(8,128)(2,1)}), bf16[16,6,12,128]{3,2,1,0:T(8,128)(2,1)S(1)}, u32[]{:S(2)}, u32[]{:S(2)}) async-start(bf16[16,6,12,128]{3,2,1,0:T(8,128)(2,1)} %pad_maximum_fusion.1), calls=%async_computation.5 | async-start | bytes 786432 | tf_op jit(solution)/shard_map/all_to_all | solution.py:112
  255.4 1.3 collective-permute-start.1

commit v14 on v12

--- a/solution.py
+++ b/solution.py
@@ -77,6 +77,14 @@
     write_col = jax.nn.sigmoid(gate_logit[:, 1])[:, :, None]
     weight_col = prompt_weight[:, :, None]
     ridge_col = ridge_term[None, :, None]
+    lane_shape = (row_count, head_count, head_size)
+    decay_b = jnp.broadcast_to(decay_col, lane_shape)
+    write_b = jnp.broadcast_to(write_col, lane_shape)
+    weight_b = jnp.broadcast_to(weight_col, lane_shape)
+    ridge_b = jnp.broadcast_to(ridge_col, lane_shape)
+
+    def lane_sum(values):
+        return jnp.broadcast_to(jnp.sum(values, axis=2, keepdims=True), values.shape)
 
     peer_count = lax.axis_size("req")
     group_count = prompt_keys.shape[0]
@@ -126,16 +134,16 @@
     def cg_step(arrived, carry):
         solution, residual, direction, norm_now = carry
         shares = unpack(exchange(owner_apply(prompt_keys, arrived, chosen)))
-        shared = weight_col * shares + own_matvec(own_keys, direction)
+        shared = weight_b * shares + own_matvec(own_keys, direction)
         product = (
-            decay_col * shared
-            + write_col * key_now * jnp.sum(key_now * direction, axis=2, keepdims=True)
-            + ridge_col * direction
-        )
-        step_size = norm_now / jnp.sum(direction * product, axis=2, keepdims=True)
+            decay_b * shared
+            + write_b * key_now * lane_sum(key_now * direction)
+            + ridge_b * direction
+        )
+        step_size = norm_now / lane_sum(direction * product)
         solution = solution + step_size * direction
         residual = residual - step_size * product
-        norm_next = jnp.sum(residual * residual, axis=2, keepdims=True)
+        norm_next = lane_sum(residual * residual)
         direction = residual + norm_next / norm_now * direction
         return solution, residual, direction, norm_next
 
@@ -149,7 +157,7 @@
         jnp.zeros_like(queries),
         queries,
         queries,
-        jnp.sum(queries * queries, axis=2, keepdims=True),
+        lane_sum(queries * queries),
     )
     carry = cg_step(first[:, :head_count], carry)
     carry = lax.fori_loop(
@@ -172,13 +180,13 @@
     own_out_direction = own_matvec(own_values, direction)
     partial = solution
     shares = returned[:, :head_count]
-    shared = weight_col * shares + own_matvec(own_keys, direction)
+    shared = weight_b * shares + own_matvec(own_keys, direction)
     product = (
-        decay_col * shared
-        + write_col * key_now * jnp.sum(key_now * direction, axis=2, keepdims=True)
-        + ridge_col * direction
-    )
-    step_last = norm_now / jnp.sum(direction * product, axis=2, keepdims=True)
+        decay_b * shared
+        + write_b * key_now * lane_sum(key_now * direction)
+        + ridge_b * direction
+    )
+    step_last = norm_now / lane_sum(direction * product)
     solution = partial + step_last * direction
     value_sum = returned[:, head_count : 2 * head_count] + step_last * returned[:, 2 * head_count :]
     own_out = own_out_partial + step_last * own_out_direction

time: 264 us -> 268 us (1.015)
  starting transfers between devices: 58.3 us -> 63.7 us
  local copies, waits for them, and re-layouts: 32 us -> 29.3 us
    all_to_all x15, starting transfers between devices: 57.8 us -> 63.1 us  [exchange(): lax.all_to_all(shaped, 'req', split_axis=0, concat_axis=0, tiled=True)]
    broadcast_in_dim x0 -> x14, other arithmetic: none -> 4.51 us  [lane_sum(): jnp.broadcast_to(jnp.sum(values, axis=2, keepdims=True), values.shape)]
    mul x22 -> x1, other arithmetic: 3.7 us -> 0.11 us  [cg_step(): write_b * key_now * lane_sum(key_now * direction)]
    unnamed x19 -> x26, local copies, waits for them, and re-layouts: 6.13 us -> 6.37 us
  transfers between devices with their start and end apart: 17 -> 17, of which waited for: 16 -> 16; matrix products, arithmetic and copies ran while one was open for 20% -> 19% of each run, Pallas kernels for 0% -> 0%
where the time goes in v14:
time: 268 us; the launch traced here: 267 us
  waiting for transfers between devices  90.1 us (34%)
  starting transfers between devices  63.7 us (24%)
  other arithmetic  58.1 us (22%)
  local copies, waits for them, and re-layouts  29.3 us (11%)
  blocking collectives  14.3 us (5%)
  matrix products  9.69 us (4%)
    all_to_all x15, waiting for transfers between devices, exchange(): lax.all_to_all(shaped, 'req', split_axis=0, concat_axis=0, tiled=True)  88.9 us
    all_to_all x15, starting transfers between devices, exchange(): lax.all_to_all(shaped, 'req', split_axis=0, concat_axis=0, tiled=True)  63.1 us
    reduce_sum x8, other arithmetic, own_matvec(): return jnp.sum(matrices * vectors[:, :, None, :], axis=3)  39.3 us
    all_to_all x1, blocking collectives, exchange(): lax.all_to_all(shaped, 'req', split_axis=0, concat_axis=0, tiled=True)  14.3 us
    gather x9, local copies, waits for them, and re-layouts, pack(): return jnp.take(padded, source, axis=0, mode='clip')  10.3 us
    add x8, other arithmetic, owner_apply(): total + jnp.where(chosen[group][:, None, None], products[group], 0.0)  6.94 us
    unnamed x26, local copies, waits for them, and re-layouts  6.37 us
    dot_general x10, matrix products, owner_apply(): products = jnp.einsum('shj,ghij->gshi', incoming, states, precision=highest)  6.33 us
  transfers between devices with their start and end apart: 17, of which 16 were waited for; matrix products, arithmetic and copies ran while one was open for 19% of the time, Pallas kernels for 0%

profile of v14, /device:TPU:0, one launch (start us, length us, event | category | flops | bytes accessed | tf_op | source)
XLA Modules:
  0.0 266.5 jit_solution(12231236072044128328)
XLA Ops:
  5.4 6.0 %copy.142 = bf16[1024,4,3,128]{0,3,2,1:T(8,128)(2,1)} copy(bf16[1024,4,3,128]{3,1,2,0:T(4,128)(2,1)} %param.19) | data formatting | bytes 6291456 | tf_op args[2]
  16.8 7.9 %all-to-all-start.2 = ((f32[16,6,5,128]{3,1,2,0:T(8,128)}), f32[16,6,5,128]{3,1,2,0:T(8,128)S(1)}, u32[]{:S(2)}, u32[]{:S(2)}) async-start(f32[16,6,5,128]{3,1,2,0:T(8,128)} %copy.152), calls=%async_computation.2 | async-start | bytes 655360 | tf_op jit(solution)/shard_map/all_to_all | solution.py:120
  24.9 11.8 %all-to-all-done.2 = f32[16,6,5,128]{3,1,2,0:T(8,128)S(1)} async-done(((f32[16,6,5,128]{3,1,2,0:T(8,128)}), f32[16,6,5,128]{3,1,2,0:T(8,128)S(1)}, u32[]{:S(2)}, u32[]{:S(2)}) %all-to-all-start.2) | async-done | bytes 245792 | tf_op jit(solution)/shard_map/all_to_all | solution.py:120
  39.0 3.5 %all-to-all-start.3 = ((f32[16,6,4,128]{3,2,1,0:T(4,128)}), f32[16,6,4,128]{3,2,1,0:T(4,128)S(1)}, u32[]{:S(2)}, u32[]{:S(2)}) async-start(f32[16,6,4,128]{3,2,1,0:T(4,128)} %select_add_fusion.4), calls=%async_computation.3 | async-start | bytes 393216 | tf_op jit(solution)/shard_map/all_to_all | solution.py:120
  42.7 4.5 %multiply_reduce_fusion.7 = f32[24,4,128]{2,1,0:T(4,128)S(1)} fusion(f32[24,4,128,128]{3,2,1,0:T(8,128)} %param.25, f32[24,4,128]{2,1,0:T(4,128)S(1)} %copy.158), kind=kLoop, calls=%fused_computation.38 | loop fusion | flops 3133440 | bytes 6389760 | tf_op jit(solution)/shard_map/reduce_sum | solution.py:16
  52.0 168.1 %while.19 = (s32[]{:T(128)}, f32[24,4,128]{2,1,0:T(4,128)S(1)}, f32[24,4,128]{2,1,0:T(4,128)S(1)}, f32[24,4,128]{2,1,0:T(4,128)S(1)}, f32[24,4,128]{2,1,0:T(4,12...) while((s32[]{:T(128)}, f32[24,4,128]{2,1,0:T(4,128)S(1)}, ...), condition=%wide.region_17.18_spmd.clone, body=%wide.region_12.17_spmd.clone.sunk | while | flops 154524000 | bytes 12433049 | solution.py:163
  53.4 3.6 %all-to-all-start = ((f32[16,6,4,128]{3,2,1,0:T(4,128)}), f32[16,6,4,128]{3,2,1,0:T(4,128)S(1)}, u32[]{:S(2)}, u32[]{:S(2)}) async-start(f32[16,6,4,128]{3,2,1,0:T(4,128)} %bitcast.144), calls=%async_computation | async-start | bytes 393216 | tf_op jit(solution)/shard_map/while/body/eval_jaxpr/all_to_all | solution.py:120
  57.2 7.9 %all-to-all-done = f32[16,6,4,128]{3,2,1,0:T(4,128)S(1)} async-done(((f32[16,6,4,128]{3,2,1,0:T(4,128)}), f32[16,6,4,128]{3,2,1,0:T(4,128)S(1)}, u32[]{:S(2)}, u32[]{:S(2)}) %all-to-all-start) | async-done | bytes 196640 | tf_op jit(solution)/shard_map/while/body/eval_jaxpr/all_to_all | solution.py:120
  67.0 3.5 %all-to-all-start.1 = ((f32[16,6,4,128]{3,2,1,0:T(4,128)}), f32[16,6,4,128]{3,2,1,0:T(4,128)S(1)}, u32[]{:S(2)}, u32[]{:S(2)}) async-start(f32[16,6,4,128]{3,2,1,0:T(4,128)} %select_add_fusion.7), calls=%async_computation.1 | async-start | bytes 393216 | tf_op jit(solution)/shard_map/while/body/eval_jaxpr/all_to_all | solution.py:120
  70.5 4.5 %multiply_reduce_fusion.16 = f32[24,4,128]{2,1,0:T(4,128)S(1)} fusion(f32[24,4,128,128]{3,2,1,0:T(8,128)} %get-tuple-element.570, f32[24,4,128]{2,1,0:T(4,128)S(1)} %get-tuple-element.543), kind=kLoop, calls=%fused_computation.12.clone.1 | loop fusion | flops 3133440 | bytes 6389760 | tf_op jit(solution)/shard_map/while/body/eval_jaxpr/reduce_sum | solution.py:16
  75.0 3.5 %all-to-all-done.1 = f32[16,6,4,128]{3,2,1,0:T(4,128)S(1)} async-done(((f32[16,6,4,128]{3,2,1,0:T(4,128)}), f32[16,6,4,128]{3,2,1,0:T(4,128)S(1)}, u32[]{:S(2)}, u32[]{:S(2)}) %all-to-all-start.1) | async-done | bytes 196640 | tf_op jit(solution)/shard_map/while/body/eval_jaxpr/all_to_all | solution.py:120
  81.4 3.5 %all-to-all-start = ((f32[16,6,4,128]{3,2,1,0:T(4,128)}), f32[16,6,4,128]{3,2,1,0:T(4,128)S(1)}, u32[]{:S(2)}, u32[]{:S(2)}) async-start(f32[16,6,4,128]{3,2,1,0:T(4,128)} %bitcast.144), calls=%async_computation | async-start | bytes 393216 | tf_op jit(solution)/shard_map/while/body/eval_jaxpr/all_to_all | solution.py:120
  85.1 7.9 %all-to-all-done = f32[16,6,4,128]{3,2,1,0:T(4,128)S(1)} async-done(((f32[16,6,4,128]{3,2,1,0:T(4,128)}), f32[16,6,4,128]{3,2,1,0:T(4,128)S(1)}, u32[]{:S(2)}, u32[]{:S(2)}) %all-to-all-start) | async-done | bytes 196640 | tf_op jit(solution)/shard_map/while/body/eval_jaxpr/all_to_all | solution.py:120
  98.4 4.5 %multiply_reduce_fusion.16 = f32[24,4,128]{2,1,0:T(4,128)S(1)} fusion(f32[24,4,128,128]{3,2,1,0:T(8,128)} %get-tuple-element.570, f32[24,4,128]{2,1,0:T(4,128)S(1)} %get-tuple-element.543), kind=kLoop, calls=%fused_computation.12.clone.1 | loop fusion | flops 3133440 | bytes 6389760 | tf_op jit(solution)/shard_map/while/body/eval_jaxpr/reduce_sum | solution.py:16
  102.9 3.5 %all-to-all-done.1 = f32[16,6,4,128]{3,2,1,0:T(4,128)S(1)} async-done(((f32[16,6,4,128]{3,2,1,0:T(4,128)}), f32[16,6,4,128]{3,2,1,0:T(4,128)S(1)}, u32[]{:S(2)}, u32[]{:S(2)}) %all-to-all-start.1) | async-done | bytes 196640 | tf_op jit(solution)/shard_map/while/body/eval_jaxpr/all_to_all | solution.py:120
  113.1 7.9 %all-to-all-done = f32[16,6,4,128]{3,2,1,0:T(4,128)S(1)} async-done(((f32[16,6,4,128]{3,2,1,0:T(4,128)}), f32[16,6,4,128]{3,2,1,0:T(4,128)S(1)}, u32[]{:S(2)}, u32[]{:S(2)}) %all-to-all-start) | async-done | bytes 196640 | tf_op jit(solution)/shard_map/while/body/eval_jaxpr/all_to_all | solution.py:120
  126.3 4.5 %multiply_reduce_fusion.16 = f32[24,4,128]{2,1,0:T(4,128)S(1)} fusion(f32[24,4,128,128]{3,2,1,0:T(8,128)} %get-tuple-element.570, f32[24,4,128]{2,1,0:T(4,128)S(1)} %get-tuple-element.543), kind=kLoop, calls=%fused_computation.12.clone.1 | loop fusion | flops 3133440 | bytes 6389760 | tf_op jit(solution)/shard_map/while/body/eval_jaxpr/reduce_sum | solution.py:16
  130.8 3.5 %all-to-all-done.1 = f32[16,6,4,128]{3,2,1,0:T(4,128)S(1)} async-done(((f32[16,6,4,128]{3,2,1,0:T(4,128)}), f32[16,6,4,128]{3,2,1,0:T(4,128)S(1)}, u32[]{:S(2)}, u32[]{:S(2)}) %all-to-all-start.1) | async-done | bytes 196640 | tf_op jit(solution)/shard_map/while/body/eval_jaxpr/all_to_all | solution.py:120
  141.0 7.9 %all-to-all-done = f32[16,6,4,128]{3,2,1,0:T(4,128)S(1)} async-done(((f32[16,6,4,128]{3,2,1,0:T(4,128)}), f32[16,6,4,128]{3,2,1,0:T(4,128)S(1)}, u32[]{:S(2)}, u32[]{:S(2)}) %all-to-all-start) | async-done | bytes 196640 | tf_op jit(solution)/shard_map/while/body/eval_jaxpr/all_to_all | solution.py:120
  154.3 4.5 %multiply_reduce_fusion.16 = f32[24,4,128]{2,1,0:T(4,128)S(1)} fusion(f32[24,4,128,128]{3,2,1,0:T(8,128)} %get-tuple-element.570, f32[24,4,128]{2,1,0:T(4,128)S(1)} %get-tuple-element.543), kind=kLoop, calls=%fused_computation.12.clone.1 | loop fusion | flops 3133440 | bytes 6389760 | tf_op jit(solution)/shard_map/while/body/eval_jaxpr/reduce_sum | solution.py:16
  158.8 3.5 %all-to-all-done.1 = f32[16,6,4,128]{3,2,1,0:T(4,128)S(1)} async-done(((f32[16,6,4,128]{3,2,1,0:T(4,128)}), f32[16,6,4,128]{3,2,1,0:T(4,128)S(1)}, u32[]{:S(2)}, u32[]{:S(2)}) %all-to-all-start.1) | async-done | bytes 196640 | tf_op jit(solution)/shard_map/while/body/eval_jaxpr/all_to_all | solution.py:120
  168.9 7.9 %all-to-all-done = f32[16,6,4,128]{3,2,1,0:T(4,128)S(1)} async-done(((f32[16,6,4,128]{3,2,1,0:T(4,128)}), f32[16,6,4,128]{3,2,1,0:T(4,128)S(1)}, u32[]{:S(2)}, u32[]{:S(2)}) %all-to-all-start) | async-done | bytes 196640 | tf_op jit(solution)/shard_map/while/body/eval_jaxpr/all_to_all | solution.py:120
  182.2 4.5 %multiply_reduce_fusion.16 = f32[24,4,128]{2,1,0:T(4,128)S(1)} fusion(f32[24,4,128,128]{3,2,1,0:T(8,128)} %get-tuple-element.570, f32[24,4,128]{2,1,0:T(4,128)S(1)} %get-tuple-element.543), kind=kLoop, calls=%fused_computation.12.clone.1 | loop fusion | flops 3133440 | bytes 6389760 | tf_op jit(solution)/shard_map/while/body/eval_jaxpr/reduce_sum | solution.py:16
  186.7 3.6 %all-to-all-done.1 = f32[16,6,4,128]{3,2,1,0:T(4,128)S(1)} async-done(((f32[16,6,4,128]{3,2,1,0:T(4,128)}), f32[16,6,4,128]{3,2,1,0:T(4,128)S(1)}, u32[]{:S(2)}, u32[]{:S(2)}) %all-to-all-start.1) | async-done | bytes 196640 | tf_op jit(solution)/shard_map/while/body/eval_jaxpr/all_to_all | solution.py:120
  196.9 7.9 %all-to-all-done = f32[16,6,4,128]{3,2,1,0:T(4,128)S(1)} async-done(((f32[16,6,4,128]{3,2,1,0:T(4,128)}), f32[16,6,4,128]{3,2,1,0:T(4,128)S(1)}, u32[]{:S(2)}, u32[]{:S(2)}) %all-to-all-start) | async-done | bytes 196640 | tf_op jit(solution)/shard_map/while/body/eval_jaxpr/all_to_all | solution.py:120
  206.6 3.9 %all-to-all-start.1 = ((f32[16,6,4,128]{3,2,1,0:T(4,128)}), f32[16,6,4,128]{3,2,1,0:T(4,128)S(1)}, u32[]{:S(2)}, u32[]{:S(2)}) async-start(f32[16,6,4,128]{3,2,1,0:T(4,128)} %select_add_fusion.7), calls=%async_computation.1 | async-start | bytes 393216 | tf_op jit(solution)/shard_map/while/body/eval_jaxpr/all_to_all | solution.py:120
  210.5 4.5 %multiply_reduce_fusion.16 = f32[24,4,128]{2,1,0:T(4,128)S(1)} fusion(f32[24,4,128,128]{3,2,1,0:T(8,128)} %get-tuple-element.570, f32[24,4,128]{2,1,0:T(4,128)S(1)} %get-tuple-element.543), kind=kLoop, calls=%fused_computation.12.clone.1 | loop fusion | flops 3133440 | bytes 6389760 | tf_op jit(solution)/shard_map/while/body/eval_jaxpr/reduce_sum | solution.py:16
  215.0 3.6 %all-to-all-done.1 = f32[16,6,4,128]{3,2,1,0:T(4,128)S(1)} async-done(((f32[16,6,4,128]{3,2,1,0:T(4,128)}), f32[16,6,4,128]{3,2,1,0:T(4,128)S(1)}, u32[]{:S(2)}, u32[]{:S(2)}) %all-to-all-start.1) | async-done | bytes 196640 | tf_op jit(solution)/shard_map/while/body/eval_jaxpr/all_to_all | solution.py:120
  221.7 14.3 %all_to_all.38 = f32[16,6,8,128]{3,2,1,0:T(8,128)S(1)} all-to-all(f32[16,6,8,128]{3,2,1,0:T(8,128)S(1)} %bitcast.154), channel_id=1, replica_groups=mesh['req'=16,'head'=2] {'req'}, dimensions={0} | all-to-all | bytes 786432 | tf_op jit(solution)/shard_map/all_to_all | solution.py:120
  240.3 9.0 %all-to-all-start.5 = ((f32[16,6,12,128]{3,2,1,0:T(8,128)}), f32[16,6,12,128]{3,2,1,0:T(8,128)S(1)}, u32[]{:S(2)}, u32[]{:S(2)}) async-start(f32[16,6,12,128]{3,2,1,0:T(8,128)} %pad_maximum_fusion), calls=%async_computation.5 | async-start | bytes 1572864 | tf_op jit(solution)/shard_map/all_to_all | solution.py:120
  249.3 7.9 %multiply_reduce_fusion.4 = (f32[24,4,128]{2,1,0:T(4,128)S(1)}, f32[24,4,128]{2,1,0:T(4,128)S(1)}, f32[24,4,128]{2,1,0:T(4,128)S(1)}) fusion(f32[24,4,128,128]{3,2,1,0:T(8,128)} %param.26, f32[24,4,128]{2,1,0:T(4,128)S(1)} %get-tuple-element.201, f32[24,4,128]{2,1,0:T(4,128)S(1)} %get-tuple-element.202, f32[24,4,128,128]{3,2,1,0:T(8,128)} %get-tuple-element.578), kind=kLoop, calls=%fused_computation.35 | loop fusion | flops 9400320 | bytes 12828672 | tf_op jit(solution)/shard_map/reduce_sum | solution.py:16
  257.2 5.3 %all-to-all-done.5 = f32[16,6,12,128]{3,2,1,0:T(8,128)S(1)} async-done(((f32[16,6,12,128]{3,2,1,0:T(8,128)}), f32[16,6,12,128]{3,2,1,0:T(8,128)S(1)}, u32[]{:S(2)}, u32[]{:S(2)}) %all-to-all-start.5) | async-done | bytes 589856 | tf_op jit(solution)/shard_map/all_to_all | solution.py:120
  (214 shorter events, 85.0 us)
Async XLA Ops:
  0.0 264.2 %copy-start = (bf16[4,128,1024]{2,1,0:T(8,128)(2,1)S(1)}, bf16[4,128,1024]{2,1,0:T(8,128)(2,1)}, u32[]{:S(2)}) copy-start(bf16[4,128,1024]{2,1,0:T(8,128)(2,1)} %param.31) | copy-start | bytes 3145732
  0.0 11.5 %copy-start.3 = (bf16[24,512]{1,0:T(8,128)(2,1)S(1)}, bf16[24,512]{1,0:T(8,128)(2,1)}, u32[]{:S(2)}) copy-start(bf16[24,512]{1,0:T(8,128)(2,1)} %param.17) | copy-start | bytes 73732
  0.0 11.5 %copy-start.4 = (bf16[1024,2,4]{0,2,1:T(4,128)(2,1)S(1)}, bf16[1024,2,4]{0,2,1:T(4,128)(2,1)}, u32[]{:S(2)}) copy-start(bf16[1024,2,4]{0,2,1:T(4,128)(2,1)} %param.22) | copy-start | bytes 49156
  0.0 11.7 %copy-start.6 = (f32[1024]{0:T(1024)S(1)}, f32[1024]{0:T(1024)}, u32[]{:S(2)}) copy-start(f32[1024]{0:T(1024)} %param.18) | copy-start | bytes 12292
  0.0 11.5 %collective-permute-start = (bf16[24,512]{1,0:T(8,128)(2,1)}, bf16[24,512]{1,0:T(8,128)(2,1)S(1)}, u32[]{:S(2)}, u32[]{:S(2)}) collective-permute-start(bf16[24,512]{1,0:T(8,128)(2,1)} %param.17), channel_id=1, source_target_pairs={{0,1},{1,0},{2,3},{3,2},{4,5},{5,4},{6,7},{7,6},{8,9},{9,8},{10,11... | collective-permute-start | bytes 73736 | tf_op jit(solution)/shard_map/ppermute | solution.py:37
  5.4 19.3 %copy-start.1 = (f32[2,4,128,128]{3,2,1,0:T(8,128)S(1)}, f32[2,4,128,128]{3,2,1,0:T(8,128)}, u32[]{:S(2)}) copy-start(f32[2,4,128,128]{3,2,1,0:T(8,128)} %param.27) | copy-start | bytes 1572868
  5.4 19.4 %copy-start.5 = (f32[24,4]{0,1:T(4,128)S(1)}, f32[24,4]{0,1:T(4,128)}, u32[]{:S(2)}) copy-start(f32[24,4]{0,1:T(4,128)} %param.23) | copy-start | bytes 1156
  16.8 19.9 %all-to-all-start.2 = ((f32[16,6,5,128]{3,1,2,0:T(8,128)}), f32[16,6,5,128]{3,1,2,0:T(8,128)S(1)}, u32[]{:S(2)}, u32[]{:S(2)}) async-start(f32[16,6,5,128]{3,1,2,0:T(8,128)} %copy.152), calls=%async_computation.2 | async-start | bytes 655360 | tf_op jit(solution)/shard_map/all_to_all | solution.py:120
  24.8 26.4 %copy-start.7 = (f32[4]{0:T(128)S(1)}, f32[4]{0:T(128)}, u32[]{:S(2)}) copy-start(f32[4]{0:T(128)} %param.24) | copy-start | bytes 52
  39.0 11.6 %all-to-all-start.3 = ((f32[16,6,4,128]{3,2,1,0:T(4,128)}), f32[16,6,4,128]{3,2,1,0:T(4,128)S(1)}, u32[]{:S(2)}, u32[]{:S(2)}) async-start(f32[16,6,4,128]{3,2,1,0:T(4,128)} %select_add_fusion.4), calls=%async_computation.3 | async-start | bytes 393216 | tf_op jit(solution)/shard_map/all_to_all | solution.py:120
  53.4 11.7 %all-to-all-start = ((f32[16,6,4,128]{3,2,1,0:T(4,128)}), f32[16,6,4,128]{3,2,1,0:T(4,128)S(1)}, u32[]{:S(2)}, u32[]{:S(2)}) async-start(f32[16,6,4,128]{3,2,1,0:T(4,128)} %bitcast.144), calls=%async_computation | async-start | bytes 393216 | tf_op jit(solution)/shard_map/while/body/eval_jaxpr/all_to_all | solution.py:120
  67.0 11.6 %all-to-all-start.1 = ((f32[16,6,4,128]{3,2,1,0:T(4,128)}), f32[16,6,4,128]{3,2,1,0:T(4,128)S(1)}, u32[]{:S(2)}, u32[]{:S(2)}) async-start(f32[16,6,4,128]{3,2,1,0:T(4,128)} %select_add_fusion.7), calls=%async_computation.1 | async-start | bytes 393216 | tf_op jit(solution)/shard_map/while/body/eval_jaxpr/all_to_all | solution.py:120
  81.4 11.6 %all-to-all-start = ((f32[16,6,4,128]{3,2,1,0:T(4,128)}), f32[16,6,4,128]{3,2,1,0:T(4,128)S(1)}, u32[]{:S(2)}, u32[]{:S(2)}) async-start(f32[16,6,4,128]{3,2,1,0:T(4,128)} %bitcast.144), calls=%async_computation | async-start | bytes 393216 | tf_op jit(solution)/shard_map/while/body/eval_jaxpr/all_to_all | solution.py:120
  94.9 11.6 %all-to-all-start.1 = ((f32[16,6,4,128]{3,2,1,0:T(4,128)}), f32[16,6,4,128]{3,2,1,0:T(4,128)S(1)}, u32[]{:S(2)}, u32[]{:S(2)}) async-start(f32[16,6,4,128]{3,2,1,0:T(4,128)} %select_add_fusion.7), calls=%async_computation.1 | async-start | bytes 393216 | tf_op jit(solution)/shard_map/while/body/eval_jaxpr/all_to_all | solution.py:120
  109.3 11.6 %all-to-all-start = ((f32[16,6,4,128]{3,2,1,0:T(4,128)}), f32[16,6,4,128]{3,2,1,0:T(4,128)S(1)}, u32[]{:S(2)}, u32[]{:S(2)}) async-start(f32[16,6,4,128]{3,2,1,0:T(4,128)} %bitcast.144), calls=%async_computation | async-start | bytes 393216 | tf_op jit(solution)/shard_map/while/body/eval_jaxpr/all_to_all | solution.py:120
  122.8 11.6 %all-to-all-start.1 = ((f32[16,6,4,128]{3,2,1,0:T(4,128)}), f32[16,6,4,128]{3,2,1,0:T(4,128)S(1)}, u32[]{:S(2)}, u32[]{:S(2)}) async-start(f32[16,6,4,128]{3,2,1,0:T(4,128)} %select_add_fusion.7), calls=%async_computation.1 | async-start | bytes 393216 | tf_op jit(solution)/shard_map/while/body/eval_jaxpr/all_to_all | solution.py:120
  137.3 11.6 %all-to-all-start = ((f32[16,6,4,128]{3,2,1,0:T(4,128)}), f32[16,6,4,128]{3,2,1,0:T(4,128)S(1)}, u32[]{:S(2)}, u32[]{:S(2)}) async-start(f32[16,6,4,128]{3,2,1,0:T(4,128)} %bitcast.144), calls=%async_computation | async-start | bytes 393216 | tf_op jit(solution)/shard_map/while/body/eval_jaxpr/all_to_all | solution.py:120
  150.7 11.6 %all-to-all-start.1 = ((f32[16,6,4,128]{3,2,1,0:T(4,128)}), f32[16,6,4,128]{3,2,1,0:T(4,128)S(1)}, u32[]{:S(2)}, u32[]{:S(2)}) async-start(f32[16,6,4,128]{3,2,1,0:T(4,128)} %select_add_fusion.7), calls=%async_computation.1 | async-start | bytes 393216 | tf_op jit(solution)/shard_map/while/body/eval_jaxpr/all_to_all | solution.py:120
  165.2 11.6 %all-to-all-start = ((f32[16,6,4,128]{3,2,1,0:T(4,128)}), f32[16,6,4,128]{3,2,1,0:T(4,128)S(1)}, u32[]{:S(2)}, u32[]{:S(2)}) async-start(f32[16,6,4,128]{3,2,1,0:T(4,128)} %bitcast.144), calls=%async_computation | async-start | bytes 393216 | tf_op jit(solution)/shard_map/while/body/eval_jaxpr/all_to_all | solution.py:120
  178.7 11.6 %all-to-all-start.1 = ((f32[16,6,4,128]{3,2,1,0:T(4,128)}), f32[16,6,4,128]{3,2,1,0:T(4,128)S(1)}, u32[]{:S(2)}, u32[]{:S(2)}) async-start(f32[16,6,4,128]{3,2,1,0:T(4,128)} %select_add_fusion.7), calls=%async_computation.1 | async-start | bytes 393216 | tf_op jit(solution)/shard_map/while/body/eval_jaxpr/all_to_all | solution.py:120
  193.1 11.6 %all-to-all-start = ((f32[16,6,4,128]{3,2,1,0:T(4,128)}), f32[16,6,4,128]{3,2,1,0:T(4,128)S(1)}, u32[]{:S(2)}, u32[]{:S(2)}) async-start(f32[16,6,4,128]{3,2,1,0:T(4,128)} %bitcast.144), calls=%async_computation | async-start | bytes 393216 | tf_op jit(solution)/shard_map/while/body/eval_jaxpr/all_to_all | solution.py:120
  206.6 12.0 %all-to-all-start.1 = ((f32[16,6,4,128]{3,2,1,0:T(4,128)}), f32[16,6,4,128]{3,2,1,0:T(4,128)S(1)}, u32[]{:S(2)}, u32[]{:S(2)}) async-start(f32[16,6,4,128]{3,2,1,0:T(4,128)} %select_add_fusion.7), calls=%async_computation.1 | async-start | bytes 393216 | tf_op jit(solution)/shard_map/while/body/eval_jaxpr/all_to_all | solution.py:120
  220.1 16.9 %copy-start.2 = (f32[2,4,128,128]{3,2,1,0:T(8,128)S(1)}, f32[2,4,128,128]{3,2,1,0:T(8,128)}, u32[]{:S(2)}) copy-start(f32[2,4,128,128]{3,2,1,0:T(8,128)} %param.28) | copy-start | bytes 1572868
  240.3 22.3 %all-to-all-start.5 = ((f32[16,6,12,128]{3,2,1,0:T(8,128)}), f32[16,6,12,128]{3,2,1,0:T(8,128)S(1)}, u32[]{:S(2)}, u32[]{:S(2)}) async-start(f32[16,6,12,128]{3,2,1,0:T(8,128)} %pad_maximum_fusion), calls=%async_computation.5 | async-start | bytes 1572864 | tf_op jit(solution)/shard_map/all_to_all | solution.py:120
  264.5 1.3 collective-permute-start.1

commit v15 on v14

--- a/solution.py
+++ b/solution.py
@@ -180,13 +180,13 @@
     own_out_direction = own_matvec(own_values, direction)
     partial = solution
     shares = returned[:, :head_count]
-    shared = weight_b * shares + own_matvec(own_keys, direction)
+    shared = weight_col * shares + own_matvec(own_keys, direction)
     product = (
-        decay_b * shared
-        + write_b * key_now * lane_sum(key_now * direction)
-        + ridge_b * direction
-    )
-    step_last = norm_now / lane_sum(direction * product)
+        decay_col * shared
+        + write_col * key_now * jnp.sum(key_now * direction, axis=2, keepdims=True)
+        + ridge_col * direction
+    )
+    step_last = norm_now[:, :, :1] / jnp.sum(direction * product, axis=2, keepdims=True)
     solution = partial + step_last * direction
     value_sum = returned[:, head_count : 2 * head_count] + step_last * returned[:, 2 * head_count :]
     own_out = own_out_partial + step_last * own_out_direction

time: 268 us -> 269 us (level)
  no operation moved by 1% of the time
where the time goes in v15:
time: 269 us; the launch traced here: 267 us
  waiting for transfers between devices  90 us (33%)
  starting transfers between devices  63.7 us (24%)
  other arithmetic  58.4 us (22%)
  local copies, waits for them, and re-layouts  29.4 us (11%)
  blocking collectives  14.3 us (5%)
  matrix products  9.7 us (4%)
    all_to_all x15, waiting for transfers between devices, exchange(): lax.all_to_all(shaped, 'req', split_axis=0, concat_axis=0, tiled=True)  88.7 us
    all_to_all x15, starting transfers between devices, exchange(): lax.all_to_all(shaped, 'req', split_axis=0, concat_axis=0, tiled=True)  63.1 us
    reduce_sum x8, other arithmetic, own_matvec(): return jnp.sum(matrices * vectors[:, :, None, :], axis=3)  39.3 us
    all_to_all x1, blocking collectives, exchange(): lax.all_to_all(shaped, 'req', split_axis=0, concat_axis=0, tiled=True)  14.3 us
    gather x9, local copies, waits for them, and re-layouts, pack(): return jnp.take(padded, source, axis=0, mode='clip')  10.3 us
    add x8, other arithmetic, owner_apply(): total + jnp.where(chosen[group][:, None, None], products[group], 0.0)  6.94 us
    unnamed x26, local copies, waits for them, and re-layouts  6.37 us
    dot_general x10, matrix products, owner_apply(): products = jnp.einsum('shj,ghij->gshi', incoming, states, precision=highest)  6.33 us
  transfers between devices with their start and end apart: 17, of which 16 were waited for; matrix products, arithmetic and copies ran while one was open for 19% of the time, Pallas kernels for 0%

profile of v15, /device:TPU:0, one launch (start us, length us, event | category | flops | bytes accessed | tf_op | source)
XLA Modules:
  0.0 266.8 jit_solution(13402622639683498236)
XLA Ops:
  5.4 6.0 %copy.143 = bf16[1024,4,3,128]{0,3,2,1:T(8,128)(2,1)} copy(bf16[1024,4,3,128]{3,1,2,0:T(4,128)(2,1)} %param.19) | data formatting | bytes 6291456 | tf_op args[2]
  16.8 7.9 %all-to-all-start.2 = ((f32[16,6,5,128]{3,1,2,0:T(8,128)}), f32[16,6,5,128]{3,1,2,0:T(8,128)S(1)}, u32[]{:S(2)}, u32[]{:S(2)}) async-start(f32[16,6,5,128]{3,1,2,0:T(8,128)} %copy.153), calls=%async_computation.2 | async-start | bytes 655360 | tf_op jit(solution)/shard_map/all_to_all | solution.py:120
  24.9 11.8 %all-to-all-done.2 = f32[16,6,5,128]{3,1,2,0:T(8,128)S(1)} async-done(((f32[16,6,5,128]{3,1,2,0:T(8,128)}), f32[16,6,5,128]{3,1,2,0:T(8,128)S(1)}, u32[]{:S(2)}, u32[]{:S(2)}) %all-to-all-start.2) | async-done | bytes 245792 | tf_op jit(solution)/shard_map/all_to_all | solution.py:120
  39.0 3.5 %all-to-all-start.3 = ((f32[16,6,4,128]{3,2,1,0:T(4,128)}), f32[16,6,4,128]{3,2,1,0:T(4,128)S(1)}, u32[]{:S(2)}, u32[]{:S(2)}) async-start(f32[16,6,4,128]{3,2,1,0:T(4,128)} %select_add_fusion.4), calls=%async_computation.3 | async-start | bytes 393216 | tf_op jit(solution)/shard_map/all_to_all | solution.py:120
  42.7 4.5 %multiply_reduce_fusion.7 = f32[24,4,128]{2,1,0:T(4,128)S(1)} fusion(f32[24,4,128,128]{3,2,1,0:T(8,128)} %param.25, f32[24,4,128]{2,1,0:T(4,128)S(1)} %copy.159), kind=kLoop, calls=%fused_computation.37 | loop fusion | flops 3133440 | bytes 6389760 | tf_op jit(solution)/shard_map/reduce_sum | solution.py:16
  52.0 168.1 %while.19 = (s32[]{:T(128)}, f32[24,4,128]{2,1,0:T(4,128)S(1)}, f32[24,4,128]{2,1,0:T(4,128)S(1)}, f32[24,4,128]{2,1,0:T(4,128)S(1)}, f32[24,4,128]{2,1,0:T(4,12...) while((s32[]{:T(128)}, f32[24,4,128]{2,1,0:T(4,128)S(1)}, ...), condition=%wide.region_17.18_spmd.clone, body=%wide.region_12.17_spmd.clone.sunk | while | flops 154524000 | bytes 12433049 | solution.py:163
  53.4 3.6 %all-to-all-start = ((f32[16,6,4,128]{3,2,1,0:T(4,128)}), f32[16,6,4,128]{3,2,1,0:T(4,128)S(1)}, u32[]{:S(2)}, u32[]{:S(2)}) async-start(f32[16,6,4,128]{3,2,1,0:T(4,128)} %bitcast.150), calls=%async_computation | async-start | bytes 393216 | tf_op jit(solution)/shard_map/while/body/eval_jaxpr/all_to_all | solution.py:120
  57.2 7.9 %all-to-all-done = f32[16,6,4,128]{3,2,1,0:T(4,128)S(1)} async-done(((f32[16,6,4,128]{3,2,1,0:T(4,128)}), f32[16,6,4,128]{3,2,1,0:T(4,128)S(1)}, u32[]{:S(2)}, u32[]{:S(2)}) %all-to-all-start) | async-done | bytes 196640 | tf_op jit(solution)/shard_map/while/body/eval_jaxpr/all_to_all | solution.py:120
  67.0 3.5 %all-to-all-start.1 = ((f32[16,6,4,128]{3,2,1,0:T(4,128)}), f32[16,6,4,128]{3,2,1,0:T(4,128)S(1)}, u32[]{:S(2)}, u32[]{:S(2)}) async-start(f32[16,6,4,128]{3,2,1,0:T(4,128)} %select_add_fusion.7), calls=%async_computation.1 | async-start | bytes 393216 | tf_op jit(solution)/shard_map/while/body/eval_jaxpr/all_to_all | solution.py:120
  70.5 4.5 %multiply_reduce_fusion.16 = f32[24,4,128]{2,1,0:T(4,128)S(1)} fusion(f32[24,4,128,128]{3,2,1,0:T(8,128)} %get-tuple-element.570, f32[24,4,128]{2,1,0:T(4,128)S(1)} %get-tuple-element.543), kind=kLoop, calls=%fused_computation.12.clone.1 | loop fusion | flops 3133440 | bytes 6389760 | tf_op jit(solution)/shard_map/while/body/eval_jaxpr/reduce_sum | solution.py:16
  75.0 3.5 %all-to-all-done.1 = f32[16,6,4,128]{3,2,1,0:T(4,128)S(1)} async-done(((f32[16,6,4,128]{3,2,1,0:T(4,128)}), f32[16,6,4,128]{3,2,1,0:T(4,128)S(1)}, u32[]{:S(2)}, u32[]{:S(2)}) %all-to-all-start.1) | async-done | bytes 196640 | tf_op jit(solution)/shard_map/while/body/eval_jaxpr/all_to_all | solution.py:120
  85.1 7.9 %all-to-all-done = f32[16,6,4,128]{3,2,1,0:T(4,128)S(1)} async-done(((f32[16,6,4,128]{3,2,1,0:T(4,128)}), f32[16,6,4,128]{3,2,1,0:T(4,128)S(1)}, u32[]{:S(2)}, u32[]{:S(2)}) %all-to-all-start) | async-done | bytes 196640 | tf_op jit(solution)/shard_map/while/body/eval_jaxpr/all_to_all | solution.py:120
  94.9 3.5 %all-to-all-start.1 = ((f32[16,6,4,128]{3,2,1,0:T(4,128)}), f32[16,6,4,128]{3,2,1,0:T(4,128)S(1)}, u32[]{:S(2)}, u32[]{:S(2)}) async-start(f32[16,6,4,128]{3,2,1,0:T(4,128)} %select_add_fusion.7), calls=%async_computation.1 | async-start | bytes 393216 | tf_op jit(solution)/shard_map/while/body/eval_jaxpr/all_to_all | solution.py:120
  98.4 4.5 %multiply_reduce_fusion.16 = f32[24,4,128]{2,1,0:T(4,128)S(1)} fusion(f32[24,4,128,128]{3,2,1,0:T(8,128)} %get-tuple-element.570, f32[24,4,128]{2,1,0:T(4,128)S(1)} %get-tuple-element.543), kind=kLoop, calls=%fused_computation.12.clone.1 | loop fusion | flops 3133440 | bytes 6389760 | tf_op jit(solution)/shard_map/while/body/eval_jaxpr/reduce_sum | solution.py:16
  102.9 3.5 %all-to-all-done.1 = f32[16,6,4,128]{3,2,1,0:T(4,128)S(1)} async-done(((f32[16,6,4,128]{3,2,1,0:T(4,128)}), f32[16,6,4,128]{3,2,1,0:T(4,128)S(1)}, u32[]{:S(2)}, u32[]{:S(2)}) %all-to-all-start.1) | async-done | bytes 196640 | tf_op jit(solution)/shard_map/while/body/eval_jaxpr/all_to_all | solution.py:120
  113.1 7.9 %all-to-all-done = f32[16,6,4,128]{3,2,1,0:T(4,128)S(1)} async-done(((f32[16,6,4,128]{3,2,1,0:T(4,128)}), f32[16,6,4,128]{3,2,1,0:T(4,128)S(1)}, u32[]{:S(2)}, u32[]{:S(2)}) %all-to-all-start) | async-done | bytes 196640 | tf_op jit(solution)/shard_map/while/body/eval_jaxpr/all_to_all | solution.py:120
  126.3 4.5 %multiply_reduce_fusion.16 = f32[24,4,128]{2,1,0:T(4,128)S(1)} fusion(f32[24,4,128,128]{3,2,1,0:T(8,128)} %get-tuple-element.570, f32[24,4,128]{2,1,0:T(4,128)S(1)} %get-tuple-element.543), kind=kLoop, calls=%fused_computation.12.clone.1 | loop fusion | flops 3133440 | bytes 6389760 | tf_op jit(solution)/shard_map/while/body/eval_jaxpr/reduce_sum | solution.py:16
  130.8 3.5 %all-to-all-done.1 = f32[16,6,4,128]{3,2,1,0:T(4,128)S(1)} async-done(((f32[16,6,4,128]{3,2,1,0:T(4,128)}), f32[16,6,4,128]{3,2,1,0:T(4,128)S(1)}, u32[]{:S(2)}, u32[]{:S(2)}) %all-to-all-start.1) | async-done | bytes 196640 | tf_op jit(solution)/shard_map/while/body/eval_jaxpr/all_to_all | solution.py:120
  141.0 7.9 %all-to-all-done = f32[16,6,4,128]{3,2,1,0:T(4,128)S(1)} async-done(((f32[16,6,4,128]{3,2,1,0:T(4,128)}), f32[16,6,4,128]{3,2,1,0:T(4,128)S(1)}, u32[]{:S(2)}, u32[]{:S(2)}) %all-to-all-start) | async-done | bytes 196640 | tf_op jit(solution)/shard_map/while/body/eval_jaxpr/all_to_all | solution.py:120
  154.3 4.5 %multiply_reduce_fusion.16 = f32[24,4,128]{2,1,0:T(4,128)S(1)} fusion(f32[24,4,128,128]{3,2,1,0:T(8,128)} %get-tuple-element.570, f32[24,4,128]{2,1,0:T(4,128)S(1)} %get-tuple-element.543), kind=kLoop, calls=%fused_computation.12.clone.1 | loop fusion | flops 3133440 | bytes 6389760 | tf_op jit(solution)/shard_map/while/body/eval_jaxpr/reduce_sum | solution.py:16
  158.8 3.5 %all-to-all-done.1 = f32[16,6,4,128]{3,2,1,0:T(4,128)S(1)} async-done(((f32[16,6,4,128]{3,2,1,0:T(4,128)}), f32[16,6,4,128]{3,2,1,0:T(4,128)S(1)}, u32[]{:S(2)}, u32[]{:S(2)}) %all-to-all-start.1) | async-done | bytes 196640 | tf_op jit(solution)/shard_map/while/body/eval_jaxpr/all_to_all | solution.py:120
  168.9 7.9 %all-to-all-done = f32[16,6,4,128]{3,2,1,0:T(4,128)S(1)} async-done(((f32[16,6,4,128]{3,2,1,0:T(4,128)}), f32[16,6,4,128]{3,2,1,0:T(4,128)S(1)}, u32[]{:S(2)}, u32[]{:S(2)}) %all-to-all-start) | async-done | bytes 196640 | tf_op jit(solution)/shard_map/while/body/eval_jaxpr/all_to_all | solution.py:120
  182.2 4.5 %multiply_reduce_fusion.16 = f32[24,4,128]{2,1,0:T(4,128)S(1)} fusion(f32[24,4,128,128]{3,2,1,0:T(8,128)} %get-tuple-element.570, f32[24,4,128]{2,1,0:T(4,128)S(1)} %get-tuple-element.543), kind=kLoop, calls=%fused_computation.12.clone.1 | loop fusion | flops 3133440 | bytes 6389760 | tf_op jit(solution)/shard_map/while/body/eval_jaxpr/reduce_sum | solution.py:16
  186.7 3.6 %all-to-all-done.1 = f32[16,6,4,128]{3,2,1,0:T(4,128)S(1)} async-done(((f32[16,6,4,128]{3,2,1,0:T(4,128)}), f32[16,6,4,128]{3,2,1,0:T(4,128)S(1)}, u32[]{:S(2)}, u32[]{:S(2)}) %all-to-all-start.1) | async-done | bytes 196640 | tf_op jit(solution)/shard_map/while/body/eval_jaxpr/all_to_all | solution.py:120
  196.9 7.9 %all-to-all-done = f32[16,6,4,128]{3,2,1,0:T(4,128)S(1)} async-done(((f32[16,6,4,128]{3,2,1,0:T(4,128)}), f32[16,6,4,128]{3,2,1,0:T(4,128)S(1)}, u32[]{:S(2)}, u32[]{:S(2)}) %all-to-all-start) | async-done | bytes 196640 | tf_op jit(solution)/shard_map/while/body/eval_jaxpr/all_to_all | solution.py:120
  206.6 3.9 %all-to-all-start.1 = ((f32[16,6,4,128]{3,2,1,0:T(4,128)}), f32[16,6,4,128]{3,2,1,0:T(4,128)S(1)}, u32[]{:S(2)}, u32[]{:S(2)}) async-start(f32[16,6,4,128]{3,2,1,0:T(4,128)} %select_add_fusion.7), calls=%async_computation.1 | async-start | bytes 393216 | tf_op jit(solution)/shard_map/while/body/eval_jaxpr/all_to_all | solution.py:120
  210.5 4.5 %multiply_reduce_fusion.16 = f32[24,4,128]{2,1,0:T(4,128)S(1)} fusion(f32[24,4,128,128]{3,2,1,0:T(8,128)} %get-tuple-element.570, f32[24,4,128]{2,1,0:T(4,128)S(1)} %get-tuple-element.543), kind=kLoop, calls=%fused_computation.12.clone.1 | loop fusion | flops 3133440 | bytes 6389760 | tf_op jit(solution)/shard_map/while/body/eval_jaxpr/reduce_sum | solution.py:16
  215.0 3.6 %all-to-all-done.1 = f32[16,6,4,128]{3,2,1,0:T(4,128)S(1)} async-done(((f32[16,6,4,128]{3,2,1,0:T(4,128)}), f32[16,6,4,128]{3,2,1,0:T(4,128)S(1)}, u32[]{:S(2)}, u32[]{:S(2)}) %all-to-all-start.1) | async-done | bytes 196640 | tf_op jit(solution)/shard_map/while/body/eval_jaxpr/all_to_all | solution.py:120
  221.7 14.3 %all_to_all.38 = f32[16,6,8,128]{3,2,1,0:T(8,128)S(1)} all-to-all(f32[16,6,8,128]{3,2,1,0:T(8,128)S(1)} %bitcast.160), channel_id=1, replica_groups=mesh['req'=16,'head'=2] {'req'}, dimensions={0} | all-to-all | bytes 786432 | tf_op jit(solution)/shard_map/all_to_all | solution.py:120
  240.3 9.0 %all-to-all-start.5 = ((f32[16,6,12,128]{3,2,1,0:T(8,128)}), f32[16,6,12,128]{3,2,1,0:T(8,128)S(1)}, u32[]{:S(2)}, u32[]{:S(2)}) async-start(f32[16,6,12,128]{3,2,1,0:T(8,128)} %pad_maximum_fusion), calls=%async_computation.5 | async-start | bytes 1572864 | tf_op jit(solution)/shard_map/all_to_all | solution.py:120
  249.4 7.9 %multiply_reduce_fusion.4 = (f32[24,4,128]{2,1,0:T(4,128)S(1)}, f32[24,4,128]{2,1,0:T(4,128)S(1)}, f32[24,4,128]{2,1,0:T(4,128)S(1)}) fusion(f32[24,4,128,128]{3,2,1,0:T(8,128)} %param.26, f32[24,4,128]{2,1,0:T(4,128)S(1)} %get-tuple-element.201, f32[24,4,128]{2,1,0:T(4,128)S(1)} %get-tuple-element.202, f32[24,4,128,128]{3,2,1,0:T(8,128)} %get-tuple-element.578), kind=kLoop, calls=%fused_computation.34 | loop fusion | flops 9400320 | bytes 12828672 | tf_op jit(solution)/shard_map/reduce_sum | solution.py:16
  257.4 5.2 %all-to-all-done.5 = f32[16,6,12,128]{3,2,1,0:T(8,128)S(1)} async-done(((f32[16,6,12,128]{3,2,1,0:T(8,128)}), f32[16,6,12,128]{3,2,1,0:T(8,128)S(1)}, u32[]{:S(2)}, u32[]{:S(2)}) %all-to-all-start.5) | async-done | bytes 589856 | tf_op jit(solution)/shard_map/all_to_all | solution.py:120
  (216 shorter events, 85.4 us)
Async XLA Ops:
  0.0 264.5 %copy-start = (bf16[4,128,1024]{2,1,0:T(8,128)(2,1)S(1)}, bf16[4,128,1024]{2,1,0:T(8,128)(2,1)}, u32[]{:S(2)}) copy-start(bf16[4,128,1024]{2,1,0:T(8,128)(2,1)} %param.31) | copy-start | bytes 3145732
  0.0 11.5 %copy-start.3 = (bf16[24,512]{1,0:T(8,128)(2,1)S(1)}, bf16[24,512]{1,0:T(8,128)(2,1)}, u32[]{:S(2)}) copy-start(bf16[24,512]{1,0:T(8,128)(2,1)} %param.17) | copy-start | bytes 73732
  0.0 11.5 %copy-start.4 = (bf16[1024,2,4]{0,2,1:T(4,128)(2,1)S(1)}, bf16[1024,2,4]{0,2,1:T(4,128)(2,1)}, u32[]{:S(2)}) copy-start(bf16[1024,2,4]{0,2,1:T(4,128)(2,1)} %param.22) | copy-start | bytes 49156
  0.0 11.7 %copy-start.6 = (f32[1024]{0:T(1024)S(1)}, f32[1024]{0:T(1024)}, u32[]{:S(2)}) copy-start(f32[1024]{0:T(1024)} %param.18) | copy-start | bytes 12292
  0.0 11.5 %collective-permute-start = (bf16[24,512]{1,0:T(8,128)(2,1)}, bf16[24,512]{1,0:T(8,128)(2,1)S(1)}, u32[]{:S(2)}, u32[]{:S(2)}) collective-permute-start(bf16[24,512]{1,0:T(8,128)(2,1)} %param.17), channel_id=1, source_target_pairs={{0,1},{1,0},{2,3},{3,2},{4,5},{5,4},{6,7},{7,6},{8,9},{9,8},{10,11... | collective-permute-start | bytes 73736 | tf_op jit(solution)/shard_map/ppermute | solution.py:37
  5.4 19.3 %copy-start.1 = (f32[2,4,128,128]{3,2,1,0:T(8,128)S(1)}, f32[2,4,128,128]{3,2,1,0:T(8,128)}, u32[]{:S(2)}) copy-start(f32[2,4,128,128]{3,2,1,0:T(8,128)} %param.27) | copy-start | bytes 1572868
  5.4 19.4 %copy-start.5 = (f32[24,4]{0,1:T(4,128)S(1)}, f32[24,4]{0,1:T(4,128)}, u32[]{:S(2)}) copy-start(f32[24,4]{0,1:T(4,128)} %param.23) | copy-start | bytes 1156
  16.8 19.9 %all-to-all-start.2 = ((f32[16,6,5,128]{3,1,2,0:T(8,128)}), f32[16,6,5,128]{3,1,2,0:T(8,128)S(1)}, u32[]{:S(2)}, u32[]{:S(2)}) async-start(f32[16,6,5,128]{3,1,2,0:T(8,128)} %copy.153), calls=%async_computation.2 | async-start | bytes 655360 | tf_op jit(solution)/shard_map/all_to_all | solution.py:120
  24.8 26.4 %copy-start.7 = (f32[4]{0:T(128)S(1)}, f32[4]{0:T(128)}, u32[]{:S(2)}) copy-start(f32[4]{0:T(128)} %param.24) | copy-start | bytes 52
  39.0 11.6 %all-to-all-start.3 = ((f32[16,6,4,128]{3,2,1,0:T(4,128)}), f32[16,6,4,128]{3,2,1,0:T(4,128)S(1)}, u32[]{:S(2)}, u32[]{:S(2)}) async-start(f32[16,6,4,128]{3,2,1,0:T(4,128)} %select_add_fusion.4), calls=%async_computation.3 | async-start | bytes 393216 | tf_op jit(solution)/shard_map/all_to_all | solution.py:120
  53.4 11.7 %all-to-all-start = ((f32[16,6,4,128]{3,2,1,0:T(4,128)}), f32[16,6,4,128]{3,2,1,0:T(4,128)S(1)}, u32[]{:S(2)}, u32[]{:S(2)}) async-start(f32[16,6,4,128]{3,2,1,0:T(4,128)} %bitcast.150), calls=%async_computation | async-start | bytes 393216 | tf_op jit(solution)/shard_map/while/body/eval_jaxpr/all_to_all | solution.py:120
  67.0 11.6 %all-to-all-start.1 = ((f32[16,6,4,128]{3,2,1,0:T(4,128)}), f32[16,6,4,128]{3,2,1,0:T(4,128)S(1)}, u32[]{:S(2)}, u32[]{:S(2)}) async-start(f32[16,6,4,128]{3,2,1,0:T(4,128)} %select_add_fusion.7), calls=%async_computation.1 | async-start | bytes 393216 | tf_op jit(solution)/shard_map/while/body/eval_jaxpr/all_to_all | solution.py:120
  81.4 11.6 %all-to-all-start = ((f32[16,6,4,128]{3,2,1,0:T(4,128)}), f32[16,6,4,128]{3,2,1,0:T(4,128)S(1)}, u32[]{:S(2)}, u32[]{:S(2)}) async-start(f32[16,6,4,128]{3,2,1,0:T(4,128)} %bitcast.150), calls=%async_computation | async-start | bytes 393216 | tf_op jit(solution)/shard_map/while/body/eval_jaxpr/all_to_all | solution.py:120
  94.9 11.6 %all-to-all-start.1 = ((f32[16,6,4,128]{3,2,1,0:T(4,128)}), f32[16,6,4,128]{3,2,1,0:T(4,128)S(1)}, u32[]{:S(2)}, u32[]{:S(2)}) async-start(f32[16,6,4,128]{3,2,1,0:T(4,128)} %select_add_fusion.7), calls=%async_computation.1 | async-start | bytes 393216 | tf_op jit(solution)/shard_map/while/body/eval_jaxpr/all_to_all | solution.py:120
  109.3 11.6 %all-to-all-start = ((f32[16,6,4,128]{3,2,1,0:T(4,128)}), f32[16,6,4,128]{3,2,1,0:T(4,128)S(1)}, u32[]{:S(2)}, u32[]{:S(2)}) async-start(f32[16,6,4,128]{3,2,1,0:T(4,128)} %bitcast.150), calls=%async_computation | async-start | bytes 393216 | tf_op jit(solution)/shard_map/while/body/eval_jaxpr/all_to_all | solution.py:120
  122.8 11.6 %all-to-all-start.1 = ((f32[16,6,4,128]{3,2,1,0:T(4,128)}), f32[16,6,4,128]{3,2,1,0:T(4,128)S(1)}, u32[]{:S(2)}, u32[]{:S(2)}) async-start(f32[16,6,4,128]{3,2,1,0:T(4,128)} %select_add_fusion.7), calls=%async_computation.1 | async-start | bytes 393216 | tf_op jit(solution)/shard_map/while/body/eval_jaxpr/all_to_all | solution.py:120
  137.3 11.6 %all-to-all-start = ((f32[16,6,4,128]{3,2,1,0:T(4,128)}), f32[16,6,4,128]{3,2,1,0:T(4,128)S(1)}, u32[]{:S(2)}, u32[]{:S(2)}) async-start(f32[16,6,4,128]{3,2,1,0:T(4,128)} %bitcast.150), calls=%async_computation | async-start | bytes 393216 | tf_op jit(solution)/shard_map/while/body/eval_jaxpr/all_to_all | solution.py:120
  150.7 11.6 %all-to-all-start.1 = ((f32[16,6,4,128]{3,2,1,0:T(4,128)}), f32[16,6,4,128]{3,2,1,0:T(4,128)S(1)}, u32[]{:S(2)}, u32[]{:S(2)}) async-start(f32[16,6,4,128]{3,2,1,0:T(4,128)} %select_add_fusion.7), calls=%async_computation.1 | async-start | bytes 393216 | tf_op jit(solution)/shard_map/while/body/eval_jaxpr/all_to_all | solution.py:120
  165.2 11.6 %all-to-all-start = ((f32[16,6,4,128]{3,2,1,0:T(4,128)}), f32[16,6,4,128]{3,2,1,0:T(4,128)S(1)}, u32[]{:S(2)}, u32[]{:S(2)}) async-start(f32[16,6,4,128]{3,2,1,0:T(4,128)} %bitcast.150), calls=%async_computation | async-start | bytes 393216 | tf_op jit(solution)/shard_map/while/body/eval_jaxpr/all_to_all | solution.py:120
  178.7 11.6 %all-to-all-start.1 = ((f32[16,6,4,128]{3,2,1,0:T(4,128)}), f32[16,6,4,128]{3,2,1,0:T(4,128)S(1)}, u32[]{:S(2)}, u32[]{:S(2)}) async-start(f32[16,6,4,128]{3,2,1,0:T(4,128)} %select_add_fusion.7), calls=%async_computation.1 | async-start | bytes 393216 | tf_op jit(solution)/shard_map/while/body/eval_jaxpr/all_to_all | solution.py:120
  193.2 11.6 %all-to-all-start = ((f32[16,6,4,128]{3,2,1,0:T(4,128)}), f32[16,6,4,128]{3,2,1,0:T(4,128)S(1)}, u32[]{:S(2)}, u32[]{:S(2)}) async-start(f32[16,6,4,128]{3,2,1,0:T(4,128)} %bitcast.150), calls=%async_computation | async-start | bytes 393216 | tf_op jit(solution)/shard_map/while/body/eval_jaxpr/all_to_all | solution.py:120
  206.6 12.0 %all-to-all-start.1 = ((f32[16,6,4,128]{3,2,1,0:T(4,128)}), f32[16,6,4,128]{3,2,1,0:T(4,128)S(1)}, u32[]{:S(2)}, u32[]{:S(2)}) async-start(f32[16,6,4,128]{3,2,1,0:T(4,128)} %select_add_fusion.7), calls=%async_computation.1 | async-start | bytes 393216 | tf_op jit(solution)/shard_map/while/body/eval_jaxpr/all_to_all | solution.py:120
  220.1 16.9 %copy-start.2 = (f32[2,4,128,128]{3,2,1,0:T(8,128)S(1)}, f32[2,4,128,128]{3,2,1,0:T(8,128)}, u32[]{:S(2)}) copy-start(f32[2,4,128,128]{3,2,1,0:T(8,128)} %param.28) | copy-start | bytes 1572868
  240.3 22.3 %all-to-all-start.5 = ((f32[16,6,12,128]{3,2,1,0:T(8,128)}), f32[16,6,12,128]{3,2,1,0:T(8,128)S(1)}, u32[]{:S(2)}, u32[]{:S(2)}) async-start(f32[16,6,12,128]{3,2,1,0:T(8,128)} %pad_maximum_fusion), calls=%async_computation.5 | async-start | bytes 1572864 | tf_op jit(solution)/shard_map/all_to_all | solution.py:120
  264.8 1.3 collective-permute-start.1

commit v16 on v12

--- a/solution.py
+++ b/solution.py
@@ -189,19 +189,26 @@
     normalized = (
         readout * lax.rsqrt(jnp.mean(readout * readout, axis=2, keepdims=True) + epsilon)
     ).astype(jnp.bfloat16)
-    partial_value = jnp.dot(
-        normalized.reshape(row_count, head_count * head_size),
-        out_weight.reshape(head_count * head_size, model_width),
-        preferred_element_type=jnp.float32,
-    )
+    flat = normalized.reshape(row_count, head_count * head_size)
+    weight_flat = out_weight.reshape(head_count * head_size, model_width)
     head_peers = lax.axis_size("head")
     if head_peers == 2:
         me = lax.axis_index("head")
         width = model_width // 2
-        mine = lax.dynamic_slice_in_dim(partial_value, me * width, width, axis=1)
-        theirs = lax.dynamic_slice_in_dim(partial_value, (1 - me) * width, width, axis=1)
-        attended = mine + lax.ppermute(theirs, "head", [(0, 1), (1, 0)])
+        theirs = jnp.dot(
+            flat,
+            lax.dynamic_slice_in_dim(weight_flat, (1 - me) * width, width, axis=1),
+            preferred_element_type=jnp.float32,
+        )
+        arriving = lax.ppermute(theirs, "head", [(0, 1), (1, 0)])
+        mine = jnp.dot(
+            flat,
+            lax.dynamic_slice_in_dim(weight_flat, me * width, width, axis=1),
+            preferred_element_type=jnp.float32,
+        )
+        attended = mine + arriving
     else:
+        partial_value = jnp.dot(flat, weight_flat, preferred_element_type=jnp.float32)
         attended = lax.psum_scatter(
             partial_value.astype(jnp.bfloat16), "head", scatter_dimension=1, tiled=True
         ).astype(jnp.float32)

time: 264 us -> 264 us (level)
  no operation moved by 1% of the time
where the time goes in v16:
time: 264 us; the launch traced here: 262 us
  waiting for transfers between devices  88.8 us (34%)
  other arithmetic  58.5 us (22%)
  starting transfers between devices  58.3 us (22%)
  local copies, waits for them, and re-layouts  32 us (12%)
  blocking collectives  13.2 us (5%)
  matrix products  10.5 us (4%)
    all_to_all x15, waiting for transfers between devices, exchange(): lax.all_to_all(shaped, 'req', split_axis=0, concat_axis=0, tiled=True)  87.6 us
    all_to_all x15, starting transfers between devices, exchange(): lax.all_to_all(shaped, 'req', split_axis=0, concat_axis=0, tiled=True)  57.8 us
    reduce_sum x8, other arithmetic, own_matvec(): return jnp.sum(matrices * vectors[:, :, None, :], axis=3)  39.3 us
    all_to_all x1, blocking collectives, exchange(): lax.all_to_all(shaped, 'req', split_axis=0, concat_axis=0, tiled=True)  13.2 us
    gather x9, local copies, waits for them, and re-layouts, pack(): return jnp.take(padded, source, axis=0, mode='clip')  10.3 us
    add x8, other arithmetic, owner_apply(): total + jnp.where(chosen[group][:, None, None], products[group], 0.0)  6.94 us
    dot_general x10, matrix products, owner_apply(): products = jnp.einsum('shj,ghij->gshi', incoming, states, precision=highest)  6.33 us
    unnamed x19, local copies, waits for them, and re-layouts  6.13 us
  transfers between devices with their start and end apart: 17, of which 16 were waited for; matrix products, arithmetic and copies ran while one was open for 20% of the time, Pallas kernels for 0%

profile of v16, /device:TPU:0, one launch (start us, length us, event | category | flops | bytes accessed | tf_op | source)
XLA Modules:
  0.0 262.5 jit_solution(16518394848097606944)
XLA Ops:
  5.4 6.0 %copy.153 = bf16[1024,4,3,128]{0,3,2,1:T(8,128)(2,1)} copy(bf16[1024,4,3,128]{3,1,2,0:T(4,128)(2,1)} %param.19) | data formatting | bytes 6291456 | tf_op args[2]
  16.5 7.9 %all-to-all-start.2 = ((f32[16,6,5,128]{3,1,2,0:T(8,128)}), f32[16,6,5,128]{3,1,2,0:T(8,128)S(1)}, u32[]{:S(2)}, u32[]{:S(2)}) async-start(f32[16,6,5,128]{3,1,2,0:T(8,128)} %copy.163), calls=%async_computation.2 | async-start | bytes 655360 | tf_op jit(solution)/shard_map/all_to_all | solution.py:112
  24.9 11.5 %all-to-all-done.2 = f32[16,6,5,128]{3,1,2,0:T(8,128)S(1)} async-done(((f32[16,6,5,128]{3,1,2,0:T(8,128)}), f32[16,6,5,128]{3,1,2,0:T(8,128)S(1)}, u32[]{:S(2)}, u32[]{:S(2)}) %all-to-all-start.2) | async-done | bytes 245792 | tf_op jit(solution)/shard_map/all_to_all | solution.py:112
  38.6 3.5 %all-to-all-start.3 = ((f32[16,6,4,128]{3,2,1,0:T(4,128)}), f32[16,6,4,128]{3,2,1,0:T(4,128)S(1)}, u32[]{:S(2)}, u32[]{:S(2)}) async-start(f32[16,6,4,128]{3,2,1,0:T(4,128)} %select_add_fusion.4), calls=%async_computation.3 | async-start | bytes 393216 | tf_op jit(solution)/shard_map/all_to_all | solution.py:112
  42.2 4.5 %multiply_reduce_fusion.7 = f32[24,4,128]{2,1,0:T(4,128)S(1)} fusion(f32[24,4,128,128]{3,2,1,0:T(8,128)} %param.25, f32[24,4,128]{2,1,0:T(4,128)S(1)} %copy.169), kind=kLoop, calls=%fused_computation.33 | loop fusion | flops 3133440 | bytes 6389760 | tf_op jit(solution)/shard_map/reduce_sum | solution.py:16
  51.5 170.8 %while.16 = (s32[]{:T(128)}, f32[24,4,128]{2,1,0:T(4,128)S(1)}, f32[24,4,128]{2,1,0:T(4,128)S(1)}, f32[24,4,128]{2,1,0:T(4,128)S(1)}, f32[24,4,1]{0,1,2:T(4,128)...) while((s32[]{:T(128)}, f32[24,4,128]{2,1,0:T(4,128)S(1)}, ...), condition=%wide.region_17.18_spmd, body=%wide.region_12.17_spmd.sunk | while | flops 154523872 | bytes 12098585 | solution.py:155
  56.7 7.9 %all-to-all-done = f32[16,6,4,128]{3,2,1,0:T(4,128)S(1)} async-done(((f32[16,6,4,128]{3,2,1,0:T(4,128)}), f32[16,6,4,128]{3,2,1,0:T(4,128)S(1)}, u32[]{:S(2)}, u32[]{:S(2)}) %all-to-all-start) | async-done | bytes 196640 | tf_op jit(solution)/shard_map/while/body/eval_jaxpr/all_to_all | solution.py:112
  66.4 3.5 %all-to-all-start.1 = ((f32[16,6,4,128]{3,2,1,0:T(4,128)}), f32[16,6,4,128]{3,2,1,0:T(4,128)S(1)}, u32[]{:S(2)}, u32[]{:S(2)}) async-start(f32[16,6,4,128]{3,2,1,0:T(4,128)} %select_add_fusion.7), calls=%async_computation.1 | async-start | bytes 393216 | tf_op jit(solution)/shard_map/while/body/eval_jaxpr/all_to_all | solution.py:112
  70.2 4.5 %multiply_reduce_fusion.17 = f32[24,4,128]{2,1,0:T(4,128)S(1)} fusion(f32[24,4,128,128]{3,2,1,0:T(8,128)} %get-tuple-element.428, f32[24,4,128]{2,1,0:T(4,128)S(1)} %get-tuple-element.399), kind=kLoop, calls=%fused_computation.8.clone.1 | loop fusion | flops 3133440 | bytes 6389760 | tf_op jit(solution)/shard_map/while/body/eval_jaxpr/reduce_sum | solution.py:16
  81.2 3.6 %all-to-all-start = ((f32[16,6,4,128]{3,2,1,0:T(4,128)}), f32[16,6,4,128]{3,2,1,0:T(4,128)S(1)}, u32[]{:S(2)}, u32[]{:S(2)}) async-start(f32[16,6,4,128]{3,2,1,0:T(4,128)} %bitcast.194), calls=%async_computation | async-start | bytes 393216 | tf_op jit(solution)/shard_map/while/body/eval_jaxpr/all_to_all | solution.py:112
  85.1 7.9 %all-to-all-done = f32[16,6,4,128]{3,2,1,0:T(4,128)S(1)} async-done(((f32[16,6,4,128]{3,2,1,0:T(4,128)}), f32[16,6,4,128]{3,2,1,0:T(4,128)S(1)}, u32[]{:S(2)}, u32[]{:S(2)}) %all-to-all-start) | async-done | bytes 196640 | tf_op jit(solution)/shard_map/while/body/eval_jaxpr/all_to_all | solution.py:112
  94.8 3.5 %all-to-all-start.1 = ((f32[16,6,4,128]{3,2,1,0:T(4,128)}), f32[16,6,4,128]{3,2,1,0:T(4,128)S(1)}, u32[]{:S(2)}, u32[]{:S(2)}) async-start(f32[16,6,4,128]{3,2,1,0:T(4,128)} %select_add_fusion.7), calls=%async_computation.1 | async-start | bytes 393216 | tf_op jit(solution)/shard_map/while/body/eval_jaxpr/all_to_all | solution.py:112
  98.6 4.5 %multiply_reduce_fusion.17 = f32[24,4,128]{2,1,0:T(4,128)S(1)} fusion(f32[24,4,128,128]{3,2,1,0:T(8,128)} %get-tuple-element.428, f32[24,4,128]{2,1,0:T(4,128)S(1)} %get-tuple-element.399), kind=kLoop, calls=%fused_computation.8.clone.1 | loop fusion | flops 3133440 | bytes 6389760 | tf_op jit(solution)/shard_map/while/body/eval_jaxpr/reduce_sum | solution.py:16
  109.7 3.6 %all-to-all-start = ((f32[16,6,4,128]{3,2,1,0:T(4,128)}), f32[16,6,4,128]{3,2,1,0:T(4,128)S(1)}, u32[]{:S(2)}, u32[]{:S(2)}) async-start(f32[16,6,4,128]{3,2,1,0:T(4,128)} %bitcast.194), calls=%async_computation | async-start | bytes 393216 | tf_op jit(solution)/shard_map/while/body/eval_jaxpr/all_to_all | solution.py:112
  113.5 7.9 %all-to-all-done = f32[16,6,4,128]{3,2,1,0:T(4,128)S(1)} async-done(((f32[16,6,4,128]{3,2,1,0:T(4,128)}), f32[16,6,4,128]{3,2,1,0:T(4,128)S(1)}, u32[]{:S(2)}, u32[]{:S(2)}) %all-to-all-start) | async-done | bytes 196640 | tf_op jit(solution)/shard_map/while/body/eval_jaxpr/all_to_all | solution.py:112
  127.1 4.5 %multiply_reduce_fusion.17 = f32[24,4,128]{2,1,0:T(4,128)S(1)} fusion(f32[24,4,128,128]{3,2,1,0:T(8,128)} %get-tuple-element.428, f32[24,4,128]{2,1,0:T(4,128)S(1)} %get-tuple-element.399), kind=kLoop, calls=%fused_computation.8.clone.1 | loop fusion | flops 3133440 | bytes 6389760 | tf_op jit(solution)/shard_map/while/body/eval_jaxpr/reduce_sum | solution.py:16
  138.1 3.6 %all-to-all-start = ((f32[16,6,4,128]{3,2,1,0:T(4,128)}), f32[16,6,4,128]{3,2,1,0:T(4,128)S(1)}, u32[]{:S(2)}, u32[]{:S(2)}) async-start(f32[16,6,4,128]{3,2,1,0:T(4,128)} %bitcast.194), calls=%async_computation | async-start | bytes 393216 | tf_op jit(solution)/shard_map/while/body/eval_jaxpr/all_to_all | solution.py:112
  141.9 7.9 %all-to-all-done = f32[16,6,4,128]{3,2,1,0:T(4,128)S(1)} async-done(((f32[16,6,4,128]{3,2,1,0:T(4,128)}), f32[16,6,4,128]{3,2,1,0:T(4,128)S(1)}, u32[]{:S(2)}, u32[]{:S(2)}) %all-to-all-start) | async-done | bytes 196640 | tf_op jit(solution)/shard_map/while/body/eval_jaxpr/all_to_all | solution.py:112
  151.7 3.5 %all-to-all-start.1 = ((f32[16,6,4,128]{3,2,1,0:T(4,128)}), f32[16,6,4,128]{3,2,1,0:T(4,128)S(1)}, u32[]{:S(2)}, u32[]{:S(2)}) async-start(f32[16,6,4,128]{3,2,1,0:T(4,128)} %select_add_fusion.7), calls=%async_computation.1 | async-start | bytes 393216 | tf_op jit(solution)/shard_map/while/body/eval_jaxpr/all_to_all | solution.py:112
  155.5 4.5 %multiply_reduce_fusion.17 = f32[24,4,128]{2,1,0:T(4,128)S(1)} fusion(f32[24,4,128,128]{3,2,1,0:T(8,128)} %get-tuple-element.428, f32[24,4,128]{2,1,0:T(4,128)S(1)} %get-tuple-element.399), kind=kLoop, calls=%fused_computation.8.clone.1 | loop fusion | flops 3133440 | bytes 6389760 | tf_op jit(solution)/shard_map/while/body/eval_jaxpr/reduce_sum | solution.py:16
  166.5 3.6 %all-to-all-start = ((f32[16,6,4,128]{3,2,1,0:T(4,128)}), f32[16,6,4,128]{3,2,1,0:T(4,128)S(1)}, u32[]{:S(2)}, u32[]{:S(2)}) async-start(f32[16,6,4,128]{3,2,1,0:T(4,128)} %bitcast.194), calls=%async_computation | async-start | bytes 393216 | tf_op jit(solution)/shard_map/while/body/eval_jaxpr/all_to_all | solution.py:112
  170.4 7.9 %all-to-all-done = f32[16,6,4,128]{3,2,1,0:T(4,128)S(1)} async-done(((f32[16,6,4,128]{3,2,1,0:T(4,128)}), f32[16,6,4,128]{3,2,1,0:T(4,128)S(1)}, u32[]{:S(2)}, u32[]{:S(2)}) %all-to-all-start) | async-done | bytes 196640 | tf_op jit(solution)/shard_map/while/body/eval_jaxpr/all_to_all | solution.py:112
  180.2 3.5 %all-to-all-start.1 = ((f32[16,6,4,128]{3,2,1,0:T(4,128)}), f32[16,6,4,128]{3,2,1,0:T(4,128)S(1)}, u32[]{:S(2)}, u32[]{:S(2)}) async-start(f32[16,6,4,128]{3,2,1,0:T(4,128)} %select_add_fusion.7), calls=%async_computation.1 | async-start | bytes 393216 | tf_op jit(solution)/shard_map/while/body/eval_jaxpr/all_to_all | solution.py:112
  183.9 4.5 %multiply_reduce_fusion.17 = f32[24,4,128]{2,1,0:T(4,128)S(1)} fusion(f32[24,4,128,128]{3,2,1,0:T(8,128)} %get-tuple-element.428, f32[24,4,128]{2,1,0:T(4,128)S(1)} %get-tuple-element.399), kind=kLoop, calls=%fused_computation.8.clone.1 | loop fusion | flops 3133440 | bytes 6389760 | tf_op jit(solution)/shard_map/while/body/eval_jaxpr/reduce_sum | solution.py:16
  195.0 3.6 %all-to-all-start = ((f32[16,6,4,128]{3,2,1,0:T(4,128)}), f32[16,6,4,128]{3,2,1,0:T(4,128)S(1)}, u32[]{:S(2)}, u32[]{:S(2)}) async-start(f32[16,6,4,128]{3,2,1,0:T(4,128)} %bitcast.194), calls=%async_computation | async-start | bytes 393216 | tf_op jit(solution)/shard_map/while/body/eval_jaxpr/all_to_all | solution.py:112
  198.8 8.0 %all-to-all-done = f32[16,6,4,128]{3,2,1,0:T(4,128)S(1)} async-done(((f32[16,6,4,128]{3,2,1,0:T(4,128)}), f32[16,6,4,128]{3,2,1,0:T(4,128)S(1)}, u32[]{:S(2)}, u32[]{:S(2)}) %all-to-all-start) | async-done | bytes 196640 | tf_op jit(solution)/shard_map/while/body/eval_jaxpr/all_to_all | solution.py:112
  212.5 4.5 %multiply_reduce_fusion.17 = f32[24,4,128]{2,1,0:T(4,128)S(1)} fusion(f32[24,4,128,128]{3,2,1,0:T(8,128)} %get-tuple-element.428, f32[24,4,128]{2,1,0:T(4,128)S(1)} %get-tuple-element.399), kind=kLoop, calls=%fused_computation.8.clone.1 | loop fusion | flops 3133440 | bytes 6389760 | tf_op jit(solution)/shard_map/while/body/eval_jaxpr/reduce_sum | solution.py:16
  217.0 3.6 %all-to-all-done.1 = f32[16,6,4,128]{3,2,1,0:T(4,128)S(1)} async-done(((f32[16,6,4,128]{3,2,1,0:T(4,128)}), f32[16,6,4,128]{3,2,1,0:T(4,128)S(1)}, u32[]{:S(2)}, u32[]{:S(2)}) %all-to-all-start.1) | async-done | bytes 196640 | tf_op jit(solution)/shard_map/while/body/eval_jaxpr/all_to_all | solution.py:112
  223.9 13.2 %all_to_all.32 = f32[16,6,8,128]{3,2,1,0:T(8,128)S(1)} all-to-all(f32[16,6,8,128]{3,2,1,0:T(8,128)S(1)} %bitcast.209), channel_id=1, replica_groups=mesh['req'=16,'head'=2] {'req'}, dimensions={0} | all-to-all | bytes 786432 | tf_op jit(solution)/shard_map/all_to_all | solution.py:112
  241.4 3.6 %all-to-all-start.5 = ((f32[16,6,12,128]{3,2,1,0:T(8,128)}), f32[16,6,12,128]{3,2,1,0:T(8,128)S(1)}, u32[]{:S(2)}, u32[]{:S(2)}) async-start(f32[16,6,12,128]{3,2,1,0:T(8,128)} %pad_maximum_fusion), calls=%async_computation.5 | async-start | bytes 1572864 | tf_op jit(solution)/shard_map/all_to_all | solution.py:112
  245.0 7.9 %multiply_reduce_fusion.4 = (f32[24,4,128]{2,1,0:T(4,128)S(1)}, f32[24,4,128]{2,1,0:T(4,128)S(1)}, f32[24,4,128]{2,1,0:T(4,128)S(1)}) fusion(f32[24,4,128,128]{3,2,1,0:T(8,128)} %param.26, f32[24,4,128]{2,1,0:T(4,128)S(1)} %get-tuple-element.94, f32[24,4,128]{2,1,0:T(4,128)S(1)} %get-tuple-element.95, f32[24,4,128,128]{3,2,1,0:T(8,128)} %get-tuple-element.434), kind=kLoop, calls=%fused_computation.30 | loop fusion | flops 9400320 | bytes 12828672 | tf_op jit(solution)/shard_map/reduce_sum | solution.py:16
  253.0 5.3 %all-to-all-done.5 = f32[16,6,12,128]{3,2,1,0:T(8,128)S(1)} async-done(((f32[16,6,12,128]{3,2,1,0:T(8,128)}), f32[16,6,12,128]{3,2,1,0:T(8,128)S(1)}, u32[]{:S(2)}, u32[]{:S(2)}) %all-to-all-start.5) | async-done | bytes 589856 | tf_op jit(solution)/shard_map/all_to_all | solution.py:112
  (263 shorter events, 87.8 us)
Async XLA Ops:
  0.0 260.2 %copy-start = (bf16[4,128,1024]{2,1,0:T(8,128)(2,1)S(1)}, bf16[4,128,1024]{2,1,0:T(8,128)(2,1)}, u32[]{:S(2)}) copy-start(bf16[4,128,1024]{2,1,0:T(8,128)(2,1)} %param.31) | copy-start | bytes 3145732
  0.0 11.5 %copy-start.3 = (bf16[24,512]{1,0:T(8,128)(2,1)S(1)}, bf16[24,512]{1,0:T(8,128)(2,1)}, u32[]{:S(2)}) copy-start(bf16[24,512]{1,0:T(8,128)(2,1)} %param.17) | copy-start | bytes 73732
  0.0 11.6 %copy-start.6 = (f32[1024]{0:T(1024)S(1)}, f32[1024]{0:T(1024)}, u32[]{:S(2)}) copy-start(f32[1024]{0:T(1024)} %param.18) | copy-start | bytes 12292
  0.0 11.5 %collective-permute-start = (bf16[24,512]{1,0:T(8,128)(2,1)}, bf16[24,512]{1,0:T(8,128)(2,1)S(1)}, u32[]{:S(2)}, u32[]{:S(2)}) collective-permute-start(bf16[24,512]{1,0:T(8,128)(2,1)} %param.17), channel_id=1, source_target_pairs={{0,1},{1,0},{2,3},{3,2},{4,5},{5,4},{6,7},{7,6},{8,9},{9,8},{10,11... | collective-permute-start | bytes 73736 | tf_op jit(solution)/shard_map/ppermute | solution.py:37
  5.4 19.1 %copy-start.5 = (bf16[1024,2,4]{0,2,1:T(4,128)(2,1)S(1)}, bf16[1024,2,4]{0,2,1:T(4,128)(2,1)}, u32[]{:S(2)}) copy-start(bf16[1024,2,4]{0,2,1:T(4,128)(2,1)} %param.22) | copy-start | bytes 49156
  5.4 19.1 %copy-start.1 = (f32[2,4,128,128]{3,2,1,0:T(8,128)S(1)}, f32[2,4,128,128]{3,2,1,0:T(8,128)}, u32[]{:S(2)}) copy-start(f32[2,4,128,128]{3,2,1,0:T(8,128)} %param.27) | copy-start | bytes 1572868
  16.5 19.9 %all-to-all-start.2 = ((f32[16,6,5,128]{3,1,2,0:T(8,128)}), f32[16,6,5,128]{3,1,2,0:T(8,128)S(1)}, u32[]{:S(2)}, u32[]{:S(2)}) async-start(f32[16,6,5,128]{3,1,2,0:T(8,128)} %copy.163), calls=%async_computation.2 | async-start | bytes 655360 | tf_op jit(solution)/shard_map/all_to_all | solution.py:112
  24.6 26.3 %copy-start.4 = (f32[24,4]{0,1:T(4,128)S(1)}, f32[24,4]{0,1:T(4,128)}, u32[]{:S(2)}) copy-start(f32[24,4]{0,1:T(4,128)} %param.23) | copy-start | bytes 1156
  24.6 26.3 %copy-start.7 = (f32[4]{0:T(128)S(1)}, f32[4]{0:T(128)}, u32[]{:S(2)}) copy-start(f32[4]{0:T(128)} %param.24) | copy-start | bytes 52
  38.6 11.6 %all-to-all-start.3 = ((f32[16,6,4,128]{3,2,1,0:T(4,128)}), f32[16,6,4,128]{3,2,1,0:T(4,128)S(1)}, u32[]{:S(2)}, u32[]{:S(2)}) async-start(f32[16,6,4,128]{3,2,1,0:T(4,128)} %select_add_fusion.4), calls=%async_computation.3 | async-start | bytes 393216 | tf_op jit(solution)/shard_map/all_to_all | solution.py:112
  52.9 11.6 %all-to-all-start = ((f32[16,6,4,128]{3,2,1,0:T(4,128)}), f32[16,6,4,128]{3,2,1,0:T(4,128)S(1)}, u32[]{:S(2)}, u32[]{:S(2)}) async-start(f32[16,6,4,128]{3,2,1,0:T(4,128)} %bitcast.194), calls=%async_computation | async-start | bytes 393216 | tf_op jit(solution)/shard_map/while/body/eval_jaxpr/all_to_all | solution.py:112
  66.4 11.6 %all-to-all-start.1 = ((f32[16,6,4,128]{3,2,1,0:T(4,128)}), f32[16,6,4,128]{3,2,1,0:T(4,128)S(1)}, u32[]{:S(2)}, u32[]{:S(2)}) async-start(f32[16,6,4,128]{3,2,1,0:T(4,128)} %select_add_fusion.7), calls=%async_computation.1 | async-start | bytes 393216 | tf_op jit(solution)/shard_map/while/body/eval_jaxpr/all_to_all | solution.py:112
  81.2 11.7 %all-to-all-start = ((f32[16,6,4,128]{3,2,1,0:T(4,128)}), f32[16,6,4,128]{3,2,1,0:T(4,128)S(1)}, u32[]{:S(2)}, u32[]{:S(2)}) async-start(f32[16,6,4,128]{3,2,1,0:T(4,128)} %bitcast.194), calls=%async_computation | async-start | bytes 393216 | tf_op jit(solution)/shard_map/while/body/eval_jaxpr/all_to_all | solution.py:112
  94.8 11.6 %all-to-all-start.1 = ((f32[16,6,4,128]{3,2,1,0:T(4,128)}), f32[16,6,4,128]{3,2,1,0:T(4,128)S(1)}, u32[]{:S(2)}, u32[]{:S(2)}) async-start(f32[16,6,4,128]{3,2,1,0:T(4,128)} %select_add_fusion.7), calls=%async_computation.1 | async-start | bytes 393216 | tf_op jit(solution)/shard_map/while/body/eval_jaxpr/all_to_all | solution.py:112
  109.7 11.7 %all-to-all-start = ((f32[16,6,4,128]{3,2,1,0:T(4,128)}), f32[16,6,4,128]{3,2,1,0:T(4,128)S(1)}, u32[]{:S(2)}, u32[]{:S(2)}) async-start(f32[16,6,4,128]{3,2,1,0:T(4,128)} %bitcast.194), calls=%async_computation | async-start | bytes 393216 | tf_op jit(solution)/shard_map/while/body/eval_jaxpr/all_to_all | solution.py:112
  123.3 11.6 %all-to-all-start.1 = ((f32[16,6,4,128]{3,2,1,0:T(4,128)}), f32[16,6,4,128]{3,2,1,0:T(4,128)S(1)}, u32[]{:S(2)}, u32[]{:S(2)}) async-start(f32[16,6,4,128]{3,2,1,0:T(4,128)} %select_add_fusion.7), calls=%async_computation.1 | async-start | bytes 393216 | tf_op jit(solution)/shard_map/while/body/eval_jaxpr/all_to_all | solution.py:112
  138.1 11.7 %all-to-all-start = ((f32[16,6,4,128]{3,2,1,0:T(4,128)}), f32[16,6,4,128]{3,2,1,0:T(4,128)S(1)}, u32[]{:S(2)}, u32[]{:S(2)}) async-start(f32[16,6,4,128]{3,2,1,0:T(4,128)} %bitcast.194), calls=%async_computation | async-start | bytes 393216 | tf_op jit(solution)/shard_map/while/body/eval_jaxpr/all_to_all | solution.py:112
  151.7 11.6 %all-to-all-start.1 = ((f32[16,6,4,128]{3,2,1,0:T(4,128)}), f32[16,6,4,128]{3,2,1,0:T(4,128)S(1)}, u32[]{:S(2)}, u32[]{:S(2)}) async-start(f32[16,6,4,128]{3,2,1,0:T(4,128)} %select_add_fusion.7), calls=%async_computation.1 | async-start | bytes 393216 | tf_op jit(solution)/shard_map/while/body/eval_jaxpr/all_to_all | solution.py:112
  166.5 11.7 %all-to-all-start = ((f32[16,6,4,128]{3,2,1,0:T(4,128)}), f32[16,6,4,128]{3,2,1,0:T(4,128)S(1)}, u32[]{:S(2)}, u32[]{:S(2)}) async-start(f32[16,6,4,128]{3,2,1,0:T(4,128)} %bitcast.194), calls=%async_computation | async-start | bytes 393216 | tf_op jit(solution)/shard_map/while/body/eval_jaxpr/all_to_all | solution.py:112
  180.2 11.6 %all-to-all-start.1 = ((f32[16,6,4,128]{3,2,1,0:T(4,128)}), f32[16,6,4,128]{3,2,1,0:T(4,128)S(1)}, u32[]{:S(2)}, u32[]{:S(2)}) async-start(f32[16,6,4,128]{3,2,1,0:T(4,128)} %select_add_fusion.7), calls=%async_computation.1 | async-start | bytes 393216 | tf_op jit(solution)/shard_map/while/body/eval_jaxpr/all_to_all | solution.py:112
  195.0 11.8 %all-to-all-start = ((f32[16,6,4,128]{3,2,1,0:T(4,128)}), f32[16,6,4,128]{3,2,1,0:T(4,128)S(1)}, u32[]{:S(2)}, u32[]{:S(2)}) async-start(f32[16,6,4,128]{3,2,1,0:T(4,128)} %bitcast.194), calls=%async_computation | async-start | bytes 393216 | tf_op jit(solution)/shard_map/while/body/eval_jaxpr/all_to_all | solution.py:112
  208.7 11.9 %all-to-all-start.1 = ((f32[16,6,4,128]{3,2,1,0:T(4,128)}), f32[16,6,4,128]{3,2,1,0:T(4,128)S(1)}, u32[]{:S(2)}, u32[]{:S(2)}) async-start(f32[16,6,4,128]{3,2,1,0:T(4,128)} %select_add_fusion.7), calls=%async_computation.1 | async-start | bytes 393216 | tf_op jit(solution)/shard_map/while/body/eval_jaxpr/all_to_all | solution.py:112
  222.4 15.8 %copy-start.2 = (f32[2,4,128,128]{3,2,1,0:T(8,128)S(1)}, f32[2,4,128,128]{3,2,1,0:T(8,128)}, u32[]{:S(2)}) copy-start(f32[2,4,128,128]{3,2,1,0:T(8,128)} %param.28) | copy-start | bytes 1572868
  241.4 16.8 %all-to-all-start.5 = ((f32[16,6,12,128]{3,2,1,0:T(8,128)}), f32[16,6,12,128]{3,2,1,0:T(8,128)S(1)}, u32[]{:S(2)}, u32[]{:S(2)}) async-start(f32[16,6,12,128]{3,2,1,0:T(8,128)} %pad_maximum_fusion), calls=%async_computation.5 | async-start | bytes 1572864 | tf_op jit(solution)/shard_map/all_to_all | solution.py:112
  260.4 1.2 collective-permute-start.1

commit v17 on v12

--- a/solution.py
+++ b/solution.py
@@ -117,11 +117,10 @@
         return jnp.where(routed[:, None, None], taken, 0.0)
 
     def owner_apply(states, incoming, chosen):
-        products = jnp.einsum("shj,ghij->gshi", incoming, states, precision=highest)
-        total = jnp.where(chosen[0][:, None, None], products[0], 0.0)
-        for group in range(1, group_count):
-            total = total + jnp.where(chosen[group][:, None, None], products[group], 0.0)
-        return total
+        split = jnp.stack(
+            [jnp.where(chosen[group][:, None, None], incoming, 0.0) for group in range(group_count)]
+        )
+        return jnp.einsum("gshj,ghij->shi", split, states, precision=highest)
 
     def cg_step(arrived, carry):
         solution, residual, direction, norm_now = carry

time: 264 us -> 266 us (level)
  blocking collectives: 13.1 us -> 82.4 us
  waiting for transfers between devices: 88.8 us -> 41.2 us
  starting transfers between devices: 58.3 us -> 37.1 us
    all_to_all x1 -> x7, blocking collectives: 13.1 us -> 82.4 us  [exchange(): lax.all_to_all(shaped, 'req', split_axis=0, concat_axis=0, tiled=True)]
    all_to_all x15 -> x9, waiting for transfers between devices: 87.6 us -> 40 us  [exchange(): lax.all_to_all(shaped, 'req', split_axis=0, concat_axis=0, tiled=True)]
    all_to_all x15 -> x9, starting transfers between devices: 57.8 us -> 36.5 us  [exchange(): lax.all_to_all(shaped, 'req', split_axis=0, concat_axis=0, tiled=True)]
    add x8 -> x0, other arithmetic: 6.94 us -> none  [owner_apply(): total + jnp.where(chosen[group][:, None, None], products[group], 0.0)]
    transpose x0 -> x7, local copies, waits for them, and re-layouts: none -> 5.62 us  [owner_apply(): return jnp.einsum('gshj,ghij->shi', split, states, precision=highest)]
    mul x7, other arithmetic: 3.23 us -> 7.83 us  [cg_step(): write_col * key_now * jnp.sum(key_now * direction, axis=2, keepdims=True)]
    gather x9, local copies, waits for them, and re-layouts: 10.3 us -> 6.33 us  [pack(): return jnp.take(padded, source, axis=0, mode='clip')]
    slice x30 -> x0, local copies, waits for them, and re-layouts: 2.88 us -> none  [the longest x20 1.58 us: owner_apply(): total = jnp.where(chosen[0][:, None, None], products[0], 0.0)]
  transfers between devices with their start and end apart: 17 -> 11, of which waited for: 16 -> 10; matrix products, arithmetic and copies ran while one was open for 20% -> 20% of each run, Pallas kernels for 0% -> 0%
where the time goes in v17:
time: 266 us; the launch traced here: 264 us
  blocking collectives  82.4 us (31%)
  other arithmetic  59.6 us (22%)
  waiting for transfers between devices  41.2 us (15%)
  starting transfers between devices  37.1 us (14%)
  local copies, waits for them, and re-layouts  32.7 us (12%)
  matrix products  10 us (4%)
    all_to_all x7, blocking collectives, exchange(): lax.all_to_all(shaped, 'req', split_axis=0, concat_axis=0, tiled=True)  82.4 us
    all_to_all x9, waiting for transfers between devices, exchange(): lax.all_to_all(shaped, 'req', split_axis=0, concat_axis=0, tiled=True)  40 us
    reduce_sum x8, other arithmetic, own_matvec(): return jnp.sum(matrices * vectors[:, :, None, :], axis=3)  39.3 us
    all_to_all x9, starting transfers between devices, exchange(): lax.all_to_all(shaped, 'req', split_axis=0, concat_axis=0, tiled=True)  36.5 us
    mul x7, other arithmetic, cg_step(): write_col * key_now * jnp.sum(key_now * direction, axis=2, keepdims=True)  7.83 us
    dot_general x10, matrix products, owner_apply(): return jnp.einsum('gshj,ghij->shi', split, states, precision=highest)  6.65 us
    gather x9, local copies, waits for them, and re-layouts, pack(): return jnp.take(padded, source, axis=0, mode='clip')  6.33 us
    unnamed x23, local copies, waits for them, and re-layouts  6.14 us
  transfers between devices with their start and end apart: 11, of which 10 were waited for; matrix products, arithmetic and copies ran while one was open for 20% of the time, Pallas kernels for 0%

profile of v17, /device:TPU:0, one launch (start us, length us, event | category | flops | bytes accessed | tf_op | source)
XLA Modules:
  0.0 264.0 jit_solution(6738423337919055562)
XLA Ops:
  7.2 6.0 %copy.143 = bf16[1024,4,3,128]{0,3,2,1:T(8,128)(2,1)} copy(bf16[1024,4,3,128]{3,1,2,0:T(4,128)(2,1)} %param.19) | data formatting | bytes 6291456 | tf_op args[2]
  18.2 8.1 %all-to-all-start.2 = ((f32[16,6,5,128]{3,1,2,0:T(8,128)}), f32[16,6,5,128]{3,1,2,0:T(8,128)S(1)}, u32[]{:S(2)}, u32[]{:S(2)}) async-start(f32[16,6,5,128]{3,1,2,0:T(8,128)} %copy.153), calls=%async_computation.2 | async-start | bytes 655360 | tf_op jit(solution)/shard_map/all_to_all | solution.py:112
  26.7 11.5 %all-to-all-done.2 = f32[16,6,5,128]{3,1,2,0:T(8,128)S(1)} async-done(((f32[16,6,5,128]{3,1,2,0:T(8,128)}), f32[16,6,5,128]{3,1,2,0:T(8,128)S(1)}, u32[]{:S(2)}, u32[]{:S(2)}) %all-to-all-start.2) | async-done | bytes 245792 | tf_op jit(solution)/shard_map/all_to_all | solution.py:112
  40.0 3.5 %all-to-all-start.3 = ((f32[16,6,4,128]{3,2,1,0:T(4,128)}), f32[16,6,4,128]{3,2,1,0:T(4,128)S(1)}, u32[]{:S(2)}, u32[]{:S(2)}) async-start(f32[16,6,4,128]{3,2,1,0:T(4,128)} %bitcast.38), calls=%async_computation.3 | async-start | bytes 393216 | tf_op jit(solution)/shard_map/all_to_all | solution.py:112
  43.6 4.5 %multiply_reduce_fusion.7 = f32[24,4,128]{2,1,0:T(4,128)S(1)} fusion(f32[24,4,128,128]{3,2,1,0:T(8,128)} %param.25, f32[24,4,128]{2,1,0:T(4,128)S(1)} %copy.159), kind=kLoop, calls=%fused_computation.37 | loop fusion | flops 3133440 | bytes 6389760 | tf_op jit(solution)/shard_map/reduce_sum | solution.py:16
  48.1 3.5 %all-to-all-done.3 = f32[16,6,4,128]{3,2,1,0:T(4,128)S(1)} async-done(((f32[16,6,4,128]{3,2,1,0:T(4,128)}), f32[16,6,4,128]{3,2,1,0:T(4,128)S(1)}, u32[]{:S(2)}, u32[]{:S(2)}) %all-to-all-start.3) | async-done | bytes 196640 | tf_op jit(solution)/shard_map/all_to_all | solution.py:112
  53.5 167.3 %while.16 = (s32[]{:T(128)}, f32[24,4,128]{2,1,0:T(4,128)S(1)}, f32[24,4,128]{2,1,0:T(4,128)S(1)}, f32[24,4,128]{2,1,0:T(4,128)S(1)}, f32[24,4,1]{0,1,2:T(4,128)...) while((s32[]{:T(128)}, f32[24,4,128]{2,1,0:T(4,128)S(1)}, ...), condition=%wide.region_17.18_spmd, body=%wide.region_12.17_spmd.sunk | while | flops 154573024 | bytes 10721913 | solution.py:154
  54.3 11.3 %all_to_all.33 = f32[16,6,4,128]{3,2,1,0:T(4,128)S(1)} all-to-all(f32[16,6,4,128]{3,2,1,0:T(4,128)S(1)} %bitcast.196), channel_id=1, replica_groups=mesh['req'=16,'head'=2] {'req'}, dimensions={0} | all-to-all | bytes 393216 | tf_op jit(solution)/shard_map/while/body/eval_jaxpr/all_to_all | solution.py:112
  67.2 3.5 %all-to-all-start.1 = ((f32[16,6,4,128]{3,2,1,0:T(4,128)}), f32[16,6,4,128]{3,2,1,0:T(4,128)S(1)}, u32[]{:S(2)}, u32[]{:S(2)}) async-start(f32[16,6,4,128]{3,2,1,0:T(4,128)} %bitcast.191), calls=%async_computation.1 | async-start | bytes 393216 | tf_op jit(solution)/shard_map/while/body/eval_jaxpr/all_to_all | solution.py:112
  71.0 4.5 %multiply_reduce_fusion.17 = f32[24,4,128]{2,1,0:T(4,128)S(1)} fusion(f32[24,4,128,128]{3,2,1,0:T(8,128)} %get-tuple-element.425, f32[24,4,128]{2,1,0:T(4,128)S(1)} %get-tuple-element.396), kind=kLoop, calls=%fused_computation.8.clone.1 | loop fusion | flops 3133440 | bytes 6389760 | tf_op jit(solution)/shard_map/while/body/eval_jaxpr/reduce_sum | solution.py:16
  75.5 3.3 %all-to-all-done.1 = f32[16,6,4,128]{3,2,1,0:T(4,128)S(1)} async-done(((f32[16,6,4,128]{3,2,1,0:T(4,128)}), f32[16,6,4,128]{3,2,1,0:T(4,128)S(1)}, u32[]{:S(2)}, u32[]{:S(2)}) %all-to-all-start.1) | async-done | bytes 196640 | tf_op jit(solution)/shard_map/while/body/eval_jaxpr/all_to_all | solution.py:112
  82.0 11.5 %all_to_all.33 = f32[16,6,4,128]{3,2,1,0:T(4,128)S(1)} all-to-all(f32[16,6,4,128]{3,2,1,0:T(4,128)S(1)} %bitcast.196), channel_id=1, replica_groups=mesh['req'=16,'head'=2] {'req'}, dimensions={0} | all-to-all | bytes 393216 | tf_op jit(solution)/shard_map/while/body/eval_jaxpr/all_to_all | solution.py:112
  95.1 3.5 %all-to-all-start.1 = ((f32[16,6,4,128]{3,2,1,0:T(4,128)}), f32[16,6,4,128]{3,2,1,0:T(4,128)S(1)}, u32[]{:S(2)}, u32[]{:S(2)}) async-start(f32[16,6,4,128]{3,2,1,0:T(4,128)} %bitcast.191), calls=%async_computation.1 | async-start | bytes 393216 | tf_op jit(solution)/shard_map/while/body/eval_jaxpr/all_to_all | solution.py:112
  98.9 4.5 %multiply_reduce_fusion.17 = f32[24,4,128]{2,1,0:T(4,128)S(1)} fusion(f32[24,4,128,128]{3,2,1,0:T(8,128)} %get-tuple-element.425, f32[24,4,128]{2,1,0:T(4,128)S(1)} %get-tuple-element.396), kind=kLoop, calls=%fused_computation.8.clone.1 | loop fusion | flops 3133440 | bytes 6389760 | tf_op jit(solution)/shard_map/while/body/eval_jaxpr/reduce_sum | solution.py:16
  109.9 11.5 %all_to_all.33 = f32[16,6,4,128]{3,2,1,0:T(4,128)S(1)} all-to-all(f32[16,6,4,128]{3,2,1,0:T(4,128)S(1)} %bitcast.196), channel_id=1, replica_groups=mesh['req'=16,'head'=2] {'req'}, dimensions={0} | all-to-all | bytes 393216 | tf_op jit(solution)/shard_map/while/body/eval_jaxpr/all_to_all | solution.py:112
  123.0 3.5 %all-to-all-start.1 = ((f32[16,6,4,128]{3,2,1,0:T(4,128)}), f32[16,6,4,128]{3,2,1,0:T(4,128)S(1)}, u32[]{:S(2)}, u32[]{:S(2)}) async-start(f32[16,6,4,128]{3,2,1,0:T(4,128)} %bitcast.191), calls=%async_computation.1 | async-start | bytes 393216 | tf_op jit(solution)/shard_map/while/body/eval_jaxpr/all_to_all | solution.py:112
  126.8 4.5 %multiply_reduce_fusion.17 = f32[24,4,128]{2,1,0:T(4,128)S(1)} fusion(f32[24,4,128,128]{3,2,1,0:T(8,128)} %get-tuple-element.425, f32[24,4,128]{2,1,0:T(4,128)S(1)} %get-tuple-element.396), kind=kLoop, calls=%fused_computation.8.clone.1 | loop fusion | flops 3133440 | bytes 6389760 | tf_op jit(solution)/shard_map/while/body/eval_jaxpr/reduce_sum | solution.py:16
  131.3 3.3 %all-to-all-done.1 = f32[16,6,4,128]{3,2,1,0:T(4,128)S(1)} async-done(((f32[16,6,4,128]{3,2,1,0:T(4,128)}), f32[16,6,4,128]{3,2,1,0:T(4,128)S(1)}, u32[]{:S(2)}, u32[]{:S(2)}) %all-to-all-start.1) | async-done | bytes 196640 | tf_op jit(solution)/shard_map/while/body/eval_jaxpr/all_to_all | solution.py:112
  137.8 11.5 %all_to_all.33 = f32[16,6,4,128]{3,2,1,0:T(4,128)S(1)} all-to-all(f32[16,6,4,128]{3,2,1,0:T(4,128)S(1)} %bitcast.196), channel_id=1, replica_groups=mesh['req'=16,'head'=2] {'req'}, dimensions={0} | all-to-all | bytes 393216 | tf_op jit(solution)/shard_map/while/body/eval_jaxpr/all_to_all | solution.py:112
  150.9 3.5 %all-to-all-start.1 = ((f32[16,6,4,128]{3,2,1,0:T(4,128)}), f32[16,6,4,128]{3,2,1,0:T(4,128)S(1)}, u32[]{:S(2)}, u32[]{:S(2)}) async-start(f32[16,6,4,128]{3,2,1,0:T(4,128)} %bitcast.191), calls=%async_computation.1 | async-start | bytes 393216 | tf_op jit(solution)/shard_map/while/body/eval_jaxpr/all_to_all | solution.py:112
  154.7 4.5 %multiply_reduce_fusion.17 = f32[24,4,128]{2,1,0:T(4,128)S(1)} fusion(f32[24,4,128,128]{3,2,1,0:T(8,128)} %get-tuple-element.425, f32[24,4,128]{2,1,0:T(4,128)S(1)} %get-tuple-element.396), kind=kLoop, calls=%fused_computation.8.clone.1 | loop fusion | flops 3133440 | bytes 6389760 | tf_op jit(solution)/shard_map/while/body/eval_jaxpr/reduce_sum | solution.py:16
  165.7 11.5 %all_to_all.33 = f32[16,6,4,128]{3,2,1,0:T(4,128)S(1)} all-to-all(f32[16,6,4,128]{3,2,1,0:T(4,128)S(1)} %bitcast.196), channel_id=1, replica_groups=mesh['req'=16,'head'=2] {'req'}, dimensions={0} | all-to-all | bytes 393216 | tf_op jit(solution)/shard_map/while/body/eval_jaxpr/all_to_all | solution.py:112
  178.8 3.5 %all-to-all-start.1 = ((f32[16,6,4,128]{3,2,1,0:T(4,128)}), f32[16,6,4,128]{3,2,1,0:T(4,128)S(1)}, u32[]{:S(2)}, u32[]{:S(2)}) async-start(f32[16,6,4,128]{3,2,1,0:T(4,128)} %bitcast.191), calls=%async_computation.1 | async-start | bytes 393216 | tf_op jit(solution)/shard_map/while/body/eval_jaxpr/all_to_all | solution.py:112
  182.6 4.5 %multiply_reduce_fusion.17 = f32[24,4,128]{2,1,0:T(4,128)S(1)} fusion(f32[24,4,128,128]{3,2,1,0:T(8,128)} %get-tuple-element.425, f32[24,4,128]{2,1,0:T(4,128)S(1)} %get-tuple-element.396), kind=kLoop, calls=%fused_computation.8.clone.1 | loop fusion | flops 3133440 | bytes 6389760 | tf_op jit(solution)/shard_map/while/body/eval_jaxpr/reduce_sum | solution.py:16
  193.7 11.5 %all_to_all.33 = f32[16,6,4,128]{3,2,1,0:T(4,128)S(1)} all-to-all(f32[16,6,4,128]{3,2,1,0:T(4,128)S(1)} %bitcast.196), channel_id=1, replica_groups=mesh['req'=16,'head'=2] {'req'}, dimensions={0} | all-to-all | bytes 393216 | tf_op jit(solution)/shard_map/while/body/eval_jaxpr/all_to_all | solution.py:112
  206.8 3.5 %all-to-all-start.1 = ((f32[16,6,4,128]{3,2,1,0:T(4,128)}), f32[16,6,4,128]{3,2,1,0:T(4,128)S(1)}, u32[]{:S(2)}, u32[]{:S(2)}) async-start(f32[16,6,4,128]{3,2,1,0:T(4,128)} %bitcast.191), calls=%async_computation.1 | async-start | bytes 393216 | tf_op jit(solution)/shard_map/while/body/eval_jaxpr/all_to_all | solution.py:112
  210.5 4.5 %multiply_reduce_fusion.17 = f32[24,4,128]{2,1,0:T(4,128)S(1)} fusion(f32[24,4,128,128]{3,2,1,0:T(8,128)} %get-tuple-element.425, f32[24,4,128]{2,1,0:T(4,128)S(1)} %get-tuple-element.396), kind=kLoop, calls=%fused_computation.8.clone.1 | loop fusion | flops 3133440 | bytes 6389760 | tf_op jit(solution)/shard_map/while/body/eval_jaxpr/reduce_sum | solution.py:16
  215.0 3.3 %all-to-all-done.1 = f32[16,6,4,128]{3,2,1,0:T(4,128)S(1)} async-done(((f32[16,6,4,128]{3,2,1,0:T(4,128)}), f32[16,6,4,128]{3,2,1,0:T(4,128)S(1)}, u32[]{:S(2)}, u32[]{:S(2)}) %all-to-all-start.1) | async-done | bytes 196640 | tf_op jit(solution)/shard_map/while/body/eval_jaxpr/all_to_all | solution.py:112
  222.4 13.5 %all_to_all.32 = f32[16,6,8,128]{3,2,1,0:T(8,128)S(1)} all-to-all(f32[16,6,8,128]{3,2,1,0:T(8,128)S(1)} %bitcast.200), channel_id=1, replica_groups=mesh['req'=16,'head'=2] {'req'}, dimensions={0} | all-to-all | bytes 786432 | tf_op jit(solution)/shard_map/all_to_all | solution.py:112
  239.2 3.8 %all-to-all-start.5 = ((f32[16,6,12,128]{3,1,2,0:T(8,128)}), f32[16,6,12,128]{3,1,2,0:T(8,128)S(1)}, u32[]{:S(2)}, u32[]{:S(2)}) async-start(f32[16,6,12,128]{3,1,2,0:T(8,128)} %copy.169), calls=%async_computation.5 | async-start | bytes 1572864 | tf_op jit(solution)/shard_map/all_to_all | solution.py:112
  243.0 7.9 %multiply_reduce_fusion.4 = (f32[24,4,128]{2,1,0:T(4,128)S(1)}, f32[24,4,128]{2,1,0:T(4,128)S(1)}, f32[24,4,128]{2,1,0:T(4,128)S(1)}) fusion(f32[24,4,128,128]{3,2,1,0:T(8,128)} %param.26, f32[24,4,128]{2,1,0:T(4,128)S(1)} %get-tuple-element.94, f32[24,4,128]{2,1,0:T(4,128)S(1)} %get-tuple-element.95, f32[24,4,128,128]{3,2,1,0:T(8,128)} %get-tuple-element.431), kind=kLoop, calls=%fused_computation.34 | loop fusion | flops 9400320 | bytes 12828672 | tf_op jit(solution)/shard_map/reduce_sum | solution.py:16
  250.9 5.3 %all-to-all-done.5 = f32[16,6,12,128]{3,1,2,0:T(8,128)S(1)} async-done(((f32[16,6,12,128]{3,1,2,0:T(8,128)}), f32[16,6,12,128]{3,1,2,0:T(8,128)S(1)}, u32[]{:S(2)}, u32[]{:S(2)}) %all-to-all-start.5) | async-done | bytes 589856 | tf_op jit(solution)/shard_map/all_to_all | solution.py:112
  (228 shorter events, 68.6 us)
Async XLA Ops:
  0.0 261.7 %copy-start = (bf16[4,128,1024]{2,1,0:T(8,128)(2,1)S(1)}, bf16[4,128,1024]{2,1,0:T(8,128)(2,1)}, u32[]{:S(2)}) copy-start(bf16[4,128,1024]{2,1,0:T(8,128)(2,1)} %param.31) | copy-start | bytes 3145732
  0.0 13.2 %copy-start.3 = (bf16[24,512]{1,0:T(8,128)(2,1)S(1)}, bf16[24,512]{1,0:T(8,128)(2,1)}, u32[]{:S(2)}) copy-start(bf16[24,512]{1,0:T(8,128)(2,1)} %param.17) | copy-start | bytes 73732
  0.0 13.4 %copy-start.7 = (f32[1024]{0:T(1024)S(1)}, f32[1024]{0:T(1024)}, u32[]{:S(2)}) copy-start(f32[1024]{0:T(1024)} %param.18) | copy-start | bytes 12292
  0.0 13.2 %collective-permute-start = (bf16[24,512]{1,0:T(8,128)(2,1)}, bf16[24,512]{1,0:T(8,128)(2,1)S(1)}, u32[]{:S(2)}, u32[]{:S(2)}) collective-permute-start(bf16[24,512]{1,0:T(8,128)(2,1)} %param.17), channel_id=1, source_target_pairs={{0,1},{1,0},{2,3},{3,2},{4,5},{5,4},{6,7},{7,6},{8,9},{9,8},{10,11... | collective-permute-start | bytes 73736 | tf_op jit(solution)/shard_map/ppermute | solution.py:37
  1.9 1.4 copy-start.8
  7.1 19.2 %copy-start.5 = (bf16[1024,2,4]{0,2,1:T(4,128)(2,1)S(1)}, bf16[1024,2,4]{0,2,1:T(4,128)(2,1)}, u32[]{:S(2)}) copy-start(bf16[1024,2,4]{0,2,1:T(4,128)(2,1)} %param.22) | copy-start | bytes 49156
  7.2 19.2 %copy-start.1 = (f32[2,4,128,128]{3,2,1,0:T(8,128)S(1)}, f32[2,4,128,128]{3,2,1,0:T(8,128)}, u32[]{:S(2)}) copy-start(f32[2,4,128,128]{3,2,1,0:T(8,128)} %param.27) | copy-start | bytes 1572868
  18.2 33.9 %copy-start.4 = (f32[24,4]{0,1:T(4,128)S(1)}, f32[24,4]{0,1:T(4,128)}, u32[]{:S(2)}) copy-start(f32[24,4]{0,1:T(4,128)} %param.23) | copy-start | bytes 1156
  18.2 20.0 %all-to-all-start.2 = ((f32[16,6,5,128]{3,1,2,0:T(8,128)}), f32[16,6,5,128]{3,1,2,0:T(8,128)S(1)}, u32[]{:S(2)}, u32[]{:S(2)}) async-start(f32[16,6,5,128]{3,1,2,0:T(8,128)} %copy.153), calls=%async_computation.2 | async-start | bytes 655360 | tf_op jit(solution)/shard_map/all_to_all | solution.py:112
  26.3 26.9 %copy-start.6 = (s32[1024]{0:T(1024)}, s32[1024]{0:T(1024)S(1)}, u32[]{:S(2)}) copy-start(s32[1024]{0:T(1024)S(1)} %pad_clamp_fusion.2) | copy-start | bytes 12292
  40.0 11.6 %all-to-all-start.3 = ((f32[16,6,4,128]{3,2,1,0:T(4,128)}), f32[16,6,4,128]{3,2,1,0:T(4,128)S(1)}, u32[]{:S(2)}, u32[]{:S(2)}) async-start(f32[16,6,4,128]{3,2,1,0:T(4,128)} %bitcast.38), calls=%async_computation.3 | async-start | bytes 393216 | tf_op jit(solution)/shard_map/all_to_all | solution.py:112
  53.5 183.2 %copy-start.2 = (f32[2,4,128,128]{3,2,1,0:T(8,128)S(1)}, f32[2,4,128,128]{3,2,1,0:T(8,128)}, u32[]{:S(2)}) copy-start(f32[2,4,128,128]{3,2,1,0:T(8,128)} %param.28) | copy-start | bytes 1572868
  67.2 11.6 %all-to-all-start.1 = ((f32[16,6,4,128]{3,2,1,0:T(4,128)}), f32[16,6,4,128]{3,2,1,0:T(4,128)S(1)}, u32[]{:S(2)}, u32[]{:S(2)}) async-start(f32[16,6,4,128]{3,2,1,0:T(4,128)} %bitcast.191), calls=%async_computation.1 | async-start | bytes 393216 | tf_op jit(solution)/shard_map/while/body/eval_jaxpr/all_to_all | solution.py:112
  95.1 11.6 %all-to-all-start.1 = ((f32[16,6,4,128]{3,2,1,0:T(4,128)}), f32[16,6,4,128]{3,2,1,0:T(4,128)S(1)}, u32[]{:S(2)}, u32[]{:S(2)}) async-start(f32[16,6,4,128]{3,2,1,0:T(4,128)} %bitcast.191), calls=%async_computation.1 | async-start | bytes 393216 | tf_op jit(solution)/shard_map/while/body/eval_jaxpr/all_to_all | solution.py:112
  123.0 11.6 %all-to-all-start.1 = ((f32[16,6,4,128]{3,2,1,0:T(4,128)}), f32[16,6,4,128]{3,2,1,0:T(4,128)S(1)}, u32[]{:S(2)}, u32[]{:S(2)}) async-start(f32[16,6,4,128]{3,2,1,0:T(4,128)} %bitcast.191), calls=%async_computation.1 | async-start | bytes 393216 | tf_op jit(solution)/shard_map/while/body/eval_jaxpr/all_to_all | solution.py:112
  150.9 11.6 %all-to-all-start.1 = ((f32[16,6,4,128]{3,2,1,0:T(4,128)}), f32[16,6,4,128]{3,2,1,0:T(4,128)S(1)}, u32[]{:S(2)}, u32[]{:S(2)}) async-start(f32[16,6,4,128]{3,2,1,0:T(4,128)} %bitcast.191), calls=%async_computation.1 | async-start | bytes 393216 | tf_op jit(solution)/shard_map/while/body/eval_jaxpr/all_to_all | solution.py:112
  178.8 11.6 %all-to-all-start.1 = ((f32[16,6,4,128]{3,2,1,0:T(4,128)}), f32[16,6,4,128]{3,2,1,0:T(4,128)S(1)}, u32[]{:S(2)}, u32[]{:S(2)}) async-start(f32[16,6,4,128]{3,2,1,0:T(4,128)} %bitcast.191), calls=%async_computation.1 | async-start | bytes 393216 | tf_op jit(solution)/shard_map/while/body/eval_jaxpr/all_to_all | solution.py:112
  206.8 11.6 %all-to-all-start.1 = ((f32[16,6,4,128]{3,2,1,0:T(4,128)}), f32[16,6,4,128]{3,2,1,0:T(4,128)S(1)}, u32[]{:S(2)}, u32[]{:S(2)}) async-start(f32[16,6,4,128]{3,2,1,0:T(4,128)} %bitcast.191), calls=%async_computation.1 | async-start | bytes 393216 | tf_op jit(solution)/shard_map/while/body/eval_jaxpr/all_to_all | solution.py:112
  239.2 17.0 %all-to-all-start.5 = ((f32[16,6,12,128]{3,1,2,0:T(8,128)}), f32[16,6,12,128]{3,1,2,0:T(8,128)S(1)}, u32[]{:S(2)}, u32[]{:S(2)}) async-start(f32[16,6,12,128]{3,1,2,0:T(8,128)} %copy.169), calls=%async_computation.5 | async-start | bytes 1572864 | tf_op jit(solution)/shard_map/all_to_all | solution.py:112
  243.0 20.3 %copy-start.9 = (pred[24]{0:T(512)(128)(4,1)S(1)}, pred[24]{0:T(512)(128)(4,1)}, u32[]{:S(2)}) copy-start(pred[24]{0:T(512)(128)(4,1)} %copy-done.8) | copy-start | bytes 76
  262.0 1.3 collective-permute-start.1
